TPU v7x, 512 devices: a whole 4x8x8 slice. The times are simulated.
512 devices in a mesh: req: 64 (over x, y, core), tp: 8 (over z).
Axes of the slice: x: 4, y: 8, z: 8, core: 2. Of those that a mesh axis runs over, the one named last changes fastest.
Arguments:
- vit_context: bfloat16 [32768, 4096], P('req', 'tp'), may hold values from -6 to 6
- vision_residual: bfloat16 [32768, 4096], P('req', 'tp'), may hold values from -75 to 75
- out_weight: bfloat16 [4096, 4096], P('tp', 'req'), may hold values from -0.09375 to 0.09375
- layer_scale: float32 [4096], P('tp'), may hold values from 0.2 to 2
- prompt: bfloat16 [64, 256, 4096], P('req', None, 'tp'), may hold values from -75 to 75
- prompt_len: int32 [64], P('req'), may hold values from 128 to 256
- image_at: int32 [64], P('req'), may hold values from 0 to 128
- grid_sizes: int32 [128, 2], replicated, may hold values from 7 to 8, as said below
- image_owner: int32 [128], replicated, may hold values from 0 to 63, as said below
- norm_gain: float32 [4096], replicated, may hold values from 0.5 to 1.5
- qkv_weight: bfloat16 [4096, 6144], P('req', 'tp'), may hold values from -0.09375 to 0.09375
Outputs:
- qkv: bfloat16 [24576, 6144], P('req', 'tp')
Inputs may be any that keep to these rules, and one draw needn't show every extreme that they name: `image_owner`: each request owns exactly 2 images. `grid_sizes`: each side is 7 or 8; in every draw the images of some request are all 8 by 8, so that request has exactly 128 merged rows.
All inputs are finite; a program needn't handle non-finite values.
Results may differ from a plain program's by a relative error of at most 0.008.
Values may be sent and summed in bfloat16 or wider, within the bound.
No kernel may reach another device: no remote copies, remote signals or barrier semaphores. Data moves between devices by JAX's collectives and lax.ppermute only.
A program may use at most 64 MiB of HBM per device.

v0:
```python
import jax
import jax.numpy as jnp
from jax import lax
from jax.sharding import PartitionSpec as P

HEAD = 128
GROUP = 4
IMG_MAX = 128


def request_plan(grid_sizes, image_owner, requests):
    image_rows = grid_sizes[:, 0] * grid_sizes[:, 1]
    member = (image_owner[:, None] == jnp.arange(requests, dtype=jnp.int32)[None, :]).astype(
        jnp.int32
    )
    counts = jnp.sum(image_rows[:, None] * member, axis=0)
    starts = jnp.cumsum(counts) - counts
    return (counts, starts)


def rope_tables(count):
    half_size = HEAD // 2
    exponent = jnp.arange(half_size, dtype=jnp.float32) * (2.0 / HEAD)
    frequency = jnp.exp(-exponent * jnp.log(jnp.float32(500000.0)))
    angles = jnp.arange(count, dtype=jnp.float32)[:, None] * frequency[None, :]
    return (jnp.cos(angles), jnp.sin(angles))


def apply_rope(projected, cosine_table, sine_table):
    seq_rows = projected.shape[0]
    head_blocks = projected.reshape(seq_rows, -1, GROUP + 2, HEAD)
    turning = head_blocks[:, :, : GROUP + 1, :]
    first_half = turning[..., : HEAD // 2]
    second_half = turning[..., HEAD // 2 :]
    cosine_wide = cosine_table[:, None, None, :]
    sine_wide = sine_table[:, None, None, :]
    turned = jnp.concatenate(
        [
            first_half * cosine_wide - second_half * sine_wide,
            second_half * cosine_wide + first_half * sine_wide,
        ],
        axis=-1,
    )
    head_blocks = jnp.concatenate([turned, head_blocks[:, :, GROUP + 1 :, :]], axis=2)
    return head_blocks.reshape(seq_rows, -1)


def normalize(embedded, norm_gain):
    values = embedded.astype(jnp.float32)
    mean_square = jnp.mean(values * values, axis=-1, keepdims=True)
    return (values * lax.rsqrt(mean_square + 1e-05) * norm_gain[None, :]).astype(jnp.bfloat16)


def shards(
    vit_context,
    vision_residual,
    out_weight,
    layer_scale,
    prompt,
    prompt_len,
    image_at,
    grid_sizes,
    image_owner,
    norm_gain,
    qkv_weight,
):
    requests = lax.axis_size("req")
    device_index = lax.axis_index("req")
    feature_width = vit_context.shape[1]
    merged_context = jnp.mean(
        vit_context.astype(jnp.float32).reshape(-1, 4, feature_width), axis=1
    ).astype(jnp.bfloat16)
    merged_residual = jnp.mean(
        vision_residual.astype(jnp.float32).reshape(-1, 4, feature_width), axis=1
    )
    partial_value = jnp.dot(
        merged_context,
        lax.all_gather(out_weight, "req", axis=1, tiled=True),
        preferred_element_type=jnp.float32,
    )
    summed = lax.psum(partial_value.astype(jnp.bfloat16), "tp").astype(jnp.float32)
    own_share = lax.dynamic_slice_in_dim(
        summed, lax.axis_index("tp") * feature_width, feature_width, 1
    )
    merged = (merged_residual + layer_scale[None, :] * own_share).astype(jnp.bfloat16)
    merged_count = merged.shape[0]
    counts, starts = request_plan(grid_sizes, image_owner, requests)
    request_ends = starts + counts
    capacity = (IMG_MAX + requests - 1) // requests
    request_ids = jnp.arange(requests, dtype=jnp.int32)
    group_index = jnp.arange(merged_count, dtype=jnp.int32) * requests + device_index
    destination = jnp.sum((request_ends[None, :] <= group_index[:, None]).astype(jnp.int32), axis=1)
    owned_start = jnp.sum(
        jnp.where(destination[:, None] == request_ids[None, :], starts[None, :], 0), axis=1
    )
    target = destination * capacity + (group_index - owned_start) // requests
    usable = destination < requests
    send_slots = jnp.arange(requests * capacity, dtype=jnp.int32)
    placing = ((send_slots[:, None] == target[None, :]) & usable[None, :]).astype(jnp.bfloat16)
    outgoing = jnp.dot(placing, merged, preferred_element_type=jnp.float32).astype(jnp.bfloat16)
    arrived = lax.all_to_all(
        outgoing.reshape(requests, capacity, feature_width),
        "req",
        split_axis=0,
        concat_axis=0,
        tiled=True,
    )
    arrived = arrived.reshape(requests * capacity, feature_width)
    own_request = request_ids == device_index
    own_count = jnp.sum(jnp.where(own_request, counts, 0))
    own_start = jnp.sum(jnp.where(own_request, starts, 0))
    image_from = image_at[0]
    prompt_count = prompt_len[0]
    seq_slots = prompt.shape[1] + IMG_MAX
    slot_index = jnp.arange(seq_slots, dtype=jnp.int32)
    image_row = slot_index - image_from
    in_image = (image_row >= 0) & (image_row < own_count)
    is_live = slot_index < prompt_count + own_count
    from_prompt = is_live & jnp.logical_not(in_image)
    flat_index = (own_start + image_row) % requests * capacity + image_row // requests
    image_pick = ((flat_index[:, None] == send_slots[None, :]) & in_image[:, None]).astype(
        jnp.bfloat16
    )
    prompt_row = jnp.where(slot_index < image_from, slot_index, slot_index - own_count)
    prompt_ids = jnp.arange(prompt.shape[1], dtype=jnp.int32)
    prompt_pick = ((prompt_row[:, None] == prompt_ids[None, :]) & from_prompt[:, None]).astype(
        jnp.bfloat16
    )
    embedded = (
        jnp.dot(image_pick, arrived, preferred_element_type=jnp.float32)
        + jnp.dot(prompt_pick, prompt[0], preferred_element_type=jnp.float32)
    ).astype(jnp.bfloat16)
    gathered = lax.all_gather(embedded, "tp", axis=1, tiled=True)
    normed = normalize(gathered, norm_gain)
    projected = jnp.dot(
        normed,
        lax.all_gather(qkv_weight, "req", axis=0, tiled=True),
        preferred_element_type=jnp.float32,
    )
    cosine_table, sine_table = rope_tables(seq_slots)
    return apply_rope(projected, cosine_table, sine_table).astype(jnp.bfloat16)


def solution(mesh):
    in_specs = (
        P("req", "tp"),
        P("req", "tp"),
        P("tp", "req"),
        P("tp"),
        P("req", None, "tp"),
        P("req"),
        P("req"),
        P(),
        P(),
        P(),
        P("req", "tp"),
    )
    out_specs = P("req", "tp")
    return jax.shard_map(shards, mesh=mesh, in_specs=in_specs, out_specs=out_specs, check_vma=False)
```

profile of v0, /device:TPU:1, one launch (start us, length us, event | category | flops | bytes accessed | tf_op | source)
XLA Modules:
  0.0 352.9 jit_solution(7770393168710454331)
XLA Ops:
  6.5 0.7 all-gather.4.cloned.1.call-update
  7.3 1.4 reshape.205
  8.7 0.6 reduce_sum.78
  9.3 0.8 multiply_bitcast_fusion
  10.1 91.0 %all-gather.4.cloned.1.call-done = bf16[512,4096]{0,1:T(8,128)(2,1)} async-done(((bf16[512,64]{0,1:T(8,128)(2,1)}), bf16[512,4096]{0,1:T(8,128)(2,1)}) %all-gather.4.cloned.1.call-update) | async-done | bytes 4194320 | tf_op jit(solution)/shard_map/all_gather | solution.py:78
  101.1 4.6 %convolution_convert_fusion = bf16[128,4096]{1,0:T(8,128)(2,1)} fusion(bf16[512,4096]{0,1:T(8,128)(2,1)} %all-gather.4.cloned.1.call-done, f32[128,512]{1,0:T(8,128)S(1)} %reduce_sum.78), kind=kOutput, calls=%fused_computation.5 | convolution fusion | flops 537526272 | bytes 5505024 | tf_op jit(solution)/shard_map/dot_general | solution.py:76
  106.2 0.3 reshape.203
  106.5 0.6 reduce_sum.77
  107.3 0.7 fusion.38
  108.1 73.3 %all-reduce.2.cloned.1.call-done = bf16[128,4096]{1,0:T(8,128)(2,1)} async-done(((bf16[128,4096]{1,0:T(8,128)(2,1)}), bf16[128,4096]{1,0:T(8,128)(2,1)}) %all-reduce.2.cloned.1.call-update) | async-done | bytes 1048592 | tf_op jit(solution)/shard_map/psum | solution.py:81
  181.4 1.1 convolution_convert_fusion.1
  182.5 0.7 reshape.199
  183.3 14.2 %all-to-all-start = ((bf16[64,2,512]{2,1,0:T(2,128)(2,1)}), bf16[64,2,512]{2,1,0:T(2,128)(2,1)S(1)}, u32[]{:S(2)}, u32[]{:S(2)}) async-start(bf16[64,2,512]{2,1,0:T(2,128)(2,1)} %reshape.199), calls=%async_computation | async-start | bytes 262144 | tf_op jit(solution)/shard_map/all_to_all | solution.py:101
  199.3 0.6 fusion.37
  199.9 1.3 fusion.30
  201.2 6.6 %all-to-all-done = bf16[64,2,512]{2,1,0:T(2,128)(2,1)S(1)} async-done(((bf16[64,2,512]{2,1,0:T(2,128)(2,1)}), bf16[64,2,512]{2,1,0:T(2,128)(2,1)S(1)}, u32[]{:S(2)}, u32[]{:S(2)}) %all-to-all-start) | async-done | bytes 131104 | tf_op jit(solution)/shard_map/all_to_all | solution.py:101
  208.2 1.1 fusion.7
  209.3 0.5 all-gather.8.cloned.1.call-update
  209.9 0.4 fusion.21
  210.3 40.0 %all-gather.6.cloned.1.call-done = bf16[384,4096]{1,0:T(8,128)(2,1)} async-done(((bf16[384,512]{1,0:T(8,128)(2,1)}), bf16[384,4096]{1,0:T(8,128)(2,1)}) %all-gather.6.cloned.1.call-update) | async-done | bytes 3145744 | tf_op jit(solution)/shard_map/all_gather | solution.py:133
  250.3 2.6 fusion
  252.9 85.4 %all-gather.8.cloned.1.call-done = bf16[4096,768]{1,0:T(8,128)(2,1)} async-done(((bf16[64,768]{1,0:T(8,128)(2,1)}), bf16[4096,768]{1,0:T(8,128)(2,1)}) %all-gather.8.cloned.1.call-update) | async-done | bytes 6291472 | tf_op jit(solution)/shard_map/all_gather | solution.py:137
  338.3 6.7 %fusion.3 = f32[384,768]{0,1:T(8,128)S(1)} fusion(bf16[4096,768]{1,0:T(8,128)(2,1)} %all-gather.8.cloned.1.call-done, bf16[384,4096]{1,0:T(8,128)(2,1)} %all-gather.6.cloned.1.call-done, f32[4096]{0:T(1024)S(1)} %copy-done.3, f32[384]{0:T(512)S(1)} %add_rsqrt_fusion), kind=kOutput, calls=%fused_computation.6 | convolution fusion | flops 2422210560 | bytes 10634752 | tf_op jit(solution)/shard_map/dot_general | solution.py:135
  345.2 1.1 copy.18
  (32 shorter events, 1.4 us)
Async XLA Ops:
  6.5 201.7 %copy-start = (bf16[1,256,512]{2,1,0:T(8,128)(2,1)S(1)}, bf16[1,256,512]{2,1,0:T(8,128)(2,1)}, u32[]{:S(2)}) copy-start(bf16[1,256,512]{2,1,0:T(8,128)(2,1)} %param.15) | copy-start | bytes 786436
  6.5 94.5 %all-gather.4.cloned.1.call-start = ((), (), s32[]{:S(2)}) async-start(), calls=%async_computation.1 | async-start | bytes 4259840 | tf_op jit(solution)/shard_map/all_gather | solution.py:78
  7.3 174.2 %all-reduce.2.cloned.1.call-start = ((), (), s32[]{:S(2)}) async-start(), calls=%async_computation.2 | async-start | bytes 2097152 | tf_op jit(solution)/shard_map/psum | solution.py:81
  8.7 97.0 %copy-start.4 = (s32[128]{0:T(128)S(1)}, s32[128]{0:T(128)}, u32[]{:S(2)}) copy-start(s32[128]{0:T(128)} %param.19) | copy-start | bytes 1540
  8.7 97.5 %copy-start.1 = (bf16[512,512]{1,0:T(8,128)(2,1)S(1)}, bf16[512,512]{1,0:T(8,128)(2,1)}, u32[]{:S(2)}) copy-start(bf16[512,512]{1,0:T(8,128)(2,1)} %param.12) | copy-start | bytes 1572868
  10.1 171.3 %copy-start.2 = (f32[512]{0:T(512)S(1)}, f32[512]{0:T(512)}, u32[]{:S(2)}) copy-start(f32[512]{0:T(512)} %param.14) | copy-start | bytes 6148
  106.5 231.8 %copy-start.3 = (f32[4096]{0:T(1024)S(1)}, f32[4096]{0:T(1024)}, u32[]{:S(2)}) copy-start(f32[4096]{0:T(1024)} %param.20) | copy-start | bytes 49156
  183.3 24.5 %all-to-all-start = ((bf16[64,2,512]{2,1,0:T(2,128)(2,1)}), bf16[64,2,512]{2,1,0:T(2,128)(2,1)S(1)}, u32[]{:S(2)}, u32[]{:S(2)}) async-start(bf16[64,2,512]{2,1,0:T(2,128)(2,1)} %reshape.199), calls=%async_computation | async-start | bytes 262144 | tf_op jit(solution)/shard_map/all_to_all | solution.py:101
  197.4 52.9 %all-gather.6.cloned.1.call-start = ((), (), s32[]{:S(2)}) async-start(), calls=%async_computation.3 | async-start | bytes 3538944 | tf_op jit(solution)/shard_map/all_gather | solution.py:133
  209.3 129.0 %all-gather.8.cloned.1.call-start = ((), (), s32[]{:S(2)}) async-start(), calls=%async_computation.4 | async-start | bytes 6389760 | tf_op jit(solution)/shard_map/all_gather | solution.py:137
Sparse Core Ops, SparseCore 0:
  10.7 90.2 all-gather.3
  105.8 75.5 all-reduce.1
  209.4 40.8 all-gather.5
  253.5 84.7 all-gather.7
where the time goes:
time: 353 us
  waiting for transfers between devices  298 us (84%)
  between operations  15.2 us (4%)
  starting transfers between devices  14.3 us (4%)
  matrix products  13.8 us (4%)
  other arithmetic  8.27 us (2%)
  local copies, waits for them, and re-layouts  3.69 us (1%)
    all_gather x1, waiting for transfers between devices, shards(): lax.all_gather(out_weight, 'req', axis=1, tiled=True)  91 us
    all_gather x1, waiting for transfers between devices, shards(): lax.all_gather(qkv_weight, 'req', axis=0, tiled=True)  85.4 us
    psum x1, waiting for transfers between devices, shards(): lax.psum(partial_value.astype(jnp.bfloat16), 'tp').astype(jnp.float32)  73.3 us
    all_gather x1, waiting for transfers between devices, shards(): gathered = lax.all_gather(embedded, 'tp', axis=1, tiled=True)  40 us
    all_to_all x1, starting transfers between devices, shards(): lax.all_to_all(outgoing.reshape(requests, capacity, feature_width), 'req'...  14.2 us
  transfers between devices with their start and end apart: 5, of which 5 were waited for; matrix products, arithmetic and copies ran while one was open for 3% of the time, Pallas kernels for 0%

commit v1 on v0

--- a/solution.py
+++ b/solution.py
@@ -78,9 +78,12 @@
         lax.all_gather(out_weight, "req", axis=1, tiled=True),
         preferred_element_type=jnp.float32,
     )
-    summed = lax.psum(partial_value.astype(jnp.bfloat16), "tp").astype(jnp.float32)
-    own_share = lax.dynamic_slice_in_dim(
-        summed, lax.axis_index("tp") * feature_width, feature_width, 1
+    tp_count = lax.axis_size("tp")
+    block_terms = partial_value.astype(jnp.bfloat16).reshape(
+        -1, tp_count, feature_width
+    ).transpose(1, 0, 2)
+    own_share = jnp.sum(
+        lax.all_to_all(block_terms, "tp", 0, 0, tiled=True).astype(jnp.float32), axis=0
     )
     merged = (merged_residual + layer_scale[None, :] * own_share).astype(jnp.bfloat16)
     merged_count = merged.shape[0]
@@ -130,13 +133,11 @@
         jnp.dot(image_pick, arrived, preferred_element_type=jnp.float32)
         + jnp.dot(prompt_pick, prompt[0], preferred_element_type=jnp.float32)
     ).astype(jnp.bfloat16)
+    full_weight = lax.all_gather(qkv_weight, "req", axis=0, tiled=True)
+    embedded, full_weight = lax.optimization_barrier((embedded, full_weight))
     gathered = lax.all_gather(embedded, "tp", axis=1, tiled=True)
     normed = normalize(gathered, norm_gain)
-    projected = jnp.dot(
-        normed,
-        lax.all_gather(qkv_weight, "req", axis=0, tiled=True),
-        preferred_element_type=jnp.float32,
-    )
+    projected = jnp.dot(normed, full_weight, preferred_element_type=jnp.float32)
     cosine_table, sine_table = rope_tables(seq_slots)
     return apply_rope(projected, cosine_table, sine_table).astype(jnp.bfloat16)
 

time: 353 us -> 252 us (0.71)
  waiting for transfers between devices: 298 us -> 199 us
    psum x1 -> x0, waiting for transfers between devices: 73.3 us -> none  [shards(): lax.psum(partial_value.astype(jnp.bfloat16), 'tp').astype(jnp.float32)]
    all_gather x1, waiting for transfers between devices: 85.4 us -> 26.6 us  [shards(): full_weight = lax.all_gather(qkv_weight, 'req', axis=0, tiled=True)]
    all_to_all x0 -> x1, waiting for transfers between devices: none -> 25 us  [shards(): lax.all_to_all(block_terms, 'tp', 0, 0, tiled=True).astype(jnp.float32)]
    all_to_all x1, starting transfers between devices: 14.2 us -> 6.44 us  [shards(): lax.all_to_all(outgoing.reshape(requests, capacity, feature_width), 'req'...]
    all_to_all x0 -> x1, starting transfers between devices: none -> 7.23 us  [shards(): lax.all_to_all(block_terms, 'tp', 0, 0, tiled=True).astype(jnp.float32)]
    all_gather x1, waiting for transfers between devices: 40 us -> 46.6 us  [shards(): gathered = lax.all_gather(embedded, 'tp', axis=1, tiled=True)]
  transfers between devices with their start and end apart: 5 -> 5, of which waited for: 5 -> 5; matrix products, arithmetic and copies ran while one was open for 3% -> 5% of each run, Pallas kernels for 0% -> 0%
where the time goes in v1:
time: 252 us
  waiting for transfers between devices  199 us (79%)
  between operations  15.2 us (6%)
  starting transfers between devices  13.8 us (5%)
  matrix products  11 us (4%)
  other arithmetic  7.76 us (3%)
  local copies, waits for them, and re-layouts  4.89 us (2%)
    all_gather x1, waiting for transfers between devices, shards(): lax.all_gather(out_weight, 'req', axis=1, tiled=True)  91 us
    all_gather x1, waiting for transfers between devices, shards(): gathered = lax.all_gather(embedded, 'tp', axis=1, tiled=True)  46.6 us
    all_gather x1, waiting for transfers between devices, shards(): full_weight = lax.all_gather(qkv_weight, 'req', axis=0, tiled=True)  26.6 us
    all_to_all x1, waiting for transfers between devices, shards(): lax.all_to_all(block_terms, 'tp', 0, 0, tiled=True).astype(jnp.float32)  25 us
    all_to_all x1, waiting for transfers between devices, shards(): lax.all_to_all(outgoing.reshape(requests, capacity, feature_width), 'req'...  8.47 us
    all_to_all x1, starting transfers between devices, shards(): lax.all_to_all(block_terms, 'tp', 0, 0, tiled=True).astype(jnp.float32)  7.23 us
    all_to_all x1, starting transfers between devices, shards(): lax.all_to_all(outgoing.reshape(requests, capacity, feature_width), 'req'...  6.44 us
    dot_general x1, matrix products, shards(): projected = jnp.dot(normed, full_weight, preferred_element_type=jnp.float32)  5.75 us
  transfers between devices with their start and end apart: 5, of which 5 were waited for; matrix products, arithmetic and copies ran while one was open for 5% of the time, Pallas kernels for 0%

profile of v1, /device:TPU:1, one launch (start us, length us, event | category | flops | bytes accessed | tf_op | source)
XLA Modules:
  0.0 251.8 jit_solution(14725650613513382910)
XLA Ops:
  6.5 0.7 all-gather.4.cloned.1.call-update
  7.3 0.7 all-gather.6.cloned.1.call-update
  8.0 1.4 reshape.209
  9.4 0.6 reduce_sum.87
  10.0 91.0 %all-gather.4.cloned.1.call-done = bf16[512,4096]{0,1:T(8,128)(2,1)} async-done(((bf16[512,64]{0,1:T(8,128)(2,1)}), bf16[512,4096]{0,1:T(8,128)(2,1)}) %all-gather.4.cloned.1.call-update) | async-done | bytes 4194320 | tf_op jit(solution)/shard_map/all_gather | solution.py:78
  101.0 3.7 %convolution_convert_fusion = bf16[128,4096]{1,0:T(8,128)(2,1)S(1)} fusion(bf16[512,4096]{0,1:T(8,128)(2,1)} %all-gather.4.cloned.1.call-done, f32[128,512]{1,0:T(8,128)S(1)} %reduce_sum.87), kind=kOutput, calls=%fused_computation.5 | convolution fusion | flops 537526272 | bytes 5505024 | tf_op jit(solution)/shard_map/dot_general | solution.py:76
  104.7 1.1 copy.27
  105.8 7.2 %all-to-all-start = ((bf16[8,128,512]{2,1,0:T(8,128)(2,1)}), bf16[8,128,512]{2,1,0:T(8,128)(2,1)S(1)}, u32[]{:S(2)}, u32[]{:S(2)}) async-start(bf16[8,128,512]{2,1,0:T(8,128)(2,1)} %bitcast.19), calls=%async_computation | async-start | bytes 2097152 | tf_op jit(solution)/shard_map/all_to_all | solution.py:86
  113.9 0.6 reduce_sum.86
  115.8 0.7 fusion.37
  117.3 25.0 %all-to-all-done = bf16[8,128,512]{2,1,0:T(8,128)(2,1)S(1)} async-done(((bf16[8,128,512]{2,1,0:T(8,128)(2,1)}), bf16[8,128,512]{2,1,0:T(8,128)(2,1)S(1)}, u32[]{:S(2)}, u32[]{:S(2)}) %all-to-all-start) | async-done | bytes 1048608 | tf_op jit(solution)/shard_map/all_to_all | solution.py:86
  142.7 0.7 reshape.203
  143.4 6.4 %all-to-all-start.1 = ((bf16[64,2,512]{2,1,0:T(2,128)(2,1)}), bf16[64,2,512]{2,1,0:T(2,128)(2,1)S(1)}, u32[]{:S(2)}, u32[]{:S(2)}) async-start(bf16[64,2,512]{2,1,0:T(2,128)(2,1)} %reshape.203), calls=%async_computation.1 | async-start | bytes 262144 | tf_op jit(solution)/shard_map/all_to_all | solution.py:104
  149.9 0.6 fusion.36
  150.5 0.6 subtract_select_fusion
  151.1 0.6 fusion.29
  151.7 8.5 %all-to-all-done.1 = bf16[64,2,512]{2,1,0:T(2,128)(2,1)S(1)} async-done(((bf16[64,2,512]{2,1,0:T(2,128)(2,1)}), bf16[64,2,512]{2,1,0:T(2,128)(2,1)S(1)}, u32[]{:S(2)}, u32[]{:S(2)}) %all-to-all-start.1) | async-done | bytes 131104 | tf_op jit(solution)/shard_map/all_to_all | solution.py:104
  160.6 1.1 fusion.7
  161.6 26.6 %all-gather.6.cloned.1.call-done = bf16[4096,768]{1,0:T(8,128)(2,1)} async-done(((bf16[64,768]{1,0:T(8,128)(2,1)}), bf16[4096,768]{1,0:T(8,128)(2,1)}) %all-gather.6.cloned.1.call-update) | async-done | bytes 6291472 | tf_op jit(solution)/shard_map/all_gather | solution.py:136
  188.3 0.4 fusion.20
  188.7 46.6 %all-gather.8.cloned.1.call-done = bf16[384,4096]{1,0:T(8,128)(2,1)} async-done(((bf16[384,512]{1,0:T(8,128)(2,1)}), bf16[384,4096]{1,0:T(8,128)(2,1)}) %all-gather.8.cloned.1.call-update) | async-done | bytes 3145744 | tf_op jit(solution)/shard_map/all_gather | solution.py:138
  235.3 2.7 %fusion = f32[384]{0:T(512)S(1)} fusion(bf16[384,4096]{1,0:T(8,128)(2,1)} %all-gather.8.cloned.1.call-done), kind=kLoop, calls=%fused_computation.2 | loop fusion | flops 4718208 | bytes 3147264 | tf_op jit(solution)/shard_map/reduce_sum | solution.py:50
  238.2 5.8 %fusion.3 = f32[384,768]{0,1:T(8,128)S(1)} fusion(bf16[4096,768]{1,0:T(8,128)(2,1)} %all-gather.6.cloned.1.call-done, bf16[384,4096]{1,0:T(8,128)(2,1)S(1)} %copy-done.1, f32[4096]{0:T(1024)S(1)} %copy-done.4, f32[384]{0:T(512)S(1)} %add_rsqrt_fusion), kind=kOutput, calls=%fused_computation.6 | convolution fusion | flops 2422210560 | bytes 10634752 | tf_op jit(solution)/shard_map/dot_general | solution.py:140
  244.2 1.1 copy.23
  (38 shorter events, 2.1 us)
Async XLA Ops:
  6.5 154.0 %copy-start = (bf16[1,256,512]{2,1,0:T(8,128)(2,1)S(1)}, bf16[1,256,512]{2,1,0:T(8,128)(2,1)}, u32[]{:S(2)}) copy-start(bf16[1,256,512]{2,1,0:T(8,128)(2,1)} %param.15) | copy-start | bytes 786436
  6.5 94.5 %all-gather.4.cloned.1.call-start = ((), (), s32[]{:S(2)}) async-start(), calls=%async_computation.2 | async-start | bytes 4259840 | tf_op jit(solution)/shard_map/all_gather | solution.py:78
  7.3 181.0 %all-gather.6.cloned.1.call-start = ((), (), s32[]{:S(2)}) async-start(), calls=%async_computation.3 | async-start | bytes 6389760 | tf_op jit(solution)/shard_map/all_gather | solution.py:136
  104.7 8.4 %copy-start.5 = (s32[128,2]{0,1:T(2,128)S(1)}, s32[128,2]{0,1:T(2,128)}, u32[]{:S(2)}) copy-start(s32[128,2]{0,1:T(2,128)} %param.18) | copy-start | bytes 3076
  104.7 8.4 %copy-start.6 = (s32[128]{0:T(128)S(1)}, s32[128]{0:T(128)}, u32[]{:S(2)}) copy-start(s32[128]{0:T(128)} %param.19) | copy-start | bytes 1540
  104.7 8.8 %copy-start.2 = (bf16[512,512]{1,0:T(8,128)(2,1)S(1)}, bf16[512,512]{1,0:T(8,128)(2,1)}, u32[]{:S(2)}) copy-start(bf16[512,512]{1,0:T(8,128)(2,1)} %param.12) | copy-start | bytes 1572868
  105.8 36.6 %copy-start.3 = (f32[512]{0:T(512)S(1)}, f32[512]{0:T(512)}, u32[]{:S(2)}) copy-start(f32[512]{0:T(512)} %param.14) | copy-start | bytes 6148
  105.8 36.5 %all-to-all-start = ((bf16[8,128,512]{2,1,0:T(8,128)(2,1)}), bf16[8,128,512]{2,1,0:T(8,128)(2,1)S(1)}, u32[]{:S(2)}, u32[]{:S(2)}) async-start(bf16[8,128,512]{2,1,0:T(8,128)(2,1)} %bitcast.19), calls=%async_computation | async-start | bytes 2097152 | tf_op jit(solution)/shard_map/all_to_all | solution.py:86
  143.4 16.8 %all-to-all-start.1 = ((bf16[64,2,512]{2,1,0:T(2,128)(2,1)}), bf16[64,2,512]{2,1,0:T(2,128)(2,1)S(1)}, u32[]{:S(2)}, u32[]{:S(2)}) async-start(bf16[64,2,512]{2,1,0:T(2,128)(2,1)} %reshape.203), calls=%async_computation.1 | async-start | bytes 262144 | tf_op jit(solution)/shard_map/all_to_all | solution.py:104
  149.8 85.5 %all-gather.8.cloned.1.call-start = ((), (), s32[]{:S(2)}) async-start(), calls=%async_computation.4 | async-start | bytes 3538944 | tf_op jit(solution)/shard_map/all_gather | solution.py:138
  151.7 86.4 %copy-start.4 = (f32[4096]{0:T(1024)S(1)}, f32[4096]{0:T(1024)}, u32[]{:S(2)}) copy-start(f32[4096]{0:T(1024)} %param.20) | copy-start | bytes 49156
  235.3 2.8 %copy-start.1 = (bf16[384,4096]{1,0:T(8,128)(2,1)S(1)}, bf16[384,4096]{1,0:T(8,128)(2,1)}, u32[]{:S(2)}) copy-start(bf16[384,4096]{1,0:T(8,128)(2,1)} %all-gather.8.cloned.1.call-done) | copy-start | bytes 9437188
Sparse Core Ops, SparseCore 0:
  10.7 90.2 all-gather.3
  104.3 83.8 all-gather.5
  190.4 44.9 all-gather.7

commit v2 on v1

--- a/solution.py
+++ b/solution.py
@@ -51,6 +51,12 @@
     return (values * lax.rsqrt(mean_square + 1e-05) * norm_gain[None, :]).astype(jnp.bfloat16)
 
 
+def gather_features(rows, tp_count):
+    copies = jnp.broadcast_to(rows[None], (tp_count,) + rows.shape)
+    blocks = lax.all_to_all(copies, "tp", 0, 0, tiled=True)
+    return blocks.transpose(1, 0, 2).reshape(rows.shape[0], -1)
+
+
 def shards(
     vit_context,
     vision_residual,
@@ -73,6 +79,8 @@
     merged_residual = jnp.mean(
         vision_residual.astype(jnp.float32).reshape(-1, 4, feature_width), axis=1
     )
+    full_prompt = gather_features(prompt[0], lax.axis_size("tp"))
+    full_prompt, merged_context = lax.optimization_barrier((full_prompt, merged_context))
     partial_value = jnp.dot(
         merged_context,
         lax.all_gather(out_weight, "req", axis=1, tiled=True),
@@ -129,14 +137,13 @@
     prompt_pick = ((prompt_row[:, None] == prompt_ids[None, :]) & from_prompt[:, None]).astype(
         jnp.bfloat16
     )
+    full_image = gather_features(arrived, tp_count)
     embedded = (
-        jnp.dot(image_pick, arrived, preferred_element_type=jnp.float32)
-        + jnp.dot(prompt_pick, prompt[0], preferred_element_type=jnp.float32)
+        jnp.dot(image_pick, full_image, preferred_element_type=jnp.float32)
+        + jnp.dot(prompt_pick, full_prompt, preferred_element_type=jnp.float32)
     ).astype(jnp.bfloat16)
     full_weight = lax.all_gather(qkv_weight, "req", axis=0, tiled=True)
-    embedded, full_weight = lax.optimization_barrier((embedded, full_weight))
-    gathered = lax.all_gather(embedded, "tp", axis=1, tiled=True)
-    normed = normalize(gathered, norm_gain)
+    normed = normalize(embedded, norm_gain)
     projected = jnp.dot(normed, full_weight, preferred_element_type=jnp.float32)
     cosine_table, sine_table = rope_tables(seq_slots)
     return apply_rope(projected, cosine_table, sine_table).astype(jnp.bfloat16)

time: 252 us -> 213 us (0.85)
  waiting for transfers between devices: 199 us -> 127 us
  blocking collectives: 0 us -> 16.6 us
  starting transfers between devices: 13.8 us -> 21.7 us
  local copies, waits for them, and re-layouts: 4.89 us -> 9.92 us
  matrix products: 11 us -> 14.5 us
    all_to_all x1 -> x2, waiting for transfers between devices: 8.47 us -> 71.1 us  [gather_features(): blocks = lax.all_to_all(copies, 'tp', 0, 0, tiled=True)]
    all_gather x1, waiting for transfers between devices: 91 us -> 31.2 us  [shards(): lax.all_gather(out_weight, 'req', axis=1, tiled=True)]
    all_gather x1 -> x0, waiting for transfers between devices: 46.6 us -> none  [shards(): gathered = lax.all_gather(embedded, 'tp', axis=1, tiled=True)]
    all_gather x1, waiting for transfers between devices: 26.6 us -> 0.01 us  [shards(): full_weight = lax.all_gather(qkv_weight, 'req', axis=0, tiled=True)]
    all_to_all x0 -> x1, blocking collectives: none -> 16.6 us  [shards(): lax.all_to_all(outgoing.reshape(requests, capacity, feature_width), 'req'...]
    all_to_all x1 -> x2, starting transfers between devices: 6.44 us -> 14.4 us  [gather_features(): blocks = lax.all_to_all(copies, 'tp', 0, 0, tiled=True)]
    broadcast_in_dim x0 -> x5, local copies, waits for them, and re-layouts: none -> 3.83 us  [gather_features(): copies = jnp.broadcast_to(rows[None], (tp_count,) + rows.shape)]
    reduce_sum x1 -> x0, other arithmetic: 2.73 us -> none  [normalize(): mean_square = jnp.mean(values * values, axis=-1, keepdims=True)]
  transfers between devices with their start and end apart: 5 -> 5, of which waited for: 5 -> 4; matrix products, arithmetic and copies ran while one was open for 5% -> 11% of each run, Pallas kernels for 0% -> 0%
where the time goes in v2:
time: 213 us; the launch traced here: 212 us
  waiting for transfers between devices  127 us (60%)
  starting transfers between devices  21.7 us (10%)
  blocking collectives  16.6 us (8%)
  between operations  15.6 us (7%)
  matrix products  14.5 us (7%)
  local copies, waits for them, and re-layouts  9.92 us (5%)
  other arithmetic  6.58 us (3%)
    all_to_all x2, waiting for transfers between devices, gather_features(): blocks = lax.all_to_all(copies, 'tp', 0, 0, tiled=True)  71.1 us
    all_gather x1, waiting for transfers between devices, shards(): lax.all_gather(out_weight, 'req', axis=1, tiled=True)  31.2 us
    all_to_all x1, waiting for transfers between devices, shards(): lax.all_to_all(block_terms, 'tp', 0, 0, tiled=True).astype(jnp.float32)  23.6 us
    all_to_all x1, blocking collectives, shards(): lax.all_to_all(outgoing.reshape(requests, capacity, feature_width), 'req'...  16.6 us
    all_to_all x2, starting transfers between devices, gather_features(): blocks = lax.all_to_all(copies, 'tp', 0, 0, tiled=True)  14.4 us
    all_to_all x1, starting transfers between devices, shards(): lax.all_to_all(block_terms, 'tp', 0, 0, tiled=True).astype(jnp.float32)  7.24 us
    dot_general x1, matrix products, shards(): projected = jnp.dot(normed, full_weight, preferred_element_type=jnp.float32)  6.71 us
  transfers between devices with their start and end apart: 5, of which 4 were waited for; matrix products, arithmetic and copies ran while one was open for 11% of the time, Pallas kernels for 0%

profile of v2, /device:TPU:1, one launch (start us, length us, event | category | flops | bytes accessed | tf_op | source)
XLA Modules:
  0.0 212.2 jit_solution(16004944551827687252)
XLA Ops:
  6.5 0.7 all-gather.3.cloned.1.call-update
  8.0 1.1 copy.25
  9.1 1.4 broadcast_in_dim.26
  10.5 10.9 %all-to-all-start = ((bf16[8,256,512]{1,2,0:T(8,128)(2,1)}), bf16[8,256,512]{1,2,0:T(8,128)(2,1)S(1)}, u32[]{:S(2)}, u32[]{:S(2)}) async-start(bf16[8,256,512]{1,2,0:T(8,128)(2,1)} %broadcast_in_dim.26), calls=%async_computation | async-start | bytes 4194304 | tf_op jit(solution)/shard_map/all_to_all | solution.py:56
  21.4 1.4 reshape.214
  23.4 46.4 %all-to-all-done = bf16[8,256,512]{1,2,0:T(8,128)(2,1)S(1)} async-done(((bf16[8,256,512]{1,2,0:T(8,128)(2,1)}), bf16[8,256,512]{1,2,0:T(8,128)(2,1)S(1)}, u32[]{:S(2)}, u32[]{:S(2)}) %all-to-all-start) | async-done | bytes 2097184 | tf_op jit(solution)/shard_map/all_to_all | solution.py:56
  69.8 31.2 %all-gather.3.cloned.1.call-done = bf16[512,4096]{0,1:T(8,128)(2,1)} async-done(((bf16[512,64]{0,1:T(8,128)(2,1)}), bf16[512,4096]{0,1:T(8,128)(2,1)}) %all-gather.3.cloned.1.call-update) | async-done | bytes 4194320 | tf_op jit(solution)/shard_map/all_gather | solution.py:86
  101.0 3.7 %convolution_convert_fusion = bf16[128,4096]{1,0:T(8,128)(2,1)S(1)} fusion(bf16[128,512]{1,0:T(8,128)(2,1)S(1)} %multiply_convert_fusion, bf16[512,4096]{0,1:T(8,128)(2,1)} %all-gather.3.cloned.1.call-done), kind=kOutput, calls=%fused_computation.6 | convolution fusion | flops 537395200 | bytes 5373952 | tf_op jit(solution)/shard_map/dot_general | solution.py:84
  104.7 1.1 copy.33
  105.8 7.2 %all-to-all-start.1 = ((bf16[8,128,512]{2,1,0:T(8,128)(2,1)}), bf16[8,128,512]{2,1,0:T(8,128)(2,1)S(1)}, u32[]{:S(2)}, u32[]{:S(2)}) async-start(bf16[8,128,512]{2,1,0:T(8,128)(2,1)} %bitcast.31), calls=%async_computation.1 | async-start | bytes 2097152 | tf_op jit(solution)/shard_map/all_to_all | solution.py:94
  113.5 2.4 %reshape.212 = f32[128,4,512]{2,1,0:T(4,128)} reshape(bf16[512,512]{1,0:T(8,128)(2,1)} %param.12) | data formatting | bytes 1572864 | tf_op jit(solution)/shard_map/reshape | solution.py:80
  115.9 1.9 reduce_sum.86
  117.8 0.7 fusion.34
  118.7 23.6 %all-to-all-done.1 = bf16[8,128,512]{2,1,0:T(8,128)(2,1)S(1)} async-done(((bf16[8,128,512]{2,1,0:T(8,128)(2,1)}), bf16[8,128,512]{2,1,0:T(8,128)(2,1)S(1)}, u32[]{:S(2)}, u32[]{:S(2)}) %all-to-all-start.1) | async-done | bytes 1048608 | tf_op jit(solution)/shard_map/all_to_all | solution.py:94
  142.7 16.6 %all_to_all.20 = bf16[64,2,512]{2,1,0:T(2,128)(2,1)S(1)} all-to-all(bf16[64,2,512]{2,1,0:T(2,128)(2,1)S(1)} %reshape.208), channel_id=1, replica_groups=mesh['req'=64,'tp'=8] {'req'}, dimensions={0} | all-to-all | bytes 262144 | tf_op jit(solution)/shard_map/all_to_all | solution.py:112
  159.5 1.1 broadcast_in_dim.28
  160.6 3.6 %all-to-all-start.3 = ((bf16[8,128,512]{1,2,0:T(8,128)(2,1)}), bf16[8,128,512]{1,2,0:T(8,128)(2,1)S(1)}, u32[]{:S(2)}, u32[]{:S(2)}) async-start(bf16[8,128,512]{1,2,0:T(8,128)(2,1)} %broadcast_in_dim.28), calls=%async_computation.3 | async-start | bytes 2097152 | tf_op jit(solution)/shard_map/all_to_all | solution.py:56
  166.2 0.7 fusion.33
  166.9 1.4 fusion.26
  168.7 24.7 %all-to-all-done.3 = bf16[8,128,512]{1,2,0:T(8,128)(2,1)S(1)} async-done(((bf16[8,128,512]{1,2,0:T(8,128)(2,1)}), bf16[8,128,512]{1,2,0:T(8,128)(2,1)S(1)}, u32[]{:S(2)}, u32[]{:S(2)}) %all-to-all-start.3) | async-done | bytes 1048608 | tf_op jit(solution)/shard_map/all_to_all | solution.py:56
  193.4 1.0 fusion.12
  194.5 2.9 %fusion = (f32[384]{0:T(512)S(1)}, bf16[384,4096]{1,0:T(8,128)(2,1)}) fusion(f32[384,4096]{1,0:T(8,128)S(1)} %fusion.12, bf16[256,4096]{0,1:T(8,128)(2,1)S(1)} %bitcast.29, s32[384]{0:T(512)S(1)} %get-tuple-element.21, pred[384]{0:T(512)(128)(4,1)S(1)} %get-tuple-element.9), kind=kOutput, calls=%fused_computation.2 | convolution fusion | flops 813366912 | bytes 11537792 | tf_op jit(solution)/shard_map/dot_general | solution.py:143
  197.4 6.7 %fusion.3 = f32[384,768]{0,1:T(8,128)S(1)} fusion(bf16[4096,768]{1,0:T(8,128)(2,1)} %all-gather.5.cloned.1.call-done, bf16[384,4096]{1,0:T(8,128)(2,1)} %get-tuple-element.19, f32[4096]{0:T(1024)S(1)} %copy-done.1, f32[384]{0:T(512)S(1)} %add_rsqrt_fusion), kind=kOutput, calls=%fused_computation.7 | convolution fusion | flops 2422210560 | bytes 10634752 | tf_op jit(solution)/shard_map/dot_general | solution.py:147
  204.3 1.1 copy.29
  (35 shorter events, 3.2 us)
Async XLA Ops:
  6.5 94.5 %all-gather.3.cloned.1.call-start = ((), (), s32[]{:S(2)}) async-start(), calls=%async_computation.4 | async-start | bytes 4259840 | tf_op jit(solution)/shard_map/all_gather | solution.py:86
  7.3 190.1 %all-gather.5.cloned.1.call-start = ((), (), s32[]{:S(2)}) async-start(), calls=%async_computation.5 | async-start | bytes 6389760 | tf_op jit(solution)/shard_map/all_gather | solution.py:145
  10.5 59.3 %all-to-all-start = ((bf16[8,256,512]{1,2,0:T(8,128)(2,1)}), bf16[8,256,512]{1,2,0:T(8,128)(2,1)S(1)}, u32[]{:S(2)}, u32[]{:S(2)}) async-start(bf16[8,256,512]{1,2,0:T(8,128)(2,1)} %broadcast_in_dim.26), calls=%async_computation | async-start | bytes 4194304 | tf_op jit(solution)/shard_map/all_to_all | solution.py:56
  104.7 8.4 %copy-start.2 = (s32[128,2]{0,1:T(2,128)S(1)}, s32[128,2]{0,1:T(2,128)}, u32[]{:S(2)}) copy-start(s32[128,2]{0,1:T(2,128)} %param.18) | copy-start | bytes 3076
  104.7 8.4 %copy-start.3 = (s32[128]{0:T(128)S(1)}, s32[128]{0:T(128)}, u32[]{:S(2)}) copy-start(s32[128]{0:T(128)} %param.19) | copy-start | bytes 1540
  105.8 36.6 %copy-start = (f32[512]{0:T(512)S(1)}, f32[512]{0:T(512)}, u32[]{:S(2)}) copy-start(f32[512]{0:T(512)} %param.14) | copy-start | bytes 6148
  105.8 36.5 %all-to-all-start.1 = ((bf16[8,128,512]{2,1,0:T(8,128)(2,1)}), bf16[8,128,512]{2,1,0:T(8,128)(2,1)S(1)}, u32[]{:S(2)}, u32[]{:S(2)}) async-start(bf16[8,128,512]{2,1,0:T(8,128)(2,1)} %bitcast.31), calls=%async_computation.1 | async-start | bytes 2097152 | tf_op jit(solution)/shard_map/all_to_all | solution.py:94
  160.6 32.8 %all-to-all-start.3 = ((bf16[8,128,512]{1,2,0:T(8,128)(2,1)}), bf16[8,128,512]{1,2,0:T(8,128)(2,1)S(1)}, u32[]{:S(2)}, u32[]{:S(2)}) async-start(bf16[8,128,512]{1,2,0:T(8,128)(2,1)} %broadcast_in_dim.28), calls=%async_computation.3 | async-start | bytes 2097152 | tf_op jit(solution)/shard_map/all_to_all | solution.py:56
  194.5 2.9 %copy-start.1 = (f32[4096]{0:T(1024)S(1)}, f32[4096]{0:T(1024)}, u32[]{:S(2)}) copy-start(f32[4096]{0:T(1024)} %param.20) | copy-start | bytes 49156
Sparse Core Ops, SparseCore 0:
  10.7 90.2 all-gather.2
  104.3 83.8 all-gather.4

commit v3 on v2

--- a/solution.py
+++ b/solution.py
@@ -1,11 +1,12 @@
 import jax
 import jax.numpy as jnp
 from jax import lax
-from jax.sharding import PartitionSpec as P
+from jax.sharding import Mesh, PartitionSpec as P
 
 HEAD = 128
 GROUP = 4
 IMG_MAX = 128
+REQ = ("rxy", "rc")
 
 
 def request_plan(grid_sizes, image_owner, requests):
@@ -70,8 +71,8 @@
     norm_gain,
     qkv_weight,
 ):
-    requests = lax.axis_size("req")
-    device_index = lax.axis_index("req")
+    requests = lax.axis_size(REQ)
+    device_index = lax.axis_index(REQ)
     feature_width = vit_context.shape[1]
     merged_context = jnp.mean(
         vit_context.astype(jnp.float32).reshape(-1, 4, feature_width), axis=1
@@ -81,11 +82,17 @@
     )
     full_prompt = gather_features(prompt[0], lax.axis_size("tp"))
     full_prompt, merged_context = lax.optimization_barrier((full_prompt, merged_context))
-    partial_value = jnp.dot(
-        merged_context,
-        lax.all_gather(out_weight, "req", axis=1, tiled=True),
-        preferred_element_type=jnp.float32,
-    )
+    core = lax.axis_index("rc")
+    own_half = lax.all_gather(out_weight, "rxy", axis=1, tiled=True)
+    other_half = lax.ppermute(own_half, "rc", [(0, 1), (1, 0)])
+    own_part = jnp.dot(merged_context, own_half, preferred_element_type=jnp.float32)
+    other_part = jnp.dot(merged_context, other_half, preferred_element_type=jnp.float32)
+    own_part = own_part.reshape(own_part.shape[0], -1, 1, out_weight.shape[1])
+    other_part = other_part.reshape(own_part.shape)
+    partial_value = jnp.concatenate(
+        [jnp.where(core == 0, own_part, other_part), jnp.where(core == 0, other_part, own_part)],
+        axis=2,
+    ).reshape(own_part.shape[0], -1)
     tp_count = lax.axis_size("tp")
     block_terms = partial_value.astype(jnp.bfloat16).reshape(
         -1, tp_count, feature_width
@@ -111,7 +118,7 @@
     outgoing = jnp.dot(placing, merged, preferred_element_type=jnp.float32).astype(jnp.bfloat16)
     arrived = lax.all_to_all(
         outgoing.reshape(requests, capacity, feature_width),
-        "req",
+        REQ,
         split_axis=0,
         concat_axis=0,
         tiled=True,
@@ -142,7 +149,7 @@
         jnp.dot(image_pick, full_image, preferred_element_type=jnp.float32)
         + jnp.dot(prompt_pick, full_prompt, preferred_element_type=jnp.float32)
     ).astype(jnp.bfloat16)
-    full_weight = lax.all_gather(qkv_weight, "req", axis=0, tiled=True)
+    full_weight = lax.all_gather(qkv_weight, REQ, axis=0, tiled=True)
     normed = normalize(embedded, norm_gain)
     projected = jnp.dot(normed, full_weight, preferred_element_type=jnp.float32)
     cosine_table, sine_table = rope_tables(seq_slots)
@@ -164,4 +171,13 @@
         P("req", "tp"),
     )
     out_specs = P("req", "tp")
-    return jax.shard_map(shards, mesh=mesh, in_specs=in_specs, out_specs=out_specs, check_vma=False)
+    rows, columns = mesh.devices.shape
+    split_mesh = Mesh(mesh.devices.reshape(rows // 2, 2, columns), ("rxy", "rc", "tp"))
+    rename = lambda spec: P(*(REQ if axis == "req" else axis for axis in spec))
+    return jax.shard_map(
+        shards,
+        mesh=split_mesh,
+        in_specs=tuple(rename(spec) for spec in in_specs),
+        out_specs=rename(out_specs),
+        check_vma=False,
+    )

time: 213 us -> 222 us (1.042)
  starting transfers between devices: 21.7 us -> 28 us
  waiting for transfers between devices: 127 us -> 124 us
  local copies, waits for them, and re-layouts: 9.92 us -> 12.3 us
    all_to_all x2, waiting for transfers between devices: 71.1 us -> 25 us  [gather_features(): blocks = lax.all_to_all(copies, 'tp', 0, 0, tiled=True)]
    all_gather x2, waiting for transfers between devices: 31.2 us -> 74.2 us  [the longest x1 74.2 us: shards(): own_half = lax.all_gather(out_weight, 'rxy', axis=1, tiled=True)]
    ppermute x0 -> x1, starting transfers between devices: none -> 6.33 us  [shards(): other_half = lax.ppermute(own_half, 'rc', [(0, 1), (1, 0)])]
    dot_general x1 -> x2, matrix products: 3.66 us -> 4.81 us  [the longest x1 2.41 us: shards(): jnp.dot(merged_context, other_half, preferred_element_type=jnp.float32)]
  transfers between devices with their start and end apart: 5 -> 6, of which waited for: 4 -> 3; matrix products, arithmetic and copies ran while one was open for 11% -> 13% of each run, Pallas kernels for 0% -> 0%
where the time goes in v3:
time: 222 us; the launch traced here: 221 us
  waiting for transfers between devices  124 us (56%)
  starting transfers between devices  28 us (13%)
  blocking collectives  17 us (8%)
  matrix products  15.6 us (7%)
  between operations  15.5 us (7%)
  local copies, waits for them, and re-layouts  12.3 us (6%)
  other arithmetic  8.23 us (4%)
    all_gather x1, waiting for transfers between devices, shards(): own_half = lax.all_gather(out_weight, 'rxy', axis=1, tiled=True)  74.2 us
    all_to_all x2, waiting for transfers between devices, gather_features(): blocks = lax.all_to_all(copies, 'tp', 0, 0, tiled=True)  25 us
    all_to_all x1, waiting for transfers between devices, shards(): lax.all_to_all(block_terms, 'tp', 0, 0, tiled=True).astype(jnp.float32)  23.7 us
    all_to_all x1, blocking collectives, shards(): lax.all_to_all(outgoing.reshape(requests, capacity, feature_width), REQ,...  17 us
    all_to_all x2, starting transfers between devices, gather_features(): blocks = lax.all_to_all(copies, 'tp', 0, 0, tiled=True)  14.4 us
    all_to_all x1, starting transfers between devices, shards(): lax.all_to_all(block_terms, 'tp', 0, 0, tiled=True).astype(jnp.float32)  7.23 us
    dot_general x1, matrix products, shards(): projected = jnp.dot(normed, full_weight, preferred_element_type=jnp.float32)  6.73 us
    ppermute x1, starting transfers between devices, shards(): other_half = lax.ppermute(own_half, 'rc', [(0, 1), (1, 0)])  6.33 us
  transfers between devices with their start and end apart: 6, of which 3 were waited for; matrix products, arithmetic and copies ran while one was open for 13% of the time, Pallas kernels for 0%

profile of v3, /device:TPU:1, one launch (start us, length us, event | category | flops | bytes accessed | tf_op | source)
XLA Modules:
  0.0 221.0 jit_solution(6815497697525344568)
XLA Ops:
  8.0 1.1 copy.39
  9.1 1.4 broadcast_in_dim.26
  10.5 10.9 %all-to-all-start = ((bf16[8,256,512]{1,2,0:T(8,128)(2,1)}), bf16[8,256,512]{1,2,0:T(8,128)(2,1)S(1)}, u32[]{:S(2)}, u32[]{:S(2)}) async-start(bf16[8,256,512]{1,2,0:T(8,128)(2,1)} %broadcast_in_dim.26), calls=%async_computation | async-start | bytes 4194304 | tf_op jit(solution)/shard_map/all_to_all | solution.py:57
  21.4 74.2 %all-gather.3.cloned.1.call-done = bf16[512,2048]{0,1:T(8,128)(2,1)} async-done(((bf16[512,64]{0,1:T(8,128)(2,1)}), bf16[512,2048]{0,1:T(8,128)(2,1)}) %all-gather.3.cloned.1.call-update) | async-done | bytes 2097168 | tf_op jit(solution)/shard_map/all_gather | solution.py:86
  95.6 6.3 %collective-permute-start = (bf16[512,2048]{0,1:T(8,128)(2,1)}, bf16[512,2048]{0,1:T(8,128)(2,1)}, u32[]{:S(2)}, u32[]{:S(2)}) collective-permute-start(bf16[512,2048]{0,1:T(8,128)(2,1)} %all-gather.3.cloned.1.call-done), channel_id=1, source_target_pairs={{0,8},{8,0},{1,9},{9,1},{2,10},{10,2},{3,11},{11,3},{4,12},{12,4},... | collective-permute-start | bytes 6291464 | tf_op jit(solution)/shard_map/ppermute | solution.py:87
  101.9 1.4 reshape.262
  103.9 2.4 %fusion.39 = bf16[128,2048]{1,0:T(8,128)(2,1)S(1)} fusion(bf16[128,512]{1,0:T(8,128)(2,1)S(1)} %multiply_convert_fusion, bf16[512,2048]{0,1:T(8,128)(2,1)} %all-gather.3.cloned.1.call-done), kind=kOutput, calls=%fused_computation.80 | convolution fusion | flops 268435456 | bytes 2752512 | tf_op jit(solution)/shard_map/dot_general | solution.py:88
  106.4 2.4 %select_convert_fusion.1 = (bf16[128,2048]{1,0:T(8,128)(2,1)S(1)}, bf16[128,2048]{1,0:T(8,128)(2,1)S(1)}) fusion(bf16[128,2048]{1,0:T(8,128)(2,1)S(1)} %fusion.39, pred[]{:T(512)S(6)} %eq.91, bf16[128,512]{1,0:T(8,128)(2,1)S(1)} %multiply_convert_fusion, bf16[512,2048]{0,1:T(8,128)(2,1)} %collective-permute-done), kind=kOutput, calls=%fused_computation.13 | convolution fusion | flops 268959744 | bytes 3801089 | tf_op jit(solution)/shard_map/dot_general | solution.py:89
  110.1 1.2 pad_maximum_fusion
  111.2 1.1 copy.42
  112.3 7.2 %all-to-all-start.1 = ((bf16[8,128,512]{1,2,0:T(8,128)(2,1)}), bf16[8,128,512]{1,2,0:T(8,128)(2,1)S(1)}, u32[]{:S(2)}, u32[]{:S(2)}) async-start(bf16[8,128,512]{1,2,0:T(8,128)(2,1)} %bitcast.31), calls=%async_computation.1 | async-start | bytes 2097152 | tf_op jit(solution)/shard_map/all_to_all | solution.py:101
  120.0 2.4 %reshape.260 = f32[128,4,512]{2,1,0:T(4,128)} reshape(bf16[512,512]{1,0:T(8,128)(2,1)} %param.12) | data formatting | bytes 1572864 | tf_op jit(solution)/shard_map/reshape | solution.py:81
  122.4 1.8 reduce_sum.86
  125.2 23.7 %all-to-all-done.1 = bf16[8,128,512]{1,2,0:T(8,128)(2,1)S(1)} async-done(((bf16[8,128,512]{1,2,0:T(8,128)(2,1)}), bf16[8,128,512]{1,2,0:T(8,128)(2,1)S(1)}, u32[]{:S(2)}, u32[]{:S(2)}) %all-to-all-start.1) | async-done | bytes 1048608 | tf_op jit(solution)/shard_map/all_to_all | solution.py:101
  149.7 1.1 copy.43
  151.1 17.0 %all_to_all.20 = bf16[64,2,512]{2,1,0:T(2,128)(2,1)S(1)} all-to-all(bf16[64,2,512]{2,1,0:T(2,128)(2,1)S(1)} %reshape.256), channel_id=1, replica_groups=mesh['rxy'=32,'rc'=2,'tp'=8] {'rxy','rc'}, dimensions={0} | all-to-all | bytes 262144 | tf_op jit(solution)/shard_map/all_to_all | solution.py:119
  168.3 1.1 broadcast_in_dim.28
  169.4 3.6 %all-to-all-start.3 = ((bf16[8,128,512]{1,2,0:T(8,128)(2,1)}), bf16[8,128,512]{1,2,0:T(8,128)(2,1)S(1)}, u32[]{:S(2)}, u32[]{:S(2)}) async-start(bf16[8,128,512]{1,2,0:T(8,128)(2,1)} %broadcast_in_dim.28), calls=%async_computation.3 | async-start | bytes 2097152 | tf_op jit(solution)/shard_map/all_to_all | solution.py:57
  175.5 1.3 fusion.26
  177.2 25.0 %all-to-all-done.3 = bf16[8,128,512]{1,2,0:T(8,128)(2,1)S(1)} async-done(((bf16[8,128,512]{1,2,0:T(8,128)(2,1)}), bf16[8,128,512]{1,2,0:T(8,128)(2,1)S(1)}, u32[]{:S(2)}, u32[]{:S(2)}) %all-to-all-start.3) | async-done | bytes 1048608 | tf_op jit(solution)/shard_map/all_to_all | solution.py:57
  202.2 1.0 fusion.12
  203.2 2.9 %fusion = (f32[384]{0:T(512)S(1)}, bf16[384,4096]{1,0:T(8,128)(2,1)}) fusion(f32[384,4096]{1,0:T(8,128)S(1)} %fusion.12, bf16[256,4096]{0,1:T(8,128)(2,1)S(1)} %bitcast.29, s32[384]{0:T(512)S(1)} %get-tuple-element.23, pred[384]{0:T(512)(128)(4,1)S(1)} %get-tuple-element.9), kind=kOutput, calls=%fused_computation.2 | convolution fusion | flops 813366912 | bytes 11537792 | tf_op jit(solution)/shard_map/dot_general | solution.py:150
  206.1 6.7 %fusion.3 = f32[384,768]{0,1:T(8,128)S(1)} fusion(bf16[4096,768]{1,0:T(8,128)(2,1)} %all-gather.5.cloned.1.call-done, bf16[384,4096]{1,0:T(8,128)(2,1)} %get-tuple-element.21, f32[4096]{0:T(1024)S(1)} %copy-done.1, f32[384]{0:T(512)S(1)} %add_rsqrt_fusion), kind=kOutput, calls=%fused_computation.6 | convolution fusion | flops 2422210560 | bytes 10634752 | tf_op jit(solution)/shard_map/dot_general | solution.py:154
  213.1 1.1 copy.46
  (42 shorter events, 7.2 us)
Async XLA Ops:
  6.5 89.0 %all-gather.3.cloned.1.call-start = ((), (), s32[]{:S(2)}) async-start(), calls=%async_computation.4 | async-start | bytes 2162688 | tf_op jit(solution)/shard_map/all_gather | solution.py:86
  7.3 198.9 %all-gather.5.cloned.1.call-start = ((), (), s32[]{:S(2)}) async-start(), calls=%async_computation.5 | async-start | bytes 6389760 | tf_op jit(solution)/shard_map/all_gather | solution.py:152
  10.5 93.4 %all-to-all-start = ((bf16[8,256,512]{1,2,0:T(8,128)(2,1)}), bf16[8,256,512]{1,2,0:T(8,128)(2,1)S(1)}, u32[]{:S(2)}, u32[]{:S(2)}) async-start(bf16[8,256,512]{1,2,0:T(8,128)(2,1)} %broadcast_in_dim.26), calls=%async_computation | async-start | bytes 4194304 | tf_op jit(solution)/shard_map/all_to_all | solution.py:57
  95.6 10.8 %collective-permute-start = (bf16[512,2048]{0,1:T(8,128)(2,1)}, bf16[512,2048]{0,1:T(8,128)(2,1)}, u32[]{:S(2)}, u32[]{:S(2)}) collective-permute-start(bf16[512,2048]{0,1:T(8,128)(2,1)} %all-gather.3.cloned.1.call-done), channel_id=1, source_target_pairs={{0,8},{8,0},{1,9},{9,1},{2,10},{10,2},{3,11},{11,3},{4,12},{12,4},... | collective-permute-start | bytes 6291464 | tf_op jit(solution)/shard_map/ppermute | solution.py:87
  110.0 9.5 %copy-start.2 = (s32[128,2]{0,1:T(2,128)S(1)}, s32[128,2]{0,1:T(2,128)}, u32[]{:S(2)}) copy-start(s32[128,2]{0,1:T(2,128)} %param.18) | copy-start | bytes 3076
  110.1 9.5 %copy-start.3 = (s32[128]{0:T(128)S(1)}, s32[128]{0:T(128)}, u32[]{:S(2)}) copy-start(s32[128]{0:T(128)} %param.19) | copy-start | bytes 1540
  112.3 38.5 %copy-start = (f32[512]{0:T(512)S(1)}, f32[512]{0:T(512)}, u32[]{:S(2)}) copy-start(f32[512]{0:T(512)} %param.14) | copy-start | bytes 6148
  112.3 36.5 %all-to-all-start.1 = ((bf16[8,128,512]{1,2,0:T(8,128)(2,1)}), bf16[8,128,512]{1,2,0:T(8,128)(2,1)S(1)}, u32[]{:S(2)}, u32[]{:S(2)}) async-start(bf16[8,128,512]{1,2,0:T(8,128)(2,1)} %bitcast.31), calls=%async_computation.1 | async-start | bytes 2097152 | tf_op jit(solution)/shard_map/all_to_all | solution.py:101
  169.4 32.8 %all-to-all-start.3 = ((bf16[8,128,512]{1,2,0:T(8,128)(2,1)}), bf16[8,128,512]{1,2,0:T(8,128)(2,1)S(1)}, u32[]{:S(2)}, u32[]{:S(2)}) async-start(bf16[8,128,512]{1,2,0:T(8,128)(2,1)} %broadcast_in_dim.28), calls=%async_computation.3 | async-start | bytes 2097152 | tf_op jit(solution)/shard_map/all_to_all | solution.py:57
  203.2 2.9 %copy-start.1 = (f32[4096]{0:T(1024)S(1)}, f32[4096]{0:T(1024)}, u32[]{:S(2)}) copy-start(f32[4096]{0:T(1024)} %param.20) | copy-start | bytes 49156
Sparse Core Ops, SparseCore 0:
  10.5 84.9 all-gather.2
  98.9 88.2 all-gather.4

commit v4 on v3

--- a/solution.py
+++ b/solution.py
@@ -6,7 +6,7 @@
 HEAD = 128
 GROUP = 4
 IMG_MAX = 128
-REQ = ("rxy", "rc")
+REQ = ("rx", "ry", "rc")
 
 
 def request_plan(grid_sizes, image_owner, requests):
@@ -56,6 +56,35 @@
     copies = jnp.broadcast_to(rows[None], (tp_count,) + rows.shape)
     blocks = lax.all_to_all(copies, "tp", 0, 0, tiled=True)
     return blocks.transpose(1, 0, 2).reshape(rows.shape[0], -1)
+
+
+def shift(value, axis, step):
+    size = lax.axis_size(axis)
+    return lax.ppermute(value, axis, [(k, (k + step) % size) for k in range(size)])
+
+
+def ring_gather(value, axis):
+    size = lax.axis_size(axis)
+    forward, backward = value, value
+    after = {}
+    for step in range(1, size // 2 + 1):
+        if step == size // 2 and size % 2 == 0:
+            half = value.shape[-1] // 2
+            left = shift(forward[..., :half], axis, 1)
+            right = shift(backward[..., half:], axis, -1)
+            after[step] = jnp.concatenate([left, right], axis=-1)
+            break
+        forward = shift(forward, axis, 1)
+        backward = shift(backward, axis, -1)
+        after[size - step] = forward
+        after[step] = backward
+    relative = jnp.stack([value] + [after[step] for step in range(1, size)], axis=0)
+    return jnp.roll(relative, lax.axis_index(axis), axis=0)
+
+
+def gather_plane(shard):
+    by_y = ring_gather(shard, "ry")
+    return ring_gather(by_y, "rx")
 
 
 def shards(
@@ -80,20 +109,22 @@
     merged_residual = jnp.mean(
         vision_residual.astype(jnp.float32).reshape(-1, 4, feature_width), axis=1
     )
-    full_prompt = gather_features(prompt[0], lax.axis_size("tp"))
-    full_prompt, merged_context = lax.optimization_barrier((full_prompt, merged_context))
+    own_half = gather_plane(out_weight)
+    other_half = lax.ppermute(own_half, "rc", [(0, 1), (1, 0)])
     core = lax.axis_index("rc")
-    own_half = lax.all_gather(out_weight, "rxy", axis=1, tiled=True)
-    other_half = lax.ppermute(own_half, "rc", [(0, 1), (1, 0)])
-    own_part = jnp.dot(merged_context, own_half, preferred_element_type=jnp.float32)
-    other_part = jnp.dot(merged_context, other_half, preferred_element_type=jnp.float32)
-    own_part = own_part.reshape(own_part.shape[0], -1, 1, out_weight.shape[1])
-    other_part = other_part.reshape(own_part.shape)
-    partial_value = jnp.concatenate(
+    own_part = jnp.einsum(
+        "gk,xykn->gxyn", merged_context, own_half, preferred_element_type=jnp.float32
+    )
+    other_part = jnp.einsum(
+        "gk,xykn->gxyn", merged_context, other_half, preferred_element_type=jnp.float32
+    )
+    partial_value = jnp.stack(
         [jnp.where(core == 0, own_part, other_part), jnp.where(core == 0, other_part, own_part)],
-        axis=2,
+        axis=3,
     ).reshape(own_part.shape[0], -1)
     tp_count = lax.axis_size("tp")
+    full_prompt = gather_features(prompt[0], tp_count)
+    full_prompt, partial_value = lax.optimization_barrier((full_prompt, partial_value))
     block_terms = partial_value.astype(jnp.bfloat16).reshape(
         -1, tp_count, feature_width
     ).transpose(1, 0, 2)
@@ -172,7 +203,10 @@
     )
     out_specs = P("req", "tp")
     rows, columns = mesh.devices.shape
-    split_mesh = Mesh(mesh.devices.reshape(rows // 2, 2, columns), ("rxy", "rc", "tp"))
+    x_size = len({device.coords[0] for device in mesh.devices.flat})
+    split_mesh = Mesh(
+        mesh.devices.reshape(x_size, rows // (2 * x_size), 2, columns), REQ + ("tp",)
+    )
     rename = lambda spec: P(*(REQ if axis == "req" else axis for axis in spec))
     return jax.shard_map(
         shards,

time: 222 us -> 221 us (level)
  waiting for transfers between devices: 124 us -> 82 us
  starting transfers between devices: 28 us -> 67.4 us
  local copies, waits for them, and re-layouts: 12.3 us -> 16.1 us
  matrix products: 15.6 us -> 12.9 us
    all_gather x1 -> x0, waiting for transfers between devices: 74.2 us -> none  [shards(): own_half = lax.all_gather(out_weight, 'rxy', axis=1, tiled=True)]
    ppermute x0 -> x12, starting transfers between devices: none -> 40.4 us  [shift(): lax.ppermute(value, axis, [(k, (k + step) % size) for k in range(size)])]
    all_to_all x2, waiting for transfers between devices: 25 us -> 46.5 us  [gather_features(): blocks = lax.all_to_all(copies, 'tp', 0, 0, tiled=True)]
    ppermute x0 -> x12, waiting for transfers between devices: none -> 10.4 us  [shift(): lax.ppermute(value, axis, [(k, (k + step) % size) for k in range(size)])]
    unnamed x8 -> x30, local copies, waits for them, and re-layouts: 0.02 us -> 6.27 us
    all_to_all x1, starting transfers between devices: 7.23 us -> 3.9 us  [shards(): lax.all_to_all(block_terms, 'tp', 0, 0, tiled=True).astype(jnp.float32)]
  transfers between devices with their start and end apart: 6 -> 17, of which waited for: 3 -> 7; matrix products, arithmetic and copies ran while one was open for 13% -> 13% of each run, Pallas kernels for 0% -> 0%
where the time goes in v4:
time: 221 us; the launch traced here: 220 us
  waiting for transfers between devices  82 us (37%)
  starting transfers between devices  67.4 us (30%)
  blocking collectives  19.2 us (9%)
  local copies, waits for them, and re-layouts  16.1 us (7%)
  between operations  15.9 us (7%)
  matrix products  12.9 us (6%)
  other arithmetic  6.97 us (3%)
    all_to_all x2, waiting for transfers between devices, gather_features(): blocks = lax.all_to_all(copies, 'tp', 0, 0, tiled=True)  46.5 us
    ppermute x12, starting transfers between devices, shift(): lax.ppermute(value, axis, [(k, (k + step) % size) for k in range(size)])  40.4 us
    all_to_all x1, waiting for transfers between devices, shards(): lax.all_to_all(block_terms, 'tp', 0, 0, tiled=True).astype(jnp.float32)  23.1 us
    all_to_all x1, blocking collectives, shards(): lax.all_to_all(outgoing.reshape(requests, capacity, feature_width), REQ,...  19.2 us
    all_to_all x2, starting transfers between devices, gather_features(): blocks = lax.all_to_all(copies, 'tp', 0, 0, tiled=True)  15.8 us
    ppermute x12, waiting for transfers between devices, shift(): lax.ppermute(value, axis, [(k, (k + step) % size) for k in range(size)])  10.4 us
    ppermute x1, starting transfers between devices, shards(): other_half = lax.ppermute(own_half, 'rc', [(0, 1), (1, 0)])  7.36 us
    unnamed x30, local copies, waits for them, and re-layouts  6.27 us
  transfers between devices with their start and end apart: 17, of which 7 were waited for; matrix products, arithmetic and copies ran while one was open for 13% of the time, Pallas kernels for 0%

profile of v4, /device:TPU:1, one launch (start us, length us, event | category | flops | bytes accessed | tf_op | source)
XLA Modules:
  0.0 220.4 jit_solution(4139865889153867305)
XLA Ops:
  6.5 6.0 %collective-permute-start = (bf16[512,64]{0,1:T(8,128)(2,1)}, bf16[512,64]{0,1:T(8,128)(2,1)S(1)}, u32[]{:S(2)}, u32[]{:S(2)}) collective-permute-start(bf16[512,64]{0,1:T(8,128)(2,1)} %param.13), channel_id=1, source_target_pairs={{0,112},{16,0},{32,16},{48,32},{64,48},{80,64},{96,80},{112,96},{1... | collective-permute-start | bytes 196616 | tf_op jit(solution)/shard_map/ppermute | solution.py:63
  12.6 1.9 collective-permute-start.3
  15.4 4.6 %collective-permute-start.1 = (bf16[512,64]{0,1:T(8,128)(2,1)S(1)}, bf16[512,64]{0,1:T(8,128)(2,1)S(1)}, u32[]{:S(2)}, u32[]{:S(2)}) collective-permute-start(bf16[512,64]{0,1:T(8,128)(2,1)S(1)} %collective-permute-done), channel_id=1, source_target_pairs={{0,112},{16,0},{32,16},{48,32},{64,48},{80,64},{96,80},{112,96},{1... | collective-permute-start | bytes 196616 | tf_op jit(solution)/shard_map/ppermute | solution.py:63
  20.0 1.9 collective-permute-start.4
  22.0 4.6 %collective-permute-start.2 = (bf16[512,64]{0,1:T(8,128)(2,1)S(1)}, bf16[512,64]{0,1:T(8,128)(2,1)S(1)}, u32[]{:S(2)}, u32[]{:S(2)}) collective-permute-start(bf16[512,64]{0,1:T(8,128)(2,1)S(1)} %collective-permute-done.1), channel_id=1, source_target_pairs={{0,112},{16,0},{32,16},{48,32},{64,48},{80,64},{96,80},{112,96},{1... | collective-permute-start | bytes 196616 | tf_op jit(solution)/shard_map/ppermute | solution.py:63
  26.5 1.9 collective-permute-start.5
  28.5 4.3 %collective-permute-done.5 = bf16[512,64]{0,1:T(8,128)(2,1)S(1)} collective-permute-done((bf16[512,64]{0,1:T(8,128)(2,1)S(1)}, bf16[512,64]{0,1:T(8,128)(2,1)S(1)}, u32[]{:S(2)}, u32[]{:S(2)}) %collective-permute-start.5) | collective-permute-done | bytes 65568 | tf_op jit(solution)/shard_map/ppermute | solution.py:63
  34.7 4.6 %collective-permute-start.7 = (bf16[512,32]{0,1:T(8,128)(2,1)S(1)}, bf16[512,32]{0,1:T(8,128)(2,1)S(1)}, u32[]{:S(2)}, u32[]{:S(2)}) collective-permute-start(bf16[512,32]{0,1:T(8,128)(2,1)S(1)} %slice.41), channel_id=1, source_target_pairs={{0,112},{16,0},{32,16},{48,32},{64,48},{80,64},{96,80},{112,96},{1... | collective-permute-start | bytes 98312 | tf_op jit(solution)/shard_map/ppermute | solution.py:63
  42.3 3.1 %collective-permute-start.9 = (bf16[8,512,64]{1,2,0:T(8,128)(2,1)S(1)}, bf16[8,512,64]{1,2,0:T(8,128)(2,1)S(1)}, u32[]{:S(2)}, u32[]{:S(2)}) collective-permute-start(bf16[8,512,64]{1,2,0:T(8,128)(2,1)S(1)} %get-tuple-element.14), channel_id=1, source_target_pairs={{0,128},{128,256},{256,384},{384,0},{1,129},{129,257},{257,385},{3... | collective-permute-start | bytes 1572872 | tf_op jit(solution)/shard_map/ppermute | solution.py:63
  45.4 3.4 %collective-permute-start.8 = (bf16[8,512,64]{1,2,0:T(8,128)(2,1)S(1)}, bf16[8,512,64]{1,2,0:T(8,128)(2,1)S(1)}, u32[]{:S(2)}, u32[]{:S(2)}) collective-permute-start(bf16[8,512,64]{1,2,0:T(8,128)(2,1)S(1)} %get-tuple-element.14), channel_id=1, source_target_pairs={{0,384},{128,0},{256,128},{384,256},{1,385},{129,1},{257,129},{385... | collective-permute-start | bytes 1572872 | tf_op jit(solution)/shard_map/ppermute | solution.py:63
  48.8 5.0 %collective-permute-done.9 = bf16[8,512,64]{1,2,0:T(8,128)(2,1)S(1)} collective-permute-done((bf16[8,512,64]{1,2,0:T(8,128)(2,1)S(1)}, bf16[8,512,64]{1,2,0:T(8,128)(2,1)S(1)}, u32[]{:S(2)}, u32[]{:S(2)}) %collective-permute-start.9) | collective-permute-done | bytes 524320 | tf_op jit(solution)/shard_map/ppermute | solution.py:63
  53.8 2.3 %collective-permute-start.10 = (bf16[8,512,32]{1,2,0:T(8,128)(2,1)S(1)}, bf16[8,512,32]{1,2,0:T(8,128)(2,1)S(1)}, u32[]{:S(2)}, u32[]{:S(2)}) collective-permute-start(bf16[8,512,32]{1,2,0:T(8,128)(2,1)S(1)} %slice.42), channel_id=1, source_target_pairs={{0,128},{128,256},{256,384},{384,0},{1,129},{129,257},{257,385},{3... | collective-permute-start | bytes 786440 | tf_op jit(solution)/shard_map/ppermute | solution.py:63
  56.1 4.2 %collective-permute-start.11 = (bf16[8,512,32]{1,2,0:T(8,128)(2,1)S(1)}, bf16[8,512,32]{1,2,0:T(8,128)(2,1)S(1)}, u32[]{:S(2)}, u32[]{:S(2)}) collective-permute-start(bf16[8,512,32]{1,2,0:T(8,128)(2,1)S(1)} %slice.43), channel_id=1, source_target_pairs={{0,384},{128,0},{256,128},{384,256},{1,385},{129,1},{257,129},{385... | collective-permute-start | bytes 786440 | tf_op jit(solution)/shard_map/ppermute | solution.py:63
  62.0 12.0 %all-to-all-start = ((bf16[8,256,512]{1,2,0:T(8,128)(2,1)}), bf16[8,256,512]{1,2,0:T(8,128)(2,1)}, u32[]{:S(2)}, u32[]{:S(2)}) async-start(bf16[8,256,512]{1,2,0:T(8,128)(2,1)} %broadcast_in_dim.26), calls=%async_computation | async-start | bytes 4194304 | tf_op jit(solution)/shard_map/all_to_all | solution.py:57
  81.9 7.4 %collective-permute-start.12 = (bf16[4,8,512,64]{2,3,1,0:T(8,128)(2,1)S(1)}, bf16[4,8,512,64]{2,3,1,0:T(8,128)(2,1)}, u32[]{:S(2)}, u32[]{:S(2)}) collective-permute-start(bf16[4,8,512,64]{2,3,1,0:T(8,128)(2,1)S(1)} %constant_dynamic-slice_fusion), channel_id=1, source_target_pairs={{0,8},{8,0},{1,9},{9,1},{2,10},{10,2},{3,11},{11,3},{4,12},{12,4},... | collective-permute-start | bytes 6291464 | tf_op jit(solution)/shard_map/ppermute | solution.py:113
  93.2 2.3 %fusion.25 = bf16[128,4,8,64]{0,3,2,1:T(8,128)(2,1)S(1)} fusion(bf16[4,8,512,64]{2,3,1,0:T(8,128)(2,1)} %collective-permute-done.12, f32[128,512]{1,0:T(8,128)S(1)} %reduce_sum.87), kind=kOutput, calls=%fused_computation.63 | convolution fusion | flops 268566528 | bytes 2883584 | tf_op jit(solution)/shard_map/gk,xykn->gxyn/dot_general | solution.py:118
  97.4 24.0 %all-to-all-done = bf16[8,256,512]{1,2,0:T(8,128)(2,1)} async-done(((bf16[8,256,512]{1,2,0:T(8,128)(2,1)}), bf16[8,256,512]{1,2,0:T(8,128)(2,1)}, u32[]{:S(2)}, u32[]{:S(2)}) %all-to-all-start) | async-done | bytes 2097184 | tf_op jit(solution)/shard_map/all_to_all | solution.py:57
  121.5 3.9 %all-to-all-start.1 = ((bf16[8,128,512]{1,2,0:T(8,128)(2,1)}), bf16[8,128,512]{1,2,0:T(8,128)(2,1)S(1)}, u32[]{:S(2)}, u32[]{:S(2)}) async-start(bf16[8,128,512]{1,2,0:T(8,128)(2,1)} %bitcast.25), calls=%async_computation.1 | async-start | bytes 2097152 | tf_op jit(solution)/shard_map/all_to_all | solution.py:132
  127.7 23.1 %all-to-all-done.1 = bf16[8,128,512]{1,2,0:T(8,128)(2,1)S(1)} async-done(((bf16[8,128,512]{1,2,0:T(8,128)(2,1)}), bf16[8,128,512]{1,2,0:T(8,128)(2,1)S(1)}, u32[]{:S(2)}, u32[]{:S(2)}) %all-to-all-start.1) | async-done | bytes 1048608 | tf_op jit(solution)/shard_map/all_to_all | solution.py:132
  151.4 19.2 %all_to_all.20 = bf16[64,2,512]{2,1,0:T(2,128)(2,1)S(1)} all-to-all(bf16[64,2,512]{2,1,0:T(2,128)(2,1)S(1)} %reshape.212), channel_id=1, replica_groups=mesh['rx'=4,'ry'=8,'rc'=2,'tp'=8] {'rx','ry','rc'}, dimensions={0} | all-to-all | bytes 262144 | tf_op jit(solution)/shard_map/all_to_all | solution.py:150
  171.9 3.7 %all-to-all-start.3 = ((bf16[8,128,512]{1,2,0:T(8,128)(2,1)}), bf16[8,128,512]{1,2,0:T(8,128)(2,1)S(1)}, u32[]{:S(2)}, u32[]{:S(2)}) async-start(bf16[8,128,512]{1,2,0:T(8,128)(2,1)} %broadcast_in_dim.28), calls=%async_computation.3 | async-start | bytes 2097152 | tf_op jit(solution)/shard_map/all_to_all | solution.py:57
  180.0 22.5 %all-to-all-done.3 = bf16[8,128,512]{1,2,0:T(8,128)(2,1)S(1)} async-done(((bf16[8,128,512]{1,2,0:T(8,128)(2,1)}), bf16[8,128,512]{1,2,0:T(8,128)(2,1)S(1)}, u32[]{:S(2)}, u32[]{:S(2)}) %all-to-all-start.3) | async-done | bytes 1048608 | tf_op jit(solution)/shard_map/all_to_all | solution.py:57
  203.5 2.9 %fusion = (f32[384]{0:T(512)S(1)}, bf16[384,4096]{1,0:T(8,128)(2,1)S(1)}) fusion(f32[384,4096]{1,0:T(8,128)S(1)} %fusion.14, bf16[256,4096]{0,1:T(8,128)(2,1)} %bitcast.5, s32[384]{0:T(512)S(1)} %get-tuple-element.25, pred[384]{0:T(512)(128)(4,1)S(1)} %get-tuple-element.9), kind=kOutput, calls=%fused_computation.2 | convolution fusion | flops 813366912 | bytes 11537792 | tf_op jit(solution)/shard_map/dot_general | solution.py:181
  206.5 5.8 %fusion.3 = f32[384,768]{0,1:T(8,128)S(1)} fusion(bf16[4096,768]{1,0:T(8,128)(2,1)} %all-gather.2.cloned.1.call-done, bf16[384,4096]{1,0:T(8,128)(2,1)S(1)} %get-tuple-element.23, f32[4096]{0:T(1024)S(1)} %copy-done.3, f32[384]{0:T(512)S(1)} %add_rsqrt_fusion), kind=kOutput, calls=%fused_computation.6 | convolution fusion | flops 2422210560 | bytes 10634752 | tf_op jit(solution)/shard_map/dot_general | solution.py:185
  (93 shorter events, 29.9 us)
Async XLA Ops:
  6.5 53.8 %copy-start.1 = (bf16[1,256,512]{2,1,0:T(8,128)(2,1)S(1)}, bf16[1,256,512]{2,1,0:T(8,128)(2,1)}, u32[]{:S(2)}) copy-start(bf16[1,256,512]{2,1,0:T(8,128)(2,1)} %param.15) | copy-start | bytes 786436
  6.5 199.9 %all-gather.2.cloned.1.call-start = ((), (), s32[]{:S(2)}) async-start(), calls=%async_computation.4 | async-start | bytes 6389760 | tf_op jit(solution)/shard_map/all_gather | solution.py:183
  6.5 8.9 %collective-permute-start = (bf16[512,64]{0,1:T(8,128)(2,1)}, bf16[512,64]{0,1:T(8,128)(2,1)S(1)}, u32[]{:S(2)}, u32[]{:S(2)}) collective-permute-start(bf16[512,64]{0,1:T(8,128)(2,1)} %param.13), channel_id=1, source_target_pairs={{0,112},{16,0},{32,16},{48,32},{64,48},{80,64},{96,80},{112,96},{1... | collective-permute-start | bytes 196616 | tf_op jit(solution)/shard_map/ppermute | solution.py:63
  12.6 7.4 %collective-permute-start.3 = (bf16[512,64]{0,1:T(8,128)(2,1)}, bf16[512,64]{0,1:T(8,128)(2,1)S(1)}, u32[]{:S(2)}, u32[]{:S(2)}) collective-permute-start(bf16[512,64]{0,1:T(8,128)(2,1)} %param.13), channel_id=1, source_target_pairs={{0,16},{16,32},{32,48},{48,64},{64,80},{80,96},{96,112},{112,0},{1... | collective-permute-start | bytes 196616 | tf_op jit(solution)/shard_map/ppermute | solution.py:63
  15.4 6.5 %collective-permute-start.1 = (bf16[512,64]{0,1:T(8,128)(2,1)S(1)}, bf16[512,64]{0,1:T(8,128)(2,1)S(1)}, u32[]{:S(2)}, u32[]{:S(2)}) collective-permute-start(bf16[512,64]{0,1:T(8,128)(2,1)S(1)} %collective-permute-done), channel_id=1, source_target_pairs={{0,112},{16,0},{32,16},{48,32},{64,48},{80,64},{96,80},{112,96},{1... | collective-permute-start | bytes 196616 | tf_op jit(solution)/shard_map/ppermute | solution.py:63
  20.0 6.5 %collective-permute-start.4 = (bf16[512,64]{0,1:T(8,128)(2,1)S(1)}, bf16[512,64]{0,1:T(8,128)(2,1)S(1)}, u32[]{:S(2)}, u32[]{:S(2)}) collective-permute-start(bf16[512,64]{0,1:T(8,128)(2,1)S(1)} %collective-permute-done.3), channel_id=1, source_target_pairs={{0,16},{16,32},{32,48},{48,64},{64,80},{80,96},{96,112},{112,0},{1... | collective-permute-start | bytes 196616 | tf_op jit(solution)/shard_map/ppermute | solution.py:63
  22.0 12.7 %collective-permute-start.2 = (bf16[512,64]{0,1:T(8,128)(2,1)S(1)}, bf16[512,64]{0,1:T(8,128)(2,1)S(1)}, u32[]{:S(2)}, u32[]{:S(2)}) collective-permute-start(bf16[512,64]{0,1:T(8,128)(2,1)S(1)} %collective-permute-done.1), channel_id=1, source_target_pairs={{0,112},{16,0},{32,16},{48,32},{64,48},{80,64},{96,80},{112,96},{1... | collective-permute-start | bytes 196616 | tf_op jit(solution)/shard_map/ppermute | solution.py:63
  26.5 6.2 %collective-permute-start.5 = (bf16[512,64]{0,1:T(8,128)(2,1)S(1)}, bf16[512,64]{0,1:T(8,128)(2,1)S(1)}, u32[]{:S(2)}, u32[]{:S(2)}) collective-permute-start(bf16[512,64]{0,1:T(8,128)(2,1)S(1)} %collective-permute-done.4), channel_id=1, source_target_pairs={{0,16},{16,32},{32,48},{48,64},{64,80},{80,96},{96,112},{112,0},{1... | collective-permute-start | bytes 196616 | tf_op jit(solution)/shard_map/ppermute | solution.py:63
  32.8 6.5 %collective-permute-start.6 = (bf16[512,32]{0,1:T(8,128)(2,1)S(1)}, bf16[512,32]{0,1:T(8,128)(2,1)S(1)}, u32[]{:S(2)}, u32[]{:S(2)}) collective-permute-start(bf16[512,32]{0,1:T(8,128)(2,1)S(1)} %slice.40), channel_id=1, source_target_pairs={{0,16},{16,32},{32,48},{48,64},{64,80},{80,96},{96,112},{112,0},{1... | collective-permute-start | bytes 98312 | tf_op jit(solution)/shard_map/ppermute | solution.py:63
  34.7 5.7 %collective-permute-start.7 = (bf16[512,32]{0,1:T(8,128)(2,1)S(1)}, bf16[512,32]{0,1:T(8,128)(2,1)S(1)}, u32[]{:S(2)}, u32[]{:S(2)}) collective-permute-start(bf16[512,32]{0,1:T(8,128)(2,1)S(1)} %slice.41), channel_id=1, source_target_pairs={{0,112},{16,0},{32,16},{48,32},{64,48},{80,64},{96,80},{112,96},{1... | collective-permute-start | bytes 98312 | tf_op jit(solution)/shard_map/ppermute | solution.py:63
  42.3 11.5 %collective-permute-start.9 = (bf16[8,512,64]{1,2,0:T(8,128)(2,1)S(1)}, bf16[8,512,64]{1,2,0:T(8,128)(2,1)S(1)}, u32[]{:S(2)}, u32[]{:S(2)}) collective-permute-start(bf16[8,512,64]{1,2,0:T(8,128)(2,1)S(1)} %get-tuple-element.14), channel_id=1, source_target_pairs={{0,128},{128,256},{256,384},{384,0},{1,129},{129,257},{257,385},{3... | collective-permute-start | bytes 1572872 | tf_op jit(solution)/shard_map/ppermute | solution.py:63
  45.4 10.7 %collective-permute-start.8 = (bf16[8,512,64]{1,2,0:T(8,128)(2,1)S(1)}, bf16[8,512,64]{1,2,0:T(8,128)(2,1)S(1)}, u32[]{:S(2)}, u32[]{:S(2)}) collective-permute-start(bf16[8,512,64]{1,2,0:T(8,128)(2,1)S(1)} %get-tuple-element.14), channel_id=1, source_target_pairs={{0,384},{128,0},{256,128},{384,256},{1,385},{129,1},{257,129},{385... | collective-permute-start | bytes 1572872 | tf_op jit(solution)/shard_map/ppermute | solution.py:63
  53.8 21.0 %collective-permute-start.10 = (bf16[8,512,32]{1,2,0:T(8,128)(2,1)S(1)}, bf16[8,512,32]{1,2,0:T(8,128)(2,1)S(1)}, u32[]{:S(2)}, u32[]{:S(2)}) collective-permute-start(bf16[8,512,32]{1,2,0:T(8,128)(2,1)S(1)} %slice.42), channel_id=1, source_target_pairs={{0,128},{128,256},{256,384},{384,0},{1,129},{129,257},{257,385},{3... | collective-permute-start | bytes 786440 | tf_op jit(solution)/shard_map/ppermute | solution.py:63
  56.1 18.7 %collective-permute-start.11 = (bf16[8,512,32]{1,2,0:T(8,128)(2,1)S(1)}, bf16[8,512,32]{1,2,0:T(8,128)(2,1)S(1)}, u32[]{:S(2)}, u32[]{:S(2)}) collective-permute-start(bf16[8,512,32]{1,2,0:T(8,128)(2,1)S(1)} %slice.43), channel_id=1, source_target_pairs={{0,384},{128,0},{256,128},{384,256},{1,385},{129,1},{257,129},{385... | collective-permute-start | bytes 786440 | tf_op jit(solution)/shard_map/ppermute | solution.py:63
  62.0 59.5 %all-to-all-start = ((bf16[8,256,512]{1,2,0:T(8,128)(2,1)}), bf16[8,256,512]{1,2,0:T(8,128)(2,1)}, u32[]{:S(2)}, u32[]{:S(2)}) async-start(bf16[8,256,512]{1,2,0:T(8,128)(2,1)} %broadcast_in_dim.26), calls=%async_computation | async-start | bytes 4194304 | tf_op jit(solution)/shard_map/all_to_all | solution.py:57
  81.9 11.3 %collective-permute-start.12 = (bf16[4,8,512,64]{2,3,1,0:T(8,128)(2,1)S(1)}, bf16[4,8,512,64]{2,3,1,0:T(8,128)(2,1)}, u32[]{:S(2)}, u32[]{:S(2)}) collective-permute-start(bf16[4,8,512,64]{2,3,1,0:T(8,128)(2,1)S(1)} %constant_dynamic-slice_fusion), channel_id=1, source_target_pairs={{0,8},{8,0},{1,9},{9,1},{2,10},{10,2},{3,11},{11,3},{4,12},{12,4},... | collective-permute-start | bytes 6291464 | tf_op jit(solution)/shard_map/ppermute | solution.py:113
  95.5 29.9 %copy-start.4 = (s32[128,2]{0,1:T(2,128)S(1)}, s32[128,2]{0,1:T(2,128)}, u32[]{:S(2)}) copy-start(s32[128,2]{0,1:T(2,128)} %param.18) | copy-start | bytes 3076
  95.5 29.9 %copy-start.5 = (s32[128]{0:T(128)S(1)}, s32[128]{0:T(128)}, u32[]{:S(2)}) copy-start(s32[128]{0:T(128)} %param.19) | copy-start | bytes 1540
  96.2 29.6 %copy-start = (bf16[512,512]{1,0:T(8,128)(2,1)S(1)}, bf16[512,512]{1,0:T(8,128)(2,1)}, u32[]{:S(2)}) copy-start(bf16[512,512]{1,0:T(8,128)(2,1)} %param.12) | copy-start | bytes 1572868
  96.3 54.8 %copy-start.2 = (f32[512]{0:T(512)S(1)}, f32[512]{0:T(512)}, u32[]{:S(2)}) copy-start(f32[512]{0:T(512)} %param.14) | copy-start | bytes 6148
  121.5 29.4 %all-to-all-start.1 = ((bf16[8,128,512]{1,2,0:T(8,128)(2,1)}), bf16[8,128,512]{1,2,0:T(8,128)(2,1)S(1)}, u32[]{:S(2)}, u32[]{:S(2)}) async-start(bf16[8,128,512]{1,2,0:T(8,128)(2,1)} %bitcast.25), calls=%async_computation.1 | async-start | bytes 2097152 | tf_op jit(solution)/shard_map/all_to_all | solution.py:132
  171.9 30.6 %all-to-all-start.3 = ((bf16[8,128,512]{1,2,0:T(8,128)(2,1)}), bf16[8,128,512]{1,2,0:T(8,128)(2,1)S(1)}, u32[]{:S(2)}, u32[]{:S(2)}) async-start(bf16[8,128,512]{1,2,0:T(8,128)(2,1)} %broadcast_in_dim.28), calls=%async_computation.3 | async-start | bytes 2097152 | tf_op jit(solution)/shard_map/all_to_all | solution.py:57
  203.5 2.9 %copy-start.3 = (f32[4096]{0:T(1024)S(1)}, f32[4096]{0:T(1024)}, u32[]{:S(2)}) copy-start(f32[4096]{0:T(1024)} %param.20) | copy-start | bytes 49156
Sparse Core Ops, SparseCore 0:
  14.7 90.4 all-gather.1

commit v5 on v2

--- a/solution.py
+++ b/solution.py
@@ -87,14 +87,7 @@
         preferred_element_type=jnp.float32,
     )
     tp_count = lax.axis_size("tp")
-    block_terms = partial_value.astype(jnp.bfloat16).reshape(
-        -1, tp_count, feature_width
-    ).transpose(1, 0, 2)
-    own_share = jnp.sum(
-        lax.all_to_all(block_terms, "tp", 0, 0, tiled=True).astype(jnp.float32), axis=0
-    )
-    merged = (merged_residual + layer_scale[None, :] * own_share).astype(jnp.bfloat16)
-    merged_count = merged.shape[0]
+    merged_count = merged_context.shape[0]
     counts, starts = request_plan(grid_sizes, image_owner, requests)
     request_ends = starts + counts
     capacity = (IMG_MAX + requests - 1) // requests
@@ -107,16 +100,25 @@
     target = destination * capacity + (group_index - owned_start) // requests
     usable = destination < requests
     send_slots = jnp.arange(requests * capacity, dtype=jnp.int32)
-    placing = ((send_slots[:, None] == target[None, :]) & usable[None, :]).astype(jnp.bfloat16)
-    outgoing = jnp.dot(placing, merged, preferred_element_type=jnp.float32).astype(jnp.bfloat16)
-    arrived = lax.all_to_all(
-        outgoing.reshape(requests, capacity, feature_width),
-        "req",
-        split_axis=0,
-        concat_axis=0,
+    sends = (send_slots[:, None] == target[None, :]) & usable[None, :]
+    slot_used = jnp.any(sends, axis=1)
+    source_group = jnp.sum(jnp.where(sends, jnp.arange(merged_count)[None, :], 0), axis=1)
+    residual_out = jnp.where(slot_used[:, None], merged_residual[source_group], 0.0)
+    residual_in = lax.all_to_all(
+        residual_out.reshape(requests, capacity, feature_width), "req", 0, 0, tiled=True
+    ).reshape(requests * capacity, feature_width)
+    terms = partial_value.astype(jnp.bfloat16)
+    terms_out = jnp.where(slot_used[:, None], terms[source_group], jnp.zeros_like(terms[:1]))
+    terms_out = terms_out.reshape(requests, capacity, tp_count, feature_width).transpose(0, 2, 1, 3)
+    terms_in = lax.all_to_all(
+        terms_out.reshape(requests * tp_count, capacity, feature_width),
+        ("req", "tp"),
+        0,
+        0,
         tiled=True,
-    )
-    arrived = arrived.reshape(requests * capacity, feature_width)
+    ).reshape(requests, tp_count, capacity, feature_width)
+    image_sum = jnp.sum(terms_in.astype(jnp.float32), axis=1).reshape(-1, feature_width)
+    arrived = (residual_in + layer_scale[None, :] * image_sum).astype(jnp.bfloat16)
     own_request = request_ids == device_index
     own_count = jnp.sum(jnp.where(own_request, counts, 0))
     own_start = jnp.sum(jnp.where(own_request, starts, 0))

time: 213 us -> 219 us (1.028)
  starting transfers between devices: 21.7 us -> 42.9 us
  blocking collectives: 16.6 us -> 0 us
  waiting for transfers between devices: 127 us -> 119 us
  local copies, waits for them, and re-layouts: 9.92 us -> 16.9 us
  other arithmetic: 6.58 us -> 9.47 us
    all_to_all x1 -> x2, starting transfers between devices: 7.24 us -> 28.4 us  [the longest x1 14.5 us: shards(): lax.all_to_all(terms_out.reshape(requests * tp_count, capacity, feature_w...]
    all_to_all x1 -> x0, blocking collectives: 16.6 us -> none  [shards(): lax.all_to_all(outgoing.reshape(requests, capacity, feature_width), 'req'...]
    all_gather x1, waiting for transfers between devices: 31.2 us -> 19.3 us  [shards(): lax.all_gather(out_weight, 'req', axis=1, tiled=True)]
    all_to_all x1 -> x2, waiting for transfers between devices: 23.6 us -> 34.4 us  [the longest x1 34.4 us: shards(): lax.all_to_all(terms_out.reshape(requests * tp_count, capacity, feature_w...]
    all_to_all x2, waiting for transfers between devices: 71.1 us -> 63.6 us  [gather_features(): blocks = lax.all_to_all(copies, 'tp', 0, 0, tiled=True)]
    gather x0 -> x3, local copies, waits for them, and re-layouts: none -> 3.1 us  [the longest x1 2.2 us: shards(): terms[source_group]]
  transfers between devices with their start and end apart: 5 -> 6, of which waited for: 4 -> 4; matrix products, arithmetic and copies ran while one was open for 11% -> 15% of each run, Pallas kernels for 0% -> 0%
where the time goes in v5:
time: 219 us; the launch traced here: 218 us
  waiting for transfers between devices  119 us (54%)
  starting transfers between devices  42.9 us (20%)
  local copies, waits for them, and re-layouts  16.9 us (8%)
  between operations  15.5 us (7%)
  matrix products  14.3 us (7%)
  other arithmetic  9.47 us (4%)
    all_to_all x2, waiting for transfers between devices, gather_features(): blocks = lax.all_to_all(copies, 'tp', 0, 0, tiled=True)  63.6 us
    all_to_all x1, waiting for transfers between devices, shards(): lax.all_to_all(terms_out.reshape(requests * tp_count, capacity, feature_w...  34.4 us
    all_gather x1, waiting for transfers between devices, shards(): lax.all_gather(out_weight, 'req', axis=1, tiled=True)  19.3 us
    all_to_all x1, starting transfers between devices, shards(): lax.all_to_all(terms_out.reshape(requests * tp_count, capacity, feature_w...  14.5 us
    all_to_all x2, starting transfers between devices, gather_features(): blocks = lax.all_to_all(copies, 'tp', 0, 0, tiled=True)  14.4 us
    all_to_all x1, starting transfers between devices, shards(): lax.all_to_all(residual_out.reshape(requests, capacity, feature_width), '...  13.8 us
    dot_general x1, matrix products, shards(): projected = jnp.dot(normed, full_weight, preferred_element_type=jnp.float32)  6.71 us
  transfers between devices with their start and end apart: 6, of which 4 were waited for; matrix products, arithmetic and copies ran while one was open for 15% of the time, Pallas kernels for 0%

profile of v5, /device:TPU:1, one launch (start us, length us, event | category | flops | bytes accessed | tf_op | source)
XLA Modules:
  0.0 217.9 jit_solution(3483023960812004679)
XLA Ops:
  8.0 1.1 copy.39
  9.1 1.4 broadcast_in_dim.72
  10.6 10.9 %all-to-all-start.1 = ((bf16[8,256,512]{1,2,0:T(8,128)(2,1)}), bf16[8,256,512]{1,2,0:T(8,128)(2,1)S(1)}, u32[]{:S(2)}, u32[]{:S(2)}) async-start(bf16[8,256,512]{1,2,0:T(8,128)(2,1)} %broadcast_in_dim.72), calls=%async_computation.1 | async-start | bytes 4194304 | tf_op jit(solution)/shard_map/all_to_all | solution.py:56
  21.9 1.4 reshape.275
  24.5 2.4 %reshape.273 = f32[128,4,512]{2,1,0:T(4,128)} reshape(bf16[512,512]{1,0:T(8,128)(2,1)} %param.12) | data formatting | bytes 1572864 | tf_op jit(solution)/shard_map/reshape | solution.py:80
  27.5 1.9 reduce_sum.97
  31.4 38.5 %all-to-all-done.1 = bf16[8,256,512]{1,2,0:T(8,128)(2,1)S(1)} async-done(((bf16[8,256,512]{1,2,0:T(8,128)(2,1)}), bf16[8,256,512]{1,2,0:T(8,128)(2,1)S(1)}, u32[]{:S(2)}, u32[]{:S(2)}) %all-to-all-start.1) | async-done | bytes 2097184 | tf_op jit(solution)/shard_map/all_to_all | solution.py:56
  69.8 13.8 %all-to-all-start = ((f32[64,2,512]{2,1,0:T(2,128)}), f32[64,2,512]{2,1,0:T(2,128)S(1)}, u32[]{:S(2)}, u32[]{:S(2)}) async-start(f32[64,2,512]{2,1,0:T(2,128)} %broadcast_select_fusion), calls=%async_computation | async-start | bytes 524288 | tf_op jit(solution)/shard_map/all_to_all | solution.py:107
  83.7 19.3 %all-gather.3.cloned.1.call-done = bf16[512,4096]{0,1:T(8,128)(2,1)} async-done(((bf16[512,64]{0,1:T(8,128)(2,1)}), bf16[512,4096]{0,1:T(8,128)(2,1)}) %all-gather.3.cloned.1.call-update) | async-done | bytes 4194320 | tf_op jit(solution)/shard_map/all_gather | solution.py:86
  103.0 3.7 %convolution_convert_fusion = bf16[128,4096]{1,0:T(8,128)(2,1)S(1)} fusion(bf16[128,512]{1,0:T(8,128)(2,1)S(1)} %multiply_convert_fusion, bf16[512,4096]{0,1:T(8,128)(2,1)} %all-gather.3.cloned.1.call-done), kind=kOutput, calls=%fused_computation.8 | convolution fusion | flops 537395200 | bytes 5373952 | tf_op jit(solution)/shard_map/dot_general | solution.py:84
  106.7 2.2 %gather_fusion.1 = bf16[128,4096]{1,0:T(8,128)(2,1)} fusion(bf16[128,4096]{1,0:T(8,128)(2,1)S(1)} %convolution_convert_fusion, s32[1024]{0:T(1024)S(1)} %pad_clamp_fusion), kind=kCustom, calls=%fused_computation.1 | custom fusion | bytes 2097664 | tf_op jit(solution)/shard_map/gather | solution.py:111
  108.9 1.6 copy.49
  110.7 2.1 copy.41
  112.8 14.5 %all-to-all-start.2 = ((bf16[512,2,512]{2,1,0:T(2,128)(2,1)}), bf16[512,2,512]{2,1,0:T(2,128)(2,1)S(1)}, u32[]{:S(2)}, u32[]{:S(2)}) async-start(bf16[512,2,512]{2,1,0:T(2,128)(2,1)} %copy.41), calls=%async_computation.2 | async-start | bytes 2097152 | tf_op jit(solution)/shard_map/all_to_all | solution.py:113
  128.3 34.4 %all-to-all-done.2 = bf16[512,2,512]{2,1,0:T(2,128)(2,1)S(1)} async-done(((bf16[512,2,512]{2,1,0:T(2,128)(2,1)}), bf16[512,2,512]{2,1,0:T(2,128)(2,1)S(1)}, u32[]{:S(2)}, u32[]{:S(2)}) %all-to-all-start.2) | async-done | bytes 1048608 | tf_op jit(solution)/shard_map/all_to_all | solution.py:113
  162.7 1.1 convert_reduce_fusion
  165.2 1.1 broadcast_in_dim.74
  166.3 3.6 %all-to-all-start.3 = ((bf16[8,128,512]{1,2,0:T(8,128)(2,1)}), bf16[8,128,512]{1,2,0:T(8,128)(2,1)S(1)}, u32[]{:S(2)}, u32[]{:S(2)}) async-start(bf16[8,128,512]{1,2,0:T(8,128)(2,1)} %broadcast_in_dim.74), calls=%async_computation.3 | async-start | bytes 2097152 | tf_op jit(solution)/shard_map/all_to_all | solution.py:56
  172.3 1.1 fusion.23
  173.9 25.1 %all-to-all-done.3 = bf16[8,128,512]{1,2,0:T(8,128)(2,1)S(1)} async-done(((bf16[8,128,512]{1,2,0:T(8,128)(2,1)}), bf16[8,128,512]{1,2,0:T(8,128)(2,1)S(1)}, u32[]{:S(2)}, u32[]{:S(2)}) %all-to-all-start.3) | async-done | bytes 1048608 | tf_op jit(solution)/shard_map/all_to_all | solution.py:56
  199.0 1.0 fusion.13
  200.1 2.9 %fusion = (f32[384]{0:T(512)S(1)}, bf16[384,4096]{1,0:T(8,128)(2,1)}) fusion(f32[384,4096]{1,0:T(8,128)S(1)} %fusion.13, bf16[256,4096]{0,1:T(8,128)(2,1)S(1)} %bitcast.36, s32[384]{0:T(512)S(1)} %get-tuple-element.21, pred[384]{0:T(512)(128)(4,1)S(1)} %get-tuple-element.9), kind=kOutput, calls=%fused_computation.4 | convolution fusion | flops 813366912 | bytes 11537792 | tf_op jit(solution)/shard_map/dot_general | solution.py:145
  203.0 6.7 %fusion.3 = f32[384,768]{0,1:T(8,128)S(1)} fusion(bf16[4096,768]{1,0:T(8,128)(2,1)} %all-gather.5.cloned.1.call-done, bf16[384,4096]{1,0:T(8,128)(2,1)} %get-tuple-element.19, f32[4096]{0:T(1024)S(1)} %copy-done.1, f32[384]{0:T(512)S(1)} %add_rsqrt_fusion), kind=kOutput, calls=%fused_computation.9 | convolution fusion | flops 2422210560 | bytes 10634752 | tf_op jit(solution)/shard_map/dot_general | solution.py:149
  209.9 1.1 copy.46
  (49 shorter events, 9.3 us)
Async XLA Ops:
  6.5 96.5 %all-gather.3.cloned.1.call-start = ((), (), s32[]{:S(2)}) async-start(), calls=%async_computation.4 | async-start | bytes 4259840 | tf_op jit(solution)/shard_map/all_gather | solution.py:86
  7.3 195.7 %all-gather.5.cloned.1.call-start = ((), (), s32[]{:S(2)}) async-start(), calls=%async_computation.5 | async-start | bytes 6389760 | tf_op jit(solution)/shard_map/all_gather | solution.py:147
  9.1 12.3 %copy-start.2 = (s32[128,2]{0,1:T(2,128)S(1)}, s32[128,2]{0,1:T(2,128)}, u32[]{:S(2)}) copy-start(s32[128,2]{0,1:T(2,128)} %param.18) | copy-start | bytes 3076
  9.1 12.3 %copy-start.3 = (s32[128]{0:T(128)S(1)}, s32[128]{0:T(128)}, u32[]{:S(2)}) copy-start(s32[128]{0:T(128)} %param.19) | copy-start | bytes 1540
  10.6 59.3 %all-to-all-start.1 = ((bf16[8,256,512]{1,2,0:T(8,128)(2,1)}), bf16[8,256,512]{1,2,0:T(8,128)(2,1)S(1)}, u32[]{:S(2)}, u32[]{:S(2)}) async-start(bf16[8,256,512]{1,2,0:T(8,128)(2,1)} %broadcast_in_dim.72), calls=%async_computation.1 | async-start | bytes 4194304 | tf_op jit(solution)/shard_map/all_to_all | solution.py:56
  69.8 43.0 %all-to-all-start = ((f32[64,2,512]{2,1,0:T(2,128)}), f32[64,2,512]{2,1,0:T(2,128)S(1)}, u32[]{:S(2)}, u32[]{:S(2)}) async-start(f32[64,2,512]{2,1,0:T(2,128)} %broadcast_select_fusion), calls=%async_computation | async-start | bytes 524288 | tf_op jit(solution)/shard_map/all_to_all | solution.py:107
  110.7 53.3 %copy-start = (f32[512]{0:T(512)S(1)}, f32[512]{0:T(512)}, u32[]{:S(2)}) copy-start(f32[512]{0:T(512)} %param.14) | copy-start | bytes 6148
  112.8 49.9 %all-to-all-start.2 = ((bf16[512,2,512]{2,1,0:T(2,128)(2,1)}), bf16[512,2,512]{2,1,0:T(2,128)(2,1)S(1)}, u32[]{:S(2)}, u32[]{:S(2)}) async-start(bf16[512,2,512]{2,1,0:T(2,128)(2,1)} %copy.41), calls=%async_computation.2 | async-start | bytes 2097152 | tf_op jit(solution)/shard_map/all_to_all | solution.py:113
  166.3 32.7 %all-to-all-start.3 = ((bf16[8,128,512]{1,2,0:T(8,128)(2,1)}), bf16[8,128,512]{1,2,0:T(8,128)(2,1)S(1)}, u32[]{:S(2)}, u32[]{:S(2)}) async-start(bf16[8,128,512]{1,2,0:T(8,128)(2,1)} %broadcast_in_dim.74), calls=%async_computation.3 | async-start | bytes 2097152 | tf_op jit(solution)/shard_map/all_to_all | solution.py:56
  200.1 2.9 %copy-start.1 = (f32[4096]{0:T(1024)S(1)}, f32[4096]{0:T(1024)}, u32[]{:S(2)}) copy-start(f32[4096]{0:T(1024)} %param.20) | copy-start | bytes 49156
Sparse Core Ops, SparseCore 0:
  10.7 92.2 all-gather.2
  106.4 87.6 all-gather.4

commit v6 on v4

--- a/solution.py
+++ b/solution.py
@@ -123,8 +123,6 @@
         axis=3,
     ).reshape(own_part.shape[0], -1)
     tp_count = lax.axis_size("tp")
-    full_prompt = gather_features(prompt[0], tp_count)
-    full_prompt, partial_value = lax.optimization_barrier((full_prompt, partial_value))
     block_terms = partial_value.astype(jnp.bfloat16).reshape(
         -1, tp_count, feature_width
     ).transpose(1, 0, 2)
@@ -176,6 +174,7 @@
         jnp.bfloat16
     )
     full_image = gather_features(arrived, tp_count)
+    full_prompt = lax.all_gather(prompt[0], "tp", axis=1, tiled=True)
     embedded = (
         jnp.dot(image_pick, full_image, preferred_element_type=jnp.float32)
         + jnp.dot(prompt_pick, full_prompt, preferred_element_type=jnp.float32)

time: 221 us -> 203 us (0.919)
  waiting for transfers between devices: 82 us -> 66 us
  starting transfers between devices: 67.4 us -> 62.1 us
  matrix products: 12.9 us -> 17.3 us
    all_to_all x2 -> x1, waiting for transfers between devices: 46.5 us -> 22.5 us  [gather_features(): blocks = lax.all_to_all(copies, 'tp', 0, 0, tiled=True)]
    all_to_all x2 -> x1, starting transfers between devices: 15.8 us -> 3.74 us  [gather_features(): blocks = lax.all_to_all(copies, 'tp', 0, 0, tiled=True)]
    all_to_all x1, starting transfers between devices: 3.9 us -> 7.87 us  [shards(): lax.all_to_all(block_terms, 'tp', 0, 0, tiled=True).astype(jnp.float32)]
    all_to_all x1, waiting for transfers between devices: 23.1 us -> 26.9 us  [shards(): lax.all_to_all(block_terms, 'tp', 0, 0, tiled=True).astype(jnp.float32)]
    ppermute x12, waiting for transfers between devices: 10.4 us -> 14 us  [shift(): lax.ppermute(value, axis, [(k, (k + step) % size) for k in range(size)])]
    ppermute x1, starting transfers between devices: 7.36 us -> 10.2 us  [shards(): other_half = lax.ppermute(own_half, 'rc', [(0, 1), (1, 0)])]
    dot_general x1, matrix products: 1.03 us -> 3.69 us  [shards(): jnp.dot(image_pick, full_image, preferred_element_type=jnp.float32)]
    unnamed x30 -> x28, local copies, waits for them, and re-layouts: 6.27 us -> 6.26 us
  transfers between devices with their start and end apart: 17 -> 17, of which waited for: 7 -> 8; matrix products, arithmetic and copies ran while one was open for 13% -> 16% of each run, Pallas kernels for 0% -> 0%
where the time goes in v6:
time: 203 us; the launch traced here: 202 us
  waiting for transfers between devices  66 us (33%)
  starting transfers between devices  62.1 us (31%)
  blocking collectives  19.4 us (10%)
  matrix products  17.3 us (9%)
  between operations  15.9 us (8%)
  local copies, waits for them, and re-layouts  14.4 us (7%)
  other arithmetic  6.97 us (3%)
    ppermute x12, starting transfers between devices, shift(): lax.ppermute(value, axis, [(k, (k + step) % size) for k in range(size)])  40.3 us
    all_to_all x1, waiting for transfers between devices, shards(): lax.all_to_all(block_terms, 'tp', 0, 0, tiled=True).astype(jnp.float32)  26.9 us
    all_to_all x1, waiting for transfers between devices, gather_features(): blocks = lax.all_to_all(copies, 'tp', 0, 0, tiled=True)  22.5 us
    all_to_all x1, blocking collectives, shards(): lax.all_to_all(outgoing.reshape(requests, capacity, feature_width), REQ,...  19.4 us
    ppermute x12, waiting for transfers between devices, shift(): lax.ppermute(value, axis, [(k, (k + step) % size) for k in range(size)])  14 us
    ppermute x1, starting transfers between devices, shards(): other_half = lax.ppermute(own_half, 'rc', [(0, 1), (1, 0)])  10.2 us
    all_to_all x1, starting transfers between devices, shards(): lax.all_to_all(block_terms, 'tp', 0, 0, tiled=True).astype(jnp.float32)  7.87 us
    unnamed x28, local copies, waits for them, and re-layouts  6.26 us
  transfers between devices with their start and end apart: 17, of which 8 were waited for; matrix products, arithmetic and copies ran while one was open for 16% of the time, Pallas kernels for 0%

profile of v6, /device:TPU:1, one launch (start us, length us, event | category | flops | bytes accessed | tf_op | source)
XLA Modules:
  0.0 202.1 jit_solution(6564715590776921020)
XLA Ops:
  7.3 5.9 %collective-permute-start = (bf16[512,64]{0,1:T(8,128)(2,1)}, bf16[512,64]{0,1:T(8,128)(2,1)S(1)}, u32[]{:S(2)}, u32[]{:S(2)}) collective-permute-start(bf16[512,64]{0,1:T(8,128)(2,1)} %param.13), channel_id=1, source_target_pairs={{0,112},{16,0},{32,16},{48,32},{64,48},{80,64},{96,80},{112,96},{1... | collective-permute-start | bytes 196616 | tf_op jit(solution)/shard_map/ppermute | solution.py:63
  13.2 1.9 collective-permute-start.3
  16.1 4.6 %collective-permute-start.1 = (bf16[512,64]{0,1:T(8,128)(2,1)S(1)}, bf16[512,64]{0,1:T(8,128)(2,1)S(1)}, u32[]{:S(2)}, u32[]{:S(2)}) collective-permute-start(bf16[512,64]{0,1:T(8,128)(2,1)S(1)} %collective-permute-done), channel_id=1, source_target_pairs={{0,112},{16,0},{32,16},{48,32},{64,48},{80,64},{96,80},{112,96},{1... | collective-permute-start | bytes 196616 | tf_op jit(solution)/shard_map/ppermute | solution.py:63
  20.6 1.9 collective-permute-start.4
  22.6 4.6 %collective-permute-start.2 = (bf16[512,64]{0,1:T(8,128)(2,1)S(1)}, bf16[512,64]{0,1:T(8,128)(2,1)S(1)}, u32[]{:S(2)}, u32[]{:S(2)}) collective-permute-start(bf16[512,64]{0,1:T(8,128)(2,1)S(1)} %collective-permute-done.1), channel_id=1, source_target_pairs={{0,112},{16,0},{32,16},{48,32},{64,48},{80,64},{96,80},{112,96},{1... | collective-permute-start | bytes 196616 | tf_op jit(solution)/shard_map/ppermute | solution.py:63
  27.2 1.9 collective-permute-start.5
  29.1 4.3 %collective-permute-done.5 = bf16[512,64]{0,1:T(8,128)(2,1)S(1)} collective-permute-done((bf16[512,64]{0,1:T(8,128)(2,1)S(1)}, bf16[512,64]{0,1:T(8,128)(2,1)S(1)}, u32[]{:S(2)}, u32[]{:S(2)}) %collective-permute-start.5) | collective-permute-done | bytes 65568 | tf_op jit(solution)/shard_map/ppermute | solution.py:63
  35.4 4.6 %collective-permute-start.7 = (bf16[512,32]{0,1:T(8,128)(2,1)S(1)}, bf16[512,32]{0,1:T(8,128)(2,1)S(1)}, u32[]{:S(2)}, u32[]{:S(2)}) collective-permute-start(bf16[512,32]{0,1:T(8,128)(2,1)S(1)} %slice.41), channel_id=1, source_target_pairs={{0,112},{16,0},{32,16},{48,32},{64,48},{80,64},{96,80},{112,96},{1... | collective-permute-start | bytes 98312 | tf_op jit(solution)/shard_map/ppermute | solution.py:63
  42.8 3.1 %collective-permute-start.9 = (bf16[8,512,64]{1,2,0:T(8,128)(2,1)S(1)}, bf16[8,512,64]{1,2,0:T(8,128)(2,1)S(1)}, u32[]{:S(2)}, u32[]{:S(2)}) collective-permute-start(bf16[8,512,64]{1,2,0:T(8,128)(2,1)S(1)} %get-tuple-element.10), channel_id=1, source_target_pairs={{0,128},{128,256},{256,384},{384,0},{1,129},{129,257},{257,385},{3... | collective-permute-start | bytes 1572872 | tf_op jit(solution)/shard_map/ppermute | solution.py:63
  46.0 3.4 %collective-permute-start.8 = (bf16[8,512,64]{1,2,0:T(8,128)(2,1)S(1)}, bf16[8,512,64]{1,2,0:T(8,128)(2,1)S(1)}, u32[]{:S(2)}, u32[]{:S(2)}) collective-permute-start(bf16[8,512,64]{1,2,0:T(8,128)(2,1)S(1)} %get-tuple-element.10), channel_id=1, source_target_pairs={{0,384},{128,0},{256,128},{384,256},{1,385},{129,1},{257,129},{385... | collective-permute-start | bytes 1572872 | tf_op jit(solution)/shard_map/ppermute | solution.py:63
  49.3 5.0 %collective-permute-done.9 = bf16[8,512,64]{1,2,0:T(8,128)(2,1)S(1)} collective-permute-done((bf16[8,512,64]{1,2,0:T(8,128)(2,1)S(1)}, bf16[8,512,64]{1,2,0:T(8,128)(2,1)S(1)}, u32[]{:S(2)}, u32[]{:S(2)}) %collective-permute-start.9) | collective-permute-done | bytes 524320 | tf_op jit(solution)/shard_map/ppermute | solution.py:63
  54.4 1.9 collective-permute-start.10
  56.3 4.6 %collective-permute-start.11 = (bf16[8,512,32]{1,2,0:T(8,128)(2,1)S(1)}, bf16[8,512,32]{1,2,0:T(8,128)(2,1)S(1)}, u32[]{:S(2)}, u32[]{:S(2)}) collective-permute-start(bf16[8,512,32]{1,2,0:T(8,128)(2,1)S(1)} %slice.43), channel_id=1, source_target_pairs={{0,384},{128,0},{256,128},{384,256},{1,385},{129,1},{257,129},{385... | collective-permute-start | bytes 786440 | tf_op jit(solution)/shard_map/ppermute | solution.py:63
  61.8 1.9 collective-permute-done.10
  72.5 10.2 %collective-permute-start.12 = (bf16[4,8,512,64]{2,3,1,0:T(8,128)(2,1)S(1)}, bf16[4,8,512,64]{2,3,1,0:T(8,128)(2,1)}, u32[]{:S(2)}, u32[]{:S(2)}) collective-permute-start(bf16[4,8,512,64]{2,3,1,0:T(8,128)(2,1)S(1)} %constant_dynamic-slice_fusion), channel_id=1, source_target_pairs={{0,8},{8,0},{1,9},{9,1},{2,10},{10,2},{3,11},{11,3},{4,12},{12,4},... | collective-permute-start | bytes 6291464 | tf_op jit(solution)/shard_map/ppermute | solution.py:113
  86.6 2.3 %fusion.28 = bf16[128,4,8,64]{0,3,2,1:T(8,128)(2,1)S(1)} fusion(bf16[4,8,512,64]{2,3,1,0:T(8,128)(2,1)} %collective-permute-done.12, f32[128,512]{1,0:T(8,128)S(1)} %reduce_sum.87), kind=kOutput, calls=%fused_computation.66 | convolution fusion | flops 268566528 | bytes 2883584 | tf_op jit(solution)/shard_map/gk,xykn->gxyn/dot_general | solution.py:118
  90.8 7.9 %all-to-all-start = ((bf16[8,128,512]{1,2,0:T(8,128)(2,1)}), bf16[8,128,512]{1,2,0:T(8,128)(2,1)S(1)}, u32[]{:S(2)}, u32[]{:S(2)}) async-start(bf16[8,128,512]{1,2,0:T(8,128)(2,1)} %bitcast.21), calls=%async_computation | async-start | bytes 2097152 | tf_op jit(solution)/shard_map/all_to_all | solution.py:130
  101.1 26.9 %all-to-all-done = bf16[8,128,512]{1,2,0:T(8,128)(2,1)S(1)} async-done(((bf16[8,128,512]{1,2,0:T(8,128)(2,1)}), bf16[8,128,512]{1,2,0:T(8,128)(2,1)S(1)}, u32[]{:S(2)}, u32[]{:S(2)}) %all-to-all-start) | async-done | bytes 1048608 | tf_op jit(solution)/shard_map/all_to_all | solution.py:130
  128.5 19.4 %all_to_all.15 = bf16[64,2,512]{2,1,0:T(2,128)(2,1)S(1)} all-to-all(bf16[64,2,512]{2,1,0:T(2,128)(2,1)S(1)} %reshape.204), channel_id=1, replica_groups=mesh['rx'=4,'ry'=8,'rc'=2,'tp'=8] {'rx','ry','rc'}, dimensions={0} | all-to-all | bytes 262144 | tf_op jit(solution)/shard_map/all_to_all | solution.py:148
  149.2 3.7 %all-to-all-start.2 = ((bf16[8,128,512]{1,2,0:T(8,128)(2,1)}), bf16[8,128,512]{1,2,0:T(8,128)(2,1)S(1)}, u32[]{:S(2)}, u32[]{:S(2)}) async-start(bf16[8,128,512]{1,2,0:T(8,128)(2,1)} %broadcast_in_dim.22), calls=%async_computation.2 | async-start | bytes 2097152 | tf_op jit(solution)/shard_map/all_to_all | solution.py:57
  157.3 22.5 %all-to-all-done.2 = bf16[8,128,512]{1,2,0:T(8,128)(2,1)S(1)} async-done(((bf16[8,128,512]{1,2,0:T(8,128)(2,1)}), bf16[8,128,512]{1,2,0:T(8,128)(2,1)S(1)}, u32[]{:S(2)}, u32[]{:S(2)}) %all-to-all-start.2) | async-done | bytes 1048608 | tf_op jit(solution)/shard_map/all_to_all | solution.py:57
  179.8 3.7 %fusion.17 = f32[384,4096]{1,0:T(8,128)} fusion(bf16[128,4096]{0,1:T(8,128)(2,1)S(1)} %bitcast.79, s32[384]{0:T(512)S(1)} %get-tuple-element.20, pred[384]{0:T(512)(128)(4,1)S(1)} %get-tuple-element.6), kind=kOutput, calls=%fused_computation.38 | convolution fusion | flops 402751488 | bytes 7341952 | tf_op jit(solution)/shard_map/dot_general | solution.py:179
  183.5 4.6 %fusion = (f32[384]{0:T(512)S(1)}, bf16[384,4096]{1,0:T(8,128)(2,1)S(1)}) fusion(f32[384,4096]{1,0:T(8,128)} %fusion.17, bf16[1,256,4096]{2,1,0:T(8,128)(2,1)} %all-gather.6.cloned.1.call-done, s32[384]{0:T(512)S(1)} %get-tuple-element.21, pred[384]{0:T(512)(128)(4,1)S(1)} %get-tuple-element.5), kind=kOutput, calls=%fused_computation.2 | convolution fusion | flops 813366912 | bytes 11537792 | tf_op jit(solution)/shard_map/dot_general | solution.py:180
  188.1 5.8 %fusion.3 = f32[384,768]{0,1:T(8,128)S(1)} fusion(bf16[4096,768]{1,0:T(8,128)(2,1)} %all-gather.4.cloned.1.call-done, bf16[384,4096]{1,0:T(8,128)(2,1)S(1)} %get-tuple-element.19, f32[4096]{0:T(1024)S(1)} %copy-done.2, f32[384]{0:T(512)S(1)} %add_rsqrt_fusion), kind=kOutput, calls=%fused_computation.6 | convolution fusion | flops 2422210560 | bytes 10634752 | tf_op jit(solution)/shard_map/dot_general | solution.py:184
  (90 shorter events, 29.6 us)
Async XLA Ops:
  6.5 176.9 %all-gather.6.cloned.1.call-start = ((), (), s32[]{:S(2)}) async-start(), calls=%async_computation.4 | async-start | bytes 2359296 | tf_op jit(solution)/shard_map/all_gather | solution.py:177
  7.3 180.9 %all-gather.4.cloned.1.call-start = ((), (), s32[]{:S(2)}) async-start(), calls=%async_computation.3 | async-start | bytes 6389760 | tf_op jit(solution)/shard_map/all_gather | solution.py:182
  7.3 8.8 %collective-permute-start = (bf16[512,64]{0,1:T(8,128)(2,1)}, bf16[512,64]{0,1:T(8,128)(2,1)S(1)}, u32[]{:S(2)}, u32[]{:S(2)}) collective-permute-start(bf16[512,64]{0,1:T(8,128)(2,1)} %param.13), channel_id=1, source_target_pairs={{0,112},{16,0},{32,16},{48,32},{64,48},{80,64},{96,80},{112,96},{1... | collective-permute-start | bytes 196616 | tf_op jit(solution)/shard_map/ppermute | solution.py:63
  13.2 7.4 %collective-permute-start.3 = (bf16[512,64]{0,1:T(8,128)(2,1)}, bf16[512,64]{0,1:T(8,128)(2,1)S(1)}, u32[]{:S(2)}, u32[]{:S(2)}) collective-permute-start(bf16[512,64]{0,1:T(8,128)(2,1)} %param.13), channel_id=1, source_target_pairs={{0,16},{16,32},{32,48},{48,64},{64,80},{80,96},{96,112},{112,0},{1... | collective-permute-start | bytes 196616 | tf_op jit(solution)/shard_map/ppermute | solution.py:63
  16.1 6.5 %collective-permute-start.1 = (bf16[512,64]{0,1:T(8,128)(2,1)S(1)}, bf16[512,64]{0,1:T(8,128)(2,1)S(1)}, u32[]{:S(2)}, u32[]{:S(2)}) collective-permute-start(bf16[512,64]{0,1:T(8,128)(2,1)S(1)} %collective-permute-done), channel_id=1, source_target_pairs={{0,112},{16,0},{32,16},{48,32},{64,48},{80,64},{96,80},{112,96},{1... | collective-permute-start | bytes 196616 | tf_op jit(solution)/shard_map/ppermute | solution.py:63
  20.6 6.5 %collective-permute-start.4 = (bf16[512,64]{0,1:T(8,128)(2,1)S(1)}, bf16[512,64]{0,1:T(8,128)(2,1)S(1)}, u32[]{:S(2)}, u32[]{:S(2)}) collective-permute-start(bf16[512,64]{0,1:T(8,128)(2,1)S(1)} %collective-permute-done.3), channel_id=1, source_target_pairs={{0,16},{16,32},{32,48},{48,64},{64,80},{80,96},{96,112},{112,0},{1... | collective-permute-start | bytes 196616 | tf_op jit(solution)/shard_map/ppermute | solution.py:63
  22.6 12.7 %collective-permute-start.2 = (bf16[512,64]{0,1:T(8,128)(2,1)S(1)}, bf16[512,64]{0,1:T(8,128)(2,1)S(1)}, u32[]{:S(2)}, u32[]{:S(2)}) collective-permute-start(bf16[512,64]{0,1:T(8,128)(2,1)S(1)} %collective-permute-done.1), channel_id=1, source_target_pairs={{0,112},{16,0},{32,16},{48,32},{64,48},{80,64},{96,80},{112,96},{1... | collective-permute-start | bytes 196616 | tf_op jit(solution)/shard_map/ppermute | solution.py:63
  27.2 6.2 %collective-permute-start.5 = (bf16[512,64]{0,1:T(8,128)(2,1)S(1)}, bf16[512,64]{0,1:T(8,128)(2,1)S(1)}, u32[]{:S(2)}, u32[]{:S(2)}) collective-permute-start(bf16[512,64]{0,1:T(8,128)(2,1)S(1)} %collective-permute-done.4), channel_id=1, source_target_pairs={{0,16},{16,32},{32,48},{48,64},{64,80},{80,96},{96,112},{112,0},{1... | collective-permute-start | bytes 196616 | tf_op jit(solution)/shard_map/ppermute | solution.py:63
  33.4 6.5 %collective-permute-start.6 = (bf16[512,32]{0,1:T(8,128)(2,1)S(1)}, bf16[512,32]{0,1:T(8,128)(2,1)S(1)}, u32[]{:S(2)}, u32[]{:S(2)}) collective-permute-start(bf16[512,32]{0,1:T(8,128)(2,1)S(1)} %slice.40), channel_id=1, source_target_pairs={{0,16},{16,32},{32,48},{48,64},{64,80},{80,96},{96,112},{112,0},{1... | collective-permute-start | bytes 98312 | tf_op jit(solution)/shard_map/ppermute | solution.py:63
  35.4 5.6 %collective-permute-start.7 = (bf16[512,32]{0,1:T(8,128)(2,1)S(1)}, bf16[512,32]{0,1:T(8,128)(2,1)S(1)}, u32[]{:S(2)}, u32[]{:S(2)}) collective-permute-start(bf16[512,32]{0,1:T(8,128)(2,1)S(1)} %slice.41), channel_id=1, source_target_pairs={{0,112},{16,0},{32,16},{48,32},{64,48},{80,64},{96,80},{112,96},{1... | collective-permute-start | bytes 98312 | tf_op jit(solution)/shard_map/ppermute | solution.py:63
  42.8 11.5 %collective-permute-start.9 = (bf16[8,512,64]{1,2,0:T(8,128)(2,1)S(1)}, bf16[8,512,64]{1,2,0:T(8,128)(2,1)S(1)}, u32[]{:S(2)}, u32[]{:S(2)}) collective-permute-start(bf16[8,512,64]{1,2,0:T(8,128)(2,1)S(1)} %get-tuple-element.10), channel_id=1, source_target_pairs={{0,128},{128,256},{256,384},{384,0},{1,129},{129,257},{257,385},{3... | collective-permute-start | bytes 1572872 | tf_op jit(solution)/shard_map/ppermute | solution.py:63
  46.0 10.4 %collective-permute-start.8 = (bf16[8,512,64]{1,2,0:T(8,128)(2,1)S(1)}, bf16[8,512,64]{1,2,0:T(8,128)(2,1)S(1)}, u32[]{:S(2)}, u32[]{:S(2)}) collective-permute-start(bf16[8,512,64]{1,2,0:T(8,128)(2,1)S(1)} %get-tuple-element.10), channel_id=1, source_target_pairs={{0,384},{128,0},{256,128},{384,256},{1,385},{129,1},{257,129},{385... | collective-permute-start | bytes 1572872 | tf_op jit(solution)/shard_map/ppermute | solution.py:63
  54.4 9.4 %collective-permute-start.10 = (bf16[8,512,32]{1,2,0:T(8,128)(2,1)S(1)}, bf16[8,512,32]{1,2,0:T(8,128)(2,1)S(1)}, u32[]{:S(2)}, u32[]{:S(2)}) collective-permute-start(bf16[8,512,32]{1,2,0:T(8,128)(2,1)S(1)} %slice.42), channel_id=1, source_target_pairs={{0,128},{128,256},{256,384},{384,0},{1,129},{129,257},{257,385},{3... | collective-permute-start | bytes 786440 | tf_op jit(solution)/shard_map/ppermute | solution.py:63
  56.3 9.2 %collective-permute-start.11 = (bf16[8,512,32]{1,2,0:T(8,128)(2,1)S(1)}, bf16[8,512,32]{1,2,0:T(8,128)(2,1)S(1)}, u32[]{:S(2)}, u32[]{:S(2)}) collective-permute-start(bf16[8,512,32]{1,2,0:T(8,128)(2,1)S(1)} %slice.43), channel_id=1, source_target_pairs={{0,384},{128,0},{256,128},{384,256},{1,385},{129,1},{257,129},{385... | collective-permute-start | bytes 786440 | tf_op jit(solution)/shard_map/ppermute | solution.py:63
  72.5 14.1 %collective-permute-start.12 = (bf16[4,8,512,64]{2,3,1,0:T(8,128)(2,1)S(1)}, bf16[4,8,512,64]{2,3,1,0:T(8,128)(2,1)}, u32[]{:S(2)}, u32[]{:S(2)}) collective-permute-start(bf16[4,8,512,64]{2,3,1,0:T(8,128)(2,1)S(1)} %constant_dynamic-slice_fusion), channel_id=1, source_target_pairs={{0,8},{8,0},{1,9},{9,1},{2,10},{10,2},{3,11},{11,3},{4,12},{12,4},... | collective-permute-start | bytes 6291464 | tf_op jit(solution)/shard_map/ppermute | solution.py:113
  88.9 9.8 %copy-start.3 = (s32[128,2]{0,1:T(2,128)S(1)}, s32[128,2]{0,1:T(2,128)}, u32[]{:S(2)}) copy-start(s32[128,2]{0,1:T(2,128)} %param.18) | copy-start | bytes 3076
  88.9 9.8 %copy-start.4 = (s32[128]{0:T(128)S(1)}, s32[128]{0:T(128)}, u32[]{:S(2)}) copy-start(s32[128]{0:T(128)} %param.19) | copy-start | bytes 1540
  89.6 9.5 %copy-start = (bf16[512,512]{1,0:T(8,128)(2,1)S(1)}, bf16[512,512]{1,0:T(8,128)(2,1)}, u32[]{:S(2)}) copy-start(bf16[512,512]{1,0:T(8,128)(2,1)} %param.12) | copy-start | bytes 1572868
  89.7 38.5 %copy-start.1 = (f32[512]{0:T(512)S(1)}, f32[512]{0:T(512)}, u32[]{:S(2)}) copy-start(f32[512]{0:T(512)} %param.14) | copy-start | bytes 6148
  90.8 37.1 %all-to-all-start = ((bf16[8,128,512]{1,2,0:T(8,128)(2,1)}), bf16[8,128,512]{1,2,0:T(8,128)(2,1)S(1)}, u32[]{:S(2)}, u32[]{:S(2)}) async-start(bf16[8,128,512]{1,2,0:T(8,128)(2,1)} %bitcast.21), calls=%async_computation | async-start | bytes 2097152 | tf_op jit(solution)/shard_map/all_to_all | solution.py:130
  149.2 30.5 %all-to-all-start.2 = ((bf16[8,128,512]{1,2,0:T(8,128)(2,1)}), bf16[8,128,512]{1,2,0:T(8,128)(2,1)S(1)}, u32[]{:S(2)}, u32[]{:S(2)}) async-start(bf16[8,128,512]{1,2,0:T(8,128)(2,1)} %broadcast_in_dim.22), calls=%async_computation.2 | async-start | bytes 2097152 | tf_op jit(solution)/shard_map/all_to_all | solution.py:57
  183.5 4.7 %copy-start.2 = (f32[4096]{0:T(1024)S(1)}, f32[4096]{0:T(1024)}, u32[]{:S(2)}) copy-start(f32[4096]{0:T(1024)} %param.20) | copy-start | bytes 49156
Sparse Core Ops, SparseCore 0:
  9.4 46.0 all-gather.5
  58.9 90.3 all-gather.3

commit v7 on v6

--- a/solution.py
+++ b/solution.py
@@ -65,20 +65,7 @@
 
 def ring_gather(value, axis):
     size = lax.axis_size(axis)
-    forward, backward = value, value
-    after = {}
-    for step in range(1, size // 2 + 1):
-        if step == size // 2 and size % 2 == 0:
-            half = value.shape[-1] // 2
-            left = shift(forward[..., :half], axis, 1)
-            right = shift(backward[..., half:], axis, -1)
-            after[step] = jnp.concatenate([left, right], axis=-1)
-            break
-        forward = shift(forward, axis, 1)
-        backward = shift(backward, axis, -1)
-        after[size - step] = forward
-        after[step] = backward
-    relative = jnp.stack([value] + [after[step] for step in range(1, size)], axis=0)
+    relative = jnp.stack([value] + [shift(value, axis, -step) for step in range(1, size)], axis=0)
     return jnp.roll(relative, lax.axis_index(axis), axis=0)
 
 

time: 203 us -> 203 us (level)
  waiting for transfers between devices: 66 us -> 78.9 us
  starting transfers between devices: 62.1 us -> 52.2 us
  blocking collectives: 19.4 us -> 16.9 us
    ppermute x12 -> x10, waiting for transfers between devices: 14 us -> 26.8 us  [shift(): lax.ppermute(value, axis, [(k, (k + step) % size) for k in range(size)])]
    ppermute x1, starting transfers between devices: 10.2 us -> 2.4 us  [shards(): other_half = lax.ppermute(own_half, 'rc', [(0, 1), (1, 0)])]
    ppermute x12 -> x10, starting transfers between devices: 40.3 us -> 36 us  [shift(): lax.ppermute(value, axis, [(k, (k + step) % size) for k in range(size)])]
    all_to_all x1, blocking collectives: 19.4 us -> 16.9 us  [shards(): lax.all_to_all(outgoing.reshape(requests, capacity, feature_width), REQ,...]
    all_to_all x1, starting transfers between devices: 7.87 us -> 10 us  [shards(): lax.all_to_all(block_terms, 'tp', 0, 0, tiled=True).astype(jnp.float32)]
    unnamed x28 -> x32, local copies, waits for them, and re-layouts: 6.26 us -> 7.96 us
  transfers between devices with their start and end apart: 17 -> 15, of which waited for: 8 -> 8; matrix products, arithmetic and copies ran while one was open for 16% -> 16% of each run, Pallas kernels for 0% -> 0%
where the time goes in v7:
time: 203 us; the launch traced here: 202 us
  waiting for transfers between devices  78.9 us (39%)
  starting transfers between devices  52.2 us (26%)
  matrix products  17.3 us (9%)
  blocking collectives  16.9 us (8%)
  local copies, waits for them, and re-layouts  16 us (8%)
  between operations  15.8 us (8%)
  other arithmetic  5.2 us (3%)
    ppermute x10, starting transfers between devices, shift(): lax.ppermute(value, axis, [(k, (k + step) % size) for k in range(size)])  36 us
    all_to_all x1, waiting for transfers between devices, shards(): lax.all_to_all(block_terms, 'tp', 0, 0, tiled=True).astype(jnp.float32)  26.9 us
    ppermute x10, waiting for transfers between devices, shift(): lax.ppermute(value, axis, [(k, (k + step) % size) for k in range(size)])  26.8 us
    all_to_all x1, waiting for transfers between devices, gather_features(): blocks = lax.all_to_all(copies, 'tp', 0, 0, tiled=True)  22.6 us
    all_to_all x1, blocking collectives, shards(): lax.all_to_all(outgoing.reshape(requests, capacity, feature_width), REQ,...  16.9 us
    all_to_all x1, starting transfers between devices, shards(): lax.all_to_all(block_terms, 'tp', 0, 0, tiled=True).astype(jnp.float32)  10 us
    unnamed x32, local copies, waits for them, and re-layouts  7.96 us
    dot_general x1, matrix products, shards(): projected = jnp.dot(normed, full_weight, preferred_element_type=jnp.float32)  5.77 us
  transfers between devices with their start and end apart: 15, of which 8 were waited for; matrix products, arithmetic and copies ran while one was open for 16% of the time, Pallas kernels for 0%

profile of v7, /device:TPU:1, one launch (start us, length us, event | category | flops | bytes accessed | tf_op | source)
XLA Modules:
  0.0 202.4 jit_solution(6001533092742010005)
XLA Ops:
  7.3 5.9 %collective-permute-start = (bf16[512,64]{0,1:T(8,128)(2,1)}, bf16[512,64]{0,1:T(8,128)(2,1)S(1)}, u32[]{:S(2)}, u32[]{:S(2)}) collective-permute-start(bf16[512,64]{0,1:T(8,128)(2,1)} %param.13), channel_id=1, source_target_pairs={{0,112},{16,0},{32,16},{48,32},{64,48},{80,64},{96,80},{112,96},{1... | collective-permute-start | bytes 196616 | tf_op jit(solution)/shard_map/ppermute | solution.py:63
  13.2 3.8 %collective-permute-start.1 = (bf16[512,64]{0,1:T(8,128)(2,1)}, bf16[512,64]{0,1:T(8,128)(2,1)S(1)}, u32[]{:S(2)}, u32[]{:S(2)}) collective-permute-start(bf16[512,64]{0,1:T(8,128)(2,1)} %param.13), channel_id=1, source_target_pairs={{0,96},{16,112},{32,0},{48,16},{64,32},{80,48},{96,64},{112,80},{1... | collective-permute-start | bytes 196616 | tf_op jit(solution)/shard_map/ppermute | solution.py:63
  17.0 2.8 %collective-permute-start.2 = (bf16[512,64]{0,1:T(8,128)(2,1)}, bf16[512,64]{0,1:T(8,128)(2,1)S(1)}, u32[]{:S(2)}, u32[]{:S(2)}) collective-permute-start(bf16[512,64]{0,1:T(8,128)(2,1)} %param.13), channel_id=1, source_target_pairs={{0,80},{16,96},{32,112},{48,0},{64,16},{80,32},{96,48},{112,64},{1... | collective-permute-start | bytes 196616 | tf_op jit(solution)/shard_map/ppermute | solution.py:63
  19.8 5.7 %collective-permute-start.3 = (bf16[512,64]{0,1:T(8,128)(2,1)}, bf16[512,64]{0,1:T(8,128)(2,1)S(1)}, u32[]{:S(2)}, u32[]{:S(2)}) collective-permute-start(bf16[512,64]{0,1:T(8,128)(2,1)} %param.13), channel_id=1, source_target_pairs={{0,64},{16,80},{32,96},{48,112},{64,0},{80,16},{96,32},{112,48},{1... | collective-permute-start | bytes 196616 | tf_op jit(solution)/shard_map/ppermute | solution.py:63
  25.4 1.9 collective-permute-start.4
  28.3 4.8 %collective-permute-start.5 = (bf16[512,64]{0,1:T(8,128)(2,1)}, bf16[512,64]{0,1:T(8,128)(2,1)S(1)}, u32[]{:S(2)}, u32[]{:S(2)}) collective-permute-start(bf16[512,64]{0,1:T(8,128)(2,1)} %param.13), channel_id=1, source_target_pairs={{0,32},{16,48},{32,64},{48,80},{64,96},{80,112},{96,0},{112,16},{1... | collective-permute-start | bytes 196616 | tf_op jit(solution)/shard_map/ppermute | solution.py:63
  33.1 3.2 %collective-permute-start.6 = (bf16[512,64]{0,1:T(8,128)(2,1)}, bf16[512,64]{0,1:T(8,128)(2,1)S(1)}, u32[]{:S(2)}, u32[]{:S(2)}) collective-permute-start(bf16[512,64]{0,1:T(8,128)(2,1)} %param.13), channel_id=1, source_target_pairs={{0,16},{16,32},{32,48},{48,64},{64,80},{80,96},{96,112},{112,0},{1... | collective-permute-start | bytes 196616 | tf_op jit(solution)/shard_map/ppermute | solution.py:63
  36.7 4.7 %collective-permute-done.6 = bf16[512,64]{0,1:T(8,128)(2,1)S(1)} collective-permute-done((bf16[512,64]{0,1:T(8,128)(2,1)}, bf16[512,64]{0,1:T(8,128)(2,1)S(1)}, u32[]{:S(2)}, u32[]{:S(2)}) %collective-permute-start.6) | collective-permute-done | bytes 65568 | tf_op jit(solution)/shard_map/ppermute | solution.py:63
  43.3 3.0 %collective-permute-start.7 = (bf16[8,512,64]{1,2,0:T(8,128)(2,1)S(1)}, bf16[8,512,64]{1,2,0:T(8,128)(2,1)S(1)}, u32[]{:S(2)}, u32[]{:S(2)}) collective-permute-start(bf16[8,512,64]{1,2,0:T(8,128)(2,1)S(1)} %get-tuple-element.10), channel_id=1, source_target_pairs={{0,384},{128,0},{256,128},{384,256},{1,385},{129,1},{257,129},{385... | collective-permute-start | bytes 1572872 | tf_op jit(solution)/shard_map/ppermute | solution.py:63
  46.3 2.4 %collective-permute-start.8 = (bf16[8,512,64]{1,2,0:T(8,128)(2,1)S(1)}, bf16[8,512,64]{1,2,0:T(8,128)(2,1)S(1)}, u32[]{:S(2)}, u32[]{:S(2)}) collective-permute-start(bf16[8,512,64]{1,2,0:T(8,128)(2,1)S(1)} %get-tuple-element.10), channel_id=1, source_target_pairs={{0,256},{128,384},{256,0},{384,128},{1,257},{129,385},{257,1},{385... | collective-permute-start | bytes 1572872 | tf_op jit(solution)/shard_map/ppermute | solution.py:63
  48.7 2.5 %collective-permute-start.9 = (bf16[8,512,64]{1,2,0:T(8,128)(2,1)S(1)}, bf16[8,512,64]{1,2,0:T(8,128)(2,1)S(1)}, u32[]{:S(2)}, u32[]{:S(2)}) collective-permute-start(bf16[8,512,64]{1,2,0:T(8,128)(2,1)S(1)} %get-tuple-element.10), channel_id=1, source_target_pairs={{0,128},{128,256},{256,384},{384,0},{1,129},{129,257},{257,385},{3... | collective-permute-start | bytes 1572872 | tf_op jit(solution)/shard_map/ppermute | solution.py:63
  51.3 5.2 %collective-permute-done.7 = bf16[8,512,64]{1,2,0:T(8,128)(2,1)S(1)} collective-permute-done((bf16[8,512,64]{1,2,0:T(8,128)(2,1)S(1)}, bf16[8,512,64]{1,2,0:T(8,128)(2,1)S(1)}, u32[]{:S(2)}, u32[]{:S(2)}) %collective-permute-start.7) | collective-permute-done | bytes 524320 | tf_op jit(solution)/shard_map/ppermute | solution.py:63
  57.3 2.5 %collective-permute-done.8 = bf16[8,512,64]{1,2,0:T(8,128)(2,1)S(1)} collective-permute-done((bf16[8,512,64]{1,2,0:T(8,128)(2,1)S(1)}, bf16[8,512,64]{1,2,0:T(8,128)(2,1)S(1)}, u32[]{:S(2)}, u32[]{:S(2)}) %collective-permute-start.8) | collective-permute-done | bytes 524320 | tf_op jit(solution)/shard_map/ppermute | solution.py:63
  60.7 14.1 %collective-permute-done.9 = bf16[8,512,64]{1,2,0:T(8,128)(2,1)S(1)} collective-permute-done((bf16[8,512,64]{1,2,0:T(8,128)(2,1)S(1)}, bf16[8,512,64]{1,2,0:T(8,128)(2,1)S(1)}, u32[]{:S(2)}, u32[]{:S(2)}) %collective-permute-start.9) | collective-permute-done | bytes 524320 | tf_op jit(solution)/shard_map/ppermute | solution.py:63
  80.9 2.4 %collective-permute-start.10 = (bf16[4,8,512,64]{2,3,1,0:T(8,128)(2,1)S(1)}, bf16[4,8,512,64]{2,3,1,0:T(8,128)(2,1)}, u32[]{:S(2)}, u32[]{:S(2)}) collective-permute-start(bf16[4,8,512,64]{2,3,1,0:T(8,128)(2,1)S(1)} %constant_dynamic-slice_fusion), channel_id=1, source_target_pairs={{0,8},{8,0},{1,9},{9,1},{2,10},{10,2},{3,11},{11,3},{4,12},{12,4},... | collective-permute-start | bytes 6291464 | tf_op jit(solution)/shard_map/ppermute | solution.py:100
  87.2 2.3 %fusion.26 = bf16[128,4,8,64]{0,3,2,1:T(8,128)(2,1)S(1)} fusion(bf16[4,8,512,64]{2,3,1,0:T(8,128)(2,1)} %collective-permute-done.10, f32[128,512]{1,0:T(8,128)S(1)} %reduce_sum.87), kind=kOutput, calls=%fused_computation.64 | convolution fusion | flops 268566528 | bytes 2883584 | tf_op jit(solution)/shard_map/gk,xykn->gxyn/dot_general | solution.py:105
  91.5 10.0 %all-to-all-start = ((bf16[8,128,512]{1,2,0:T(8,128)(2,1)}), bf16[8,128,512]{1,2,0:T(8,128)(2,1)S(1)}, u32[]{:S(2)}, u32[]{:S(2)}) async-start(bf16[8,128,512]{1,2,0:T(8,128)(2,1)} %bitcast.21), calls=%async_computation | async-start | bytes 2097152 | tf_op jit(solution)/shard_map/all_to_all | solution.py:117
  103.8 26.9 %all-to-all-done = bf16[8,128,512]{1,2,0:T(8,128)(2,1)S(1)} async-done(((bf16[8,128,512]{1,2,0:T(8,128)(2,1)}), bf16[8,128,512]{1,2,0:T(8,128)(2,1)S(1)}, u32[]{:S(2)}, u32[]{:S(2)}) %all-to-all-start) | async-done | bytes 1048608 | tf_op jit(solution)/shard_map/all_to_all | solution.py:117
  131.3 16.9 %all_to_all.15 = bf16[64,2,512]{2,1,0:T(2,128)(2,1)S(1)} all-to-all(bf16[64,2,512]{2,1,0:T(2,128)(2,1)S(1)} %reshape.204), channel_id=1, replica_groups=mesh['rx'=4,'ry'=8,'rc'=2,'tp'=8] {'rx','ry','rc'}, dimensions={0} | all-to-all | bytes 262144 | tf_op jit(solution)/shard_map/all_to_all | solution.py:135
  149.5 3.7 %all-to-all-start.2 = ((bf16[8,128,512]{1,2,0:T(8,128)(2,1)}), bf16[8,128,512]{1,2,0:T(8,128)(2,1)S(1)}, u32[]{:S(2)}, u32[]{:S(2)}) async-start(bf16[8,128,512]{1,2,0:T(8,128)(2,1)} %broadcast_in_dim.22), calls=%async_computation.2 | async-start | bytes 2097152 | tf_op jit(solution)/shard_map/all_to_all | solution.py:57
  157.5 22.6 %all-to-all-done.2 = bf16[8,128,512]{1,2,0:T(8,128)(2,1)S(1)} async-done(((bf16[8,128,512]{1,2,0:T(8,128)(2,1)}), bf16[8,128,512]{1,2,0:T(8,128)(2,1)S(1)}, u32[]{:S(2)}, u32[]{:S(2)}) %all-to-all-start.2) | async-done | bytes 1048608 | tf_op jit(solution)/shard_map/all_to_all | solution.py:57
  180.1 3.7 %fusion.15 = f32[384,4096]{1,0:T(8,128)} fusion(bf16[128,4096]{0,1:T(8,128)(2,1)S(1)} %bitcast.73, s32[384]{0:T(512)S(1)} %get-tuple-element.20, pred[384]{0:T(512)(128)(4,1)S(1)} %get-tuple-element.6), kind=kOutput, calls=%fused_computation.37 | convolution fusion | flops 402751488 | bytes 7341952 | tf_op jit(solution)/shard_map/dot_general | solution.py:166
  183.8 4.6 %fusion = (f32[384]{0:T(512)S(1)}, bf16[384,4096]{1,0:T(8,128)(2,1)S(1)}) fusion(f32[384,4096]{1,0:T(8,128)} %fusion.15, bf16[1,256,4096]{2,1,0:T(8,128)(2,1)} %all-gather.6.cloned.1.call-done, s32[384]{0:T(512)S(1)} %get-tuple-element.21, pred[384]{0:T(512)(128)(4,1)S(1)} %get-tuple-element.5), kind=kOutput, calls=%fused_computation.2 | convolution fusion | flops 813366912 | bytes 11537792 | tf_op jit(solution)/shard_map/dot_general | solution.py:167
  188.5 5.8 %fusion.3 = f32[384,768]{0,1:T(8,128)S(1)} fusion(bf16[4096,768]{1,0:T(8,128)(2,1)} %all-gather.4.cloned.1.call-done, bf16[384,4096]{1,0:T(8,128)(2,1)S(1)} %get-tuple-element.19, f32[4096]{0:T(1024)S(1)} %copy-done.2, f32[384]{0:T(512)S(1)} %add_rsqrt_fusion), kind=kOutput, calls=%fused_computation.6 | convolution fusion | flops 2422210560 | bytes 10634752 | tf_op jit(solution)/shard_map/dot_general | solution.py:171
  (82 shorter events, 25.1 us)
Async XLA Ops:
  6.5 177.2 %all-gather.6.cloned.1.call-start = ((), (), s32[]{:S(2)}) async-start(), calls=%async_computation.4 | async-start | bytes 2359296 | tf_op jit(solution)/shard_map/all_gather | solution.py:164
  7.3 181.2 %all-gather.4.cloned.1.call-start = ((), (), s32[]{:S(2)}) async-start(), calls=%async_computation.3 | async-start | bytes 6389760 | tf_op jit(solution)/shard_map/all_gather | solution.py:169
  7.3 21.0 %collective-permute-start = (bf16[512,64]{0,1:T(8,128)(2,1)}, bf16[512,64]{0,1:T(8,128)(2,1)S(1)}, u32[]{:S(2)}, u32[]{:S(2)}) collective-permute-start(bf16[512,64]{0,1:T(8,128)(2,1)} %param.13), channel_id=1, source_target_pairs={{0,112},{16,0},{32,16},{48,32},{64,48},{80,64},{96,80},{112,96},{1... | collective-permute-start | bytes 196616 | tf_op jit(solution)/shard_map/ppermute | solution.py:63
  13.2 19.9 %collective-permute-start.1 = (bf16[512,64]{0,1:T(8,128)(2,1)}, bf16[512,64]{0,1:T(8,128)(2,1)S(1)}, u32[]{:S(2)}, u32[]{:S(2)}) collective-permute-start(bf16[512,64]{0,1:T(8,128)(2,1)} %param.13), channel_id=1, source_target_pairs={{0,96},{16,112},{32,0},{48,16},{64,32},{80,48},{96,64},{112,80},{1... | collective-permute-start | bytes 196616 | tf_op jit(solution)/shard_map/ppermute | solution.py:63
  17.0 19.3 %collective-permute-start.2 = (bf16[512,64]{0,1:T(8,128)(2,1)}, bf16[512,64]{0,1:T(8,128)(2,1)S(1)}, u32[]{:S(2)}, u32[]{:S(2)}) collective-permute-start(bf16[512,64]{0,1:T(8,128)(2,1)} %param.13), channel_id=1, source_target_pairs={{0,80},{16,96},{32,112},{48,0},{64,16},{80,32},{96,48},{112,64},{1... | collective-permute-start | bytes 196616 | tf_op jit(solution)/shard_map/ppermute | solution.py:63
  19.8 16.6 %collective-permute-start.3 = (bf16[512,64]{0,1:T(8,128)(2,1)}, bf16[512,64]{0,1:T(8,128)(2,1)S(1)}, u32[]{:S(2)}, u32[]{:S(2)}) collective-permute-start(bf16[512,64]{0,1:T(8,128)(2,1)} %param.13), channel_id=1, source_target_pairs={{0,64},{16,80},{32,96},{48,112},{64,0},{80,16},{96,32},{112,48},{1... | collective-permute-start | bytes 196616 | tf_op jit(solution)/shard_map/ppermute | solution.py:63
  25.4 11.0 %collective-permute-start.4 = (bf16[512,64]{0,1:T(8,128)(2,1)}, bf16[512,64]{0,1:T(8,128)(2,1)S(1)}, u32[]{:S(2)}, u32[]{:S(2)}) collective-permute-start(bf16[512,64]{0,1:T(8,128)(2,1)} %param.13), channel_id=1, source_target_pairs={{0,48},{16,64},{32,80},{48,96},{64,112},{80,0},{96,16},{112,32},{1... | collective-permute-start | bytes 196616 | tf_op jit(solution)/shard_map/ppermute | solution.py:63
  28.3 8.4 %collective-permute-start.5 = (bf16[512,64]{0,1:T(8,128)(2,1)}, bf16[512,64]{0,1:T(8,128)(2,1)S(1)}, u32[]{:S(2)}, u32[]{:S(2)}) collective-permute-start(bf16[512,64]{0,1:T(8,128)(2,1)} %param.13), channel_id=1, source_target_pairs={{0,32},{16,48},{32,64},{48,80},{64,96},{80,112},{96,0},{112,16},{1... | collective-permute-start | bytes 196616 | tf_op jit(solution)/shard_map/ppermute | solution.py:63
  33.1 8.3 %collective-permute-start.6 = (bf16[512,64]{0,1:T(8,128)(2,1)}, bf16[512,64]{0,1:T(8,128)(2,1)S(1)}, u32[]{:S(2)}, u32[]{:S(2)}) collective-permute-start(bf16[512,64]{0,1:T(8,128)(2,1)} %param.13), channel_id=1, source_target_pairs={{0,16},{16,32},{32,48},{48,64},{64,80},{80,96},{96,112},{112,0},{1... | collective-permute-start | bytes 196616 | tf_op jit(solution)/shard_map/ppermute | solution.py:63
  43.3 13.2 %collective-permute-start.7 = (bf16[8,512,64]{1,2,0:T(8,128)(2,1)S(1)}, bf16[8,512,64]{1,2,0:T(8,128)(2,1)S(1)}, u32[]{:S(2)}, u32[]{:S(2)}) collective-permute-start(bf16[8,512,64]{1,2,0:T(8,128)(2,1)S(1)} %get-tuple-element.10), channel_id=1, source_target_pairs={{0,384},{128,0},{256,128},{384,256},{1,385},{129,1},{257,129},{385... | collective-permute-start | bytes 1572872 | tf_op jit(solution)/shard_map/ppermute | solution.py:63
  46.3 13.6 %collective-permute-start.8 = (bf16[8,512,64]{1,2,0:T(8,128)(2,1)S(1)}, bf16[8,512,64]{1,2,0:T(8,128)(2,1)S(1)}, u32[]{:S(2)}, u32[]{:S(2)}) collective-permute-start(bf16[8,512,64]{1,2,0:T(8,128)(2,1)S(1)} %get-tuple-element.10), channel_id=1, source_target_pairs={{0,256},{128,384},{256,0},{384,128},{1,257},{129,385},{257,1},{385... | collective-permute-start | bytes 1572872 | tf_op jit(solution)/shard_map/ppermute | solution.py:63
  48.7 26.0 %collective-permute-start.9 = (bf16[8,512,64]{1,2,0:T(8,128)(2,1)S(1)}, bf16[8,512,64]{1,2,0:T(8,128)(2,1)S(1)}, u32[]{:S(2)}, u32[]{:S(2)}) collective-permute-start(bf16[8,512,64]{1,2,0:T(8,128)(2,1)S(1)} %get-tuple-element.10), channel_id=1, source_target_pairs={{0,128},{128,256},{256,384},{384,0},{1,129},{129,257},{257,385},{3... | collective-permute-start | bytes 1572872 | tf_op jit(solution)/shard_map/ppermute | solution.py:63
  80.9 6.3 %collective-permute-start.10 = (bf16[4,8,512,64]{2,3,1,0:T(8,128)(2,1)S(1)}, bf16[4,8,512,64]{2,3,1,0:T(8,128)(2,1)}, u32[]{:S(2)}, u32[]{:S(2)}) collective-permute-start(bf16[4,8,512,64]{2,3,1,0:T(8,128)(2,1)S(1)} %constant_dynamic-slice_fusion), channel_id=1, source_target_pairs={{0,8},{8,0},{1,9},{9,1},{2,10},{10,2},{3,11},{11,3},{4,12},{12,4},... | collective-permute-start | bytes 6291464 | tf_op jit(solution)/shard_map/ppermute | solution.py:100
  89.5 12.0 %copy-start.3 = (s32[128,2]{0,1:T(2,128)S(1)}, s32[128,2]{0,1:T(2,128)}, u32[]{:S(2)}) copy-start(s32[128,2]{0,1:T(2,128)} %param.18) | copy-start | bytes 3076
  89.5 12.0 %copy-start.4 = (s32[128]{0:T(128)S(1)}, s32[128]{0:T(128)}, u32[]{:S(2)}) copy-start(s32[128]{0:T(128)} %param.19) | copy-start | bytes 1540
  90.3 11.7 %copy-start = (bf16[512,512]{1,0:T(8,128)(2,1)S(1)}, bf16[512,512]{1,0:T(8,128)(2,1)}, u32[]{:S(2)}) copy-start(bf16[512,512]{1,0:T(8,128)(2,1)} %param.12) | copy-start | bytes 1572868
  90.4 40.7 %copy-start.1 = (f32[512]{0:T(512)S(1)}, f32[512]{0:T(512)}, u32[]{:S(2)}) copy-start(f32[512]{0:T(512)} %param.14) | copy-start | bytes 6148
  91.5 39.3 %all-to-all-start = ((bf16[8,128,512]{1,2,0:T(8,128)(2,1)}), bf16[8,128,512]{1,2,0:T(8,128)(2,1)S(1)}, u32[]{:S(2)}, u32[]{:S(2)}) async-start(bf16[8,128,512]{1,2,0:T(8,128)(2,1)} %bitcast.21), calls=%async_computation | async-start | bytes 2097152 | tf_op jit(solution)/shard_map/all_to_all | solution.py:117
  149.5 30.6 %all-to-all-start.2 = ((bf16[8,128,512]{1,2,0:T(8,128)(2,1)}), bf16[8,128,512]{1,2,0:T(8,128)(2,1)S(1)}, u32[]{:S(2)}, u32[]{:S(2)}) async-start(bf16[8,128,512]{1,2,0:T(8,128)(2,1)} %broadcast_in_dim.22), calls=%async_computation.2 | async-start | bytes 2097152 | tf_op jit(solution)/shard_map/all_to_all | solution.py:57
  183.8 4.7 %copy-start.2 = (f32[4096]{0:T(1024)S(1)}, f32[4096]{0:T(1024)}, u32[]{:S(2)}) copy-start(f32[4096]{0:T(1024)} %param.20) | copy-start | bytes 49156
Sparse Core Ops, SparseCore 0:
  9.4 46.0 all-gather.5
  58.9 90.5 all-gather.3

commit v8 on v7

--- a/solution.py
+++ b/solution.py
@@ -65,8 +65,7 @@
 
 def ring_gather(value, axis):
     size = lax.axis_size(axis)
-    relative = jnp.stack([value] + [shift(value, axis, -step) for step in range(1, size)], axis=0)
-    return jnp.roll(relative, lax.axis_index(axis), axis=0)
+    return jnp.stack([value] + [shift(value, axis, -step) for step in range(1, size)], axis=0)
 
 
 def gather_plane(shard):
@@ -108,7 +107,10 @@
     partial_value = jnp.stack(
         [jnp.where(core == 0, own_part, other_part), jnp.where(core == 0, other_part, own_part)],
         axis=3,
-    ).reshape(own_part.shape[0], -1)
+    ).astype(jnp.bfloat16)
+    partial_value = jnp.roll(partial_value, lax.axis_index("rx"), axis=1)
+    partial_value = jnp.roll(partial_value, lax.axis_index("ry"), axis=2)
+    partial_value = partial_value.reshape(own_part.shape[0], -1)
     tp_count = lax.axis_size("tp")
     block_terms = partial_value.astype(jnp.bfloat16).reshape(
         -1, tp_count, feature_width
@@ -151,10 +153,6 @@
     in_image = (image_row >= 0) & (image_row < own_count)
     is_live = slot_index < prompt_count + own_count
     from_prompt = is_live & jnp.logical_not(in_image)
-    flat_index = (own_start + image_row) % requests * capacity + image_row // requests
-    image_pick = ((flat_index[:, None] == send_slots[None, :]) & in_image[:, None]).astype(
-        jnp.bfloat16
-    )
     prompt_row = jnp.where(slot_index < image_from, slot_index, slot_index - own_count)
     prompt_ids = jnp.arange(prompt.shape[1], dtype=jnp.int32)
     prompt_pick = ((prompt_row[:, None] == prompt_ids[None, :]) & from_prompt[:, None]).astype(
@@ -162,15 +160,32 @@
     )
     full_image = gather_features(arrived, tp_count)
     full_prompt = lax.all_gather(prompt[0], "tp", axis=1, tiled=True)
-    embedded = (
-        jnp.dot(image_pick, full_image, preferred_element_type=jnp.float32)
-        + jnp.dot(prompt_pick, full_prompt, preferred_element_type=jnp.float32)
-    ).astype(jnp.bfloat16)
     full_weight = lax.all_gather(qkv_weight, REQ, axis=0, tiled=True)
-    normed = normalize(embedded, norm_gain)
-    projected = jnp.dot(normed, full_weight, preferred_element_type=jnp.float32)
     cosine_table, sine_table = rope_tables(seq_slots)
-    return apply_rope(projected, cosine_table, sine_table).astype(jnp.bfloat16)
+    prompt_rows = jnp.dot(prompt_pick, full_prompt, preferred_element_type=jnp.float32)
+    prompt_normed = normalize(prompt_rows.astype(jnp.bfloat16), norm_gain)
+    prompt_out = apply_rope(
+        jnp.dot(prompt_normed, full_weight, preferred_element_type=jnp.float32),
+        cosine_table,
+        sine_table,
+    ).astype(jnp.bfloat16)
+    image_ids = jnp.arange(IMG_MAX, dtype=jnp.int32)
+    image_flat = (own_start + image_ids) % requests * capacity + image_ids // requests
+    image_order = (
+        (image_flat[:, None] == send_slots[None, :]) & (image_ids < own_count)[:, None]
+    ).astype(jnp.bfloat16)
+    image_rows = jnp.dot(image_order, full_image, preferred_element_type=jnp.float32)
+    image_normed = normalize(image_rows.astype(jnp.bfloat16), norm_gain)
+    image_out = apply_rope(
+        jnp.dot(image_normed, full_weight, preferred_element_type=jnp.float32),
+        lax.dynamic_slice_in_dim(cosine_table, image_from, IMG_MAX, 0),
+        lax.dynamic_slice_in_dim(sine_table, image_from, IMG_MAX, 0),
+    ).astype(jnp.bfloat16)
+    image_place = ((image_row[:, None] == image_ids[None, :]) & in_image[:, None]).astype(
+        jnp.bfloat16
+    )
+    placed = jnp.dot(image_place, image_out, preferred_element_type=jnp.float32)
+    return jnp.where(in_image[:, None], placed.astype(jnp.bfloat16), prompt_out)
 
 
 def solution(mesh):

time: 203 us -> 193 us (0.951)
  local copies, waits for them, and re-layouts: 16 us -> 5.69 us
  waiting for transfers between devices: 78.9 us -> 75.8 us
    unnamed x32 -> x19, local copies, waits for them, and re-layouts: 7.96 us -> 0.93 us
    all_to_all x1, waiting for transfers between devices: 22.6 us -> 17.8 us  [gather_features(): blocks = lax.all_to_all(copies, 'tp', 0, 0, tiled=True)]
    dot_general x2 -> x4, matrix products: 9.46 us -> 11.2 us  [the longest x1 6.85 us: shards(): jnp.dot(prompt_normed, full_weight, preferred_element_type=jnp.float32)]
  transfers between devices with their start and end apart: 15 -> 15, of which waited for: 8 -> 8; matrix products, arithmetic and copies ran while one was open for 16% -> 10% of each run, Pallas kernels for 0% -> 0%
where the time goes in v8:
time: 193 us; the launch traced here: 192 us
  waiting for transfers between devices  75.8 us (39%)
  starting transfers between devices  52.3 us (27%)
  matrix products  18.7 us (10%)
  blocking collectives  17.2 us (9%)
  between operations  15.8 us (8%)
  other arithmetic  6.87 us (4%)
  local copies, waits for them, and re-layouts  5.69 us (3%)
    ppermute x10, starting transfers between devices, shift(): lax.ppermute(value, axis, [(k, (k + step) % size) for k in range(size)])  35.7 us
    ppermute x10, waiting for transfers between devices, shift(): lax.ppermute(value, axis, [(k, (k + step) % size) for k in range(size)])  28.5 us
    all_to_all x1, waiting for transfers between devices, shards(): lax.all_to_all(block_terms, 'tp', 0, 0, tiled=True).astype(jnp.float32)  26.9 us
    all_to_all x1, waiting for transfers between devices, gather_features(): blocks = lax.all_to_all(copies, 'tp', 0, 0, tiled=True)  17.8 us
    all_to_all x1, blocking collectives, shards(): lax.all_to_all(outgoing.reshape(requests, capacity, feature_width), REQ,...  17.2 us
    all_to_all x1, starting transfers between devices, shards(): lax.all_to_all(block_terms, 'tp', 0, 0, tiled=True).astype(jnp.float32)  10.4 us
    dot_general x1, matrix products, shards(): jnp.dot(prompt_normed, full_weight, preferred_element_type=jnp.float32)  6.85 us
    dot_general x1, matrix products, shards(): jnp.dot(prompt_pick, full_prompt, preferred_element_type=jnp.float32)  4.34 us
  transfers between devices with their start and end apart: 15, of which 8 were waited for; matrix products, arithmetic and copies ran while one was open for 10% of the time, Pallas kernels for 0%

profile of v8, /device:TPU:1, one launch (start us, length us, event | category | flops | bytes accessed | tf_op | source)
XLA Modules:
  0.0 192.4 jit_solution(7313287858600130619)
XLA Ops:
  8.0 5.9 %collective-permute-start = (bf16[512,64]{0,1:T(8,128)(2,1)}, bf16[512,64]{0,1:T(8,128)(2,1)S(1)}, u32[]{:S(2)}, u32[]{:S(2)}) collective-permute-start(bf16[512,64]{0,1:T(8,128)(2,1)} %param.13), channel_id=1, source_target_pairs={{0,112},{16,0},{32,16},{48,32},{64,48},{80,64},{96,80},{112,96},{1... | collective-permute-start | bytes 196616 | tf_op jit(solution)/shard_map/ppermute | solution.py:63
  13.9 3.8 %collective-permute-start.1 = (bf16[512,64]{0,1:T(8,128)(2,1)}, bf16[512,64]{0,1:T(8,128)(2,1)S(1)}, u32[]{:S(2)}, u32[]{:S(2)}) collective-permute-start(bf16[512,64]{0,1:T(8,128)(2,1)} %param.13), channel_id=1, source_target_pairs={{0,96},{16,112},{32,0},{48,16},{64,32},{80,48},{96,64},{112,80},{1... | collective-permute-start | bytes 196616 | tf_op jit(solution)/shard_map/ppermute | solution.py:63
  17.7 2.8 %collective-permute-start.2 = (bf16[512,64]{0,1:T(8,128)(2,1)}, bf16[512,64]{0,1:T(8,128)(2,1)S(1)}, u32[]{:S(2)}, u32[]{:S(2)}) collective-permute-start(bf16[512,64]{0,1:T(8,128)(2,1)} %param.13), channel_id=1, source_target_pairs={{0,80},{16,96},{32,112},{48,0},{64,16},{80,32},{96,48},{112,64},{1... | collective-permute-start | bytes 196616 | tf_op jit(solution)/shard_map/ppermute | solution.py:63
  20.5 5.7 %collective-permute-start.3 = (bf16[512,64]{0,1:T(8,128)(2,1)}, bf16[512,64]{0,1:T(8,128)(2,1)S(1)}, u32[]{:S(2)}, u32[]{:S(2)}) collective-permute-start(bf16[512,64]{0,1:T(8,128)(2,1)} %param.13), channel_id=1, source_target_pairs={{0,64},{16,80},{32,96},{48,112},{64,0},{80,16},{96,32},{112,48},{1... | collective-permute-start | bytes 196616 | tf_op jit(solution)/shard_map/ppermute | solution.py:63
  26.1 1.9 collective-permute-start.4
  28.9 4.8 %collective-permute-start.5 = (bf16[512,64]{0,1:T(8,128)(2,1)}, bf16[512,64]{0,1:T(8,128)(2,1)S(1)}, u32[]{:S(2)}, u32[]{:S(2)}) collective-permute-start(bf16[512,64]{0,1:T(8,128)(2,1)} %param.13), channel_id=1, source_target_pairs={{0,32},{16,48},{32,64},{48,80},{64,96},{80,112},{96,0},{112,16},{1... | collective-permute-start | bytes 196616 | tf_op jit(solution)/shard_map/ppermute | solution.py:63
  33.8 3.2 %collective-permute-start.6 = (bf16[512,64]{0,1:T(8,128)(2,1)}, bf16[512,64]{0,1:T(8,128)(2,1)S(1)}, u32[]{:S(2)}, u32[]{:S(2)}) collective-permute-start(bf16[512,64]{0,1:T(8,128)(2,1)} %param.13), channel_id=1, source_target_pairs={{0,16},{16,32},{32,48},{48,64},{64,80},{80,96},{96,112},{112,0},{1... | collective-permute-start | bytes 196616 | tf_op jit(solution)/shard_map/ppermute | solution.py:63
  37.3 4.7 %collective-permute-done.6 = bf16[512,64]{0,1:T(8,128)(2,1)S(1)} collective-permute-done((bf16[512,64]{0,1:T(8,128)(2,1)}, bf16[512,64]{0,1:T(8,128)(2,1)S(1)}, u32[]{:S(2)}, u32[]{:S(2)}) %collective-permute-start.6) | collective-permute-done | bytes 65568 | tf_op jit(solution)/shard_map/ppermute | solution.py:63
  42.1 2.7 %collective-permute-start.7 = (bf16[8,512,64]{1,2,0:T(8,128)(2,1)S(1)}, bf16[8,512,64]{1,2,0:T(8,128)(2,1)S(1)}, u32[]{:S(2)}, u32[]{:S(2)}) collective-permute-start(bf16[8,512,64]{1,2,0:T(8,128)(2,1)S(1)} %bitcast_dynamic-update-slice_fusion), channel_id=1, source_target_pairs={{0,384},{128,0},{256,128},{384,256},{1,385},{129,1},{257,129},{385... | collective-permute-start | bytes 1572872 | tf_op jit(solution)/shard_map/ppermute | solution.py:63
  44.7 2.4 %collective-permute-start.8 = (bf16[8,512,64]{1,2,0:T(8,128)(2,1)S(1)}, bf16[8,512,64]{1,2,0:T(8,128)(2,1)S(1)}, u32[]{:S(2)}, u32[]{:S(2)}) collective-permute-start(bf16[8,512,64]{1,2,0:T(8,128)(2,1)S(1)} %bitcast_dynamic-update-slice_fusion), channel_id=1, source_target_pairs={{0,256},{128,384},{256,0},{384,128},{1,257},{129,385},{257,1},{385... | collective-permute-start | bytes 1572872 | tf_op jit(solution)/shard_map/ppermute | solution.py:63
  47.2 2.5 %collective-permute-start.9 = (bf16[8,512,64]{1,2,0:T(8,128)(2,1)S(1)}, bf16[8,512,64]{1,2,0:T(8,128)(2,1)S(1)}, u32[]{:S(2)}, u32[]{:S(2)}) collective-permute-start(bf16[8,512,64]{1,2,0:T(8,128)(2,1)S(1)} %bitcast_dynamic-update-slice_fusion), channel_id=1, source_target_pairs={{0,128},{128,256},{256,384},{384,0},{1,129},{129,257},{257,385},{3... | collective-permute-start | bytes 1572872 | tf_op jit(solution)/shard_map/ppermute | solution.py:63
  49.7 5.5 %collective-permute-done.7 = bf16[8,512,64]{1,2,0:T(8,128)(2,1)S(1)} collective-permute-done((bf16[8,512,64]{1,2,0:T(8,128)(2,1)S(1)}, bf16[8,512,64]{1,2,0:T(8,128)(2,1)S(1)}, u32[]{:S(2)}, u32[]{:S(2)}) %collective-permute-start.7) | collective-permute-done | bytes 524320 | tf_op jit(solution)/shard_map/ppermute | solution.py:63
  55.2 2.8 %collective-permute-done.8 = bf16[8,512,64]{1,2,0:T(8,128)(2,1)S(1)} collective-permute-done((bf16[8,512,64]{1,2,0:T(8,128)(2,1)S(1)}, bf16[8,512,64]{1,2,0:T(8,128)(2,1)S(1)}, u32[]{:S(2)}, u32[]{:S(2)}) %collective-permute-start.8) | collective-permute-done | bytes 524320 | tf_op jit(solution)/shard_map/ppermute | solution.py:63
  58.0 15.2 %collective-permute-done.9 = bf16[8,512,64]{1,2,0:T(8,128)(2,1)S(1)} collective-permute-done((bf16[8,512,64]{1,2,0:T(8,128)(2,1)S(1)}, bf16[8,512,64]{1,2,0:T(8,128)(2,1)S(1)}, u32[]{:S(2)}, u32[]{:S(2)}) %collective-permute-start.9) | collective-permute-done | bytes 524320 | tf_op jit(solution)/shard_map/ppermute | solution.py:63
  73.5 2.4 %collective-permute-start.10 = (bf16[4,8,512,64]{2,3,1,0:T(8,128)(2,1)S(1)}, bf16[4,8,512,64]{2,3,1,0:T(8,128)(2,1)}, u32[]{:S(2)}, u32[]{:S(2)}) collective-permute-start(bf16[4,8,512,64]{2,3,1,0:T(8,128)(2,1)S(1)} %pad_maximum_fusion), channel_id=1, source_target_pairs={{0,8},{8,0},{1,9},{9,1},{2,10},{10,2},{3,11},{11,3},{4,12},{12,4},... | collective-permute-start | bytes 6291464 | tf_op jit(solution)/shard_map/ppermute | solution.py:99
  79.8 2.3 %fusion.18 = (bf16[128,4,8,1,64]{0,4,2,1,3:T(8,128)(2,1)S(1)}, bf16[128,4,8,1,64]{0,4,2,1,3:T(8,128)(2,1)S(1)}) fusion(bf16[128,4,8,64]{0,3,2,1:T(8,128)(2,1)S(1)} %fusion.38, pred[]{:T(512)S(6)} %eq.112, bf16[4,8,512,64]{2,3,1,0:T(8,128)(2,1)} %collective-permute-done.10, f32[128,512]{1,0:T(8,128)S(1)} %reduce_sum.96), kind=kOutput, calls=%fused_computation.36 | convolution fusion | flops 269090816 | bytes 3932161 | tf_op jit(solution)/shard_map/gk,xykn->gxyn/dot_general | solution.py:104
  84.2 10.4 %all-to-all-start = ((bf16[8,128,512]{1,2,0:T(8,128)(2,1)}), bf16[8,128,512]{1,2,0:T(8,128)(2,1)S(1)}, u32[]{:S(2)}, u32[]{:S(2)}) async-start(bf16[8,128,512]{1,2,0:T(8,128)(2,1)} %bitcast.21), calls=%async_computation | async-start | bytes 2097152 | tf_op jit(solution)/shard_map/all_to_all | solution.py:119
  96.9 26.9 %all-to-all-done = bf16[8,128,512]{1,2,0:T(8,128)(2,1)S(1)} async-done(((bf16[8,128,512]{1,2,0:T(8,128)(2,1)}), bf16[8,128,512]{1,2,0:T(8,128)(2,1)S(1)}, u32[]{:S(2)}, u32[]{:S(2)}) %all-to-all-start) | async-done | bytes 1048608 | tf_op jit(solution)/shard_map/all_to_all | solution.py:119
  124.4 17.2 %all_to_all.15 = bf16[64,2,512]{2,1,0:T(2,128)(2,1)S(1)} all-to-all(bf16[64,2,512]{2,1,0:T(2,128)(2,1)S(1)} %reshape.222), channel_id=1, replica_groups=mesh['rx'=4,'ry'=8,'rc'=2,'tp'=8] {'rx','ry','rc'}, dimensions={0} | all-to-all | bytes 262144 | tf_op jit(solution)/shard_map/all_to_all | solution.py:137
  142.9 3.7 %all-to-all-start.2 = ((bf16[8,128,512]{1,2,0:T(8,128)(2,1)}), bf16[8,128,512]{1,2,0:T(8,128)(2,1)S(1)}, u32[]{:S(2)}, u32[]{:S(2)}) async-start(bf16[8,128,512]{1,2,0:T(8,128)(2,1)} %broadcast_in_dim.28), calls=%async_computation.2 | async-start | bytes 2097152 | tf_op jit(solution)/shard_map/all_to_all | solution.py:57
  151.5 4.3 %fusion = (f32[384]{0:T(512)S(1)}, bf16[384,4096]{1,0:T(8,128)(2,1)}) fusion(bf16[1,256,4096]{2,1,0:T(8,128)(2,1)} %all-gather.6.cloned.1.call-done, s32[384]{0:T(512)S(1)} %subtract_select_fusion, pred[384]{0:T(512)(128)(4,1)S(1)} %get-tuple-element.7), kind=kOutput, calls=%fused_computation.2 | convolution fusion | flops 811794048 | bytes 5246336 | tf_op jit(solution)/shard_map/dot_general | solution.py:165
  155.9 17.8 %all-to-all-done.2 = bf16[8,128,512]{1,2,0:T(8,128)(2,1)S(1)} async-done(((bf16[8,128,512]{1,2,0:T(8,128)(2,1)}), bf16[8,128,512]{1,2,0:T(8,128)(2,1)S(1)}, u32[]{:S(2)}, u32[]{:S(2)}) %all-to-all-start.2) | async-done | bytes 1048608 | tf_op jit(solution)/shard_map/all_to_all | solution.py:57
  174.3 6.8 %fusion.4 = f32[384,768]{0,1:T(8,128)S(1)} fusion(bf16[4096,768]{1,0:T(8,128)(2,1)} %all-gather.4.cloned.1.call-done, bf16[384,4096]{1,0:T(8,128)(2,1)} %get-tuple-element.19, f32[4096]{0:T(1024)S(1)} %copy-done.2, f32[384]{0:T(512)S(1)} %add_rsqrt_fusion), kind=kOutput, calls=%fused_computation.8 | convolution fusion | flops 2422210560 | bytes 10634752 | tf_op jit(solution)/shard_map/dot_general | solution.py:168
  181.3 2.6 %fusion.10 = f32[128,768]{0,1:T(8,128)S(1)} fusion(bf16[4096,768]{1,0:T(8,128)(2,1)S(1)} %copy-done, f32[128,4096]{1,0:T(8,128)S(1)} %get-tuple-element.21, f32[4096]{0:T(1024)S(1)} %copy-done.2, f32[128]{0:T(128)S(1)} %add_rsqrt_fusion.1), kind=kOutput, calls=%fused_computation.25 | convolution fusion | flops 806879232 | bytes 8798720 | tf_op jit(solution)/shard_map/dot_general | solution.py:180
  (79 shorter events, 18.1 us)
Async XLA Ops:
  6.5 145.0 %all-gather.6.cloned.1.call-start = ((), (), s32[]{:S(2)}) async-start(), calls=%async_computation.4 | async-start | bytes 2359296 | tf_op jit(solution)/shard_map/all_gather | solution.py:162
  7.3 167.0 %all-gather.4.cloned.1.call-start = ((), (), s32[]{:S(2)}) async-start(), calls=%async_computation.3 | async-start | bytes 6389760 | tf_op jit(solution)/shard_map/all_gather | solution.py:163
  8.0 20.9 %collective-permute-start = (bf16[512,64]{0,1:T(8,128)(2,1)}, bf16[512,64]{0,1:T(8,128)(2,1)S(1)}, u32[]{:S(2)}, u32[]{:S(2)}) collective-permute-start(bf16[512,64]{0,1:T(8,128)(2,1)} %param.13), channel_id=1, source_target_pairs={{0,112},{16,0},{32,16},{48,32},{64,48},{80,64},{96,80},{112,96},{1... | collective-permute-start | bytes 196616 | tf_op jit(solution)/shard_map/ppermute | solution.py:63
  13.9 19.8 %collective-permute-start.1 = (bf16[512,64]{0,1:T(8,128)(2,1)}, bf16[512,64]{0,1:T(8,128)(2,1)S(1)}, u32[]{:S(2)}, u32[]{:S(2)}) collective-permute-start(bf16[512,64]{0,1:T(8,128)(2,1)} %param.13), channel_id=1, source_target_pairs={{0,96},{16,112},{32,0},{48,16},{64,32},{80,48},{96,64},{112,80},{1... | collective-permute-start | bytes 196616 | tf_op jit(solution)/shard_map/ppermute | solution.py:63
  17.7 19.3 %collective-permute-start.2 = (bf16[512,64]{0,1:T(8,128)(2,1)}, bf16[512,64]{0,1:T(8,128)(2,1)S(1)}, u32[]{:S(2)}, u32[]{:S(2)}) collective-permute-start(bf16[512,64]{0,1:T(8,128)(2,1)} %param.13), channel_id=1, source_target_pairs={{0,80},{16,96},{32,112},{48,0},{64,16},{80,32},{96,48},{112,64},{1... | collective-permute-start | bytes 196616 | tf_op jit(solution)/shard_map/ppermute | solution.py:63
  20.5 16.6 %collective-permute-start.3 = (bf16[512,64]{0,1:T(8,128)(2,1)}, bf16[512,64]{0,1:T(8,128)(2,1)S(1)}, u32[]{:S(2)}, u32[]{:S(2)}) collective-permute-start(bf16[512,64]{0,1:T(8,128)(2,1)} %param.13), channel_id=1, source_target_pairs={{0,64},{16,80},{32,96},{48,112},{64,0},{80,16},{96,32},{112,48},{1... | collective-permute-start | bytes 196616 | tf_op jit(solution)/shard_map/ppermute | solution.py:63
  26.1 10.9 %collective-permute-start.4 = (bf16[512,64]{0,1:T(8,128)(2,1)}, bf16[512,64]{0,1:T(8,128)(2,1)S(1)}, u32[]{:S(2)}, u32[]{:S(2)}) collective-permute-start(bf16[512,64]{0,1:T(8,128)(2,1)} %param.13), channel_id=1, source_target_pairs={{0,48},{16,64},{32,80},{48,96},{64,112},{80,0},{96,16},{112,32},{1... | collective-permute-start | bytes 196616 | tf_op jit(solution)/shard_map/ppermute | solution.py:63
  28.9 8.4 %collective-permute-start.5 = (bf16[512,64]{0,1:T(8,128)(2,1)}, bf16[512,64]{0,1:T(8,128)(2,1)S(1)}, u32[]{:S(2)}, u32[]{:S(2)}) collective-permute-start(bf16[512,64]{0,1:T(8,128)(2,1)} %param.13), channel_id=1, source_target_pairs={{0,32},{16,48},{32,64},{48,80},{64,96},{80,112},{96,0},{112,16},{1... | collective-permute-start | bytes 196616 | tf_op jit(solution)/shard_map/ppermute | solution.py:63
  33.8 8.3 %collective-permute-start.6 = (bf16[512,64]{0,1:T(8,128)(2,1)}, bf16[512,64]{0,1:T(8,128)(2,1)S(1)}, u32[]{:S(2)}, u32[]{:S(2)}) collective-permute-start(bf16[512,64]{0,1:T(8,128)(2,1)} %param.13), channel_id=1, source_target_pairs={{0,16},{16,32},{32,48},{48,64},{64,80},{80,96},{96,112},{112,0},{1... | collective-permute-start | bytes 196616 | tf_op jit(solution)/shard_map/ppermute | solution.py:63
  42.1 13.2 %collective-permute-start.7 = (bf16[8,512,64]{1,2,0:T(8,128)(2,1)S(1)}, bf16[8,512,64]{1,2,0:T(8,128)(2,1)S(1)}, u32[]{:S(2)}, u32[]{:S(2)}) collective-permute-start(bf16[8,512,64]{1,2,0:T(8,128)(2,1)S(1)} %bitcast_dynamic-update-slice_fusion), channel_id=1, source_target_pairs={{0,384},{128,0},{256,128},{384,256},{1,385},{129,1},{257,129},{385... | collective-permute-start | bytes 1572872 | tf_op jit(solution)/shard_map/ppermute | solution.py:63
  44.7 13.3 %collective-permute-start.8 = (bf16[8,512,64]{1,2,0:T(8,128)(2,1)S(1)}, bf16[8,512,64]{1,2,0:T(8,128)(2,1)S(1)}, u32[]{:S(2)}, u32[]{:S(2)}) collective-permute-start(bf16[8,512,64]{1,2,0:T(8,128)(2,1)S(1)} %bitcast_dynamic-update-slice_fusion), channel_id=1, source_target_pairs={{0,256},{128,384},{256,0},{384,128},{1,257},{129,385},{257,1},{385... | collective-permute-start | bytes 1572872 | tf_op jit(solution)/shard_map/ppermute | solution.py:63
  47.2 26.0 %collective-permute-start.9 = (bf16[8,512,64]{1,2,0:T(8,128)(2,1)S(1)}, bf16[8,512,64]{1,2,0:T(8,128)(2,1)S(1)}, u32[]{:S(2)}, u32[]{:S(2)}) collective-permute-start(bf16[8,512,64]{1,2,0:T(8,128)(2,1)S(1)} %bitcast_dynamic-update-slice_fusion), channel_id=1, source_target_pairs={{0,128},{128,256},{256,384},{384,0},{1,129},{129,257},{257,385},{3... | collective-permute-start | bytes 1572872 | tf_op jit(solution)/shard_map/ppermute | solution.py:63
  73.5 6.3 %collective-permute-start.10 = (bf16[4,8,512,64]{2,3,1,0:T(8,128)(2,1)S(1)}, bf16[4,8,512,64]{2,3,1,0:T(8,128)(2,1)}, u32[]{:S(2)}, u32[]{:S(2)}) collective-permute-start(bf16[4,8,512,64]{2,3,1,0:T(8,128)(2,1)S(1)} %pad_maximum_fusion), channel_id=1, source_target_pairs={{0,8},{8,0},{1,9},{9,1},{2,10},{10,2},{3,11},{11,3},{4,12},{12,4},... | collective-permute-start | bytes 6291464 | tf_op jit(solution)/shard_map/ppermute | solution.py:99
  83.1 11.6 %copy-start.4 = (s32[128,2]{0,1:T(2,128)S(1)}, s32[128,2]{0,1:T(2,128)}, u32[]{:S(2)}) copy-start(s32[128,2]{0,1:T(2,128)} %param.18) | copy-start | bytes 3076
  83.1 11.6 %copy-start.5 = (s32[128]{0:T(128)S(1)}, s32[128]{0:T(128)}, u32[]{:S(2)}) copy-start(s32[128]{0:T(128)} %param.19) | copy-start | bytes 1540
  83.1 12.0 %copy-start.1 = (bf16[512,512]{1,0:T(8,128)(2,1)S(1)}, bf16[512,512]{1,0:T(8,128)(2,1)}, u32[]{:S(2)}) copy-start(bf16[512,512]{1,0:T(8,128)(2,1)} %param.12) | copy-start | bytes 1572868
  84.2 39.7 %all-to-all-start = ((bf16[8,128,512]{1,2,0:T(8,128)(2,1)}), bf16[8,128,512]{1,2,0:T(8,128)(2,1)S(1)}, u32[]{:S(2)}, u32[]{:S(2)}) async-start(bf16[8,128,512]{1,2,0:T(8,128)(2,1)} %bitcast.21), calls=%async_computation | async-start | bytes 2097152 | tf_op jit(solution)/shard_map/all_to_all | solution.py:119
  95.1 29.1 %copy-start.3 = (f32[512]{0:T(512)S(1)}, f32[512]{0:T(512)}, u32[]{:S(2)}) copy-start(f32[512]{0:T(512)} %param.14) | copy-start | bytes 6148
  142.9 30.8 %all-to-all-start.2 = ((bf16[8,128,512]{1,2,0:T(8,128)(2,1)}), bf16[8,128,512]{1,2,0:T(8,128)(2,1)S(1)}, u32[]{:S(2)}, u32[]{:S(2)}) async-start(bf16[8,128,512]{1,2,0:T(8,128)(2,1)} %broadcast_in_dim.28), calls=%async_computation.2 | async-start | bytes 2097152 | tf_op jit(solution)/shard_map/all_to_all | solution.py:57
  155.9 18.4 %copy-start.2 = (f32[4096]{0:T(1024)S(1)}, f32[4096]{0:T(1024)}, u32[]{:S(2)}) copy-start(f32[4096]{0:T(1024)} %param.20) | copy-start | bytes 49156
  174.3 7.0 %copy-start = (bf16[4096,768]{1,0:T(8,128)(2,1)S(1)}, bf16[4096,768]{1,0:T(8,128)(2,1)}, u32[]{:S(2)}) copy-start(bf16[4096,768]{1,0:T(8,128)(2,1)} %all-gather.4.cloned.1.call-done) | copy-start | bytes 18874372
Sparse Core Ops, SparseCore 0:
  9.4 46.0 all-gather.5
  58.9 90.0 all-gather.3

commit v9 on v8

--- a/solution.py
+++ b/solution.py
@@ -174,6 +174,7 @@
     image_order = (
         (image_flat[:, None] == send_slots[None, :]) & (image_ids < own_count)[:, None]
     ).astype(jnp.bfloat16)
+    full_image, prompt_out = lax.optimization_barrier((full_image, prompt_out))
     image_rows = jnp.dot(image_order, full_image, preferred_element_type=jnp.float32)
     image_normed = normalize(image_rows.astype(jnp.bfloat16), norm_gain)
     image_out = apply_rope(

time: 193 us -> 190 us (0.984)
  blocking collectives: 17.2 us -> 0 us
  starting transfers between devices: 52.3 us -> 59 us
  waiting for transfers between devices: 75.8 us -> 79.1 us
  matrix products: 18.7 us -> 21.5 us
    all_to_all x1 -> x0, blocking collectives: 17.2 us -> none  [shards(): lax.all_to_all(outgoing.reshape(requests, capacity, feature_width), REQ,...]
    all_to_all x0 -> x1, waiting for transfers between devices: none -> 9.84 us  [shards(): lax.all_to_all(outgoing.reshape(requests, capacity, feature_width), REQ,...]
    all_to_all x0 -> x1, starting transfers between devices: none -> 6.71 us  [shards(): lax.all_to_all(outgoing.reshape(requests, capacity, feature_width), REQ,...]
    all_to_all x1, waiting for transfers between devices: 26.9 us -> 23.2 us  [shards(): lax.all_to_all(block_terms, 'tp', 0, 0, tiled=True).astype(jnp.float32)]
    dot_general x1, matrix products: 2.58 us -> 5.44 us  [shards(): jnp.dot(image_normed, full_weight, preferred_element_type=jnp.float32)]
    all_to_all x1, waiting for transfers between devices: 17.8 us -> 15 us  [gather_features(): blocks = lax.all_to_all(copies, 'tp', 0, 0, tiled=True)]
  transfers between devices with their start and end apart: 15 -> 16, of which waited for: 8 -> 9; matrix products, arithmetic and copies ran while one was open for 10% -> 14% of each run, Pallas kernels for 0% -> 0%
where the time goes in v9:
time: 190 us; the launch traced here: 189 us
  waiting for transfers between devices  79.1 us (42%)
  starting transfers between devices  59 us (31%)
  matrix products  21.5 us (11%)
  between operations  15.9 us (8%)
  other arithmetic  7.08 us (4%)
  local copies, waits for them, and re-layouts  6.34 us (3%)
    ppermute x10, starting transfers between devices, shift(): lax.ppermute(value, axis, [(k, (k + step) % size) for k in range(size)])  35.7 us
    ppermute x10, waiting for transfers between devices, shift(): lax.ppermute(value, axis, [(k, (k + step) % size) for k in range(size)])  28.5 us
    all_to_all x1, waiting for transfers between devices, shards(): lax.all_to_all(block_terms, 'tp', 0, 0, tiled=True).astype(jnp.float32)  23.2 us
    all_to_all x1, waiting for transfers between devices, gather_features(): blocks = lax.all_to_all(copies, 'tp', 0, 0, tiled=True)  15 us
    all_to_all x1, starting transfers between devices, shards(): lax.all_to_all(block_terms, 'tp', 0, 0, tiled=True).astype(jnp.float32)  10.4 us
    all_to_all x1, waiting for transfers between devices, shards(): lax.all_to_all(outgoing.reshape(requests, capacity, feature_width), REQ,...  9.84 us
    dot_general x1, matrix products, shards(): jnp.dot(prompt_normed, full_weight, preferred_element_type=jnp.float32)  6.72 us
    all_to_all x1, starting transfers between devices, shards(): lax.all_to_all(outgoing.reshape(requests, capacity, feature_width), REQ,...  6.71 us
  transfers between devices with their start and end apart: 16, of which 9 were waited for; matrix products, arithmetic and copies ran while one was open for 14% of the time, Pallas kernels for 0%

profile of v9, /device:TPU:1, one launch (start us, length us, event | category | flops | bytes accessed | tf_op | source)
XLA Modules:
  0.0 188.9 jit_solution(4241014147766476552)
XLA Ops:
  8.0 5.9 %collective-permute-start = (bf16[512,64]{0,1:T(8,128)(2,1)}, bf16[512,64]{0,1:T(8,128)(2,1)S(1)}, u32[]{:S(2)}, u32[]{:S(2)}) collective-permute-start(bf16[512,64]{0,1:T(8,128)(2,1)} %param.13), channel_id=1, source_target_pairs={{0,112},{16,0},{32,16},{48,32},{64,48},{80,64},{96,80},{112,96},{1... | collective-permute-start | bytes 196616 | tf_op jit(solution)/shard_map/ppermute | solution.py:63
  13.9 3.8 %collective-permute-start.1 = (bf16[512,64]{0,1:T(8,128)(2,1)}, bf16[512,64]{0,1:T(8,128)(2,1)S(1)}, u32[]{:S(2)}, u32[]{:S(2)}) collective-permute-start(bf16[512,64]{0,1:T(8,128)(2,1)} %param.13), channel_id=1, source_target_pairs={{0,96},{16,112},{32,0},{48,16},{64,32},{80,48},{96,64},{112,80},{1... | collective-permute-start | bytes 196616 | tf_op jit(solution)/shard_map/ppermute | solution.py:63
  17.7 2.8 %collective-permute-start.2 = (bf16[512,64]{0,1:T(8,128)(2,1)}, bf16[512,64]{0,1:T(8,128)(2,1)S(1)}, u32[]{:S(2)}, u32[]{:S(2)}) collective-permute-start(bf16[512,64]{0,1:T(8,128)(2,1)} %param.13), channel_id=1, source_target_pairs={{0,80},{16,96},{32,112},{48,0},{64,16},{80,32},{96,48},{112,64},{1... | collective-permute-start | bytes 196616 | tf_op jit(solution)/shard_map/ppermute | solution.py:63
  20.5 5.7 %collective-permute-start.3 = (bf16[512,64]{0,1:T(8,128)(2,1)}, bf16[512,64]{0,1:T(8,128)(2,1)S(1)}, u32[]{:S(2)}, u32[]{:S(2)}) collective-permute-start(bf16[512,64]{0,1:T(8,128)(2,1)} %param.13), channel_id=1, source_target_pairs={{0,64},{16,80},{32,96},{48,112},{64,0},{80,16},{96,32},{112,48},{1... | collective-permute-start | bytes 196616 | tf_op jit(solution)/shard_map/ppermute | solution.py:63
  28.9 4.8 %collective-permute-start.5 = (bf16[512,64]{0,1:T(8,128)(2,1)}, bf16[512,64]{0,1:T(8,128)(2,1)S(1)}, u32[]{:S(2)}, u32[]{:S(2)}) collective-permute-start(bf16[512,64]{0,1:T(8,128)(2,1)} %param.13), channel_id=1, source_target_pairs={{0,32},{16,48},{32,64},{48,80},{64,96},{80,112},{96,0},{112,16},{1... | collective-permute-start | bytes 196616 | tf_op jit(solution)/shard_map/ppermute | solution.py:63
  33.8 3.2 %collective-permute-start.6 = (bf16[512,64]{0,1:T(8,128)(2,1)}, bf16[512,64]{0,1:T(8,128)(2,1)S(1)}, u32[]{:S(2)}, u32[]{:S(2)}) collective-permute-start(bf16[512,64]{0,1:T(8,128)(2,1)} %param.13), channel_id=1, source_target_pairs={{0,16},{16,32},{32,48},{48,64},{64,80},{80,96},{96,112},{112,0},{1... | collective-permute-start | bytes 196616 | tf_op jit(solution)/shard_map/ppermute | solution.py:63
  37.3 4.7 %collective-permute-done.6 = bf16[512,64]{0,1:T(8,128)(2,1)S(1)} collective-permute-done((bf16[512,64]{0,1:T(8,128)(2,1)}, bf16[512,64]{0,1:T(8,128)(2,1)S(1)}, u32[]{:S(2)}, u32[]{:S(2)}) %collective-permute-start.6) | collective-permute-done | bytes 65568 | tf_op jit(solution)/shard_map/ppermute | solution.py:63
  42.1 2.7 %collective-permute-start.7 = (bf16[8,512,64]{1,2,0:T(8,128)(2,1)S(1)}, bf16[8,512,64]{1,2,0:T(8,128)(2,1)S(1)}, u32[]{:S(2)}, u32[]{:S(2)}) collective-permute-start(bf16[8,512,64]{1,2,0:T(8,128)(2,1)S(1)} %bitcast_dynamic-update-slice_fusion), channel_id=1, source_target_pairs={{0,384},{128,0},{256,128},{384,256},{1,385},{129,1},{257,129},{385... | collective-permute-start | bytes 1572872 | tf_op jit(solution)/shard_map/ppermute | solution.py:63
  44.7 2.4 %collective-permute-start.8 = (bf16[8,512,64]{1,2,0:T(8,128)(2,1)S(1)}, bf16[8,512,64]{1,2,0:T(8,128)(2,1)S(1)}, u32[]{:S(2)}, u32[]{:S(2)}) collective-permute-start(bf16[8,512,64]{1,2,0:T(8,128)(2,1)S(1)} %bitcast_dynamic-update-slice_fusion), channel_id=1, source_target_pairs={{0,256},{128,384},{256,0},{384,128},{1,257},{129,385},{257,1},{385... | collective-permute-start | bytes 1572872 | tf_op jit(solution)/shard_map/ppermute | solution.py:63
  47.2 2.5 %collective-permute-start.9 = (bf16[8,512,64]{1,2,0:T(8,128)(2,1)S(1)}, bf16[8,512,64]{1,2,0:T(8,128)(2,1)S(1)}, u32[]{:S(2)}, u32[]{:S(2)}) collective-permute-start(bf16[8,512,64]{1,2,0:T(8,128)(2,1)S(1)} %bitcast_dynamic-update-slice_fusion), channel_id=1, source_target_pairs={{0,128},{128,256},{256,384},{384,0},{1,129},{129,257},{257,385},{3... | collective-permute-start | bytes 1572872 | tf_op jit(solution)/shard_map/ppermute | solution.py:63
  49.7 5.5 %collective-permute-done.7 = bf16[8,512,64]{1,2,0:T(8,128)(2,1)S(1)} collective-permute-done((bf16[8,512,64]{1,2,0:T(8,128)(2,1)S(1)}, bf16[8,512,64]{1,2,0:T(8,128)(2,1)S(1)}, u32[]{:S(2)}, u32[]{:S(2)}) %collective-permute-start.7) | collective-permute-done | bytes 524320 | tf_op jit(solution)/shard_map/ppermute | solution.py:63
  55.2 2.8 %collective-permute-done.8 = bf16[8,512,64]{1,2,0:T(8,128)(2,1)S(1)} collective-permute-done((bf16[8,512,64]{1,2,0:T(8,128)(2,1)S(1)}, bf16[8,512,64]{1,2,0:T(8,128)(2,1)S(1)}, u32[]{:S(2)}, u32[]{:S(2)}) %collective-permute-start.8) | collective-permute-done | bytes 524320 | tf_op jit(solution)/shard_map/ppermute | solution.py:63
  58.0 15.2 %collective-permute-done.9 = bf16[8,512,64]{1,2,0:T(8,128)(2,1)S(1)} collective-permute-done((bf16[8,512,64]{1,2,0:T(8,128)(2,1)S(1)}, bf16[8,512,64]{1,2,0:T(8,128)(2,1)S(1)}, u32[]{:S(2)}, u32[]{:S(2)}) %collective-permute-start.9) | collective-permute-done | bytes 524320 | tf_op jit(solution)/shard_map/ppermute | solution.py:63
  73.5 2.4 %collective-permute-start.10 = (bf16[4,8,512,64]{2,3,1,0:T(8,128)(2,1)S(1)}, bf16[4,8,512,64]{2,3,1,0:T(8,128)(2,1)}, u32[]{:S(2)}, u32[]{:S(2)}) collective-permute-start(bf16[4,8,512,64]{2,3,1,0:T(8,128)(2,1)S(1)} %pad_maximum_fusion), channel_id=1, source_target_pairs={{0,8},{8,0},{1,9},{9,1},{2,10},{10,2},{3,11},{11,3},{4,12},{12,4},... | collective-permute-start | bytes 6291464 | tf_op jit(solution)/shard_map/ppermute | solution.py:99
  79.8 2.3 %fusion.18 = (bf16[128,4,8,1,64]{0,4,2,1,3:T(8,128)(2,1)S(1)}, bf16[128,4,8,1,64]{0,4,2,1,3:T(8,128)(2,1)S(1)}) fusion(bf16[128,4,8,64]{0,3,2,1:T(8,128)(2,1)S(1)} %fusion.38, pred[]{:T(512)S(6)} %eq.112, bf16[4,8,512,64]{2,3,1,0:T(8,128)(2,1)} %collective-permute-done.10, f32[128,512]{1,0:T(8,128)S(1)} %reduce_sum.96), kind=kOutput, calls=%fused_computation.36 | convolution fusion | flops 269090816 | bytes 3932161 | tf_op jit(solution)/shard_map/gk,xykn->gxyn/dot_general | solution.py:104
  84.2 10.4 %all-to-all-start = ((bf16[8,128,512]{1,2,0:T(8,128)(2,1)}), bf16[8,128,512]{1,2,0:T(8,128)(2,1)S(1)}, u32[]{:S(2)}, u32[]{:S(2)}) async-start(bf16[8,128,512]{1,2,0:T(8,128)(2,1)} %bitcast.21), calls=%async_computation | async-start | bytes 2097152 | tf_op jit(solution)/shard_map/all_to_all | solution.py:119
  100.7 23.2 %all-to-all-done = bf16[8,128,512]{1,2,0:T(8,128)(2,1)S(1)} async-done(((bf16[8,128,512]{1,2,0:T(8,128)(2,1)}), bf16[8,128,512]{1,2,0:T(8,128)(2,1)S(1)}, u32[]{:S(2)}, u32[]{:S(2)}) %all-to-all-start) | async-done | bytes 1048608 | tf_op jit(solution)/shard_map/all_to_all | solution.py:119
  125.1 6.7 %all-to-all-start.1 = ((bf16[64,2,512]{2,1,0:T(2,128)(2,1)}), bf16[64,2,512]{2,1,0:T(2,128)(2,1)S(1)}, u32[]{:S(2)}, u32[]{:S(2)}) async-start(bf16[64,2,512]{2,1,0:T(2,128)(2,1)} %reshape.222), calls=%async_computation.1 | async-start | bytes 262144 | tf_op jit(solution)/shard_map/all_to_all | solution.py:137
  132.5 9.8 %all-to-all-done.1 = bf16[64,2,512]{2,1,0:T(2,128)(2,1)S(1)} async-done(((bf16[64,2,512]{2,1,0:T(2,128)(2,1)}), bf16[64,2,512]{2,1,0:T(2,128)(2,1)S(1)}, u32[]{:S(2)}, u32[]{:S(2)}) %all-to-all-start.1) | async-done | bytes 131104 | tf_op jit(solution)/shard_map/all_to_all | solution.py:137
  143.7 3.7 %all-to-all-start.2 = ((bf16[8,128,512]{1,2,0:T(8,128)(2,1)}), bf16[8,128,512]{1,2,0:T(8,128)(2,1)S(1)}, u32[]{:S(2)}, u32[]{:S(2)}) async-start(bf16[8,128,512]{1,2,0:T(8,128)(2,1)} %broadcast_in_dim.28), calls=%async_computation.2 | async-start | bytes 2097152 | tf_op jit(solution)/shard_map/all_to_all | solution.py:57
  148.1 4.3 %fusion = (f32[384]{0:T(512)S(1)}, bf16[384,4096]{1,0:T(8,128)(2,1)}) fusion(bf16[1,256,4096]{2,1,0:T(8,128)(2,1)} %all-gather.6.cloned.1.call-done, s32[384]{0:T(512)S(1)} %subtract_select_fusion, pred[384]{0:T(512)(128)(4,1)S(1)} %get-tuple-element.11), kind=kOutput, calls=%fused_computation.2 | convolution fusion | flops 811794048 | bytes 5246336 | tf_op jit(solution)/shard_map/dot_general | solution.py:165
  152.4 6.7 %fusion.4 = f32[384,768]{0,1:T(8,128)S(1)} fusion(bf16[4096,768]{1,0:T(8,128)(2,1)} %all-gather.4.cloned.1.call-done, bf16[384,4096]{1,0:T(8,128)(2,1)} %get-tuple-element.23, f32[4096]{0:T(1024)S(1)} %copy-done.1, f32[384]{0:T(512)S(1)} %add_rsqrt_fusion), kind=kOutput, calls=%fused_computation.8 | convolution fusion | flops 2422210560 | bytes 10634752 | tf_op jit(solution)/shard_map/dot_general | solution.py:168
  159.4 15.0 %all-to-all-done.2 = bf16[8,128,512]{1,2,0:T(8,128)(2,1)S(1)} async-done(((bf16[8,128,512]{1,2,0:T(8,128)(2,1)}), bf16[8,128,512]{1,2,0:T(8,128)(2,1)S(1)}, u32[]{:S(2)}, u32[]{:S(2)}) %all-to-all-start.2) | async-done | bytes 1048608 | tf_op jit(solution)/shard_map/all_to_all | solution.py:57
  175.0 5.4 %fusion.10 = f32[128,768]{0,1:T(8,128)S(1)} fusion(bf16[4096,768]{1,0:T(8,128)(2,1)} %all-gather.4.cloned.1.call-done, f32[128,4096]{1,0:T(8,128)S(1)} %get-tuple-element.25, f32[4096]{0:T(1024)S(1)} %copy-done.1, f32[128]{0:T(128)S(1)} %add_rsqrt_fusion.1), kind=kOutput, calls=%fused_computation.25 | convolution fusion | flops 806879232 | bytes 8798720 | tf_op jit(solution)/shard_map/dot_general | solution.py:181
  (78 shorter events, 20.8 us)
Async XLA Ops:
  6.5 141.5 %all-gather.6.cloned.1.call-start = ((), (), s32[]{:S(2)}) async-start(), calls=%async_computation.4 | async-start | bytes 2359296 | tf_op jit(solution)/shard_map/all_gather | solution.py:162
  7.3 145.2 %all-gather.4.cloned.1.call-start = ((), (), s32[]{:S(2)}) async-start(), calls=%async_computation.3 | async-start | bytes 6389760 | tf_op jit(solution)/shard_map/all_gather | solution.py:163
  8.0 20.9 %collective-permute-start = (bf16[512,64]{0,1:T(8,128)(2,1)}, bf16[512,64]{0,1:T(8,128)(2,1)S(1)}, u32[]{:S(2)}, u32[]{:S(2)}) collective-permute-start(bf16[512,64]{0,1:T(8,128)(2,1)} %param.13), channel_id=1, source_target_pairs={{0,112},{16,0},{32,16},{48,32},{64,48},{80,64},{96,80},{112,96},{1... | collective-permute-start | bytes 196616 | tf_op jit(solution)/shard_map/ppermute | solution.py:63
  13.9 19.8 %collective-permute-start.1 = (bf16[512,64]{0,1:T(8,128)(2,1)}, bf16[512,64]{0,1:T(8,128)(2,1)S(1)}, u32[]{:S(2)}, u32[]{:S(2)}) collective-permute-start(bf16[512,64]{0,1:T(8,128)(2,1)} %param.13), channel_id=1, source_target_pairs={{0,96},{16,112},{32,0},{48,16},{64,32},{80,48},{96,64},{112,80},{1... | collective-permute-start | bytes 196616 | tf_op jit(solution)/shard_map/ppermute | solution.py:63
  17.7 19.3 %collective-permute-start.2 = (bf16[512,64]{0,1:T(8,128)(2,1)}, bf16[512,64]{0,1:T(8,128)(2,1)S(1)}, u32[]{:S(2)}, u32[]{:S(2)}) collective-permute-start(bf16[512,64]{0,1:T(8,128)(2,1)} %param.13), channel_id=1, source_target_pairs={{0,80},{16,96},{32,112},{48,0},{64,16},{80,32},{96,48},{112,64},{1... | collective-permute-start | bytes 196616 | tf_op jit(solution)/shard_map/ppermute | solution.py:63
  20.5 16.6 %collective-permute-start.3 = (bf16[512,64]{0,1:T(8,128)(2,1)}, bf16[512,64]{0,1:T(8,128)(2,1)S(1)}, u32[]{:S(2)}, u32[]{:S(2)}) collective-permute-start(bf16[512,64]{0,1:T(8,128)(2,1)} %param.13), channel_id=1, source_target_pairs={{0,64},{16,80},{32,96},{48,112},{64,0},{80,16},{96,32},{112,48},{1... | collective-permute-start | bytes 196616 | tf_op jit(solution)/shard_map/ppermute | solution.py:63
  26.1 10.9 %collective-permute-start.4 = (bf16[512,64]{0,1:T(8,128)(2,1)}, bf16[512,64]{0,1:T(8,128)(2,1)S(1)}, u32[]{:S(2)}, u32[]{:S(2)}) collective-permute-start(bf16[512,64]{0,1:T(8,128)(2,1)} %param.13), channel_id=1, source_target_pairs={{0,48},{16,64},{32,80},{48,96},{64,112},{80,0},{96,16},{112,32},{1... | collective-permute-start | bytes 196616 | tf_op jit(solution)/shard_map/ppermute | solution.py:63
  28.9 8.4 %collective-permute-start.5 = (bf16[512,64]{0,1:T(8,128)(2,1)}, bf16[512,64]{0,1:T(8,128)(2,1)S(1)}, u32[]{:S(2)}, u32[]{:S(2)}) collective-permute-start(bf16[512,64]{0,1:T(8,128)(2,1)} %param.13), channel_id=1, source_target_pairs={{0,32},{16,48},{32,64},{48,80},{64,96},{80,112},{96,0},{112,16},{1... | collective-permute-start | bytes 196616 | tf_op jit(solution)/shard_map/ppermute | solution.py:63
  33.8 8.3 %collective-permute-start.6 = (bf16[512,64]{0,1:T(8,128)(2,1)}, bf16[512,64]{0,1:T(8,128)(2,1)S(1)}, u32[]{:S(2)}, u32[]{:S(2)}) collective-permute-start(bf16[512,64]{0,1:T(8,128)(2,1)} %param.13), channel_id=1, source_target_pairs={{0,16},{16,32},{32,48},{48,64},{64,80},{80,96},{96,112},{112,0},{1... | collective-permute-start | bytes 196616 | tf_op jit(solution)/shard_map/ppermute | solution.py:63
  42.1 13.2 %collective-permute-start.7 = (bf16[8,512,64]{1,2,0:T(8,128)(2,1)S(1)}, bf16[8,512,64]{1,2,0:T(8,128)(2,1)S(1)}, u32[]{:S(2)}, u32[]{:S(2)}) collective-permute-start(bf16[8,512,64]{1,2,0:T(8,128)(2,1)S(1)} %bitcast_dynamic-update-slice_fusion), channel_id=1, source_target_pairs={{0,384},{128,0},{256,128},{384,256},{1,385},{129,1},{257,129},{385... | collective-permute-start | bytes 1572872 | tf_op jit(solution)/shard_map/ppermute | solution.py:63
  44.7 13.3 %collective-permute-start.8 = (bf16[8,512,64]{1,2,0:T(8,128)(2,1)S(1)}, bf16[8,512,64]{1,2,0:T(8,128)(2,1)S(1)}, u32[]{:S(2)}, u32[]{:S(2)}) collective-permute-start(bf16[8,512,64]{1,2,0:T(8,128)(2,1)S(1)} %bitcast_dynamic-update-slice_fusion), channel_id=1, source_target_pairs={{0,256},{128,384},{256,0},{384,128},{1,257},{129,385},{257,1},{385... | collective-permute-start | bytes 1572872 | tf_op jit(solution)/shard_map/ppermute | solution.py:63
  47.2 26.0 %collective-permute-start.9 = (bf16[8,512,64]{1,2,0:T(8,128)(2,1)S(1)}, bf16[8,512,64]{1,2,0:T(8,128)(2,1)S(1)}, u32[]{:S(2)}, u32[]{:S(2)}) collective-permute-start(bf16[8,512,64]{1,2,0:T(8,128)(2,1)S(1)} %bitcast_dynamic-update-slice_fusion), channel_id=1, source_target_pairs={{0,128},{128,256},{256,384},{384,0},{1,129},{129,257},{257,385},{3... | collective-permute-start | bytes 1572872 | tf_op jit(solution)/shard_map/ppermute | solution.py:63
  73.5 6.3 %collective-permute-start.10 = (bf16[4,8,512,64]{2,3,1,0:T(8,128)(2,1)S(1)}, bf16[4,8,512,64]{2,3,1,0:T(8,128)(2,1)}, u32[]{:S(2)}, u32[]{:S(2)}) collective-permute-start(bf16[4,8,512,64]{2,3,1,0:T(8,128)(2,1)S(1)} %pad_maximum_fusion), channel_id=1, source_target_pairs={{0,8},{8,0},{1,9},{9,1},{2,10},{10,2},{3,11},{11,3},{4,12},{12,4},... | collective-permute-start | bytes 6291464 | tf_op jit(solution)/shard_map/ppermute | solution.py:99
  83.1 11.6 %copy-start.3 = (s32[128,2]{0,1:T(2,128)S(1)}, s32[128,2]{0,1:T(2,128)}, u32[]{:S(2)}) copy-start(s32[128,2]{0,1:T(2,128)} %param.18) | copy-start | bytes 3076
  83.1 11.6 %copy-start.4 = (s32[128]{0:T(128)S(1)}, s32[128]{0:T(128)}, u32[]{:S(2)}) copy-start(s32[128]{0:T(128)} %param.19) | copy-start | bytes 1540
  83.1 13.3 %copy-start = (bf16[512,512]{1,0:T(8,128)(2,1)S(1)}, bf16[512,512]{1,0:T(8,128)(2,1)}, u32[]{:S(2)}) copy-start(bf16[512,512]{1,0:T(8,128)(2,1)} %param.12) | copy-start | bytes 1572868
  84.2 39.7 %all-to-all-start = ((bf16[8,128,512]{1,2,0:T(8,128)(2,1)}), bf16[8,128,512]{1,2,0:T(8,128)(2,1)S(1)}, u32[]{:S(2)}, u32[]{:S(2)}) async-start(bf16[8,128,512]{1,2,0:T(8,128)(2,1)} %bitcast.21), calls=%async_computation | async-start | bytes 2097152 | tf_op jit(solution)/shard_map/all_to_all | solution.py:119
  96.4 27.8 %copy-start.2 = (f32[512]{0:T(512)S(1)}, f32[512]{0:T(512)}, u32[]{:S(2)}) copy-start(f32[512]{0:T(512)} %param.14) | copy-start | bytes 6148
  125.1 17.3 %all-to-all-start.1 = ((bf16[64,2,512]{2,1,0:T(2,128)(2,1)}), bf16[64,2,512]{2,1,0:T(2,128)(2,1)S(1)}, u32[]{:S(2)}, u32[]{:S(2)}) async-start(bf16[64,2,512]{2,1,0:T(2,128)(2,1)} %reshape.222), calls=%async_computation.1 | async-start | bytes 262144 | tf_op jit(solution)/shard_map/all_to_all | solution.py:137
  143.7 30.8 %all-to-all-start.2 = ((bf16[8,128,512]{1,2,0:T(8,128)(2,1)}), bf16[8,128,512]{1,2,0:T(8,128)(2,1)S(1)}, u32[]{:S(2)}, u32[]{:S(2)}) async-start(bf16[8,128,512]{1,2,0:T(8,128)(2,1)} %broadcast_in_dim.28), calls=%async_computation.2 | async-start | bytes 2097152 | tf_op jit(solution)/shard_map/all_to_all | solution.py:57
  148.1 4.4 %copy-start.1 = (f32[4096]{0:T(1024)S(1)}, f32[4096]{0:T(1024)}, u32[]{:S(2)}) copy-start(f32[4096]{0:T(1024)} %param.20) | copy-start | bytes 49156
Sparse Core Ops, SparseCore 0:
  9.4 46.0 all-gather.5
  58.9 90.3 all-gather.3

commit v10 on v9

--- a/solution.py
+++ b/solution.py
@@ -68,8 +68,20 @@
     return jnp.stack([value] + [shift(value, axis, -step) for step in range(1, size)], axis=0)
 
 
+def eight_gather(value, axis):
+    from_next = shift(value, axis, -1)
+    from_last = shift(value, axis, 1)
+    three = jnp.stack([from_last, value, from_next], axis=0)
+    far_next = shift(three, axis, -3)
+    far_last = shift(three, axis, 3)
+    return jnp.stack(
+        [value, from_next, far_next[0], far_next[1], far_next[2], far_last[1], far_last[2], from_last],
+        axis=0,
+    )
+
+
 def gather_plane(shard):
-    by_y = ring_gather(shard, "ry")
+    by_y = eight_gather(shard, "ry") if lax.axis_size("ry") == 8 else ring_gather(shard, "ry")
     return ring_gather(by_y, "rx")
 
 

time: 190 us -> 187 us (0.984)
  starting transfers between devices: 59 us -> 54 us
  waiting for transfers between devices: 79.1 us -> 81.1 us
    ppermute x10 -> x7, starting transfers between devices: 35.7 us -> 25.7 us  [shift(): lax.ppermute(value, axis, [(k, (k + step) % size) for k in range(size)])]
    all_to_all x1, starting transfers between devices: 6.71 us -> 9.71 us  [shards(): lax.all_to_all(outgoing.reshape(requests, capacity, feature_width), REQ,...]
    ppermute x1, starting transfers between devices: 2.4 us -> 5.01 us  [shards(): other_half = lax.ppermute(own_half, 'rc', [(0, 1), (1, 0)])]
    ppermute x10 -> x7, waiting for transfers between devices: 28.5 us -> 30.2 us  [shift(): lax.ppermute(value, axis, [(k, (k + step) % size) for k in range(size)])]
  transfers between devices with their start and end apart: 16 -> 13, of which waited for: 9 -> 9; matrix products, arithmetic and copies ran while one was open for 14% -> 15% of each run, Pallas kernels for 0% -> 0%
where the time goes in v10:
time: 187 us
  waiting for transfers between devices  81.1 us (43%)
  starting transfers between devices  54 us (29%)
  matrix products  21.5 us (11%)
  between operations  15.8 us (8%)
  other arithmetic  7.96 us (4%)
  local copies, waits for them, and re-layouts  6.33 us (3%)
    ppermute x7, waiting for transfers between devices, shift(): lax.ppermute(value, axis, [(k, (k + step) % size) for k in range(size)])  30.2 us
    ppermute x7, starting transfers between devices, shift(): lax.ppermute(value, axis, [(k, (k + step) % size) for k in range(size)])  25.7 us
    all_to_all x1, waiting for transfers between devices, shards(): lax.all_to_all(block_terms, 'tp', 0, 0, tiled=True).astype(jnp.float32)  23.3 us
    all_to_all x1, waiting for transfers between devices, gather_features(): blocks = lax.all_to_all(copies, 'tp', 0, 0, tiled=True)  14.9 us
    all_to_all x1, waiting for transfers between devices, shards(): lax.all_to_all(outgoing.reshape(requests, capacity, feature_width), REQ,...  10.2 us
    all_to_all x1, starting transfers between devices, shards(): lax.all_to_all(block_terms, 'tp', 0, 0, tiled=True).astype(jnp.float32)  9.74 us
    all_to_all x1, starting transfers between devices, shards(): lax.all_to_all(outgoing.reshape(requests, capacity, feature_width), REQ,...  9.71 us
    dot_general x1, matrix products, shards(): jnp.dot(prompt_normed, full_weight, preferred_element_type=jnp.float32)  6.73 us
  transfers between devices with their start and end apart: 13, of which 9 were waited for; matrix products, arithmetic and copies ran while one was open for 15% of the time, Pallas kernels for 0%

profile of v10, /device:TPU:1, one launch (start us, length us, event | category | flops | bytes accessed | tf_op | source)
XLA Modules:
  0.0 186.7 jit_solution(6906594856635271167)
XLA Ops:
  8.0 5.9 %collective-permute-start = (bf16[512,64]{0,1:T(8,128)(2,1)}, bf16[512,64]{0,1:T(8,128)(2,1)S(1)}, u32[]{:S(2)}, u32[]{:S(2)}) collective-permute-start(bf16[512,64]{0,1:T(8,128)(2,1)} %param.13), channel_id=1, source_target_pairs={{0,112},{16,0},{32,16},{48,32},{64,48},{80,64},{96,80},{112,96},{1... | collective-permute-start | bytes 196616 | tf_op jit(solution)/shard_map/ppermute | solution.py:63
  13.9 1.9 %collective-permute-start.1 = (bf16[512,64]{0,1:T(8,128)(2,1)}, bf16[512,64]{0,1:T(8,128)(2,1)S(1)}, u32[]{:S(2)}, u32[]{:S(2)}) collective-permute-start(bf16[512,64]{0,1:T(8,128)(2,1)} %param.13), channel_id=1, source_target_pairs={{0,16},{16,32},{32,48},{48,64},{64,80},{80,96},{96,112},{112,0},{1... | collective-permute-start | bytes 196616 | tf_op jit(solution)/shard_map/ppermute | solution.py:63
  16.7 3.6 %collective-permute-done.1 = bf16[512,64]{0,1:T(8,128)(2,1)S(1)} collective-permute-done((bf16[512,64]{0,1:T(8,128)(2,1)}, bf16[512,64]{0,1:T(8,128)(2,1)S(1)}, u32[]{:S(2)}, u32[]{:S(2)}) %collective-permute-start.1) | collective-permute-done | bytes 65568 | tf_op jit(solution)/shard_map/ppermute | solution.py:63
  21.2 3.3 %collective-permute-start.2 = (bf16[3,512,64]{1,2,0:T(8,128)(2,1)S(1)}, bf16[3,512,64]{1,2,0:T(8,128)(2,1)S(1)}, u32[]{:S(2)}, u32[]{:S(2)}) collective-permute-start(bf16[3,512,64]{1,2,0:T(8,128)(2,1)S(1)} %pad_maximum_fusion.2), channel_id=1, source_target_pairs={{0,80},{16,96},{32,112},{48,0},{64,16},{80,32},{96,48},{112,64},{1... | collective-permute-start | bytes 589832 | tf_op jit(solution)/shard_map/ppermute | solution.py:63
  24.6 3.7 %collective-permute-start.3 = (bf16[3,512,64]{1,2,0:T(8,128)(2,1)S(1)}, bf16[3,512,64]{1,2,0:T(8,128)(2,1)S(1)}, u32[]{:S(2)}, u32[]{:S(2)}) collective-permute-start(bf16[3,512,64]{1,2,0:T(8,128)(2,1)S(1)} %pad_maximum_fusion.2), channel_id=1, source_target_pairs={{0,48},{16,64},{32,80},{48,96},{64,112},{80,0},{96,16},{112,32},{1... | collective-permute-start | bytes 589832 | tf_op jit(solution)/shard_map/ppermute | solution.py:63
  28.4 6.7 %collective-permute-done.2 = bf16[3,512,64]{1,2,0:T(8,128)(2,1)S(1)} collective-permute-done((bf16[3,512,64]{1,2,0:T(8,128)(2,1)S(1)}, bf16[3,512,64]{1,2,0:T(8,128)(2,1)S(1)}, u32[]{:S(2)}, u32[]{:S(2)}) %collective-permute-start.2) | collective-permute-done | bytes 196640 | tf_op jit(solution)/shard_map/ppermute | solution.py:63
  35.1 4.8 %collective-permute-done.3 = bf16[3,512,64]{1,2,0:T(8,128)(2,1)S(1)} collective-permute-done((bf16[3,512,64]{1,2,0:T(8,128)(2,1)S(1)}, bf16[3,512,64]{1,2,0:T(8,128)(2,1)S(1)}, u32[]{:S(2)}, u32[]{:S(2)}) %collective-permute-start.3) | collective-permute-done | bytes 196640 | tf_op jit(solution)/shard_map/ppermute | solution.py:63
  39.9 4.3 %collective-permute-start.5 = (bf16[8,512,64]{1,2,0:T(8,128)(2,1)S(1)}, bf16[8,512,64]{1,2,0:T(8,128)(2,1)S(1)}, u32[]{:S(2)}, u32[]{:S(2)}) collective-permute-start(bf16[8,512,64]{1,2,0:T(8,128)(2,1)S(1)} %constant_dynamic-update-slice_fusion), channel_id=1, source_target_pairs={{0,256},{128,384},{256,0},{384,128},{1,257},{129,385},{257,1},{385... | collective-permute-start | bytes 1572872 | tf_op jit(solution)/shard_map/ppermute | solution.py:63
  44.2 2.2 %collective-permute-start.6 = (bf16[8,512,64]{1,2,0:T(8,128)(2,1)S(1)}, bf16[8,512,64]{1,2,0:T(8,128)(2,1)S(1)}, u32[]{:S(2)}, u32[]{:S(2)}) collective-permute-start(bf16[8,512,64]{1,2,0:T(8,128)(2,1)S(1)} %constant_dynamic-update-slice_fusion), channel_id=1, source_target_pairs={{0,128},{128,256},{256,384},{384,0},{1,129},{129,257},{257,385},{3... | collective-permute-start | bytes 1572872 | tf_op jit(solution)/shard_map/ppermute | solution.py:63
  46.4 4.3 %collective-permute-start.4 = (bf16[8,512,64]{1,2,0:T(8,128)(2,1)S(1)}, bf16[8,512,64]{1,2,0:T(8,128)(2,1)S(1)}, u32[]{:S(2)}, u32[]{:S(2)}) collective-permute-start(bf16[8,512,64]{1,2,0:T(8,128)(2,1)S(1)} %constant_dynamic-update-slice_fusion), channel_id=1, source_target_pairs={{0,384},{128,0},{256,128},{384,256},{1,385},{129,1},{257,129},{385... | collective-permute-start | bytes 1572872 | tf_op jit(solution)/shard_map/ppermute | solution.py:63
  51.4 14.3 %collective-permute-done.6 = bf16[8,512,64]{1,2,0:T(8,128)(2,1)S(1)} collective-permute-done((bf16[8,512,64]{1,2,0:T(8,128)(2,1)S(1)}, bf16[8,512,64]{1,2,0:T(8,128)(2,1)S(1)}, u32[]{:S(2)}, u32[]{:S(2)}) %collective-permute-start.6) | collective-permute-done | bytes 524320 | tf_op jit(solution)/shard_map/ppermute | solution.py:63
  66.0 5.0 %collective-permute-start.7 = (bf16[4,8,512,64]{2,3,1,0:T(8,128)(2,1)S(1)}, bf16[4,8,512,64]{2,3,1,0:T(8,128)(2,1)}, u32[]{:S(2)}, u32[]{:S(2)}) collective-permute-start(bf16[4,8,512,64]{2,3,1,0:T(8,128)(2,1)S(1)} %pad_maximum_fusion), channel_id=1, source_target_pairs={{0,8},{8,0},{1,9},{9,1},{2,10},{10,2},{3,11},{11,3},{4,12},{12,4},... | collective-permute-start | bytes 6291464 | tf_op jit(solution)/shard_map/ppermute | solution.py:111
  71.1 1.4 reshape.229
  74.9 2.3 %fusion.18 = (bf16[128,4,8,1,64]{0,4,2,1,3:T(8,128)(2,1)S(1)}, bf16[128,4,8,1,64]{0,4,2,1,3:T(8,128)(2,1)S(1)}) fusion(bf16[128,4,8,64]{0,3,2,1:T(8,128)(2,1)S(1)} %fusion.38, pred[]{:T(512)S(6)} %eq.112, bf16[4,8,512,64]{2,3,1,0:T(8,128)(2,1)} %collective-permute-done.7, f32[128,512]{1,0:T(8,128)S(1)} %reduce_sum.96), kind=kOutput, calls=%fused_computation.36 | convolution fusion | flops 269090816 | bytes 3932161 | tf_op jit(solution)/shard_map/gk,xykn->gxyn/dot_general | solution.py:116
  79.4 9.7 %all-to-all-start = ((bf16[8,128,512]{1,2,0:T(8,128)(2,1)}), bf16[8,128,512]{1,2,0:T(8,128)(2,1)S(1)}, u32[]{:S(2)}, u32[]{:S(2)}) async-start(bf16[8,128,512]{1,2,0:T(8,128)(2,1)} %bitcast.16), calls=%async_computation | async-start | bytes 2097152 | tf_op jit(solution)/shard_map/all_to_all | solution.py:131
  95.1 23.3 %all-to-all-done = bf16[8,128,512]{1,2,0:T(8,128)(2,1)S(1)} async-done(((bf16[8,128,512]{1,2,0:T(8,128)(2,1)}), bf16[8,128,512]{1,2,0:T(8,128)(2,1)S(1)}, u32[]{:S(2)}, u32[]{:S(2)}) %all-to-all-start) | async-done | bytes 1048608 | tf_op jit(solution)/shard_map/all_to_all | solution.py:131
  119.6 9.7 %all-to-all-start.1 = ((bf16[64,2,512]{2,1,0:T(2,128)(2,1)}), bf16[64,2,512]{2,1,0:T(2,128)(2,1)S(1)}, u32[]{:S(2)}, u32[]{:S(2)}) async-start(bf16[64,2,512]{2,1,0:T(2,128)(2,1)} %reshape.222), calls=%async_computation.1 | async-start | bytes 262144 | tf_op jit(solution)/shard_map/all_to_all | solution.py:149
  130.0 10.2 %all-to-all-done.1 = bf16[64,2,512]{2,1,0:T(2,128)(2,1)S(1)} async-done(((bf16[64,2,512]{2,1,0:T(2,128)(2,1)}), bf16[64,2,512]{2,1,0:T(2,128)(2,1)S(1)}, u32[]{:S(2)}, u32[]{:S(2)}) %all-to-all-start.1) | async-done | bytes 131104 | tf_op jit(solution)/shard_map/all_to_all | solution.py:149
  141.5 3.8 %all-to-all-start.2 = ((bf16[8,128,512]{1,2,0:T(8,128)(2,1)}), bf16[8,128,512]{1,2,0:T(8,128)(2,1)S(1)}, u32[]{:S(2)}, u32[]{:S(2)}) async-start(bf16[8,128,512]{1,2,0:T(8,128)(2,1)} %broadcast_in_dim.28), calls=%async_computation.2 | async-start | bytes 2097152 | tf_op jit(solution)/shard_map/all_to_all | solution.py:57
  146.0 4.3 %fusion = (f32[384]{0:T(512)S(1)}, bf16[384,4096]{1,0:T(8,128)(2,1)}) fusion(bf16[1,256,4096]{2,1,0:T(8,128)(2,1)} %all-gather.6.cloned.1.call-done, s32[384]{0:T(512)S(1)} %subtract_select_fusion, pred[384]{0:T(512)(128)(4,1)S(1)} %get-tuple-element.11), kind=kOutput, calls=%fused_computation.2 | convolution fusion | flops 811794048 | bytes 5246336 | tf_op jit(solution)/shard_map/dot_general | solution.py:177
  150.3 6.7 %fusion.4 = f32[384,768]{0,1:T(8,128)S(1)} fusion(bf16[4096,768]{1,0:T(8,128)(2,1)} %all-gather.4.cloned.1.call-done, bf16[384,4096]{1,0:T(8,128)(2,1)} %get-tuple-element.23, f32[4096]{0:T(1024)S(1)} %copy-done.1, f32[384]{0:T(512)S(1)} %add_rsqrt_fusion), kind=kOutput, calls=%fused_computation.8 | convolution fusion | flops 2422210560 | bytes 10634752 | tf_op jit(solution)/shard_map/dot_general | solution.py:180
  157.3 14.9 %all-to-all-done.2 = bf16[8,128,512]{1,2,0:T(8,128)(2,1)S(1)} async-done(((bf16[8,128,512]{1,2,0:T(8,128)(2,1)}), bf16[8,128,512]{1,2,0:T(8,128)(2,1)S(1)}, u32[]{:S(2)}, u32[]{:S(2)}) %all-to-all-start.2) | async-done | bytes 1048608 | tf_op jit(solution)/shard_map/all_to_all | solution.py:57
  172.8 5.4 %fusion.10 = f32[128,768]{0,1:T(8,128)S(1)} fusion(bf16[4096,768]{1,0:T(8,128)(2,1)} %all-gather.4.cloned.1.call-done, f32[128,4096]{1,0:T(8,128)S(1)} %get-tuple-element.25, f32[4096]{0:T(1024)S(1)} %copy-done.1, f32[128]{0:T(128)S(1)} %add_rsqrt_fusion.1), kind=kOutput, calls=%fused_computation.25 | convolution fusion | flops 806879232 | bytes 8798720 | tf_op jit(solution)/shard_map/dot_general | solution.py:193
  178.6 1.2 fusion.9
  (70 shorter events, 17.7 us)
Async XLA Ops:
  6.5 139.4 %all-gather.6.cloned.1.call-start = ((), (), s32[]{:S(2)}) async-start(), calls=%async_computation.4 | async-start | bytes 2359296 | tf_op jit(solution)/shard_map/all_gather | solution.py:174
  7.3 143.1 %all-gather.4.cloned.1.call-start = ((), (), s32[]{:S(2)}) async-start(), calls=%async_computation.3 | async-start | bytes 6389760 | tf_op jit(solution)/shard_map/all_gather | solution.py:175
  8.0 8.7 %collective-permute-start = (bf16[512,64]{0,1:T(8,128)(2,1)}, bf16[512,64]{0,1:T(8,128)(2,1)S(1)}, u32[]{:S(2)}, u32[]{:S(2)}) collective-permute-start(bf16[512,64]{0,1:T(8,128)(2,1)} %param.13), channel_id=1, source_target_pairs={{0,112},{16,0},{32,16},{48,32},{64,48},{80,64},{96,80},{112,96},{1... | collective-permute-start | bytes 196616 | tf_op jit(solution)/shard_map/ppermute | solution.py:63
  13.9 6.4 %collective-permute-start.1 = (bf16[512,64]{0,1:T(8,128)(2,1)}, bf16[512,64]{0,1:T(8,128)(2,1)S(1)}, u32[]{:S(2)}, u32[]{:S(2)}) collective-permute-start(bf16[512,64]{0,1:T(8,128)(2,1)} %param.13), channel_id=1, source_target_pairs={{0,16},{16,32},{32,48},{48,64},{64,80},{80,96},{96,112},{112,0},{1... | collective-permute-start | bytes 196616 | tf_op jit(solution)/shard_map/ppermute | solution.py:63
  21.2 13.8 %collective-permute-start.2 = (bf16[3,512,64]{1,2,0:T(8,128)(2,1)S(1)}, bf16[3,512,64]{1,2,0:T(8,128)(2,1)S(1)}, u32[]{:S(2)}, u32[]{:S(2)}) collective-permute-start(bf16[3,512,64]{1,2,0:T(8,128)(2,1)S(1)} %pad_maximum_fusion.2), channel_id=1, source_target_pairs={{0,80},{16,96},{32,112},{48,0},{64,16},{80,32},{96,48},{112,64},{1... | collective-permute-start | bytes 589832 | tf_op jit(solution)/shard_map/ppermute | solution.py:63
  24.6 15.3 %collective-permute-start.3 = (bf16[3,512,64]{1,2,0:T(8,128)(2,1)S(1)}, bf16[3,512,64]{1,2,0:T(8,128)(2,1)S(1)}, u32[]{:S(2)}, u32[]{:S(2)}) collective-permute-start(bf16[3,512,64]{1,2,0:T(8,128)(2,1)S(1)} %pad_maximum_fusion.2), channel_id=1, source_target_pairs={{0,48},{16,64},{32,80},{48,96},{64,112},{80,0},{96,16},{112,32},{1... | collective-permute-start | bytes 589832 | tf_op jit(solution)/shard_map/ppermute | solution.py:63
  39.9 11.5 %collective-permute-start.5 = (bf16[8,512,64]{1,2,0:T(8,128)(2,1)S(1)}, bf16[8,512,64]{1,2,0:T(8,128)(2,1)S(1)}, u32[]{:S(2)}, u32[]{:S(2)}) collective-permute-start(bf16[8,512,64]{1,2,0:T(8,128)(2,1)S(1)} %constant_dynamic-update-slice_fusion), channel_id=1, source_target_pairs={{0,256},{128,384},{256,0},{384,128},{1,257},{129,385},{257,1},{385... | collective-permute-start | bytes 1572872 | tf_op jit(solution)/shard_map/ppermute | solution.py:63
  44.2 21.6 %collective-permute-start.6 = (bf16[8,512,64]{1,2,0:T(8,128)(2,1)S(1)}, bf16[8,512,64]{1,2,0:T(8,128)(2,1)S(1)}, u32[]{:S(2)}, u32[]{:S(2)}) collective-permute-start(bf16[8,512,64]{1,2,0:T(8,128)(2,1)S(1)} %constant_dynamic-update-slice_fusion), channel_id=1, source_target_pairs={{0,128},{128,256},{256,384},{384,0},{1,129},{129,257},{257,385},{3... | collective-permute-start | bytes 1572872 | tf_op jit(solution)/shard_map/ppermute | solution.py:63
  46.4 19.3 %collective-permute-start.4 = (bf16[8,512,64]{1,2,0:T(8,128)(2,1)S(1)}, bf16[8,512,64]{1,2,0:T(8,128)(2,1)S(1)}, u32[]{:S(2)}, u32[]{:S(2)}) collective-permute-start(bf16[8,512,64]{1,2,0:T(8,128)(2,1)S(1)} %constant_dynamic-update-slice_fusion), channel_id=1, source_target_pairs={{0,384},{128,0},{256,128},{384,256},{1,385},{129,1},{257,129},{385... | collective-permute-start | bytes 1572872 | tf_op jit(solution)/shard_map/ppermute | solution.py:63
  66.0 8.9 %collective-permute-start.7 = (bf16[4,8,512,64]{2,3,1,0:T(8,128)(2,1)S(1)}, bf16[4,8,512,64]{2,3,1,0:T(8,128)(2,1)}, u32[]{:S(2)}, u32[]{:S(2)}) collective-permute-start(bf16[4,8,512,64]{2,3,1,0:T(8,128)(2,1)S(1)} %pad_maximum_fusion), channel_id=1, source_target_pairs={{0,8},{8,0},{1,9},{9,1},{2,10},{10,2},{3,11},{11,3},{4,12},{12,4},... | collective-permute-start | bytes 6291464 | tf_op jit(solution)/shard_map/ppermute | solution.py:111
  78.2 10.9 %copy-start.3 = (s32[128,2]{0,1:T(2,128)S(1)}, s32[128,2]{0,1:T(2,128)}, u32[]{:S(2)}) copy-start(s32[128,2]{0,1:T(2,128)} %param.18) | copy-start | bytes 3076
  78.3 10.9 %copy-start.4 = (s32[128]{0:T(128)S(1)}, s32[128]{0:T(128)}, u32[]{:S(2)}) copy-start(s32[128]{0:T(128)} %param.19) | copy-start | bytes 1540
  78.3 12.6 %copy-start = (bf16[512,512]{1,0:T(8,128)(2,1)S(1)}, bf16[512,512]{1,0:T(8,128)(2,1)}, u32[]{:S(2)}) copy-start(bf16[512,512]{1,0:T(8,128)(2,1)} %param.12) | copy-start | bytes 1572868
  79.4 39.0 %all-to-all-start = ((bf16[8,128,512]{1,2,0:T(8,128)(2,1)}), bf16[8,128,512]{1,2,0:T(8,128)(2,1)S(1)}, u32[]{:S(2)}, u32[]{:S(2)}) async-start(bf16[8,128,512]{1,2,0:T(8,128)(2,1)} %bitcast.16), calls=%async_computation | async-start | bytes 2097152 | tf_op jit(solution)/shard_map/all_to_all | solution.py:131
  90.9 27.8 %copy-start.2 = (f32[512]{0:T(512)S(1)}, f32[512]{0:T(512)}, u32[]{:S(2)}) copy-start(f32[512]{0:T(512)} %param.14) | copy-start | bytes 6148
  119.6 20.6 %all-to-all-start.1 = ((bf16[64,2,512]{2,1,0:T(2,128)(2,1)}), bf16[64,2,512]{2,1,0:T(2,128)(2,1)S(1)}, u32[]{:S(2)}, u32[]{:S(2)}) async-start(bf16[64,2,512]{2,1,0:T(2,128)(2,1)} %reshape.222), calls=%async_computation.1 | async-start | bytes 262144 | tf_op jit(solution)/shard_map/all_to_all | solution.py:149
  141.5 30.8 %all-to-all-start.2 = ((bf16[8,128,512]{1,2,0:T(8,128)(2,1)}), bf16[8,128,512]{1,2,0:T(8,128)(2,1)S(1)}, u32[]{:S(2)}, u32[]{:S(2)}) async-start(bf16[8,128,512]{1,2,0:T(8,128)(2,1)} %broadcast_in_dim.28), calls=%async_computation.2 | async-start | bytes 2097152 | tf_op jit(solution)/shard_map/all_to_all | solution.py:57
  146.0 4.4 %copy-start.1 = (f32[4096]{0:T(1024)S(1)}, f32[4096]{0:T(1024)}, u32[]{:S(2)}) copy-start(f32[4096]{0:T(1024)} %param.20) | copy-start | bytes 49156
Sparse Core Ops, SparseCore 0:
  9.4 46.0 all-gather.5
  58.9 90.9 all-gather.3

commit v11 on v10

--- a/solution.py
+++ b/solution.py
@@ -170,7 +170,6 @@
     prompt_pick = ((prompt_row[:, None] == prompt_ids[None, :]) & from_prompt[:, None]).astype(
         jnp.bfloat16
     )
-    full_image = gather_features(arrived, tp_count)
     full_prompt = lax.all_gather(prompt[0], "tp", axis=1, tiled=True)
     full_weight = lax.all_gather(qkv_weight, REQ, axis=0, tiled=True)
     cosine_table, sine_table = rope_tables(seq_slots)
@@ -186,9 +185,10 @@
     image_order = (
         (image_flat[:, None] == send_slots[None, :]) & (image_ids < own_count)[:, None]
     ).astype(jnp.bfloat16)
-    full_image, prompt_out = lax.optimization_barrier((full_image, prompt_out))
-    image_rows = jnp.dot(image_order, full_image, preferred_element_type=jnp.float32)
-    image_normed = normalize(image_rows.astype(jnp.bfloat16), norm_gain)
+    ordered = jnp.dot(image_order, arrived, preferred_element_type=jnp.float32)
+    image_rows = gather_features(ordered.astype(jnp.bfloat16), tp_count)
+    image_rows, prompt_out = lax.optimization_barrier((image_rows, prompt_out))
+    image_normed = normalize(image_rows, norm_gain)
     image_out = apply_rope(
         jnp.dot(image_normed, full_weight, preferred_element_type=jnp.float32),
         lax.dynamic_slice_in_dim(cosine_table, image_from, IMG_MAX, 0),

time: 187 us -> 188 us (level)
  no operation moved by 1% of the time
where the time goes in v11:
time: 188 us; the launch traced here: 187 us
  waiting for transfers between devices  81.3 us (43%)
  starting transfers between devices  54 us (29%)
  matrix products  21.6 us (11%)
  between operations  15.8 us (8%)
  other arithmetic  8.3 us (4%)
  local copies, waits for them, and re-layouts  6.32 us (3%)
    ppermute x7, waiting for transfers between devices, shift(): lax.ppermute(value, axis, [(k, (k + step) % size) for k in range(size)])  30.2 us
    ppermute x7, starting transfers between devices, shift(): lax.ppermute(value, axis, [(k, (k + step) % size) for k in range(size)])  25.7 us
    all_to_all x1, waiting for transfers between devices, shards(): lax.all_to_all(block_terms, 'tp', 0, 0, tiled=True).astype(jnp.float32)  24.6 us
    all_to_all x1, waiting for transfers between devices, gather_features(): blocks = lax.all_to_all(copies, 'tp', 0, 0, tiled=True)  15 us
    all_to_all x1, starting transfers between devices, shards(): lax.all_to_all(block_terms, 'tp', 0, 0, tiled=True).astype(jnp.float32)  9.74 us
    all_to_all x1, starting transfers between devices, shards(): lax.all_to_all(outgoing.reshape(requests, capacity, feature_width), REQ,...  9.71 us
    all_to_all x1, waiting for transfers between devices, shards(): lax.all_to_all(outgoing.reshape(requests, capacity, feature_width), REQ,...  8.93 us
    dot_general x1, matrix products, shards(): jnp.dot(prompt_normed, full_weight, preferred_element_type=jnp.float32)  6.74 us
  transfers between devices with their start and end apart: 13, of which 9 were waited for; matrix products, arithmetic and copies ran while one was open for 15% of the time, Pallas kernels for 0%

profile of v11, /device:TPU:1, one launch (start us, length us, event | category | flops | bytes accessed | tf_op | source)
XLA Modules:
  0.0 187.3 jit_solution(8695837526047572514)
XLA Ops:
  8.0 5.9 %collective-permute-start = (bf16[512,64]{0,1:T(8,128)(2,1)}, bf16[512,64]{0,1:T(8,128)(2,1)S(1)}, u32[]{:S(2)}, u32[]{:S(2)}) collective-permute-start(bf16[512,64]{0,1:T(8,128)(2,1)} %param.13), channel_id=1, source_target_pairs={{0,112},{16,0},{32,16},{48,32},{64,48},{80,64},{96,80},{112,96},{1... | collective-permute-start | bytes 196616 | tf_op jit(solution)/shard_map/ppermute | solution.py:63
  13.9 1.9 %collective-permute-start.1 = (bf16[512,64]{0,1:T(8,128)(2,1)}, bf16[512,64]{0,1:T(8,128)(2,1)S(1)}, u32[]{:S(2)}, u32[]{:S(2)}) collective-permute-start(bf16[512,64]{0,1:T(8,128)(2,1)} %param.13), channel_id=1, source_target_pairs={{0,16},{16,32},{32,48},{48,64},{64,80},{80,96},{96,112},{112,0},{1... | collective-permute-start | bytes 196616 | tf_op jit(solution)/shard_map/ppermute | solution.py:63
  16.7 3.6 %collective-permute-done.1 = bf16[512,64]{0,1:T(8,128)(2,1)S(1)} collective-permute-done((bf16[512,64]{0,1:T(8,128)(2,1)}, bf16[512,64]{0,1:T(8,128)(2,1)S(1)}, u32[]{:S(2)}, u32[]{:S(2)}) %collective-permute-start.1) | collective-permute-done | bytes 65568 | tf_op jit(solution)/shard_map/ppermute | solution.py:63
  21.2 3.3 %collective-permute-start.2 = (bf16[3,512,64]{1,2,0:T(8,128)(2,1)S(1)}, bf16[3,512,64]{1,2,0:T(8,128)(2,1)S(1)}, u32[]{:S(2)}, u32[]{:S(2)}) collective-permute-start(bf16[3,512,64]{1,2,0:T(8,128)(2,1)S(1)} %pad_maximum_fusion.2), channel_id=1, source_target_pairs={{0,80},{16,96},{32,112},{48,0},{64,16},{80,32},{96,48},{112,64},{1... | collective-permute-start | bytes 589832 | tf_op jit(solution)/shard_map/ppermute | solution.py:63
  24.6 3.7 %collective-permute-start.3 = (bf16[3,512,64]{1,2,0:T(8,128)(2,1)S(1)}, bf16[3,512,64]{1,2,0:T(8,128)(2,1)S(1)}, u32[]{:S(2)}, u32[]{:S(2)}) collective-permute-start(bf16[3,512,64]{1,2,0:T(8,128)(2,1)S(1)} %pad_maximum_fusion.2), channel_id=1, source_target_pairs={{0,48},{16,64},{32,80},{48,96},{64,112},{80,0},{96,16},{112,32},{1... | collective-permute-start | bytes 589832 | tf_op jit(solution)/shard_map/ppermute | solution.py:63
  28.4 6.7 %collective-permute-done.2 = bf16[3,512,64]{1,2,0:T(8,128)(2,1)S(1)} collective-permute-done((bf16[3,512,64]{1,2,0:T(8,128)(2,1)S(1)}, bf16[3,512,64]{1,2,0:T(8,128)(2,1)S(1)}, u32[]{:S(2)}, u32[]{:S(2)}) %collective-permute-start.2) | collective-permute-done | bytes 196640 | tf_op jit(solution)/shard_map/ppermute | solution.py:63
  35.1 4.8 %collective-permute-done.3 = bf16[3,512,64]{1,2,0:T(8,128)(2,1)S(1)} collective-permute-done((bf16[3,512,64]{1,2,0:T(8,128)(2,1)S(1)}, bf16[3,512,64]{1,2,0:T(8,128)(2,1)S(1)}, u32[]{:S(2)}, u32[]{:S(2)}) %collective-permute-start.3) | collective-permute-done | bytes 196640 | tf_op jit(solution)/shard_map/ppermute | solution.py:63
  39.9 4.3 %collective-permute-start.5 = (bf16[8,512,64]{1,2,0:T(8,128)(2,1)S(1)}, bf16[8,512,64]{1,2,0:T(8,128)(2,1)S(1)}, u32[]{:S(2)}, u32[]{:S(2)}) collective-permute-start(bf16[8,512,64]{1,2,0:T(8,128)(2,1)S(1)} %constant_dynamic-update-slice_fusion), channel_id=1, source_target_pairs={{0,256},{128,384},{256,0},{384,128},{1,257},{129,385},{257,1},{385... | collective-permute-start | bytes 1572872 | tf_op jit(solution)/shard_map/ppermute | solution.py:63
  44.2 2.2 %collective-permute-start.6 = (bf16[8,512,64]{1,2,0:T(8,128)(2,1)S(1)}, bf16[8,512,64]{1,2,0:T(8,128)(2,1)S(1)}, u32[]{:S(2)}, u32[]{:S(2)}) collective-permute-start(bf16[8,512,64]{1,2,0:T(8,128)(2,1)S(1)} %constant_dynamic-update-slice_fusion), channel_id=1, source_target_pairs={{0,128},{128,256},{256,384},{384,0},{1,129},{129,257},{257,385},{3... | collective-permute-start | bytes 1572872 | tf_op jit(solution)/shard_map/ppermute | solution.py:63
  46.4 4.3 %collective-permute-start.4 = (bf16[8,512,64]{1,2,0:T(8,128)(2,1)S(1)}, bf16[8,512,64]{1,2,0:T(8,128)(2,1)S(1)}, u32[]{:S(2)}, u32[]{:S(2)}) collective-permute-start(bf16[8,512,64]{1,2,0:T(8,128)(2,1)S(1)} %constant_dynamic-update-slice_fusion), channel_id=1, source_target_pairs={{0,384},{128,0},{256,128},{384,256},{1,385},{129,1},{257,129},{385... | collective-permute-start | bytes 1572872 | tf_op jit(solution)/shard_map/ppermute | solution.py:63
  51.4 14.3 %collective-permute-done.6 = bf16[8,512,64]{1,2,0:T(8,128)(2,1)S(1)} collective-permute-done((bf16[8,512,64]{1,2,0:T(8,128)(2,1)S(1)}, bf16[8,512,64]{1,2,0:T(8,128)(2,1)S(1)}, u32[]{:S(2)}, u32[]{:S(2)}) %collective-permute-start.6) | collective-permute-done | bytes 524320 | tf_op jit(solution)/shard_map/ppermute | solution.py:63
  66.0 5.0 %collective-permute-start.7 = (bf16[4,8,512,64]{2,3,1,0:T(8,128)(2,1)S(1)}, bf16[4,8,512,64]{2,3,1,0:T(8,128)(2,1)}, u32[]{:S(2)}, u32[]{:S(2)}) collective-permute-start(bf16[4,8,512,64]{2,3,1,0:T(8,128)(2,1)S(1)} %pad_maximum_fusion), channel_id=1, source_target_pairs={{0,8},{8,0},{1,9},{9,1},{2,10},{10,2},{3,11},{11,3},{4,12},{12,4},... | collective-permute-start | bytes 6291464 | tf_op jit(solution)/shard_map/ppermute | solution.py:111
  71.1 1.4 reshape.233
  74.9 2.3 %fusion.21 = (bf16[128,4,8,1,64]{0,4,2,1,3:T(8,128)(2,1)S(1)}, bf16[128,4,8,1,64]{0,4,2,1,3:T(8,128)(2,1)S(1)}) fusion(bf16[128,4,8,64]{0,3,2,1:T(8,128)(2,1)S(1)} %fusion.41, pred[]{:T(512)S(6)} %eq.112, bf16[4,8,512,64]{2,3,1,0:T(8,128)(2,1)} %collective-permute-done.7, f32[128,512]{1,0:T(8,128)S(1)} %reduce_sum.96), kind=kOutput, calls=%fused_computation.38 | convolution fusion | flops 269090816 | bytes 3932161 | tf_op jit(solution)/shard_map/gk,xykn->gxyn/dot_general | solution.py:116
  79.4 9.7 %all-to-all-start = ((bf16[8,128,512]{1,2,0:T(8,128)(2,1)}), bf16[8,128,512]{1,2,0:T(8,128)(2,1)S(1)}, u32[]{:S(2)}, u32[]{:S(2)}) async-start(bf16[8,128,512]{1,2,0:T(8,128)(2,1)} %bitcast.16), calls=%async_computation | async-start | bytes 2097152 | tf_op jit(solution)/shard_map/all_to_all | solution.py:131
  93.7 24.6 %all-to-all-done = bf16[8,128,512]{1,2,0:T(8,128)(2,1)S(1)} async-done(((bf16[8,128,512]{1,2,0:T(8,128)(2,1)}), bf16[8,128,512]{1,2,0:T(8,128)(2,1)S(1)}, u32[]{:S(2)}, u32[]{:S(2)}) %all-to-all-start) | async-done | bytes 1048608 | tf_op jit(solution)/shard_map/all_to_all | solution.py:131
  119.6 9.7 %all-to-all-start.1 = ((bf16[64,2,512]{2,1,0:T(2,128)(2,1)}), bf16[64,2,512]{2,1,0:T(2,128)(2,1)S(1)}, u32[]{:S(2)}, u32[]{:S(2)}) async-start(bf16[64,2,512]{2,1,0:T(2,128)(2,1)} %reshape.225), calls=%async_computation.1 | async-start | bytes 262144 | tf_op jit(solution)/shard_map/all_to_all | solution.py:149
  131.2 8.9 %all-to-all-done.1 = bf16[64,2,512]{2,1,0:T(2,128)(2,1)S(1)} async-done(((bf16[64,2,512]{2,1,0:T(2,128)(2,1)}), bf16[64,2,512]{2,1,0:T(2,128)(2,1)S(1)}, u32[]{:S(2)}, u32[]{:S(2)}) %all-to-all-start.1) | async-done | bytes 131104 | tf_op jit(solution)/shard_map/all_to_all | solution.py:149
  141.7 3.7 %all-to-all-start.2 = ((bf16[8,128,512]{1,2,0:T(8,128)(2,1)}), bf16[8,128,512]{1,2,0:T(8,128)(2,1)S(1)}, u32[]{:S(2)}, u32[]{:S(2)}) async-start(bf16[8,128,512]{1,2,0:T(8,128)(2,1)} %broadcast_in_dim.25), calls=%async_computation.2 | async-start | bytes 2097152 | tf_op jit(solution)/shard_map/all_to_all | solution.py:57
  146.1 4.3 %fusion = (f32[384]{0:T(512)S(1)}, bf16[384,4096]{1,0:T(8,128)(2,1)}) fusion(bf16[1,256,4096]{2,1,0:T(8,128)(2,1)} %all-gather.6.cloned.1.call-done, s32[384]{0:T(512)S(1)} %subtract_select_fusion, pred[384]{0:T(512)(128)(4,1)S(1)} %get-tuple-element.9), kind=kOutput, calls=%fused_computation.2 | convolution fusion | flops 811794048 | bytes 5246336 | tf_op jit(solution)/shard_map/dot_general | solution.py:176
  150.4 6.7 %fusion.3 = f32[384,768]{0,1:T(8,128)S(1)} fusion(bf16[4096,768]{1,0:T(8,128)(2,1)} %all-gather.4.cloned.1.call-done, bf16[384,4096]{1,0:T(8,128)(2,1)} %get-tuple-element.23, f32[4096]{0:T(1024)S(1)} %copy-done.2, f32[384]{0:T(512)S(1)} %add_rsqrt_fusion), kind=kOutput, calls=%fused_computation.6 | convolution fusion | flops 2422210560 | bytes 10634752 | tf_op jit(solution)/shard_map/dot_general | solution.py:179
  157.4 15.0 %all-to-all-done.2 = bf16[8,128,512]{1,2,0:T(8,128)(2,1)S(1)} async-done(((bf16[8,128,512]{1,2,0:T(8,128)(2,1)}), bf16[8,128,512]{1,2,0:T(8,128)(2,1)S(1)}, u32[]{:S(2)}, u32[]{:S(2)}) %all-to-all-start.2) | async-done | bytes 1048608 | tf_op jit(solution)/shard_map/all_to_all | solution.py:57
  173.0 5.9 %fusion.16 = f32[128,768]{0,1:T(8,128)S(1)} fusion(bf16[4096,768]{1,0:T(8,128)(2,1)} %all-gather.4.cloned.1.call-done, bf16[128,4096]{0,1:T(8,128)(2,1)S(1)} %bitcast.56, f32[4096]{0:T(1024)S(1)} %copy-done.2, f32[128]{0:T(128)S(1)} %add_rsqrt_fusion.1), kind=kOutput, calls=%fused_computation.31 | convolution fusion | flops 807403520 | bytes 7750144 | tf_op jit(solution)/shard_map/dot_general | solution.py:193
  179.2 1.2 fusion.11
  (71 shorter events, 17.7 us)
Async XLA Ops:
  6.5 139.5 %all-gather.6.cloned.1.call-start = ((), (), s32[]{:S(2)}) async-start(), calls=%async_computation.4 | async-start | bytes 2359296 | tf_op jit(solution)/shard_map/all_gather | solution.py:173
  7.3 143.2 %all-gather.4.cloned.1.call-start = ((), (), s32[]{:S(2)}) async-start(), calls=%async_computation.3 | async-start | bytes 6389760 | tf_op jit(solution)/shard_map/all_gather | solution.py:174
  8.0 8.7 %collective-permute-start = (bf16[512,64]{0,1:T(8,128)(2,1)}, bf16[512,64]{0,1:T(8,128)(2,1)S(1)}, u32[]{:S(2)}, u32[]{:S(2)}) collective-permute-start(bf16[512,64]{0,1:T(8,128)(2,1)} %param.13), channel_id=1, source_target_pairs={{0,112},{16,0},{32,16},{48,32},{64,48},{80,64},{96,80},{112,96},{1... | collective-permute-start | bytes 196616 | tf_op jit(solution)/shard_map/ppermute | solution.py:63
  13.9 6.4 %collective-permute-start.1 = (bf16[512,64]{0,1:T(8,128)(2,1)}, bf16[512,64]{0,1:T(8,128)(2,1)S(1)}, u32[]{:S(2)}, u32[]{:S(2)}) collective-permute-start(bf16[512,64]{0,1:T(8,128)(2,1)} %param.13), channel_id=1, source_target_pairs={{0,16},{16,32},{32,48},{48,64},{64,80},{80,96},{96,112},{112,0},{1... | collective-permute-start | bytes 196616 | tf_op jit(solution)/shard_map/ppermute | solution.py:63
  21.2 13.8 %collective-permute-start.2 = (bf16[3,512,64]{1,2,0:T(8,128)(2,1)S(1)}, bf16[3,512,64]{1,2,0:T(8,128)(2,1)S(1)}, u32[]{:S(2)}, u32[]{:S(2)}) collective-permute-start(bf16[3,512,64]{1,2,0:T(8,128)(2,1)S(1)} %pad_maximum_fusion.2), channel_id=1, source_target_pairs={{0,80},{16,96},{32,112},{48,0},{64,16},{80,32},{96,48},{112,64},{1... | collective-permute-start | bytes 589832 | tf_op jit(solution)/shard_map/ppermute | solution.py:63
  24.6 15.3 %collective-permute-start.3 = (bf16[3,512,64]{1,2,0:T(8,128)(2,1)S(1)}, bf16[3,512,64]{1,2,0:T(8,128)(2,1)S(1)}, u32[]{:S(2)}, u32[]{:S(2)}) collective-permute-start(bf16[3,512,64]{1,2,0:T(8,128)(2,1)S(1)} %pad_maximum_fusion.2), channel_id=1, source_target_pairs={{0,48},{16,64},{32,80},{48,96},{64,112},{80,0},{96,16},{112,32},{1... | collective-permute-start | bytes 589832 | tf_op jit(solution)/shard_map/ppermute | solution.py:63
  39.9 11.5 %collective-permute-start.5 = (bf16[8,512,64]{1,2,0:T(8,128)(2,1)S(1)}, bf16[8,512,64]{1,2,0:T(8,128)(2,1)S(1)}, u32[]{:S(2)}, u32[]{:S(2)}) collective-permute-start(bf16[8,512,64]{1,2,0:T(8,128)(2,1)S(1)} %constant_dynamic-update-slice_fusion), channel_id=1, source_target_pairs={{0,256},{128,384},{256,0},{384,128},{1,257},{129,385},{257,1},{385... | collective-permute-start | bytes 1572872 | tf_op jit(solution)/shard_map/ppermute | solution.py:63
  44.2 21.6 %collective-permute-start.6 = (bf16[8,512,64]{1,2,0:T(8,128)(2,1)S(1)}, bf16[8,512,64]{1,2,0:T(8,128)(2,1)S(1)}, u32[]{:S(2)}, u32[]{:S(2)}) collective-permute-start(bf16[8,512,64]{1,2,0:T(8,128)(2,1)S(1)} %constant_dynamic-update-slice_fusion), channel_id=1, source_target_pairs={{0,128},{128,256},{256,384},{384,0},{1,129},{129,257},{257,385},{3... | collective-permute-start | bytes 1572872 | tf_op jit(solution)/shard_map/ppermute | solution.py:63
  46.4 19.3 %collective-permute-start.4 = (bf16[8,512,64]{1,2,0:T(8,128)(2,1)S(1)}, bf16[8,512,64]{1,2,0:T(8,128)(2,1)S(1)}, u32[]{:S(2)}, u32[]{:S(2)}) collective-permute-start(bf16[8,512,64]{1,2,0:T(8,128)(2,1)S(1)} %constant_dynamic-update-slice_fusion), channel_id=1, source_target_pairs={{0,384},{128,0},{256,128},{384,256},{1,385},{129,1},{257,129},{385... | collective-permute-start | bytes 1572872 | tf_op jit(solution)/shard_map/ppermute | solution.py:63
  66.0 8.9 %collective-permute-start.7 = (bf16[4,8,512,64]{2,3,1,0:T(8,128)(2,1)S(1)}, bf16[4,8,512,64]{2,3,1,0:T(8,128)(2,1)}, u32[]{:S(2)}, u32[]{:S(2)}) collective-permute-start(bf16[4,8,512,64]{2,3,1,0:T(8,128)(2,1)S(1)} %pad_maximum_fusion), channel_id=1, source_target_pairs={{0,8},{8,0},{1,9},{9,1},{2,10},{10,2},{3,11},{11,3},{4,12},{12,4},... | collective-permute-start | bytes 6291464 | tf_op jit(solution)/shard_map/ppermute | solution.py:111
  78.2 10.9 %copy-start.3 = (s32[128,2]{0,1:T(2,128)S(1)}, s32[128,2]{0,1:T(2,128)}, u32[]{:S(2)}) copy-start(s32[128,2]{0,1:T(2,128)} %param.18) | copy-start | bytes 3076
  78.3 10.9 %copy-start.4 = (s32[128]{0:T(128)S(1)}, s32[128]{0:T(128)}, u32[]{:S(2)}) copy-start(s32[128]{0:T(128)} %param.19) | copy-start | bytes 1540
  78.3 12.0 %copy-start = (bf16[512,512]{1,0:T(8,128)(2,1)S(1)}, bf16[512,512]{1,0:T(8,128)(2,1)}, u32[]{:S(2)}) copy-start(bf16[512,512]{1,0:T(8,128)(2,1)} %param.12) | copy-start | bytes 1572868
  79.4 39.0 %all-to-all-start = ((bf16[8,128,512]{1,2,0:T(8,128)(2,1)}), bf16[8,128,512]{1,2,0:T(8,128)(2,1)S(1)}, u32[]{:S(2)}, u32[]{:S(2)}) async-start(bf16[8,128,512]{1,2,0:T(8,128)(2,1)} %bitcast.16), calls=%async_computation | async-start | bytes 2097152 | tf_op jit(solution)/shard_map/all_to_all | solution.py:131
  90.2 28.4 %copy-start.1 = (f32[512]{0:T(512)S(1)}, f32[512]{0:T(512)}, u32[]{:S(2)}) copy-start(f32[512]{0:T(512)} %param.14) | copy-start | bytes 6148
  119.6 20.6 %all-to-all-start.1 = ((bf16[64,2,512]{2,1,0:T(2,128)(2,1)}), bf16[64,2,512]{2,1,0:T(2,128)(2,1)S(1)}, u32[]{:S(2)}, u32[]{:S(2)}) async-start(bf16[64,2,512]{2,1,0:T(2,128)(2,1)} %reshape.225), calls=%async_computation.1 | async-start | bytes 262144 | tf_op jit(solution)/shard_map/all_to_all | solution.py:149
  141.7 30.8 %all-to-all-start.2 = ((bf16[8,128,512]{1,2,0:T(8,128)(2,1)}), bf16[8,128,512]{1,2,0:T(8,128)(2,1)S(1)}, u32[]{:S(2)}, u32[]{:S(2)}) async-start(bf16[8,128,512]{1,2,0:T(8,128)(2,1)} %broadcast_in_dim.25), calls=%async_computation.2 | async-start | bytes 2097152 | tf_op jit(solution)/shard_map/all_to_all | solution.py:57
  146.1 4.4 %copy-start.2 = (f32[4096]{0:T(1024)S(1)}, f32[4096]{0:T(1024)}, u32[]{:S(2)}) copy-start(f32[4096]{0:T(1024)} %param.20) | copy-start | bytes 49156
Sparse Core Ops, SparseCore 0:
  9.4 46.0 all-gather.5
  58.9 90.9 all-gather.3

commit v12 on v10

--- a/solution.py
+++ b/solution.py
@@ -83,6 +83,15 @@
 def gather_plane(shard):
     by_y = eight_gather(shard, "ry") if lax.axis_size("ry") == 8 else ring_gather(shard, "ry")
     return ring_gather(by_y, "rx")
+
+
+def block_sum(part, tp_count):
+    terms = part.astype(jnp.bfloat16)
+    terms = jnp.roll(terms, lax.axis_index("rx"), axis=1)
+    terms = jnp.roll(terms, lax.axis_index("ry"), axis=2)
+    terms = terms.reshape(terms.shape[0], tp_count, -1).transpose(1, 0, 2)
+    arrived = lax.all_to_all(terms, "tp", 0, 0, tiled=True)
+    return jnp.sum(arrived.astype(jnp.float32), axis=0)
 
 
 def shards(
@@ -116,20 +125,13 @@
     other_part = jnp.einsum(
         "gk,xykn->gxyn", merged_context, other_half, preferred_element_type=jnp.float32
     )
-    partial_value = jnp.stack(
-        [jnp.where(core == 0, own_part, other_part), jnp.where(core == 0, other_part, own_part)],
-        axis=3,
-    ).astype(jnp.bfloat16)
-    partial_value = jnp.roll(partial_value, lax.axis_index("rx"), axis=1)
-    partial_value = jnp.roll(partial_value, lax.axis_index("ry"), axis=2)
-    partial_value = partial_value.reshape(own_part.shape[0], -1)
     tp_count = lax.axis_size("tp")
-    block_terms = partial_value.astype(jnp.bfloat16).reshape(
-        -1, tp_count, feature_width
-    ).transpose(1, 0, 2)
-    own_share = jnp.sum(
-        lax.all_to_all(block_terms, "tp", 0, 0, tiled=True).astype(jnp.float32), axis=0
-    )
+    own_sum = block_sum(own_part, tp_count).reshape(own_part.shape[0], -1, 1, own_part.shape[-1])
+    other_sum = block_sum(other_part, tp_count).reshape(own_sum.shape)
+    own_share = jnp.concatenate(
+        [jnp.where(core == 0, own_sum, other_sum), jnp.where(core == 0, other_sum, own_sum)],
+        axis=2,
+    ).reshape(own_part.shape[0], feature_width)
     merged = (merged_residual + layer_scale[None, :] * own_share).astype(jnp.bfloat16)
     merged_count = merged.shape[0]
     counts, starts = request_plan(grid_sizes, image_owner, requests)

time: 187 us -> 194 us (1.037)
  starting transfers between devices: 54 us -> 57.6 us
  other arithmetic: 7.96 us -> 11.2 us
    all_to_all x1 -> x2, starting transfers between devices: 9.74 us -> 13.4 us  [block_sum(): arrived = lax.all_to_all(terms, 'tp', 0, 0, tiled=True)]
    all_to_all x1 -> x2, waiting for transfers between devices: 23.3 us -> 24.7 us  [block_sum(): arrived = lax.all_to_all(terms, 'tp', 0, 0, tiled=True)]
  transfers between devices with their start and end apart: 13 -> 14, of which waited for: 9 -> 9; matrix products, arithmetic and copies ran while one was open for 15% -> 16% of each run, Pallas kernels for 0% -> 0%
where the time goes in v12:
time: 194 us; the launch traced here: 193 us
  waiting for transfers between devices  80.8 us (42%)
  starting transfers between devices  57.6 us (30%)
  matrix products  21.5 us (11%)
  between operations  15.8 us (8%)
  other arithmetic  11.2 us (6%)
  local copies, waits for them, and re-layouts  6.29 us (3%)
    ppermute x7, waiting for transfers between devices, shift(): lax.ppermute(value, axis, [(k, (k + step) % size) for k in range(size)])  30.2 us
    ppermute x7, starting transfers between devices, shift(): lax.ppermute(value, axis, [(k, (k + step) % size) for k in range(size)])  25.7 us
    all_to_all x2, waiting for transfers between devices, block_sum(): arrived = lax.all_to_all(terms, 'tp', 0, 0, tiled=True)  24.7 us
    all_to_all x1, waiting for transfers between devices, gather_features(): blocks = lax.all_to_all(copies, 'tp', 0, 0, tiled=True)  14.9 us
    all_to_all x2, starting transfers between devices, block_sum(): arrived = lax.all_to_all(terms, 'tp', 0, 0, tiled=True)  13.4 us
    all_to_all x1, starting transfers between devices, shards(): lax.all_to_all(outgoing.reshape(requests, capacity, feature_width), REQ,...  9.7 us
    all_to_all x1, waiting for transfers between devices, shards(): lax.all_to_all(outgoing.reshape(requests, capacity, feature_width), REQ,...  9.62 us
    dot_general x1, matrix products, shards(): jnp.dot(prompt_normed, full_weight, preferred_element_type=jnp.float32)  6.71 us
  transfers between devices with their start and end apart: 14, of which 9 were waited for; matrix products, arithmetic and copies ran while one was open for 16% of the time, Pallas kernels for 0%

profile of v12, /device:TPU:1, one launch (start us, length us, event | category | flops | bytes accessed | tf_op | source)
XLA Modules:
  0.0 193.2 jit_solution(2230744954209425928)
XLA Ops:
  8.0 5.9 %collective-permute-start = (bf16[512,64]{0,1:T(8,128)(2,1)}, bf16[512,64]{0,1:T(8,128)(2,1)S(1)}, u32[]{:S(2)}, u32[]{:S(2)}) collective-permute-start(bf16[512,64]{0,1:T(8,128)(2,1)} %param.17), channel_id=1, source_target_pairs={{0,112},{16,0},{32,16},{48,32},{64,48},{80,64},{96,80},{112,96},{1... | collective-permute-start | bytes 196616 | tf_op jit(solution)/shard_map/ppermute | solution.py:63
  13.9 1.9 collective-permute-start.1
  16.7 3.6 %collective-permute-done.1 = bf16[512,64]{0,1:T(8,128)(2,1)S(1)} collective-permute-done((bf16[512,64]{0,1:T(8,128)(2,1)}, bf16[512,64]{0,1:T(8,128)(2,1)S(1)}, u32[]{:S(2)}, u32[]{:S(2)}) %collective-permute-start.1) | collective-permute-done | bytes 65568 | tf_op jit(solution)/shard_map/ppermute | solution.py:63
  21.2 3.3 %collective-permute-start.2 = (bf16[3,512,64]{1,2,0:T(8,128)(2,1)S(1)}, bf16[3,512,64]{1,2,0:T(8,128)(2,1)S(1)}, u32[]{:S(2)}, u32[]{:S(2)}) collective-permute-start(bf16[3,512,64]{1,2,0:T(8,128)(2,1)S(1)} %pad_maximum_fusion.3), channel_id=1, source_target_pairs={{0,80},{16,96},{32,112},{48,0},{64,16},{80,32},{96,48},{112,64},{1... | collective-permute-start | bytes 589832 | tf_op jit(solution)/shard_map/ppermute | solution.py:63
  24.6 3.7 %collective-permute-start.3 = (bf16[3,512,64]{1,2,0:T(8,128)(2,1)S(1)}, bf16[3,512,64]{1,2,0:T(8,128)(2,1)S(1)}, u32[]{:S(2)}, u32[]{:S(2)}) collective-permute-start(bf16[3,512,64]{1,2,0:T(8,128)(2,1)S(1)} %pad_maximum_fusion.3), channel_id=1, source_target_pairs={{0,48},{16,64},{32,80},{48,96},{64,112},{80,0},{96,16},{112,32},{1... | collective-permute-start | bytes 589832 | tf_op jit(solution)/shard_map/ppermute | solution.py:63
  28.4 6.7 %collective-permute-done.2 = bf16[3,512,64]{1,2,0:T(8,128)(2,1)S(1)} collective-permute-done((bf16[3,512,64]{1,2,0:T(8,128)(2,1)S(1)}, bf16[3,512,64]{1,2,0:T(8,128)(2,1)S(1)}, u32[]{:S(2)}, u32[]{:S(2)}) %collective-permute-start.2) | collective-permute-done | bytes 196640 | tf_op jit(solution)/shard_map/ppermute | solution.py:63
  35.1 4.8 %collective-permute-done.3 = bf16[3,512,64]{1,2,0:T(8,128)(2,1)S(1)} collective-permute-done((bf16[3,512,64]{1,2,0:T(8,128)(2,1)S(1)}, bf16[3,512,64]{1,2,0:T(8,128)(2,1)S(1)}, u32[]{:S(2)}, u32[]{:S(2)}) %collective-permute-start.3) | collective-permute-done | bytes 196640 | tf_op jit(solution)/shard_map/ppermute | solution.py:63
  39.9 4.3 %collective-permute-start.5 = (bf16[8,512,64]{1,2,0:T(8,128)(2,1)S(1)}, bf16[8,512,64]{1,2,0:T(8,128)(2,1)S(1)}, u32[]{:S(2)}, u32[]{:S(2)}) collective-permute-start(bf16[8,512,64]{1,2,0:T(8,128)(2,1)S(1)} %constant_dynamic-update-slice_fusion), channel_id=1, source_target_pairs={{0,256},{128,384},{256,0},{384,128},{1,257},{129,385},{257,1},{385... | collective-permute-start | bytes 1572872 | tf_op jit(solution)/shard_map/ppermute | solution.py:63
  44.2 2.2 %collective-permute-start.6 = (bf16[8,512,64]{1,2,0:T(8,128)(2,1)S(1)}, bf16[8,512,64]{1,2,0:T(8,128)(2,1)S(1)}, u32[]{:S(2)}, u32[]{:S(2)}) collective-permute-start(bf16[8,512,64]{1,2,0:T(8,128)(2,1)S(1)} %constant_dynamic-update-slice_fusion), channel_id=1, source_target_pairs={{0,128},{128,256},{256,384},{384,0},{1,129},{129,257},{257,385},{3... | collective-permute-start | bytes 1572872 | tf_op jit(solution)/shard_map/ppermute | solution.py:63
  46.4 4.3 %collective-permute-start.4 = (bf16[8,512,64]{1,2,0:T(8,128)(2,1)S(1)}, bf16[8,512,64]{1,2,0:T(8,128)(2,1)S(1)}, u32[]{:S(2)}, u32[]{:S(2)}) collective-permute-start(bf16[8,512,64]{1,2,0:T(8,128)(2,1)S(1)} %constant_dynamic-update-slice_fusion), channel_id=1, source_target_pairs={{0,384},{128,0},{256,128},{384,256},{1,385},{129,1},{257,129},{385... | collective-permute-start | bytes 1572872 | tf_op jit(solution)/shard_map/ppermute | solution.py:63
  51.4 14.3 %collective-permute-done.6 = bf16[8,512,64]{1,2,0:T(8,128)(2,1)S(1)} collective-permute-done((bf16[8,512,64]{1,2,0:T(8,128)(2,1)S(1)}, bf16[8,512,64]{1,2,0:T(8,128)(2,1)S(1)}, u32[]{:S(2)}, u32[]{:S(2)}) %collective-permute-start.6) | collective-permute-done | bytes 524320 | tf_op jit(solution)/shard_map/ppermute | solution.py:63
  66.0 5.0 %collective-permute-start.7 = (bf16[4,8,512,64]{2,3,1,0:T(8,128)(2,1)S(1)}, bf16[4,8,512,64]{2,3,1,0:T(8,128)(2,1)}, u32[]{:S(2)}, u32[]{:S(2)}) collective-permute-start(bf16[4,8,512,64]{2,3,1,0:T(8,128)(2,1)S(1)} %pad_maximum_fusion), channel_id=1, source_target_pairs={{0,8},{8,0},{1,9},{9,1},{2,10},{10,2},{3,11},{11,3},{4,12},{12,4},... | collective-permute-start | bytes 6291464 | tf_op jit(solution)/shard_map/ppermute | solution.py:120
  76.2 9.8 %all-to-all-start = ((bf16[8,128,256]{1,2,0:T(8,128)(2,1)}), bf16[8,128,256]{1,2,0:T(8,128)(2,1)}, u32[]{:S(2)}, u32[]{:S(2)}) async-start(bf16[8,128,256]{1,2,0:T(8,128)(2,1)} %bitcast.13), calls=%async_computation | async-start | bytes 1048576 | tf_op jit(solution)/shard_map/all_to_all | solution.py:93
  91.5 2.3 %convolution_convert_fusion.3 = bf16[128,4,8,64]{0,3,2,1:T(8,128)(2,1)S(1)} fusion(bf16[4,8,512,64]{2,3,1,0:T(8,128)(2,1)} %collective-permute-done.7, f32[128,512]{1,0:T(8,128)S(1)} %reduce_sum.105), kind=kOutput, calls=%fused_computation.16 | convolution fusion | flops 268828672 | bytes 2883584 | tf_op jit(solution)/shard_map/gk,xykn->gxyn/dot_general | solution.py:125
  95.1 9.1 %all-to-all-done = bf16[8,128,256]{1,2,0:T(8,128)(2,1)} async-done(((bf16[8,128,256]{1,2,0:T(8,128)(2,1)}), bf16[8,128,256]{1,2,0:T(8,128)(2,1)}, u32[]{:S(2)}, u32[]{:S(2)}) %all-to-all-start) | async-done | bytes 524320 | tf_op jit(solution)/shard_map/all_to_all | solution.py:93
  104.1 3.6 %all-to-all-start.1 = ((bf16[8,128,256]{1,2,0:T(8,128)(2,1)}), bf16[8,128,256]{1,2,0:T(8,128)(2,1)S(1)}, u32[]{:S(2)}, u32[]{:S(2)}) async-start(bf16[8,128,256]{1,2,0:T(8,128)(2,1)} %bitcast.16), calls=%async_computation.1 | async-start | bytes 1048576 | tf_op jit(solution)/shard_map/all_to_all | solution.py:93
  110.0 15.7 %all-to-all-done.1 = bf16[8,128,256]{1,2,0:T(8,128)(2,1)S(1)} async-done(((bf16[8,128,256]{1,2,0:T(8,128)(2,1)}), bf16[8,128,256]{1,2,0:T(8,128)(2,1)S(1)}, u32[]{:S(2)}, u32[]{:S(2)}) %all-to-all-start.1) | async-done | bytes 524320 | tf_op jit(solution)/shard_map/all_to_all | solution.py:93
  126.9 9.7 %all-to-all-start.2 = ((bf16[64,2,512]{2,1,0:T(2,128)(2,1)}), bf16[64,2,512]{2,1,0:T(2,128)(2,1)S(1)}, u32[]{:S(2)}, u32[]{:S(2)}) async-start(bf16[64,2,512]{2,1,0:T(2,128)(2,1)} %reshape.280), calls=%async_computation.2 | async-start | bytes 262144 | tf_op jit(solution)/shard_map/all_to_all | solution.py:151
  137.3 9.6 %all-to-all-done.2 = bf16[64,2,512]{2,1,0:T(2,128)(2,1)S(1)} async-done(((bf16[64,2,512]{2,1,0:T(2,128)(2,1)}), bf16[64,2,512]{2,1,0:T(2,128)(2,1)S(1)}, u32[]{:S(2)}, u32[]{:S(2)}) %all-to-all-start.2) | async-done | bytes 131104 | tf_op jit(solution)/shard_map/all_to_all | solution.py:151
  148.2 3.7 %all-to-all-start.3 = ((bf16[8,128,512]{1,2,0:T(8,128)(2,1)}), bf16[8,128,512]{1,2,0:T(8,128)(2,1)S(1)}, u32[]{:S(2)}, u32[]{:S(2)}) async-start(bf16[8,128,512]{1,2,0:T(8,128)(2,1)} %broadcast_in_dim.28), calls=%async_computation.3 | async-start | bytes 2097152 | tf_op jit(solution)/shard_map/all_to_all | solution.py:57
  152.6 4.3 %fusion = (f32[384]{0:T(512)S(1)}, bf16[384,4096]{1,0:T(8,128)(2,1)}) fusion(bf16[1,256,4096]{2,1,0:T(8,128)(2,1)} %all-gather.6.cloned.1.call-done, s32[384]{0:T(512)S(1)} %subtract_select_fusion, pred[384]{0:T(512)(128)(4,1)S(1)} %get-tuple-element.13), kind=kOutput, calls=%fused_computation.2 | convolution fusion | flops 811794048 | bytes 5246336 | tf_op jit(solution)/shard_map/dot_general | solution.py:179
  157.0 6.7 %fusion.4 = f32[384,768]{0,1:T(8,128)S(1)} fusion(bf16[4096,768]{1,0:T(8,128)(2,1)} %all-gather.4.cloned.1.call-done, bf16[384,4096]{1,0:T(8,128)(2,1)} %get-tuple-element.25, f32[4096]{0:T(1024)S(1)} %copy-done.1, f32[384]{0:T(512)S(1)} %add_rsqrt_fusion), kind=kOutput, calls=%fused_computation.8 | convolution fusion | flops 2422210560 | bytes 10634752 | tf_op jit(solution)/shard_map/dot_general | solution.py:182
  163.9 14.9 %all-to-all-done.3 = bf16[8,128,512]{1,2,0:T(8,128)(2,1)S(1)} async-done(((bf16[8,128,512]{1,2,0:T(8,128)(2,1)}), bf16[8,128,512]{1,2,0:T(8,128)(2,1)S(1)}, u32[]{:S(2)}, u32[]{:S(2)}) %all-to-all-start.3) | async-done | bytes 1048608 | tf_op jit(solution)/shard_map/all_to_all | solution.py:57
  179.4 5.4 %fusion.10 = f32[128,768]{0,1:T(8,128)S(1)} fusion(bf16[4096,768]{1,0:T(8,128)(2,1)} %all-gather.4.cloned.1.call-done, f32[128,4096]{1,0:T(8,128)S(1)} %get-tuple-element.27, f32[4096]{0:T(1024)S(1)} %copy-done.1, f32[128]{0:T(128)S(1)} %add_rsqrt_fusion.1), kind=kOutput, calls=%fused_computation.20 | convolution fusion | flops 806879232 | bytes 8798720 | tf_op jit(solution)/shard_map/dot_general | solution.py:195
  (76 shorter events, 22.4 us)
Async XLA Ops:
  6.5 146.1 %all-gather.6.cloned.1.call-start = ((), (), s32[]{:S(2)}) async-start(), calls=%async_computation.5 | async-start | bytes 2359296 | tf_op jit(solution)/shard_map/all_gather | solution.py:176
  7.3 149.7 %all-gather.4.cloned.1.call-start = ((), (), s32[]{:S(2)}) async-start(), calls=%async_computation.4 | async-start | bytes 6389760 | tf_op jit(solution)/shard_map/all_gather | solution.py:177
  8.0 8.7 %collective-permute-start = (bf16[512,64]{0,1:T(8,128)(2,1)}, bf16[512,64]{0,1:T(8,128)(2,1)S(1)}, u32[]{:S(2)}, u32[]{:S(2)}) collective-permute-start(bf16[512,64]{0,1:T(8,128)(2,1)} %param.17), channel_id=1, source_target_pairs={{0,112},{16,0},{32,16},{48,32},{64,48},{80,64},{96,80},{112,96},{1... | collective-permute-start | bytes 196616 | tf_op jit(solution)/shard_map/ppermute | solution.py:63
  13.9 6.4 %collective-permute-start.1 = (bf16[512,64]{0,1:T(8,128)(2,1)}, bf16[512,64]{0,1:T(8,128)(2,1)S(1)}, u32[]{:S(2)}, u32[]{:S(2)}) collective-permute-start(bf16[512,64]{0,1:T(8,128)(2,1)} %param.17), channel_id=1, source_target_pairs={{0,16},{16,32},{32,48},{48,64},{64,80},{80,96},{96,112},{112,0},{1... | collective-permute-start | bytes 196616 | tf_op jit(solution)/shard_map/ppermute | solution.py:63
  21.2 13.8 %collective-permute-start.2 = (bf16[3,512,64]{1,2,0:T(8,128)(2,1)S(1)}, bf16[3,512,64]{1,2,0:T(8,128)(2,1)S(1)}, u32[]{:S(2)}, u32[]{:S(2)}) collective-permute-start(bf16[3,512,64]{1,2,0:T(8,128)(2,1)S(1)} %pad_maximum_fusion.3), channel_id=1, source_target_pairs={{0,80},{16,96},{32,112},{48,0},{64,16},{80,32},{96,48},{112,64},{1... | collective-permute-start | bytes 589832 | tf_op jit(solution)/shard_map/ppermute | solution.py:63
  24.6 15.3 %collective-permute-start.3 = (bf16[3,512,64]{1,2,0:T(8,128)(2,1)S(1)}, bf16[3,512,64]{1,2,0:T(8,128)(2,1)S(1)}, u32[]{:S(2)}, u32[]{:S(2)}) collective-permute-start(bf16[3,512,64]{1,2,0:T(8,128)(2,1)S(1)} %pad_maximum_fusion.3), channel_id=1, source_target_pairs={{0,48},{16,64},{32,80},{48,96},{64,112},{80,0},{96,16},{112,32},{1... | collective-permute-start | bytes 589832 | tf_op jit(solution)/shard_map/ppermute | solution.py:63
  39.9 11.5 %collective-permute-start.5 = (bf16[8,512,64]{1,2,0:T(8,128)(2,1)S(1)}, bf16[8,512,64]{1,2,0:T(8,128)(2,1)S(1)}, u32[]{:S(2)}, u32[]{:S(2)}) collective-permute-start(bf16[8,512,64]{1,2,0:T(8,128)(2,1)S(1)} %constant_dynamic-update-slice_fusion), channel_id=1, source_target_pairs={{0,256},{128,384},{256,0},{384,128},{1,257},{129,385},{257,1},{385... | collective-permute-start | bytes 1572872 | tf_op jit(solution)/shard_map/ppermute | solution.py:63
  44.2 21.6 %collective-permute-start.6 = (bf16[8,512,64]{1,2,0:T(8,128)(2,1)S(1)}, bf16[8,512,64]{1,2,0:T(8,128)(2,1)S(1)}, u32[]{:S(2)}, u32[]{:S(2)}) collective-permute-start(bf16[8,512,64]{1,2,0:T(8,128)(2,1)S(1)} %constant_dynamic-update-slice_fusion), channel_id=1, source_target_pairs={{0,128},{128,256},{256,384},{384,0},{1,129},{129,257},{257,385},{3... | collective-permute-start | bytes 1572872 | tf_op jit(solution)/shard_map/ppermute | solution.py:63
  46.4 19.3 %collective-permute-start.4 = (bf16[8,512,64]{1,2,0:T(8,128)(2,1)S(1)}, bf16[8,512,64]{1,2,0:T(8,128)(2,1)S(1)}, u32[]{:S(2)}, u32[]{:S(2)}) collective-permute-start(bf16[8,512,64]{1,2,0:T(8,128)(2,1)S(1)} %constant_dynamic-update-slice_fusion), channel_id=1, source_target_pairs={{0,384},{128,0},{256,128},{384,256},{1,385},{129,1},{257,129},{385... | collective-permute-start | bytes 1572872 | tf_op jit(solution)/shard_map/ppermute | solution.py:63
  65.8 5.3 %copy-start.3 = (s32[128,2]{0,1:T(2,128)S(1)}, s32[128,2]{0,1:T(2,128)}, u32[]{:S(2)}) copy-start(s32[128,2]{0,1:T(2,128)} %param.22) | copy-start | bytes 3076
  65.8 5.3 %copy-start.4 = (s32[128]{0:T(128)S(1)}, s32[128]{0:T(128)}, u32[]{:S(2)}) copy-start(s32[128]{0:T(128)} %param.23) | copy-start | bytes 1540
  66.0 25.4 %collective-permute-start.7 = (bf16[4,8,512,64]{2,3,1,0:T(8,128)(2,1)S(1)}, bf16[4,8,512,64]{2,3,1,0:T(8,128)(2,1)}, u32[]{:S(2)}, u32[]{:S(2)}) collective-permute-start(bf16[4,8,512,64]{2,3,1,0:T(8,128)(2,1)S(1)} %pad_maximum_fusion), channel_id=1, source_target_pairs={{0,8},{8,0},{1,9},{9,1},{2,10},{10,2},{3,11},{11,3},{4,12},{12,4},... | collective-permute-start | bytes 6291464 | tf_op jit(solution)/shard_map/ppermute | solution.py:120
  76.2 27.9 %all-to-all-start = ((bf16[8,128,256]{1,2,0:T(8,128)(2,1)}), bf16[8,128,256]{1,2,0:T(8,128)(2,1)}, u32[]{:S(2)}, u32[]{:S(2)}) async-start(bf16[8,128,256]{1,2,0:T(8,128)(2,1)} %bitcast.13), calls=%async_computation | async-start | bytes 1048576 | tf_op jit(solution)/shard_map/all_to_all | solution.py:93
  104.1 21.8 %copy-start = (f32[128,512]{1,0:T(8,128)S(1)}, f32[128,512]{1,0:T(8,128)}, u32[]{:S(2)}) copy-start(f32[128,512]{1,0:T(8,128)} %reduce_sum.104) | copy-start | bytes 786436
  104.1 21.8 %copy-start.2 = (f32[512]{0:T(512)S(1)}, f32[512]{0:T(512)}, u32[]{:S(2)}) copy-start(f32[512]{0:T(512)} %param.18) | copy-start | bytes 6148
  104.1 21.5 %all-to-all-start.1 = ((bf16[8,128,256]{1,2,0:T(8,128)(2,1)}), bf16[8,128,256]{1,2,0:T(8,128)(2,1)S(1)}, u32[]{:S(2)}, u32[]{:S(2)}) async-start(bf16[8,128,256]{1,2,0:T(8,128)(2,1)} %bitcast.16), calls=%async_computation.1 | async-start | bytes 1048576 | tf_op jit(solution)/shard_map/all_to_all | solution.py:93
  126.9 20.1 %all-to-all-start.2 = ((bf16[64,2,512]{2,1,0:T(2,128)(2,1)}), bf16[64,2,512]{2,1,0:T(2,128)(2,1)S(1)}, u32[]{:S(2)}, u32[]{:S(2)}) async-start(bf16[64,2,512]{2,1,0:T(2,128)(2,1)} %reshape.280), calls=%async_computation.2 | async-start | bytes 262144 | tf_op jit(solution)/shard_map/all_to_all | solution.py:151
  148.2 30.6 %all-to-all-start.3 = ((bf16[8,128,512]{1,2,0:T(8,128)(2,1)}), bf16[8,128,512]{1,2,0:T(8,128)(2,1)S(1)}, u32[]{:S(2)}, u32[]{:S(2)}) async-start(bf16[8,128,512]{1,2,0:T(8,128)(2,1)} %broadcast_in_dim.28), calls=%async_computation.3 | async-start | bytes 2097152 | tf_op jit(solution)/shard_map/all_to_all | solution.py:57
  152.6 4.4 %copy-start.1 = (f32[4096]{0:T(1024)S(1)}, f32[4096]{0:T(1024)}, u32[]{:S(2)}) copy-start(f32[4096]{0:T(1024)} %param.24) | copy-start | bytes 49156
Sparse Core Ops, SparseCore 0:
  9.4 46.0 all-gather.5
  58.9 90.4 all-gather.3

commit v13 on v10

--- a/solution.py
+++ b/solution.py
@@ -80,9 +80,19 @@
     )
 
 
+def four_gather(value, axis):
+    from_next = shift(value, axis, -1)
+    from_last = shift(value, axis, 1)
+    half = value.shape[-1] // 2
+    via_last = shift(from_last[..., :half], axis, 1)
+    via_next = shift(from_next[..., half:], axis, -1)
+    opposite = jnp.concatenate([via_last, via_next], axis=-1)
+    return jnp.stack([value, from_next, opposite, from_last], axis=0)
+
+
 def gather_plane(shard):
     by_y = eight_gather(shard, "ry") if lax.axis_size("ry") == 8 else ring_gather(shard, "ry")
-    return ring_gather(by_y, "rx")
+    return four_gather(by_y, "rx") if lax.axis_size("rx") == 4 else ring_gather(by_y, "rx")
 
 
 def shards(

time: 187 us -> 188 us (level)
  waiting for transfers between devices: 81.1 us -> 74.8 us
  starting transfers between devices: 54 us -> 60.2 us
    ppermute x7 -> x8, waiting for transfers between devices: 30.2 us -> 24.1 us  [shift(): lax.ppermute(value, axis, [(k, (k + step) % size) for k in range(size)])]
    ppermute x1, starting transfers between devices: 5.01 us -> 9.41 us  [shards(): other_half = lax.ppermute(own_half, 'rc', [(0, 1), (1, 0)])]
    ppermute x7 -> x8, starting transfers between devices: 25.7 us -> 27.9 us  [shift(): lax.ppermute(value, axis, [(k, (k + step) % size) for k in range(size)])]
  transfers between devices with their start and end apart: 13 -> 14, of which waited for: 9 -> 10; matrix products, arithmetic and copies ran while one was open for 15% -> 15% of each run, Pallas kernels for 0% -> 0%
where the time goes in v13:
time: 188 us; the launch traced here: 187 us
  waiting for transfers between devices  74.8 us (40%)
  starting transfers between devices  60.2 us (32%)
  matrix products  21.5 us (11%)
  between operations  15.8 us (8%)
  other arithmetic  7.99 us (4%)
  local copies, waits for them, and re-layouts  6.37 us (3%)
    ppermute x8, starting transfers between devices, shift(): lax.ppermute(value, axis, [(k, (k + step) % size) for k in range(size)])  27.9 us
    ppermute x8, waiting for transfers between devices, shift(): lax.ppermute(value, axis, [(k, (k + step) % size) for k in range(size)])  24.1 us
    all_to_all x1, waiting for transfers between devices, shards(): lax.all_to_all(block_terms, 'tp', 0, 0, tiled=True).astype(jnp.float32)  23.3 us
    all_to_all x1, waiting for transfers between devices, gather_features(): blocks = lax.all_to_all(copies, 'tp', 0, 0, tiled=True)  15 us
    all_to_all x1, starting transfers between devices, shards(): lax.all_to_all(block_terms, 'tp', 0, 0, tiled=True).astype(jnp.float32)  10.5 us
    all_to_all x1, waiting for transfers between devices, shards(): lax.all_to_all(outgoing.reshape(requests, capacity, feature_width), REQ,...  9.95 us
    ppermute x1, starting transfers between devices, shards(): other_half = lax.ppermute(own_half, 'rc', [(0, 1), (1, 0)])  9.41 us
    all_to_all x1, starting transfers between devices, shards(): lax.all_to_all(outgoing.reshape(requests, capacity, feature_width), REQ,...  8.63 us
  transfers between devices with their start and end apart: 14, of which 10 were waited for; matrix products, arithmetic and copies ran while one was open for 15% of the time, Pallas kernels for 0%

profile of v13, /device:TPU:1, one launch (start us, length us, event | category | flops | bytes accessed | tf_op | source)
XLA Modules:
  0.0 186.8 jit_solution(12274360221214758180)
XLA Ops:
  8.0 5.9 %collective-permute-start = (bf16[512,64]{0,1:T(8,128)(2,1)}, bf16[512,64]{0,1:T(8,128)(2,1)S(1)}, u32[]{:S(2)}, u32[]{:S(2)}) collective-permute-start(bf16[512,64]{0,1:T(8,128)(2,1)} %param.13), channel_id=1, source_target_pairs={{0,112},{16,0},{32,16},{48,32},{64,48},{80,64},{96,80},{112,96},{1... | collective-permute-start | bytes 196616 | tf_op jit(solution)/shard_map/ppermute | solution.py:63
  13.9 1.9 %collective-permute-start.1 = (bf16[512,64]{0,1:T(8,128)(2,1)}, bf16[512,64]{0,1:T(8,128)(2,1)S(1)}, u32[]{:S(2)}, u32[]{:S(2)}) collective-permute-start(bf16[512,64]{0,1:T(8,128)(2,1)} %param.13), channel_id=1, source_target_pairs={{0,16},{16,32},{32,48},{48,64},{64,80},{80,96},{96,112},{112,0},{1... | collective-permute-start | bytes 196616 | tf_op jit(solution)/shard_map/ppermute | solution.py:63
  16.7 3.6 %collective-permute-done.1 = bf16[512,64]{0,1:T(8,128)(2,1)S(1)} collective-permute-done((bf16[512,64]{0,1:T(8,128)(2,1)}, bf16[512,64]{0,1:T(8,128)(2,1)S(1)}, u32[]{:S(2)}, u32[]{:S(2)}) %collective-permute-start.1) | collective-permute-done | bytes 65568 | tf_op jit(solution)/shard_map/ppermute | solution.py:63
  21.2 3.3 %collective-permute-start.2 = (bf16[3,512,64]{1,2,0:T(8,128)(2,1)S(1)}, bf16[3,512,64]{1,2,0:T(8,128)(2,1)S(1)}, u32[]{:S(2)}, u32[]{:S(2)}) collective-permute-start(bf16[3,512,64]{1,2,0:T(8,128)(2,1)S(1)} %pad_maximum_fusion.2), channel_id=1, source_target_pairs={{0,80},{16,96},{32,112},{48,0},{64,16},{80,32},{96,48},{112,64},{1... | collective-permute-start | bytes 589832 | tf_op jit(solution)/shard_map/ppermute | solution.py:63
  24.6 3.7 %collective-permute-start.3 = (bf16[3,512,64]{1,2,0:T(8,128)(2,1)S(1)}, bf16[3,512,64]{1,2,0:T(8,128)(2,1)S(1)}, u32[]{:S(2)}, u32[]{:S(2)}) collective-permute-start(bf16[3,512,64]{1,2,0:T(8,128)(2,1)S(1)} %pad_maximum_fusion.2), channel_id=1, source_target_pairs={{0,48},{16,64},{32,80},{48,96},{64,112},{80,0},{96,16},{112,32},{1... | collective-permute-start | bytes 589832 | tf_op jit(solution)/shard_map/ppermute | solution.py:63
  28.4 6.7 %collective-permute-done.2 = bf16[3,512,64]{1,2,0:T(8,128)(2,1)S(1)} collective-permute-done((bf16[3,512,64]{1,2,0:T(8,128)(2,1)S(1)}, bf16[3,512,64]{1,2,0:T(8,128)(2,1)S(1)}, u32[]{:S(2)}, u32[]{:S(2)}) %collective-permute-start.2) | collective-permute-done | bytes 196640 | tf_op jit(solution)/shard_map/ppermute | solution.py:63
  35.1 4.8 %collective-permute-done.3 = bf16[3,512,64]{1,2,0:T(8,128)(2,1)S(1)} collective-permute-done((bf16[3,512,64]{1,2,0:T(8,128)(2,1)S(1)}, bf16[3,512,64]{1,2,0:T(8,128)(2,1)S(1)}, u32[]{:S(2)}, u32[]{:S(2)}) %collective-permute-start.3) | collective-permute-done | bytes 196640 | tf_op jit(solution)/shard_map/ppermute | solution.py:63
  39.9 2.8 %collective-permute-start.5 = (bf16[8,512,64]{1,2,0:T(8,128)(2,1)S(1)}, bf16[8,512,64]{1,2,0:T(8,128)(2,1)S(1)}, u32[]{:S(2)}, u32[]{:S(2)}) collective-permute-start(bf16[8,512,64]{1,2,0:T(8,128)(2,1)S(1)} %constant_dynamic-update-slice_fusion), channel_id=1, source_target_pairs={{0,128},{128,256},{256,384},{384,0},{1,129},{129,257},{257,385},{3... | collective-permute-start | bytes 1572872 | tf_op jit(solution)/shard_map/ppermute | solution.py:63
  42.7 3.7 %collective-permute-start.4 = (bf16[8,512,64]{1,2,0:T(8,128)(2,1)S(1)}, bf16[8,512,64]{1,2,0:T(8,128)(2,1)S(1)}, u32[]{:S(2)}, u32[]{:S(2)}) collective-permute-start(bf16[8,512,64]{1,2,0:T(8,128)(2,1)S(1)} %constant_dynamic-update-slice_fusion), channel_id=1, source_target_pairs={{0,384},{128,0},{256,128},{384,256},{1,385},{129,1},{257,129},{385... | collective-permute-start | bytes 1572872 | tf_op jit(solution)/shard_map/ppermute | solution.py:63
  46.4 5.0 %collective-permute-done.5 = bf16[8,512,64]{1,2,0:T(8,128)(2,1)S(1)} collective-permute-done((bf16[8,512,64]{1,2,0:T(8,128)(2,1)S(1)}, bf16[8,512,64]{1,2,0:T(8,128)(2,1)S(1)}, u32[]{:S(2)}, u32[]{:S(2)}) %collective-permute-start.5) | collective-permute-done | bytes 524320 | tf_op jit(solution)/shard_map/ppermute | solution.py:63
  51.5 1.9 %collective-permute-start.6 = (bf16[8,512,32]{1,2,0:T(8,128)(2,1)S(1)}, bf16[8,512,32]{1,2,0:T(8,128)(2,1)S(1)}, u32[]{:S(2)}, u32[]{:S(2)}) collective-permute-start(bf16[8,512,32]{1,2,0:T(8,128)(2,1)S(1)} %slice.59), channel_id=1, source_target_pairs={{0,128},{128,256},{256,384},{384,0},{1,129},{129,257},{257,385},{3... | collective-permute-start | bytes 786440 | tf_op jit(solution)/shard_map/ppermute | solution.py:63
  53.4 4.6 %collective-permute-start.7 = (bf16[8,512,32]{1,2,0:T(8,128)(2,1)S(1)}, bf16[8,512,32]{1,2,0:T(8,128)(2,1)S(1)}, u32[]{:S(2)}, u32[]{:S(2)}) collective-permute-start(bf16[8,512,32]{1,2,0:T(8,128)(2,1)S(1)} %slice.60), channel_id=1, source_target_pairs={{0,384},{128,0},{256,128},{384,256},{1,385},{129,1},{257,129},{385... | collective-permute-start | bytes 786440 | tf_op jit(solution)/shard_map/ppermute | solution.py:63
  59.8 2.2 %collective-permute-done.7 = bf16[8,512,32]{1,2,0:T(8,128)(2,1)S(1)} collective-permute-done((bf16[8,512,32]{1,2,0:T(8,128)(2,1)S(1)}, bf16[8,512,32]{1,2,0:T(8,128)(2,1)S(1)}, u32[]{:S(2)}, u32[]{:S(2)}) %collective-permute-start.7) | collective-permute-done | bytes 262176 | tf_op jit(solution)/shard_map/ppermute | solution.py:63
  62.3 9.4 %collective-permute-start.8 = (bf16[4,8,512,64]{2,3,1,0:T(8,128)(2,1)S(1)}, bf16[4,8,512,64]{2,3,1,0:T(8,128)(2,1)}, u32[]{:S(2)}, u32[]{:S(2)}) collective-permute-start(bf16[4,8,512,64]{2,3,1,0:T(8,128)(2,1)S(1)} %pad_maximum_fusion), channel_id=1, source_target_pairs={{0,8},{8,0},{1,9},{9,1},{2,10},{10,2},{3,11},{11,3},{4,12},{12,4},... | collective-permute-start | bytes 6291464 | tf_op jit(solution)/shard_map/ppermute | solution.py:121
  75.6 2.3 %fusion.18 = (bf16[128,4,8,1,64]{0,4,2,1,3:T(8,128)(2,1)S(1)}, bf16[128,4,8,1,64]{0,4,2,1,3:T(8,128)(2,1)S(1)}) fusion(bf16[128,4,8,64]{0,3,2,1:T(8,128)(2,1)S(1)} %fusion.38, pred[]{:T(512)S(6)} %eq.112, bf16[4,8,512,64]{2,3,1,0:T(8,128)(2,1)} %collective-permute-done.8, f32[128,512]{1,0:T(8,128)S(1)} %reduce_sum.96), kind=kOutput, calls=%fused_computation.36 | convolution fusion | flops 269090816 | bytes 3932161 | tf_op jit(solution)/shard_map/gk,xykn->gxyn/dot_general | solution.py:126
  80.0 10.5 %all-to-all-start = ((bf16[8,128,512]{1,2,0:T(8,128)(2,1)}), bf16[8,128,512]{1,2,0:T(8,128)(2,1)S(1)}, u32[]{:S(2)}, u32[]{:S(2)}) async-start(bf16[8,128,512]{1,2,0:T(8,128)(2,1)} %bitcast.16), calls=%async_computation | async-start | bytes 2097152 | tf_op jit(solution)/shard_map/all_to_all | solution.py:141
  96.5 23.3 %all-to-all-done = bf16[8,128,512]{1,2,0:T(8,128)(2,1)S(1)} async-done(((bf16[8,128,512]{1,2,0:T(8,128)(2,1)}), bf16[8,128,512]{1,2,0:T(8,128)(2,1)S(1)}, u32[]{:S(2)}, u32[]{:S(2)}) %all-to-all-start) | async-done | bytes 1048608 | tf_op jit(solution)/shard_map/all_to_all | solution.py:141
  121.0 8.6 %all-to-all-start.1 = ((bf16[64,2,512]{2,1,0:T(2,128)(2,1)}), bf16[64,2,512]{2,1,0:T(2,128)(2,1)S(1)}, u32[]{:S(2)}, u32[]{:S(2)}) async-start(bf16[64,2,512]{2,1,0:T(2,128)(2,1)} %reshape.222), calls=%async_computation.1 | async-start | bytes 262144 | tf_op jit(solution)/shard_map/all_to_all | solution.py:159
  130.3 10.0 %all-to-all-done.1 = bf16[64,2,512]{2,1,0:T(2,128)(2,1)S(1)} async-done(((bf16[64,2,512]{2,1,0:T(2,128)(2,1)}), bf16[64,2,512]{2,1,0:T(2,128)(2,1)S(1)}, u32[]{:S(2)}, u32[]{:S(2)}) %all-to-all-start.1) | async-done | bytes 131104 | tf_op jit(solution)/shard_map/all_to_all | solution.py:159
  141.6 3.7 %all-to-all-start.2 = ((bf16[8,128,512]{1,2,0:T(8,128)(2,1)}), bf16[8,128,512]{1,2,0:T(8,128)(2,1)S(1)}, u32[]{:S(2)}, u32[]{:S(2)}) async-start(bf16[8,128,512]{1,2,0:T(8,128)(2,1)} %broadcast_in_dim.28), calls=%async_computation.2 | async-start | bytes 2097152 | tf_op jit(solution)/shard_map/all_to_all | solution.py:57
  146.1 4.3 %fusion = (f32[384]{0:T(512)S(1)}, bf16[384,4096]{1,0:T(8,128)(2,1)}) fusion(bf16[1,256,4096]{2,1,0:T(8,128)(2,1)} %all-gather.6.cloned.1.call-done, s32[384]{0:T(512)S(1)} %subtract_select_fusion, pred[384]{0:T(512)(128)(4,1)S(1)} %get-tuple-element.11), kind=kOutput, calls=%fused_computation.2 | convolution fusion | flops 811794048 | bytes 5246336 | tf_op jit(solution)/shard_map/dot_general | solution.py:187
  150.4 6.7 %fusion.4 = f32[384,768]{0,1:T(8,128)S(1)} fusion(bf16[4096,768]{1,0:T(8,128)(2,1)} %all-gather.4.cloned.1.call-done, bf16[384,4096]{1,0:T(8,128)(2,1)} %get-tuple-element.23, f32[4096]{0:T(1024)S(1)} %copy-done.1, f32[384]{0:T(512)S(1)} %add_rsqrt_fusion), kind=kOutput, calls=%fused_computation.8 | convolution fusion | flops 2422210560 | bytes 10634752 | tf_op jit(solution)/shard_map/dot_general | solution.py:190
  157.4 15.0 %all-to-all-done.2 = bf16[8,128,512]{1,2,0:T(8,128)(2,1)S(1)} async-done(((bf16[8,128,512]{1,2,0:T(8,128)(2,1)}), bf16[8,128,512]{1,2,0:T(8,128)(2,1)S(1)}, u32[]{:S(2)}, u32[]{:S(2)}) %all-to-all-start.2) | async-done | bytes 1048608 | tf_op jit(solution)/shard_map/all_to_all | solution.py:57
  172.9 5.4 %fusion.10 = f32[128,768]{0,1:T(8,128)S(1)} fusion(bf16[4096,768]{1,0:T(8,128)(2,1)} %all-gather.4.cloned.1.call-done, f32[128,4096]{1,0:T(8,128)S(1)} %get-tuple-element.25, f32[4096]{0:T(1024)S(1)} %copy-done.1, f32[128]{0:T(128)S(1)} %add_rsqrt_fusion.1), kind=kOutput, calls=%fused_computation.25 | convolution fusion | flops 806879232 | bytes 8798720 | tf_op jit(solution)/shard_map/dot_general | solution.py:203
  (75 shorter events, 21.4 us)
Async XLA Ops:
  6.5 139.5 %all-gather.6.cloned.1.call-start = ((), (), s32[]{:S(2)}) async-start(), calls=%async_computation.4 | async-start | bytes 2359296 | tf_op jit(solution)/shard_map/all_gather | solution.py:184
  7.3 143.2 %all-gather.4.cloned.1.call-start = ((), (), s32[]{:S(2)}) async-start(), calls=%async_computation.3 | async-start | bytes 6389760 | tf_op jit(solution)/shard_map/all_gather | solution.py:185
  8.0 8.7 %collective-permute-start = (bf16[512,64]{0,1:T(8,128)(2,1)}, bf16[512,64]{0,1:T(8,128)(2,1)S(1)}, u32[]{:S(2)}, u32[]{:S(2)}) collective-permute-start(bf16[512,64]{0,1:T(8,128)(2,1)} %param.13), channel_id=1, source_target_pairs={{0,112},{16,0},{32,16},{48,32},{64,48},{80,64},{96,80},{112,96},{1... | collective-permute-start | bytes 196616 | tf_op jit(solution)/shard_map/ppermute | solution.py:63
  13.9 6.4 %collective-permute-start.1 = (bf16[512,64]{0,1:T(8,128)(2,1)}, bf16[512,64]{0,1:T(8,128)(2,1)S(1)}, u32[]{:S(2)}, u32[]{:S(2)}) collective-permute-start(bf16[512,64]{0,1:T(8,128)(2,1)} %param.13), channel_id=1, source_target_pairs={{0,16},{16,32},{32,48},{48,64},{64,80},{80,96},{96,112},{112,0},{1... | collective-permute-start | bytes 196616 | tf_op jit(solution)/shard_map/ppermute | solution.py:63
  21.2 13.8 %collective-permute-start.2 = (bf16[3,512,64]{1,2,0:T(8,128)(2,1)S(1)}, bf16[3,512,64]{1,2,0:T(8,128)(2,1)S(1)}, u32[]{:S(2)}, u32[]{:S(2)}) collective-permute-start(bf16[3,512,64]{1,2,0:T(8,128)(2,1)S(1)} %pad_maximum_fusion.2), channel_id=1, source_target_pairs={{0,80},{16,96},{32,112},{48,0},{64,16},{80,32},{96,48},{112,64},{1... | collective-permute-start | bytes 589832 | tf_op jit(solution)/shard_map/ppermute | solution.py:63
  24.6 15.3 %collective-permute-start.3 = (bf16[3,512,64]{1,2,0:T(8,128)(2,1)S(1)}, bf16[3,512,64]{1,2,0:T(8,128)(2,1)S(1)}, u32[]{:S(2)}, u32[]{:S(2)}) collective-permute-start(bf16[3,512,64]{1,2,0:T(8,128)(2,1)S(1)} %pad_maximum_fusion.2), channel_id=1, source_target_pairs={{0,48},{16,64},{32,80},{48,96},{64,112},{80,0},{96,16},{112,32},{1... | collective-permute-start | bytes 589832 | tf_op jit(solution)/shard_map/ppermute | solution.py:63
  39.9 11.5 %collective-permute-start.5 = (bf16[8,512,64]{1,2,0:T(8,128)(2,1)S(1)}, bf16[8,512,64]{1,2,0:T(8,128)(2,1)S(1)}, u32[]{:S(2)}, u32[]{:S(2)}) collective-permute-start(bf16[8,512,64]{1,2,0:T(8,128)(2,1)S(1)} %constant_dynamic-update-slice_fusion), channel_id=1, source_target_pairs={{0,128},{128,256},{256,384},{384,0},{1,129},{129,257},{257,385},{3... | collective-permute-start | bytes 1572872 | tf_op jit(solution)/shard_map/ppermute | solution.py:63
  42.7 10.7 %collective-permute-start.4 = (bf16[8,512,64]{1,2,0:T(8,128)(2,1)S(1)}, bf16[8,512,64]{1,2,0:T(8,128)(2,1)S(1)}, u32[]{:S(2)}, u32[]{:S(2)}) collective-permute-start(bf16[8,512,64]{1,2,0:T(8,128)(2,1)S(1)} %constant_dynamic-update-slice_fusion), channel_id=1, source_target_pairs={{0,384},{128,0},{256,128},{384,256},{1,385},{129,1},{257,129},{385... | collective-permute-start | bytes 1572872 | tf_op jit(solution)/shard_map/ppermute | solution.py:63
  51.5 8.3 %collective-permute-start.6 = (bf16[8,512,32]{1,2,0:T(8,128)(2,1)S(1)}, bf16[8,512,32]{1,2,0:T(8,128)(2,1)S(1)}, u32[]{:S(2)}, u32[]{:S(2)}) collective-permute-start(bf16[8,512,32]{1,2,0:T(8,128)(2,1)S(1)} %slice.59), channel_id=1, source_target_pairs={{0,128},{128,256},{256,384},{384,0},{1,129},{129,257},{257,385},{3... | collective-permute-start | bytes 786440 | tf_op jit(solution)/shard_map/ppermute | solution.py:63
  53.4 8.5 %collective-permute-start.7 = (bf16[8,512,32]{1,2,0:T(8,128)(2,1)S(1)}, bf16[8,512,32]{1,2,0:T(8,128)(2,1)S(1)}, u32[]{:S(2)}, u32[]{:S(2)}) collective-permute-start(bf16[8,512,32]{1,2,0:T(8,128)(2,1)S(1)} %slice.60), channel_id=1, source_target_pairs={{0,384},{128,0},{256,128},{384,256},{1,385},{129,1},{257,129},{385... | collective-permute-start | bytes 786440 | tf_op jit(solution)/shard_map/ppermute | solution.py:63
  62.3 13.3 %collective-permute-start.8 = (bf16[4,8,512,64]{2,3,1,0:T(8,128)(2,1)S(1)}, bf16[4,8,512,64]{2,3,1,0:T(8,128)(2,1)}, u32[]{:S(2)}, u32[]{:S(2)}) collective-permute-start(bf16[4,8,512,64]{2,3,1,0:T(8,128)(2,1)S(1)} %pad_maximum_fusion), channel_id=1, source_target_pairs={{0,8},{8,0},{1,9},{9,1},{2,10},{10,2},{3,11},{11,3},{4,12},{12,4},... | collective-permute-start | bytes 6291464 | tf_op jit(solution)/shard_map/ppermute | solution.py:121
  78.9 11.6 %copy-start.3 = (s32[128,2]{0,1:T(2,128)S(1)}, s32[128,2]{0,1:T(2,128)}, u32[]{:S(2)}) copy-start(s32[128,2]{0,1:T(2,128)} %param.18) | copy-start | bytes 3076
  78.9 11.6 %copy-start.4 = (s32[128]{0:T(128)S(1)}, s32[128]{0:T(128)}, u32[]{:S(2)}) copy-start(s32[128]{0:T(128)} %param.19) | copy-start | bytes 1540
  78.9 13.4 %copy-start = (bf16[512,512]{1,0:T(8,128)(2,1)S(1)}, bf16[512,512]{1,0:T(8,128)(2,1)}, u32[]{:S(2)}) copy-start(bf16[512,512]{1,0:T(8,128)(2,1)} %param.12) | copy-start | bytes 1572868
  80.0 39.7 %all-to-all-start = ((bf16[8,128,512]{1,2,0:T(8,128)(2,1)}), bf16[8,128,512]{1,2,0:T(8,128)(2,1)S(1)}, u32[]{:S(2)}, u32[]{:S(2)}) async-start(bf16[8,128,512]{1,2,0:T(8,128)(2,1)} %bitcast.16), calls=%async_computation | async-start | bytes 2097152 | tf_op jit(solution)/shard_map/all_to_all | solution.py:141
  92.3 27.8 %copy-start.2 = (f32[512]{0:T(512)S(1)}, f32[512]{0:T(512)}, u32[]{:S(2)}) copy-start(f32[512]{0:T(512)} %param.14) | copy-start | bytes 6148
  121.0 19.3 %all-to-all-start.1 = ((bf16[64,2,512]{2,1,0:T(2,128)(2,1)}), bf16[64,2,512]{2,1,0:T(2,128)(2,1)S(1)}, u32[]{:S(2)}, u32[]{:S(2)}) async-start(bf16[64,2,512]{2,1,0:T(2,128)(2,1)} %reshape.222), calls=%async_computation.1 | async-start | bytes 262144 | tf_op jit(solution)/shard_map/all_to_all | solution.py:159
  141.6 30.8 %all-to-all-start.2 = ((bf16[8,128,512]{1,2,0:T(8,128)(2,1)}), bf16[8,128,512]{1,2,0:T(8,128)(2,1)S(1)}, u32[]{:S(2)}, u32[]{:S(2)}) async-start(bf16[8,128,512]{1,2,0:T(8,128)(2,1)} %broadcast_in_dim.28), calls=%async_computation.2 | async-start | bytes 2097152 | tf_op jit(solution)/shard_map/all_to_all | solution.py:57
  146.1 4.4 %copy-start.1 = (f32[4096]{0:T(1024)S(1)}, f32[4096]{0:T(1024)}, u32[]{:S(2)}) copy-start(f32[4096]{0:T(1024)} %param.20) | copy-start | bytes 49156
Sparse Core Ops, SparseCore 0:
  9.4 46.0 all-gather.5
  58.9 90.8 all-gather.3

commit v14 on v10

--- a/solution.py
+++ b/solution.py
@@ -170,7 +170,7 @@
     prompt_pick = ((prompt_row[:, None] == prompt_ids[None, :]) & from_prompt[:, None]).astype(
         jnp.bfloat16
     )
-    full_image = gather_features(arrived, tp_count)
+    full_image = lax.all_gather(arrived, "tp", axis=1, tiled=True)
     full_prompt = lax.all_gather(prompt[0], "tp", axis=1, tiled=True)
     full_weight = lax.all_gather(qkv_weight, REQ, axis=0, tiled=True)
     cosine_table, sine_table = rope_tables(seq_slots)

time: 187 us -> 206 us (1.10)
  the two profiles are of different devices: /device:TPU:1 before, /device:TPU:2 now
where the time goes in v14:
time: 206 us; the launch traced here: 205 us
  waiting for transfers between devices  109 us (53%)
  starting transfers between devices  47.1 us (23%)
  matrix products  20.3 us (10%)
  between operations  15.5 us (8%)
  other arithmetic  7.95 us (4%)
  local copies, waits for them, and re-layouts  5.81 us (3%)
    all_gather x1, waiting for transfers between devices, shards(): full_image = lax.all_gather(arrived, 'tp', axis=1, tiled=True)  37.1 us
    ppermute x7, waiting for transfers between devices, shift(): lax.ppermute(value, axis, [(k, (k + step) % size) for k in range(size)])  32.4 us
    ppermute x7, starting transfers between devices, shift(): lax.ppermute(value, axis, [(k, (k + step) % size) for k in range(size)])  24.8 us
    all_to_all x1, waiting for transfers between devices, shards(): lax.all_to_all(block_terms, 'tp', 0, 0, tiled=True).astype(jnp.float32)  23 us
    all_to_all x1, starting transfers between devices, shards(): lax.all_to_all(block_terms, 'tp', 0, 0, tiled=True).astype(jnp.float32)  10.3 us
    all_to_all x1, starting transfers between devices, shards(): lax.all_to_all(outgoing.reshape(requests, capacity, feature_width), REQ,...  9.77 us
    all_to_all x1, waiting for transfers between devices, shards(): lax.all_to_all(outgoing.reshape(requests, capacity, feature_width), REQ,...  9.31 us
    dot_general x1, matrix products, shards(): jnp.dot(prompt_normed, full_weight, preferred_element_type=jnp.float32)  5.87 us
  transfers between devices with their start and end apart: 13, of which 10 were waited for; matrix products, arithmetic and copies ran while one was open for 12% of the time, Pallas kernels for 0%

profile of v14, /device:TPU:2, one launch (start us, length us, event | category | flops | bytes accessed | tf_op | source)
XLA Modules:
  0.0 205.2 jit_solution(14258118456219797865)
XLA Ops:
  8.0 5.4 %collective-permute-start = (bf16[512,64]{0,1:T(8,128)(2,1)}, bf16[512,64]{0,1:T(8,128)(2,1)S(1)}, u32[]{:S(2)}, u32[]{:S(2)}) collective-permute-start(bf16[512,64]{0,1:T(8,128)(2,1)} %param.13), channel_id=1, source_target_pairs={{0,112},{16,0},{32,16},{48,32},{64,48},{80,64},{96,80},{112,96},{1... | collective-permute-start | bytes 196616 | tf_op jit(solution)/shard_map/ppermute | solution.py:63
  13.4 1.9 collective-permute-start.1
  16.2 4.8 %collective-permute-done.1 = bf16[512,64]{0,1:T(8,128)(2,1)S(1)} collective-permute-done((bf16[512,64]{0,1:T(8,128)(2,1)}, bf16[512,64]{0,1:T(8,128)(2,1)S(1)}, u32[]{:S(2)}, u32[]{:S(2)}) %collective-permute-start.1) | collective-permute-done | bytes 65568 | tf_op jit(solution)/shard_map/ppermute | solution.py:63
  21.8 3.6 %collective-permute-start.2 = (bf16[3,512,64]{1,2,0:T(8,128)(2,1)S(1)}, bf16[3,512,64]{1,2,0:T(8,128)(2,1)S(1)}, u32[]{:S(2)}, u32[]{:S(2)}) collective-permute-start(bf16[3,512,64]{1,2,0:T(8,128)(2,1)S(1)} %pad_maximum_fusion.2), channel_id=1, source_target_pairs={{0,80},{16,96},{32,112},{48,0},{64,16},{80,32},{96,48},{112,64},{1... | collective-permute-start | bytes 589832 | tf_op jit(solution)/shard_map/ppermute | solution.py:63
  25.5 4.0 %collective-permute-start.3 = (bf16[3,512,64]{1,2,0:T(8,128)(2,1)S(1)}, bf16[3,512,64]{1,2,0:T(8,128)(2,1)S(1)}, u32[]{:S(2)}, u32[]{:S(2)}) collective-permute-start(bf16[3,512,64]{1,2,0:T(8,128)(2,1)S(1)} %pad_maximum_fusion.2), channel_id=1, source_target_pairs={{0,48},{16,64},{32,80},{48,96},{64,112},{80,0},{96,16},{112,32},{1... | collective-permute-start | bytes 589832 | tf_op jit(solution)/shard_map/ppermute | solution.py:63
  29.5 7.2 %collective-permute-done.2 = bf16[3,512,64]{1,2,0:T(8,128)(2,1)S(1)} collective-permute-done((bf16[3,512,64]{1,2,0:T(8,128)(2,1)S(1)}, bf16[3,512,64]{1,2,0:T(8,128)(2,1)S(1)}, u32[]{:S(2)}, u32[]{:S(2)}) %collective-permute-start.2) | collective-permute-done | bytes 196640 | tf_op jit(solution)/shard_map/ppermute | solution.py:63
  36.7 7.1 %collective-permute-done.3 = bf16[3,512,64]{1,2,0:T(8,128)(2,1)S(1)} collective-permute-done((bf16[3,512,64]{1,2,0:T(8,128)(2,1)S(1)}, bf16[3,512,64]{1,2,0:T(8,128)(2,1)S(1)}, u32[]{:S(2)}, u32[]{:S(2)}) %collective-permute-start.3) | collective-permute-done | bytes 196640 | tf_op jit(solution)/shard_map/ppermute | solution.py:63
  43.8 4.0 %collective-permute-start.5 = (bf16[8,512,64]{1,2,0:T(8,128)(2,1)S(1)}, bf16[8,512,64]{1,2,0:T(8,128)(2,1)S(1)}, u32[]{:S(2)}, u32[]{:S(2)}) collective-permute-start(bf16[8,512,64]{1,2,0:T(8,128)(2,1)S(1)} %constant_dynamic-update-slice_fusion), channel_id=1, source_target_pairs={{0,256},{128,384},{256,0},{384,128},{1,257},{129,385},{257,1},{385... | collective-permute-start | bytes 1572872 | tf_op jit(solution)/shard_map/ppermute | solution.py:63
  47.9 1.9 collective-permute-start.6
  49.8 3.9 %collective-permute-start.4 = (bf16[8,512,64]{1,2,0:T(8,128)(2,1)S(1)}, bf16[8,512,64]{1,2,0:T(8,128)(2,1)S(1)}, u32[]{:S(2)}, u32[]{:S(2)}) collective-permute-start(bf16[8,512,64]{1,2,0:T(8,128)(2,1)S(1)} %constant_dynamic-update-slice_fusion), channel_id=1, source_target_pairs={{0,384},{128,0},{256,128},{384,256},{1,385},{129,1},{257,129},{385... | collective-permute-start | bytes 1572872 | tf_op jit(solution)/shard_map/ppermute | solution.py:63
  53.7 7.8 %collective-permute-done.5 = bf16[8,512,64]{1,2,0:T(8,128)(2,1)S(1)} collective-permute-done((bf16[8,512,64]{1,2,0:T(8,128)(2,1)S(1)}, bf16[8,512,64]{1,2,0:T(8,128)(2,1)S(1)}, u32[]{:S(2)}, u32[]{:S(2)}) %collective-permute-start.5) | collective-permute-done | bytes 524320 | tf_op jit(solution)/shard_map/ppermute | solution.py:63
  61.5 5.6 %collective-permute-done.6 = bf16[8,512,64]{1,2,0:T(8,128)(2,1)S(1)} collective-permute-done((bf16[8,512,64]{1,2,0:T(8,128)(2,1)S(1)}, bf16[8,512,64]{1,2,0:T(8,128)(2,1)S(1)}, u32[]{:S(2)}, u32[]{:S(2)}) %collective-permute-start.6) | collective-permute-done | bytes 524320 | tf_op jit(solution)/shard_map/ppermute | solution.py:63
  67.4 1.9 collective-permute-start.7
  73.5 2.3 %fusion.18 = (bf16[128,4,8,1,64]{0,4,2,1,3:T(8,128)(2,1)S(1)}, bf16[128,4,8,1,64]{0,4,2,1,3:T(8,128)(2,1)S(1)}) fusion(bf16[128,4,8,64]{0,3,2,1:T(8,128)(2,1)S(1)} %fusion.38, pred[]{:T(512)S(6)} %eq.112, bf16[4,8,512,64]{2,3,1,0:T(8,128)(2,1)} %collective-permute-done.7, f32[128,512]{1,0:T(8,128)S(1)} %reduce_sum.96), kind=kOutput, calls=%fused_computation.36 | convolution fusion | flops 269090816 | bytes 3932161 | tf_op jit(solution)/shard_map/gk,xykn->gxyn/dot_general | solution.py:116
  78.0 10.3 %all-to-all-start = ((bf16[8,128,512]{1,2,0:T(8,128)(2,1)}), bf16[8,128,512]{1,2,0:T(8,128)(2,1)S(1)}, u32[]{:S(2)}, u32[]{:S(2)}) async-start(bf16[8,128,512]{1,2,0:T(8,128)(2,1)} %bitcast.16), calls=%async_computation | async-start | bytes 2097152 | tf_op jit(solution)/shard_map/all_to_all | solution.py:131
  94.4 23.0 %all-to-all-done = bf16[8,128,512]{1,2,0:T(8,128)(2,1)S(1)} async-done(((bf16[8,128,512]{1,2,0:T(8,128)(2,1)}), bf16[8,128,512]{1,2,0:T(8,128)(2,1)S(1)}, u32[]{:S(2)}, u32[]{:S(2)}) %all-to-all-start) | async-done | bytes 1048608 | tf_op jit(solution)/shard_map/all_to_all | solution.py:131
  118.6 9.8 %all-to-all-start.1 = ((bf16[64,2,512]{2,1,0:T(2,128)(2,1)}), bf16[64,2,512]{2,1,0:T(2,128)(2,1)S(1)}, u32[]{:S(2)}, u32[]{:S(2)}) async-start(bf16[64,2,512]{2,1,0:T(2,128)(2,1)} %reshape.221), calls=%async_computation.1 | async-start | bytes 262144 | tf_op jit(solution)/shard_map/all_to_all | solution.py:149
  129.4 9.3 %all-to-all-done.1 = bf16[64,2,512]{2,1,0:T(2,128)(2,1)S(1)} async-done(((bf16[64,2,512]{2,1,0:T(2,128)(2,1)}), bf16[64,2,512]{2,1,0:T(2,128)(2,1)S(1)}, u32[]{:S(2)}, u32[]{:S(2)}) %all-to-all-start.1) | async-done | bytes 131104 | tf_op jit(solution)/shard_map/all_to_all | solution.py:149
  140.1 2.8 %fusion = (f32[384]{0:T(512)S(1)}, bf16[384,4096]{1,0:T(8,128)(2,1)S(1)}) fusion(bf16[1,256,4096]{2,1,0:T(8,128)(2,1)} %all-gather.9.cloned.1.call-done, s32[384]{0:T(512)S(1)} %subtract_select_fusion, pred[384]{0:T(512)(128)(4,1)S(1)} %get-tuple-element.11), kind=kOutput, calls=%fused_computation.2 | convolution fusion | flops 811794048 | bytes 5246336 | tf_op jit(solution)/shard_map/dot_general | solution.py:177
  142.9 3.8 %all-gather.7.cloned.1.call-done = bf16[4096,768]{1,0:T(8,128)(2,1)} async-done(((bf16[64,768]{1,0:T(8,128)(2,1)}), bf16[4096,768]{1,0:T(8,128)(2,1)}) %all-gather.7.cloned.1.call-update) | async-done | bytes 6291472 | tf_op jit(solution)/shard_map/all_gather | solution.py:175
  146.6 5.9 %fusion.4 = f32[384,768]{0,1:T(8,128)S(1)} fusion(bf16[4096,768]{1,0:T(8,128)(2,1)} %all-gather.7.cloned.1.call-done, bf16[384,4096]{1,0:T(8,128)(2,1)S(1)} %get-tuple-element.23, f32[4096]{0:T(1024)S(1)} %copy-done.1, f32[384]{0:T(512)S(1)} %add_rsqrt_fusion), kind=kOutput, calls=%fused_computation.8 | convolution fusion | flops 2422210560 | bytes 10634752 | tf_op jit(solution)/shard_map/dot_general | solution.py:180
  152.7 37.1 %all-gather.5.cloned.1.call-done = bf16[128,4096]{1,0:T(8,128)(2,1)} async-done(((bf16[128,512]{1,0:T(8,128)(2,1)}), bf16[128,4096]{1,0:T(8,128)(2,1)}) %all-gather.5.cloned.1.call-update) | async-done | bytes 1048592 | tf_op jit(solution)/shard_map/all_gather | solution.py:173
  189.9 1.8 multiply_reduce_fusion
  191.7 5.4 %fusion.10 = f32[128,768]{0,1:T(8,128)S(1)} fusion(bf16[4096,768]{1,0:T(8,128)(2,1)} %all-gather.7.cloned.1.call-done, f32[128,4096]{1,0:T(8,128)S(1)} %get-tuple-element.25, f32[4096]{0:T(1024)S(1)} %copy-done.1, f32[128]{0:T(128)S(1)} %add_rsqrt_fusion.1), kind=kOutput, calls=%fused_computation.25 | convolution fusion | flops 806879232 | bytes 8798720 | tf_op jit(solution)/shard_map/dot_general | solution.py:193
  (69 shorter events, 19.1 us)
Async XLA Ops:
  6.5 133.5 %all-gather.9.cloned.1.call-start = ((), (), s32[]{:S(2)}) async-start(), calls=%async_computation.4 | async-start | bytes 2359296 | tf_op jit(solution)/shard_map/all_gather | solution.py:174
  7.3 139.4 %all-gather.7.cloned.1.call-start = ((), (), s32[]{:S(2)}) async-start(), calls=%async_computation.3 | async-start | bytes 6389760 | tf_op jit(solution)/shard_map/all_gather | solution.py:175
  8.0 8.2 %collective-permute-start = (bf16[512,64]{0,1:T(8,128)(2,1)}, bf16[512,64]{0,1:T(8,128)(2,1)S(1)}, u32[]{:S(2)}, u32[]{:S(2)}) collective-permute-start(bf16[512,64]{0,1:T(8,128)(2,1)} %param.13), channel_id=1, source_target_pairs={{0,112},{16,0},{32,16},{48,32},{64,48},{80,64},{96,80},{112,96},{1... | collective-permute-start | bytes 196616 | tf_op jit(solution)/shard_map/ppermute | solution.py:63
  13.4 7.6 %collective-permute-start.1 = (bf16[512,64]{0,1:T(8,128)(2,1)}, bf16[512,64]{0,1:T(8,128)(2,1)S(1)}, u32[]{:S(2)}, u32[]{:S(2)}) collective-permute-start(bf16[512,64]{0,1:T(8,128)(2,1)} %param.13), channel_id=1, source_target_pairs={{0,16},{16,32},{32,48},{48,64},{64,80},{80,96},{96,112},{112,0},{1... | collective-permute-start | bytes 196616 | tf_op jit(solution)/shard_map/ppermute | solution.py:63
  21.8 14.9 %collective-permute-start.2 = (bf16[3,512,64]{1,2,0:T(8,128)(2,1)S(1)}, bf16[3,512,64]{1,2,0:T(8,128)(2,1)S(1)}, u32[]{:S(2)}, u32[]{:S(2)}) collective-permute-start(bf16[3,512,64]{1,2,0:T(8,128)(2,1)S(1)} %pad_maximum_fusion.2), channel_id=1, source_target_pairs={{0,80},{16,96},{32,112},{48,0},{64,16},{80,32},{96,48},{112,64},{1... | collective-permute-start | bytes 589832 | tf_op jit(solution)/shard_map/ppermute | solution.py:63
  25.5 18.3 %collective-permute-start.3 = (bf16[3,512,64]{1,2,0:T(8,128)(2,1)S(1)}, bf16[3,512,64]{1,2,0:T(8,128)(2,1)S(1)}, u32[]{:S(2)}, u32[]{:S(2)}) collective-permute-start(bf16[3,512,64]{1,2,0:T(8,128)(2,1)S(1)} %pad_maximum_fusion.2), channel_id=1, source_target_pairs={{0,48},{16,64},{32,80},{48,96},{64,112},{80,0},{96,16},{112,32},{1... | collective-permute-start | bytes 589832 | tf_op jit(solution)/shard_map/ppermute | solution.py:63
  43.8 17.7 %collective-permute-start.5 = (bf16[8,512,64]{1,2,0:T(8,128)(2,1)S(1)}, bf16[8,512,64]{1,2,0:T(8,128)(2,1)S(1)}, u32[]{:S(2)}, u32[]{:S(2)}) collective-permute-start(bf16[8,512,64]{1,2,0:T(8,128)(2,1)S(1)} %constant_dynamic-update-slice_fusion), channel_id=1, source_target_pairs={{0,256},{128,384},{256,0},{384,128},{1,257},{129,385},{257,1},{385... | collective-permute-start | bytes 1572872 | tf_op jit(solution)/shard_map/ppermute | solution.py:63
  47.9 19.2 %collective-permute-start.6 = (bf16[8,512,64]{1,2,0:T(8,128)(2,1)S(1)}, bf16[8,512,64]{1,2,0:T(8,128)(2,1)S(1)}, u32[]{:S(2)}, u32[]{:S(2)}) collective-permute-start(bf16[8,512,64]{1,2,0:T(8,128)(2,1)S(1)} %constant_dynamic-update-slice_fusion), channel_id=1, source_target_pairs={{0,128},{128,256},{256,384},{384,0},{1,129},{129,257},{257,385},{3... | collective-permute-start | bytes 1572872 | tf_op jit(solution)/shard_map/ppermute | solution.py:63
  49.8 17.3 %collective-permute-start.4 = (bf16[8,512,64]{1,2,0:T(8,128)(2,1)S(1)}, bf16[8,512,64]{1,2,0:T(8,128)(2,1)S(1)}, u32[]{:S(2)}, u32[]{:S(2)}) collective-permute-start(bf16[8,512,64]{1,2,0:T(8,128)(2,1)S(1)} %constant_dynamic-update-slice_fusion), channel_id=1, source_target_pairs={{0,384},{128,0},{256,128},{384,256},{1,385},{129,1},{257,129},{385... | collective-permute-start | bytes 1572872 | tf_op jit(solution)/shard_map/ppermute | solution.py:63
  67.4 6.2 %collective-permute-start.7 = (bf16[4,8,512,64]{2,3,1,0:T(8,128)(2,1)S(1)}, bf16[4,8,512,64]{2,3,1,0:T(8,128)(2,1)}, u32[]{:S(2)}, u32[]{:S(2)}) collective-permute-start(bf16[4,8,512,64]{2,3,1,0:T(8,128)(2,1)S(1)} %pad_maximum_fusion), channel_id=1, source_target_pairs={{0,8},{8,0},{1,9},{9,1},{2,10},{10,2},{3,11},{11,3},{4,12},{12,4},... | collective-permute-start | bytes 6291464 | tf_op jit(solution)/shard_map/ppermute | solution.py:111
  76.8 11.5 %copy-start.3 = (s32[128,2]{0,1:T(2,128)S(1)}, s32[128,2]{0,1:T(2,128)}, u32[]{:S(2)}) copy-start(s32[128,2]{0,1:T(2,128)} %param.18) | copy-start | bytes 3076
  76.8 11.5 %copy-start.4 = (s32[128]{0:T(128)S(1)}, s32[128]{0:T(128)}, u32[]{:S(2)}) copy-start(s32[128]{0:T(128)} %param.19) | copy-start | bytes 1540
  76.8 13.2 %copy-start = (bf16[512,512]{1,0:T(8,128)(2,1)S(1)}, bf16[512,512]{1,0:T(8,128)(2,1)}, u32[]{:S(2)}) copy-start(bf16[512,512]{1,0:T(8,128)(2,1)} %param.12) | copy-start | bytes 1572868
  78.0 39.4 %all-to-all-start = ((bf16[8,128,512]{1,2,0:T(8,128)(2,1)}), bf16[8,128,512]{1,2,0:T(8,128)(2,1)S(1)}, u32[]{:S(2)}, u32[]{:S(2)}) async-start(bf16[8,128,512]{1,2,0:T(8,128)(2,1)} %bitcast.16), calls=%async_computation | async-start | bytes 2097152 | tf_op jit(solution)/shard_map/all_to_all | solution.py:131
  90.1 27.6 %copy-start.2 = (f32[512]{0:T(512)S(1)}, f32[512]{0:T(512)}, u32[]{:S(2)}) copy-start(f32[512]{0:T(512)} %param.14) | copy-start | bytes 6148
  118.6 20.1 %all-to-all-start.1 = ((bf16[64,2,512]{2,1,0:T(2,128)(2,1)}), bf16[64,2,512]{2,1,0:T(2,128)(2,1)S(1)}, u32[]{:S(2)}, u32[]{:S(2)}) async-start(bf16[64,2,512]{2,1,0:T(2,128)(2,1)} %reshape.221), calls=%async_computation.1 | async-start | bytes 262144 | tf_op jit(solution)/shard_map/all_to_all | solution.py:149
  128.4 61.5 %all-gather.5.cloned.1.call-start = ((), (), s32[]{:S(2)}) async-start(), calls=%async_computation.2 | async-start | bytes 1179648 | tf_op jit(solution)/shard_map/all_gather | solution.py:173
  140.1 6.6 %copy-start.1 = (f32[4096]{0:T(1024)S(1)}, f32[4096]{0:T(1024)}, u32[]{:S(2)}) copy-start(f32[4096]{0:T(1024)} %param.20) | copy-start | bytes 49156
Sparse Core Ops, SparseCore 0:
  9.4 49.2 all-gather.8
  62.1 84.4 all-gather.6
  148.7 41.1 all-gather.4

commit v15 on v10

--- a/solution.py
+++ b/solution.py
@@ -108,14 +108,15 @@
         vision_residual.astype(jnp.float32).reshape(-1, 4, feature_width), axis=1
     )
     own_half = gather_plane(out_weight)
-    other_half = lax.ppermute(own_half, "rc", [(0, 1), (1, 0)])
+    partner_context = lax.ppermute(merged_context, "rc", [(0, 1), (1, 0)])
     core = lax.axis_index("rc")
     own_part = jnp.einsum(
         "gk,xykn->gxyn", merged_context, own_half, preferred_element_type=jnp.float32
-    )
-    other_part = jnp.einsum(
-        "gk,xykn->gxyn", merged_context, other_half, preferred_element_type=jnp.float32
-    )
+    ).astype(jnp.bfloat16)
+    partner_part = jnp.einsum(
+        "gk,xykn->gxyn", partner_context, own_half, preferred_element_type=jnp.float32
+    ).astype(jnp.bfloat16)
+    other_part = lax.ppermute(partner_part, "rc", [(0, 1), (1, 0)])
     partial_value = jnp.stack(
         [jnp.where(core == 0, own_part, other_part), jnp.where(core == 0, other_part, own_part)],
         axis=3,

time: 187 us -> 184 us (0.984)
  waiting for transfers between devices: 81.1 us -> 70.1 us
  starting transfers between devices: 54 us -> 62.5 us
    ppermute x7, waiting for transfers between devices: 30.2 us -> 19.7 us  [shift(): lax.ppermute(value, axis, [(k, (k + step) % size) for k in range(size)])]
    ppermute x1 -> x2, starting transfers between devices: 5.01 us -> 13.5 us  [the longest x1 8.54 us: shards(): partner_context = lax.ppermute(merged_context, 'rc', [(0, 1), (1, 0)])]
    all_to_all x1, waiting for transfers between devices: 14.9 us -> 12.2 us  [gather_features(): blocks = lax.all_to_all(copies, 'tp', 0, 0, tiled=True)]
    all_gather x1, waiting for transfers between devices: 0.01 us -> 2.72 us  [shards(): full_weight = lax.all_gather(qkv_weight, REQ, axis=0, tiled=True)]
  transfers between devices with their start and end apart: 13 -> 14, of which waited for: 9 -> 9; matrix products, arithmetic and copies ran while one was open for 15% -> 15% of each run, Pallas kernels for 0% -> 0%
where the time goes in v15:
time: 184 us
  waiting for transfers between devices  70.1 us (38%)
  starting transfers between devices  62.5 us (34%)
  matrix products  22 us (12%)
  between operations  15.9 us (9%)
  other arithmetic  7.85 us (4%)
  local copies, waits for them, and re-layouts  5.3 us (3%)
    ppermute x7, starting transfers between devices, shift(): lax.ppermute(value, axis, [(k, (k + step) % size) for k in range(size)])  25.7 us
    all_to_all x1, waiting for transfers between devices, shards(): lax.all_to_all(block_terms, 'tp', 0, 0, tiled=True).astype(jnp.float32)  23.1 us
    ppermute x7, waiting for transfers between devices, shift(): lax.ppermute(value, axis, [(k, (k + step) % size) for k in range(size)])  19.7 us
    all_to_all x1, waiting for transfers between devices, gather_features(): blocks = lax.all_to_all(copies, 'tp', 0, 0, tiled=True)  12.2 us
    all_to_all x1, waiting for transfers between devices, shards(): lax.all_to_all(outgoing.reshape(requests, capacity, feature_width), REQ,...  9.95 us
    all_to_all x1, starting transfers between devices, shards(): lax.all_to_all(block_terms, 'tp', 0, 0, tiled=True).astype(jnp.float32)  9.9 us
    all_to_all x1, starting transfers between devices, shards(): lax.all_to_all(outgoing.reshape(requests, capacity, feature_width), REQ,...  9.57 us
    ppermute x1, starting transfers between devices, shards(): partner_context = lax.ppermute(merged_context, 'rc', [(0, 1), (1, 0)])  8.54 us
  transfers between devices with their start and end apart: 14, of which 9 were waited for; matrix products, arithmetic and copies ran while one was open for 15% of the time, Pallas kernels for 0%

profile of v15, /device:TPU:1, one launch (start us, length us, event | category | flops | bytes accessed | tf_op | source)
XLA Modules:
  0.0 183.6 jit_solution(7764514746953656127)
XLA Ops:
  8.0 5.9 %collective-permute-start = (bf16[512,64]{0,1:T(8,128)(2,1)}, bf16[512,64]{0,1:T(8,128)(2,1)S(1)}, u32[]{:S(2)}, u32[]{:S(2)}) collective-permute-start(bf16[512,64]{0,1:T(8,128)(2,1)} %param.13), channel_id=1, source_target_pairs={{0,112},{16,0},{32,16},{48,32},{64,48},{80,64},{96,80},{112,96},{1... | collective-permute-start | bytes 196616 | tf_op jit(solution)/shard_map/ppermute | solution.py:63
  13.9 1.9 %collective-permute-start.1 = (bf16[512,64]{0,1:T(8,128)(2,1)}, bf16[512,64]{0,1:T(8,128)(2,1)S(1)}, u32[]{:S(2)}, u32[]{:S(2)}) collective-permute-start(bf16[512,64]{0,1:T(8,128)(2,1)} %param.13), channel_id=1, source_target_pairs={{0,16},{16,32},{32,48},{48,64},{64,80},{80,96},{96,112},{112,0},{1... | collective-permute-start | bytes 196616 | tf_op jit(solution)/shard_map/ppermute | solution.py:63
  16.7 3.6 %collective-permute-done.1 = bf16[512,64]{0,1:T(8,128)(2,1)S(1)} collective-permute-done((bf16[512,64]{0,1:T(8,128)(2,1)}, bf16[512,64]{0,1:T(8,128)(2,1)S(1)}, u32[]{:S(2)}, u32[]{:S(2)}) %collective-permute-start.1) | collective-permute-done | bytes 65568 | tf_op jit(solution)/shard_map/ppermute | solution.py:63
  21.2 3.3 %collective-permute-start.2 = (bf16[3,512,64]{1,2,0:T(8,128)(2,1)S(1)}, bf16[3,512,64]{1,2,0:T(8,128)(2,1)S(1)}, u32[]{:S(2)}, u32[]{:S(2)}) collective-permute-start(bf16[3,512,64]{1,2,0:T(8,128)(2,1)S(1)} %pad_maximum_fusion.4), channel_id=1, source_target_pairs={{0,80},{16,96},{32,112},{48,0},{64,16},{80,32},{96,48},{112,64},{1... | collective-permute-start | bytes 589832 | tf_op jit(solution)/shard_map/ppermute | solution.py:63
  24.6 3.7 %collective-permute-start.3 = (bf16[3,512,64]{1,2,0:T(8,128)(2,1)S(1)}, bf16[3,512,64]{1,2,0:T(8,128)(2,1)S(1)}, u32[]{:S(2)}, u32[]{:S(2)}) collective-permute-start(bf16[3,512,64]{1,2,0:T(8,128)(2,1)S(1)} %pad_maximum_fusion.4), channel_id=1, source_target_pairs={{0,48},{16,64},{32,80},{48,96},{64,112},{80,0},{96,16},{112,32},{1... | collective-permute-start | bytes 589832 | tf_op jit(solution)/shard_map/ppermute | solution.py:63
  28.4 6.7 %collective-permute-done.2 = bf16[3,512,64]{1,2,0:T(8,128)(2,1)S(1)} collective-permute-done((bf16[3,512,64]{1,2,0:T(8,128)(2,1)S(1)}, bf16[3,512,64]{1,2,0:T(8,128)(2,1)S(1)}, u32[]{:S(2)}, u32[]{:S(2)}) %collective-permute-start.2) | collective-permute-done | bytes 196640 | tf_op jit(solution)/shard_map/ppermute | solution.py:63
  35.1 4.8 %collective-permute-done.3 = bf16[3,512,64]{1,2,0:T(8,128)(2,1)S(1)} collective-permute-done((bf16[3,512,64]{1,2,0:T(8,128)(2,1)S(1)}, bf16[3,512,64]{1,2,0:T(8,128)(2,1)S(1)}, u32[]{:S(2)}, u32[]{:S(2)}) %collective-permute-start.3) | collective-permute-done | bytes 196640 | tf_op jit(solution)/shard_map/ppermute | solution.py:63
  39.9 4.3 %collective-permute-start.5 = (bf16[8,512,64]{1,2,0:T(8,128)(2,1)S(1)}, bf16[8,512,64]{1,2,0:T(8,128)(2,1)S(1)}, u32[]{:S(2)}, u32[]{:S(2)}) collective-permute-start(bf16[8,512,64]{1,2,0:T(8,128)(2,1)S(1)} %constant_dynamic-update-slice_fusion), channel_id=1, source_target_pairs={{0,256},{128,384},{256,0},{384,128},{1,257},{129,385},{257,1},{385... | collective-permute-start | bytes 1572872 | tf_op jit(solution)/shard_map/ppermute | solution.py:63
  44.2 2.2 %collective-permute-start.6 = (bf16[8,512,64]{1,2,0:T(8,128)(2,1)S(1)}, bf16[8,512,64]{1,2,0:T(8,128)(2,1)S(1)}, u32[]{:S(2)}, u32[]{:S(2)}) collective-permute-start(bf16[8,512,64]{1,2,0:T(8,128)(2,1)S(1)} %constant_dynamic-update-slice_fusion), channel_id=1, source_target_pairs={{0,128},{128,256},{256,384},{384,0},{1,129},{129,257},{257,385},{3... | collective-permute-start | bytes 1572872 | tf_op jit(solution)/shard_map/ppermute | solution.py:63
  46.4 4.3 %collective-permute-start.4 = (bf16[8,512,64]{1,2,0:T(8,128)(2,1)S(1)}, bf16[8,512,64]{1,2,0:T(8,128)(2,1)}, u32[]{:S(2)}, u32[]{:S(2)}) collective-permute-start(bf16[8,512,64]{1,2,0:T(8,128)(2,1)S(1)} %constant_dynamic-update-slice_fusion), channel_id=1, source_target_pairs={{0,384},{128,0},{256,128},{384,256},{1,385},{129,1},{257,129},{385... | collective-permute-start | bytes 1572872 | tf_op jit(solution)/shard_map/ppermute | solution.py:63
  51.7 8.5 %collective-permute-start.7 = (bf16[128,512]{1,0:T(8,128)(2,1)S(1)}, bf16[128,512]{1,0:T(8,128)(2,1)S(1)}, u32[]{:S(2)}, u32[]{:S(2)}) collective-permute-start(bf16[128,512]{1,0:T(8,128)(2,1)S(1)} %multiply_convert_fusion.2), channel_id=1, source_target_pairs={{0,8},{8,0},{1,9},{9,1},{2,10},{10,2},{3,11},{11,3},{4,12},{12,4},... | collective-permute-start | bytes 393224 | tf_op jit(solution)/shard_map/ppermute | solution.py:111
  61.2 4.5 %collective-permute-done.6 = bf16[8,512,64]{1,2,0:T(8,128)(2,1)S(1)} collective-permute-done((bf16[8,512,64]{1,2,0:T(8,128)(2,1)S(1)}, bf16[8,512,64]{1,2,0:T(8,128)(2,1)S(1)}, u32[]{:S(2)}, u32[]{:S(2)}) %collective-permute-start.6) | collective-permute-done | bytes 524320 | tf_op jit(solution)/shard_map/ppermute | solution.py:63
  67.5 5.0 %collective-permute-start.8 = (bf16[128,4,8,64]{0,3,2,1:T(8,128)(2,1)S(1)}, bf16[128,4,8,64]{0,3,2,1:T(8,128)(2,1)S(1)}, u32[]{:S(2)}, u32[]{:S(2)}) collective-permute-start(bf16[128,4,8,64]{0,3,2,1:T(8,128)(2,1)S(1)} %convolution_convert_fusion.3), channel_id=1, source_target_pairs={{0,8},{8,0},{1,9},{9,1},{2,10},{10,2},{3,11},{11,3},{4,12},{12,4},... | collective-permute-start | bytes 1572872 | tf_op jit(solution)/shard_map/ppermute | solution.py:119
  72.6 1.7 convolution_convert_fusion.4
  76.5 9.9 %all-to-all-start = ((bf16[8,128,512]{1,2,0:T(8,128)(2,1)}), bf16[8,128,512]{1,2,0:T(8,128)(2,1)S(1)}, u32[]{:S(2)}, u32[]{:S(2)}) async-start(bf16[8,128,512]{1,2,0:T(8,128)(2,1)} %bitcast.17), calls=%async_computation | async-start | bytes 2097152 | tf_op jit(solution)/shard_map/all_to_all | solution.py:132
  92.6 23.1 %all-to-all-done = bf16[8,128,512]{1,2,0:T(8,128)(2,1)S(1)} async-done(((bf16[8,128,512]{1,2,0:T(8,128)(2,1)}), bf16[8,128,512]{1,2,0:T(8,128)(2,1)S(1)}, u32[]{:S(2)}, u32[]{:S(2)}) %all-to-all-start) | async-done | bytes 1048608 | tf_op jit(solution)/shard_map/all_to_all | solution.py:132
  116.9 9.6 %all-to-all-start.1 = ((bf16[64,2,512]{2,1,0:T(2,128)(2,1)}), bf16[64,2,512]{2,1,0:T(2,128)(2,1)S(1)}, u32[]{:S(2)}, u32[]{:S(2)}) async-start(bf16[64,2,512]{2,1,0:T(2,128)(2,1)} %reshape.222), calls=%async_computation.1 | async-start | bytes 262144 | tf_op jit(solution)/shard_map/all_to_all | solution.py:150
  127.3 10.0 %all-to-all-done.1 = bf16[64,2,512]{2,1,0:T(2,128)(2,1)S(1)} async-done(((bf16[64,2,512]{2,1,0:T(2,128)(2,1)}), bf16[64,2,512]{2,1,0:T(2,128)(2,1)S(1)}, u32[]{:S(2)}, u32[]{:S(2)}) %all-to-all-start.1) | async-done | bytes 131104 | tf_op jit(solution)/shard_map/all_to_all | solution.py:150
  138.5 3.7 %all-to-all-start.2 = ((bf16[8,128,512]{1,2,0:T(8,128)(2,1)}), bf16[8,128,512]{1,2,0:T(8,128)(2,1)S(1)}, u32[]{:S(2)}, u32[]{:S(2)}) async-start(bf16[8,128,512]{1,2,0:T(8,128)(2,1)} %broadcast_in_dim.28), calls=%async_computation.2 | async-start | bytes 2097152 | tf_op jit(solution)/shard_map/all_to_all | solution.py:57
  142.9 4.4 %fusion = (f32[384]{0:T(512)S(1)}, bf16[384,4096]{1,0:T(8,128)(2,1)}) fusion(bf16[1,256,4096]{2,1,0:T(8,128)(2,1)} %all-gather.6.cloned.1.call-done, s32[384]{0:T(512)S(1)} %subtract_select_fusion, pred[384]{0:T(512)(128)(4,1)S(1)} %get-tuple-element.11), kind=kOutput, calls=%fused_computation.2 | convolution fusion | flops 811794048 | bytes 5246336 | tf_op jit(solution)/shard_map/dot_general | solution.py:178
  147.3 2.7 %all-gather.4.cloned.1.call-done = bf16[4096,768]{1,0:T(8,128)(2,1)} async-done(((bf16[64,768]{1,0:T(8,128)(2,1)}), bf16[4096,768]{1,0:T(8,128)(2,1)}) %all-gather.4.cloned.1.call-update) | async-done | bytes 6291472 | tf_op jit(solution)/shard_map/all_gather | solution.py:176
  150.0 6.7 %fusion.4 = f32[384,768]{0,1:T(8,128)S(1)} fusion(bf16[4096,768]{1,0:T(8,128)(2,1)} %all-gather.4.cloned.1.call-done, bf16[384,4096]{1,0:T(8,128)(2,1)} %get-tuple-element.23, f32[4096]{0:T(1024)S(1)} %copy-done.2, f32[384]{0:T(512)S(1)} %add_rsqrt_fusion), kind=kOutput, calls=%fused_computation.8 | convolution fusion | flops 2422210560 | bytes 10634752 | tf_op jit(solution)/shard_map/dot_general | solution.py:181
  157.0 12.2 %all-to-all-done.2 = bf16[8,128,512]{1,2,0:T(8,128)(2,1)S(1)} async-done(((bf16[8,128,512]{1,2,0:T(8,128)(2,1)}), bf16[8,128,512]{1,2,0:T(8,128)(2,1)S(1)}, u32[]{:S(2)}, u32[]{:S(2)}) %all-to-all-start.2) | async-done | bytes 1048608 | tf_op jit(solution)/shard_map/all_to_all | solution.py:57
  169.7 5.4 %fusion.10 = f32[128,768]{0,1:T(8,128)S(1)} fusion(bf16[4096,768]{1,0:T(8,128)(2,1)} %all-gather.4.cloned.1.call-done, f32[128,4096]{1,0:T(8,128)S(1)} %get-tuple-element.25, f32[4096]{0:T(1024)S(1)} %copy-done.2, f32[128]{0:T(128)S(1)} %add_rsqrt_fusion.1), kind=kOutput, calls=%fused_computation.27 | convolution fusion | flops 806879232 | bytes 8798720 | tf_op jit(solution)/shard_map/dot_general | solution.py:194
  (75 shorter events, 19.3 us)
Async XLA Ops:
  6.5 44.2 %copy-start = (bf16[512,512]{1,0:T(8,128)(2,1)S(1)}, bf16[512,512]{1,0:T(8,128)(2,1)}, u32[]{:S(2)}) copy-start(bf16[512,512]{1,0:T(8,128)(2,1)} %param.11) | copy-start | bytes 1572868
  6.5 136.4 %all-gather.6.cloned.1.call-start = ((), (), s32[]{:S(2)}) async-start(), calls=%async_computation.4 | async-start | bytes 2359296 | tf_op jit(solution)/shard_map/all_gather | solution.py:175
  7.3 142.8 %all-gather.4.cloned.1.call-start = ((), (), s32[]{:S(2)}) async-start(), calls=%async_computation.3 | async-start | bytes 6389760 | tf_op jit(solution)/shard_map/all_gather | solution.py:176
  8.0 8.7 %collective-permute-start = (bf16[512,64]{0,1:T(8,128)(2,1)}, bf16[512,64]{0,1:T(8,128)(2,1)S(1)}, u32[]{:S(2)}, u32[]{:S(2)}) collective-permute-start(bf16[512,64]{0,1:T(8,128)(2,1)} %param.13), channel_id=1, source_target_pairs={{0,112},{16,0},{32,16},{48,32},{64,48},{80,64},{96,80},{112,96},{1... | collective-permute-start | bytes 196616 | tf_op jit(solution)/shard_map/ppermute | solution.py:63
  13.9 6.4 %collective-permute-start.1 = (bf16[512,64]{0,1:T(8,128)(2,1)}, bf16[512,64]{0,1:T(8,128)(2,1)S(1)}, u32[]{:S(2)}, u32[]{:S(2)}) collective-permute-start(bf16[512,64]{0,1:T(8,128)(2,1)} %param.13), channel_id=1, source_target_pairs={{0,16},{16,32},{32,48},{48,64},{64,80},{80,96},{96,112},{112,0},{1... | collective-permute-start | bytes 196616 | tf_op jit(solution)/shard_map/ppermute | solution.py:63
  21.2 13.8 %collective-permute-start.2 = (bf16[3,512,64]{1,2,0:T(8,128)(2,1)S(1)}, bf16[3,512,64]{1,2,0:T(8,128)(2,1)S(1)}, u32[]{:S(2)}, u32[]{:S(2)}) collective-permute-start(bf16[3,512,64]{1,2,0:T(8,128)(2,1)S(1)} %pad_maximum_fusion.4), channel_id=1, source_target_pairs={{0,80},{16,96},{32,112},{48,0},{64,16},{80,32},{96,48},{112,64},{1... | collective-permute-start | bytes 589832 | tf_op jit(solution)/shard_map/ppermute | solution.py:63
  24.6 15.3 %collective-permute-start.3 = (bf16[3,512,64]{1,2,0:T(8,128)(2,1)S(1)}, bf16[3,512,64]{1,2,0:T(8,128)(2,1)S(1)}, u32[]{:S(2)}, u32[]{:S(2)}) collective-permute-start(bf16[3,512,64]{1,2,0:T(8,128)(2,1)S(1)} %pad_maximum_fusion.4), channel_id=1, source_target_pairs={{0,48},{16,64},{32,80},{48,96},{64,112},{80,0},{96,16},{112,32},{1... | collective-permute-start | bytes 589832 | tf_op jit(solution)/shard_map/ppermute | solution.py:63
  39.9 21.3 %collective-permute-start.5 = (bf16[8,512,64]{1,2,0:T(8,128)(2,1)S(1)}, bf16[8,512,64]{1,2,0:T(8,128)(2,1)S(1)}, u32[]{:S(2)}, u32[]{:S(2)}) collective-permute-start(bf16[8,512,64]{1,2,0:T(8,128)(2,1)S(1)} %constant_dynamic-update-slice_fusion), channel_id=1, source_target_pairs={{0,256},{128,384},{256,0},{384,128},{1,257},{129,385},{257,1},{385... | collective-permute-start | bytes 1572872 | tf_op jit(solution)/shard_map/ppermute | solution.py:63
  44.2 21.6 %collective-permute-start.6 = (bf16[8,512,64]{1,2,0:T(8,128)(2,1)S(1)}, bf16[8,512,64]{1,2,0:T(8,128)(2,1)S(1)}, u32[]{:S(2)}, u32[]{:S(2)}) collective-permute-start(bf16[8,512,64]{1,2,0:T(8,128)(2,1)S(1)} %constant_dynamic-update-slice_fusion), channel_id=1, source_target_pairs={{0,128},{128,256},{256,384},{384,0},{1,129},{129,257},{257,385},{3... | collective-permute-start | bytes 1572872 | tf_op jit(solution)/shard_map/ppermute | solution.py:63
  46.4 19.3 %collective-permute-start.4 = (bf16[8,512,64]{1,2,0:T(8,128)(2,1)S(1)}, bf16[8,512,64]{1,2,0:T(8,128)(2,1)}, u32[]{:S(2)}, u32[]{:S(2)}) collective-permute-start(bf16[8,512,64]{1,2,0:T(8,128)(2,1)S(1)} %constant_dynamic-update-slice_fusion), channel_id=1, source_target_pairs={{0,384},{128,0},{256,128},{384,256},{1,385},{129,1},{257,129},{385... | collective-permute-start | bytes 1572872 | tf_op jit(solution)/shard_map/ppermute | solution.py:63
  51.7 9.5 %collective-permute-start.7 = (bf16[128,512]{1,0:T(8,128)(2,1)S(1)}, bf16[128,512]{1,0:T(8,128)(2,1)S(1)}, u32[]{:S(2)}, u32[]{:S(2)}) collective-permute-start(bf16[128,512]{1,0:T(8,128)(2,1)S(1)} %multiply_convert_fusion.2), channel_id=1, source_target_pairs={{0,8},{8,0},{1,9},{9,1},{2,10},{10,2},{3,11},{11,3},{4,12},{12,4},... | collective-permute-start | bytes 393224 | tf_op jit(solution)/shard_map/ppermute | solution.py:111
  67.5 6.8 %collective-permute-start.8 = (bf16[128,4,8,64]{0,3,2,1:T(8,128)(2,1)S(1)}, bf16[128,4,8,64]{0,3,2,1:T(8,128)(2,1)S(1)}, u32[]{:S(2)}, u32[]{:S(2)}) collective-permute-start(bf16[128,4,8,64]{0,3,2,1:T(8,128)(2,1)S(1)} %convolution_convert_fusion.3), channel_id=1, source_target_pairs={{0,8},{8,0},{1,9},{9,1},{2,10},{10,2},{3,11},{11,3},{4,12},{12,4},... | collective-permute-start | bytes 1572872 | tf_op jit(solution)/shard_map/ppermute | solution.py:119
  75.4 11.0 %copy-start.4 = (s32[128,2]{0,1:T(2,128)S(1)}, s32[128,2]{0,1:T(2,128)}, u32[]{:S(2)}) copy-start(s32[128,2]{0,1:T(2,128)} %param.18) | copy-start | bytes 3076
  75.4 11.0 %copy-start.5 = (s32[128]{0:T(128)S(1)}, s32[128]{0:T(128)}, u32[]{:S(2)}) copy-start(s32[128]{0:T(128)} %param.19) | copy-start | bytes 1540
  75.4 12.8 %copy-start.1 = (bf16[512,512]{1,0:T(8,128)(2,1)S(1)}, bf16[512,512]{1,0:T(8,128)(2,1)}, u32[]{:S(2)}) copy-start(bf16[512,512]{1,0:T(8,128)(2,1)} %param.12) | copy-start | bytes 1572868
  76.5 39.2 %all-to-all-start = ((bf16[8,128,512]{1,2,0:T(8,128)(2,1)}), bf16[8,128,512]{1,2,0:T(8,128)(2,1)S(1)}, u32[]{:S(2)}, u32[]{:S(2)}) async-start(bf16[8,128,512]{1,2,0:T(8,128)(2,1)} %bitcast.17), calls=%async_computation | async-start | bytes 2097152 | tf_op jit(solution)/shard_map/all_to_all | solution.py:132
  88.2 27.8 %copy-start.3 = (f32[512]{0:T(512)S(1)}, f32[512]{0:T(512)}, u32[]{:S(2)}) copy-start(f32[512]{0:T(512)} %param.14) | copy-start | bytes 6148
  116.9 20.3 %all-to-all-start.1 = ((bf16[64,2,512]{2,1,0:T(2,128)(2,1)}), bf16[64,2,512]{2,1,0:T(2,128)(2,1)S(1)}, u32[]{:S(2)}, u32[]{:S(2)}) async-start(bf16[64,2,512]{2,1,0:T(2,128)(2,1)} %reshape.222), calls=%async_computation.1 | async-start | bytes 262144 | tf_op jit(solution)/shard_map/all_to_all | solution.py:150
  138.5 30.6 %all-to-all-start.2 = ((bf16[8,128,512]{1,2,0:T(8,128)(2,1)}), bf16[8,128,512]{1,2,0:T(8,128)(2,1)S(1)}, u32[]{:S(2)}, u32[]{:S(2)}) async-start(bf16[8,128,512]{1,2,0:T(8,128)(2,1)} %broadcast_in_dim.28), calls=%async_computation.2 | async-start | bytes 2097152 | tf_op jit(solution)/shard_map/all_to_all | solution.py:57
  142.9 7.1 %copy-start.2 = (f32[4096]{0:T(1024)S(1)}, f32[4096]{0:T(1024)}, u32[]{:S(2)}) copy-start(f32[4096]{0:T(1024)} %param.20) | copy-start | bytes 49156
Sparse Core Ops, SparseCore 0:
  9.4 46.0 all-gather.5
  58.9 91.1 all-gather.3

commit v16 on v10

--- a/solution.py
+++ b/solution.py
@@ -107,21 +107,23 @@
     merged_residual = jnp.mean(
         vision_residual.astype(jnp.float32).reshape(-1, 4, feature_width), axis=1
     )
-    own_half = gather_plane(out_weight)
-    other_half = lax.ppermute(own_half, "rc", [(0, 1), (1, 0)])
+    swap = [(0, 1), (1, 0)]
     core = lax.axis_index("rc")
-    own_part = jnp.einsum(
-        "gk,xykn->gxyn", merged_context, own_half, preferred_element_type=jnp.float32
-    )
-    other_part = jnp.einsum(
-        "gk,xykn->gxyn", merged_context, other_half, preferred_element_type=jnp.float32
-    )
-    partial_value = jnp.stack(
-        [jnp.where(core == 0, own_part, other_part), jnp.where(core == 0, other_part, own_part)],
-        axis=3,
-    ).astype(jnp.bfloat16)
+    context_pair = jnp.stack([merged_context, lax.ppermute(merged_context, "rc", swap)])
+    context_ring = ring_gather(context_pair, "rx")
+    weight_ring = eight_gather(out_weight, "ry") if lax.axis_size("ry") == 8 else ring_gather(out_weight, "ry")
+    parts = jnp.einsum(
+        "dcgk,ykn->dcgyn", context_ring, weight_ring, preferred_element_type=jnp.float32
+    ).astype(jnp.bfloat16)
+    from_partner = lax.ppermute(parts[:, 1], "rc", swap)
+    both = jnp.stack([parts[:, 0], from_partner], axis=-2)
+    x_count = lax.axis_size("rx")
+    landed = [both[0]] + [shift(both[(x_count - d) % x_count], "rx", (x_count - d) % x_count) for d in range(1, x_count)]
+    partial_value = jnp.moveaxis(jnp.stack(landed, axis=0), 0, 1)
+    partial_value = jnp.where(core == 0, partial_value, partial_value[..., ::-1, :])
     partial_value = jnp.roll(partial_value, lax.axis_index("rx"), axis=1)
     partial_value = jnp.roll(partial_value, lax.axis_index("ry"), axis=2)
+    own_part = merged_context
     partial_value = partial_value.reshape(own_part.shape[0], -1)
     tp_count = lax.axis_size("tp")
     block_terms = partial_value.astype(jnp.bfloat16).reshape(

time: 187 us -> 182 us (0.973)
  waiting for transfers between devices: 81.1 us -> 74.9 us
  starting transfers between devices: 54 us -> 58.1 us
  matrix products: 21.5 us -> 19.2 us
    ppermute x7 -> x10, waiting for transfers between devices: 30.2 us -> 24.2 us  [shift(): lax.ppermute(value, axis, [(k, (k + step) % size) for k in range(size)])]
    all_gather x1, waiting for transfers between devices: 0.01 us -> 4.49 us  [shards(): full_weight = lax.all_gather(qkv_weight, REQ, axis=0, tiled=True)]
    all_to_all x1, waiting for transfers between devices: 14.9 us -> 10.5 us  [gather_features(): blocks = lax.all_to_all(copies, 'tp', 0, 0, tiled=True)]
    ppermute x1 -> x2, starting transfers between devices: 5.01 us -> 9.08 us  [the longest x1 6.78 us: shards(): lax.ppermute(merged_context, 'rc', swap)]
    ppermute x7 -> x10, starting transfers between devices: 25.7 us -> 29.3 us  [shift(): lax.ppermute(value, axis, [(k, (k + step) % size) for k in range(size)])]
    all_to_all x1, starting transfers between devices: 9.71 us -> 7.3 us  [shards(): lax.all_to_all(outgoing.reshape(requests, capacity, feature_width), REQ,...]
    dot_general x2 -> x1, matrix products: 3.04 us -> 0.74 us  [shards(): jnp.einsum('dcgk,ykn->dcgyn', context_ring, weight_ring, preferred_elemen...]
  transfers between devices with their start and end apart: 13 -> 17, of which waited for: 9 -> 10; matrix products, arithmetic and copies ran while one was open for 15% -> 14% of each run, Pallas kernels for 0% -> 0%
where the time goes in v16:
time: 182 us; the launch traced here: 181 us
  waiting for transfers between devices  74.9 us (41%)
  starting transfers between devices  58.1 us (32%)
  matrix products  19.2 us (11%)
  between operations  16 us (9%)
  other arithmetic  7.43 us (4%)
  local copies, waits for them, and re-layouts  5.56 us (3%)
    ppermute x10, starting transfers between devices, shift(): lax.ppermute(value, axis, [(k, (k + step) % size) for k in range(size)])  29.3 us
    ppermute x10, waiting for transfers between devices, shift(): lax.ppermute(value, axis, [(k, (k + step) % size) for k in range(size)])  24.2 us
    all_to_all x1, waiting for transfers between devices, shards(): lax.all_to_all(block_terms, 'tp', 0, 0, tiled=True).astype(jnp.float32)  23 us
    all_to_all x1, waiting for transfers between devices, gather_features(): blocks = lax.all_to_all(copies, 'tp', 0, 0, tiled=True)  10.5 us
    all_to_all x1, waiting for transfers between devices, shards(): lax.all_to_all(outgoing.reshape(requests, capacity, feature_width), REQ,...  9.79 us
    all_to_all x1, starting transfers between devices, shards(): lax.all_to_all(block_terms, 'tp', 0, 0, tiled=True).astype(jnp.float32)  8.64 us
    all_to_all x1, starting transfers between devices, shards(): lax.all_to_all(outgoing.reshape(requests, capacity, feature_width), REQ,...  7.3 us
    ppermute x1, starting transfers between devices, shards(): lax.ppermute(merged_context, 'rc', swap)  6.78 us
  transfers between devices with their start and end apart: 17, of which 10 were waited for; matrix products, arithmetic and copies ran while one was open for 14% of the time, Pallas kernels for 0%

profile of v16, /device:TPU:1, one launch (start us, length us, event | category | flops | bytes accessed | tf_op | source)
XLA Modules:
  0.0 181.3 jit_solution(1262390514091334798)
XLA Ops:
  8.0 5.9 %collective-permute-start.4 = (bf16[512,64]{0,1:T(8,128)(2,1)}, bf16[512,64]{0,1:T(8,128)(2,1)S(1)}, u32[]{:S(2)}, u32[]{:S(2)}) collective-permute-start(bf16[512,64]{0,1:T(8,128)(2,1)} %param.13), channel_id=1, source_target_pairs={{0,112},{16,0},{32,16},{48,32},{64,48},{80,64},{96,80},{112,96},{1... | collective-permute-start | bytes 196616 | tf_op jit(solution)/shard_map/ppermute | solution.py:63
  17.9 6.8 %collective-permute-start = (bf16[128,512]{1,0:T(8,128)(2,1)S(1)}, bf16[128,512]{1,0:T(8,128)(2,1)S(1)}, u32[]{:S(2)}, u32[]{:S(2)}) collective-permute-start(bf16[128,512]{1,0:T(8,128)(2,1)S(1)} %multiply_convert_fusion.2), channel_id=1, source_target_pairs={{0,8},{8,0},{1,9},{9,1},{2,10},{10,2},{3,11},{11,3},{4,12},{12,4},... | collective-permute-start | bytes 393224 | tf_op jit(solution)/shard_map/ppermute | solution.py:112
  24.8 1.9 %collective-permute-start.6 = (bf16[3,512,64]{1,2,0:T(8,128)(2,1)S(1)}, bf16[3,512,64]{1,2,0:T(8,128)(2,1)S(1)}, u32[]{:S(2)}, u32[]{:S(2)}) collective-permute-start(bf16[3,512,64]{1,2,0:T(8,128)(2,1)S(1)} %pad_maximum_fusion.3), channel_id=1, source_target_pairs={{0,80},{16,96},{32,112},{48,0},{64,16},{80,32},{96,48},{112,64},{1... | collective-permute-start | bytes 589832 | tf_op jit(solution)/shard_map/ppermute | solution.py:63
  26.7 5.2 %collective-permute-start.7 = (bf16[3,512,64]{1,2,0:T(8,128)(2,1)S(1)}, bf16[3,512,64]{1,2,0:T(8,128)(2,1)S(1)}, u32[]{:S(2)}, u32[]{:S(2)}) collective-permute-start(bf16[3,512,64]{1,2,0:T(8,128)(2,1)S(1)} %pad_maximum_fusion.3), channel_id=1, source_target_pairs={{0,48},{16,64},{32,80},{48,96},{64,112},{80,0},{96,16},{112,32},{1... | collective-permute-start | bytes 589832 | tf_op jit(solution)/shard_map/ppermute | solution.py:63
  32.0 1.9 %collective-permute-start.1 = (bf16[2,128,512]{2,1,0:T(8,128)(2,1)S(1)}, bf16[2,128,512]{2,1,0:T(8,128)(2,1)S(1)}, u32[]{:S(2)}, u32[]{:S(2)}) collective-permute-start(bf16[2,128,512]{2,1,0:T(8,128)(2,1)S(1)} %get-tuple-element.24), channel_id=1, source_target_pairs={{0,384},{128,0},{256,128},{384,256},{1,385},{129,1},{257,129},{385... | collective-permute-start | bytes 786440 | tf_op jit(solution)/shard_map/ppermute | solution.py:63
  35.8 3.4 %collective-permute-start.3 = (bf16[2,128,512]{2,1,0:T(8,128)(2,1)S(1)}, bf16[2,128,512]{2,1,0:T(8,128)(2,1)S(1)}, u32[]{:S(2)}, u32[]{:S(2)}) collective-permute-start(bf16[2,128,512]{2,1,0:T(8,128)(2,1)S(1)} %get-tuple-element.24), channel_id=1, source_target_pairs={{0,128},{128,256},{256,384},{384,0},{1,129},{129,257},{257,385},{3... | collective-permute-start | bytes 786440 | tf_op jit(solution)/shard_map/ppermute | solution.py:63
  39.2 7.2 %collective-permute-done.7 = bf16[3,512,64]{1,2,0:T(8,128)(2,1)S(1)} collective-permute-done((bf16[3,512,64]{1,2,0:T(8,128)(2,1)S(1)}, bf16[3,512,64]{1,2,0:T(8,128)(2,1)S(1)}, u32[]{:S(2)}, u32[]{:S(2)}) %collective-permute-start.7) | collective-permute-done | bytes 196640 | tf_op jit(solution)/shard_map/ppermute | solution.py:63
  46.5 4.8 %collective-permute-done.3 = bf16[2,128,512]{2,1,0:T(8,128)(2,1)S(1)} collective-permute-done((bf16[2,128,512]{2,1,0:T(8,128)(2,1)S(1)}, bf16[2,128,512]{2,1,0:T(8,128)(2,1)S(1)}, u32[]{:S(2)}, u32[]{:S(2)}) %collective-permute-start.3) | collective-permute-done | bytes 262176 | tf_op jit(solution)/shard_map/ppermute | solution.py:63
  52.1 2.3 %collective-permute-start.8 = (bf16[4,128,8,64]{1,3,2,0:T(8,128)(2,1)S(1)}, bf16[4,128,8,64]{1,3,2,0:T(8,128)(2,1)S(1)}, u32[]{:S(2)}, u32[]{:S(2)}) collective-permute-start(bf16[4,128,8,64]{1,3,2,0:T(8,128)(2,1)S(1)} %get-tuple-element.20), channel_id=1, source_target_pairs={{0,8},{8,0},{1,9},{9,1},{2,10},{10,2},{3,11},{11,3},{4,12},{12,4},... | collective-permute-start | bytes 1572872 | tf_op jit(solution)/shard_map/ppermute | solution.py:118
  56.0 2.2 %collective-permute-start.9 = (bf16[128,8,2,64]{0,3,1,2:T(8,128)(2,1)S(1)}, bf16[128,8,2,64]{0,3,1,2:T(8,128)(2,1)S(1)}, u32[]{:S(2)}, u32[]{:S(2)}) collective-permute-start(bf16[128,8,2,64]{0,3,1,2:T(8,128)(2,1)S(1)} %get-tuple-element.16), channel_id=1, source_target_pairs={{0,384},{128,0},{256,128},{384,256},{1,385},{129,1},{257,129},{385... | collective-permute-start | bytes 786440 | tf_op jit(solution)/shard_map/ppermute | solution.py:63
  60.1 3.1 %collective-permute-start.11 = (bf16[128,8,2,64]{0,3,1,2:T(8,128)(2,1)S(1)}, bf16[128,8,2,64]{0,3,1,2:T(8,128)(2,1)S(1)}, u32[]{:S(2)}, u32[]{:S(2)}) collective-permute-start(bf16[128,8,2,64]{0,3,1,2:T(8,128)(2,1)S(1)} %get-tuple-element.17), channel_id=1, source_target_pairs={{0,128},{128,256},{256,384},{384,0},{1,129},{129,257},{257,385},{3... | collective-permute-start | bytes 786440 | tf_op jit(solution)/shard_map/ppermute | solution.py:63
  63.2 2.2 %collective-permute-done.9 = bf16[128,8,2,64]{0,3,1,2:T(8,128)(2,1)S(1)} collective-permute-done((bf16[128,8,2,64]{0,3,1,2:T(8,128)(2,1)S(1)}, bf16[128,8,2,64]{0,3,1,2:T(8,128)(2,1)S(1)}, u32[]{:S(2)}, u32[]{:S(2)}) %collective-permute-start.9) | collective-permute-done | bytes 262176 | tf_op jit(solution)/shard_map/ppermute | solution.py:63
  65.4 3.4 %collective-permute-done.10 = bf16[128,8,2,64]{0,3,1,2:T(8,128)(2,1)S(1)} collective-permute-done((bf16[128,8,2,64]{0,3,1,2:T(8,128)(2,1)S(1)}, bf16[128,8,2,64]{0,3,1,2:T(8,128)(2,1)S(1)}, u32[]{:S(2)}, u32[]{:S(2)}) %collective-permute-start.10) | collective-permute-done | bytes 262176 | tf_op jit(solution)/shard_map/ppermute | solution.py:63
  68.8 6.6 %collective-permute-done.11 = bf16[128,8,2,64]{0,3,1,2:T(8,128)(2,1)S(1)} collective-permute-done((bf16[128,8,2,64]{0,3,1,2:T(8,128)(2,1)S(1)}, bf16[128,8,2,64]{0,3,1,2:T(8,128)(2,1)S(1)}, u32[]{:S(2)}, u32[]{:S(2)}) %collective-permute-start.11) | collective-permute-done | bytes 262176 | tf_op jit(solution)/shard_map/ppermute | solution.py:63
  77.8 8.6 %all-to-all-start = ((bf16[8,128,512]{1,2,0:T(8,128)(2,1)}), bf16[8,128,512]{1,2,0:T(8,128)(2,1)S(1)}, u32[]{:S(2)}, u32[]{:S(2)}) async-start(bf16[8,128,512]{1,2,0:T(8,128)(2,1)} %bitcast.27), calls=%async_computation | async-start | bytes 2097152 | tf_op jit(solution)/shard_map/all_to_all | solution.py:133
  92.6 23.0 %all-to-all-done = bf16[8,128,512]{1,2,0:T(8,128)(2,1)S(1)} async-done(((bf16[8,128,512]{1,2,0:T(8,128)(2,1)}), bf16[8,128,512]{1,2,0:T(8,128)(2,1)S(1)}, u32[]{:S(2)}, u32[]{:S(2)}) %all-to-all-start) | async-done | bytes 1048608 | tf_op jit(solution)/shard_map/all_to_all | solution.py:133
  116.9 7.3 %all-to-all-start.1 = ((bf16[64,2,512]{2,1,0:T(2,128)(2,1)}), bf16[64,2,512]{2,1,0:T(2,128)(2,1)S(1)}, u32[]{:S(2)}, u32[]{:S(2)}) async-start(bf16[64,2,512]{2,1,0:T(2,128)(2,1)} %reshape.235), calls=%async_computation.1 | async-start | bytes 262144 | tf_op jit(solution)/shard_map/all_to_all | solution.py:151
  125.0 9.8 %all-to-all-done.1 = bf16[64,2,512]{2,1,0:T(2,128)(2,1)S(1)} async-done(((bf16[64,2,512]{2,1,0:T(2,128)(2,1)}), bf16[64,2,512]{2,1,0:T(2,128)(2,1)S(1)}, u32[]{:S(2)}, u32[]{:S(2)}) %all-to-all-start.1) | async-done | bytes 131104 | tf_op jit(solution)/shard_map/all_to_all | solution.py:151
  136.1 3.7 %all-to-all-start.2 = ((bf16[8,128,512]{1,2,0:T(8,128)(2,1)}), bf16[8,128,512]{1,2,0:T(8,128)(2,1)S(1)}, u32[]{:S(2)}, u32[]{:S(2)}) async-start(bf16[8,128,512]{1,2,0:T(8,128)(2,1)} %broadcast_in_dim.28), calls=%async_computation.2 | async-start | bytes 2097152 | tf_op jit(solution)/shard_map/all_to_all | solution.py:57
  140.5 4.4 %fusion = (f32[384]{0:T(512)S(1)}, bf16[384,4096]{1,0:T(8,128)(2,1)}) fusion(bf16[1,256,4096]{2,1,0:T(8,128)(2,1)} %all-gather.6.cloned.1.call-done, s32[384]{0:T(512)S(1)} %subtract_select_fusion, pred[384]{0:T(512)(128)(4,1)S(1)} %get-tuple-element.11), kind=kOutput, calls=%fused_computation.2 | convolution fusion | flops 811794048 | bytes 5246336 | tf_op jit(solution)/shard_map/dot_general | solution.py:179
  144.9 4.5 %all-gather.4.cloned.1.call-done = bf16[4096,768]{1,0:T(8,128)(2,1)} async-done(((bf16[64,768]{1,0:T(8,128)(2,1)}), bf16[4096,768]{1,0:T(8,128)(2,1)}) %all-gather.4.cloned.1.call-update) | async-done | bytes 6291472 | tf_op jit(solution)/shard_map/all_gather | solution.py:177
  149.4 6.7 %fusion.4 = f32[384,768]{0,1:T(8,128)S(1)} fusion(bf16[4096,768]{1,0:T(8,128)(2,1)} %all-gather.4.cloned.1.call-done, bf16[384,4096]{1,0:T(8,128)(2,1)} %get-tuple-element.29, f32[4096]{0:T(1024)S(1)} %copy-done.2, f32[384]{0:T(512)S(1)} %add_rsqrt_fusion), kind=kOutput, calls=%fused_computation.8 | convolution fusion | flops 2422210560 | bytes 10634752 | tf_op jit(solution)/shard_map/dot_general | solution.py:182
  156.3 10.5 %all-to-all-done.2 = bf16[8,128,512]{1,2,0:T(8,128)(2,1)S(1)} async-done(((bf16[8,128,512]{1,2,0:T(8,128)(2,1)}), bf16[8,128,512]{1,2,0:T(8,128)(2,1)S(1)}, u32[]{:S(2)}, u32[]{:S(2)}) %all-to-all-start.2) | async-done | bytes 1048608 | tf_op jit(solution)/shard_map/all_to_all | solution.py:57
  167.4 5.4 %fusion.10 = f32[128,768]{0,1:T(8,128)S(1)} fusion(bf16[4096,768]{1,0:T(8,128)(2,1)} %all-gather.4.cloned.1.call-done, f32[128,4096]{1,0:T(8,128)S(1)} %get-tuple-element.31, f32[4096]{0:T(1024)S(1)} %copy-done.2, f32[128]{0:T(128)S(1)} %add_rsqrt_fusion.1), kind=kOutput, calls=%fused_computation.30 | convolution fusion | flops 806879232 | bytes 8798720 | tf_op jit(solution)/shard_map/dot_general | solution.py:195
  (85 shorter events, 24.5 us)
Async XLA Ops:
  6.5 18.2 %copy-start.1 = (bf16[512,64]{0,1:T(8,128)(2,1)S(1)}, bf16[512,64]{0,1:T(8,128)(2,1)}, u32[]{:S(2)}) copy-start(bf16[512,64]{0,1:T(8,128)(2,1)} %param.13) | copy-start | bytes 196612
  6.5 134.0 %all-gather.6.cloned.1.call-start = ((), (), s32[]{:S(2)}) async-start(), calls=%async_computation.4 | async-start | bytes 2359296 | tf_op jit(solution)/shard_map/all_gather | solution.py:176
  7.3 142.1 %all-gather.4.cloned.1.call-start = ((), (), s32[]{:S(2)}) async-start(), calls=%async_computation.3 | async-start | bytes 6389760 | tf_op jit(solution)/shard_map/all_gather | solution.py:177
  8.0 16.7 %collective-permute-start.4 = (bf16[512,64]{0,1:T(8,128)(2,1)}, bf16[512,64]{0,1:T(8,128)(2,1)S(1)}, u32[]{:S(2)}, u32[]{:S(2)}) collective-permute-start(bf16[512,64]{0,1:T(8,128)(2,1)} %param.13), channel_id=1, source_target_pairs={{0,112},{16,0},{32,16},{48,32},{64,48},{80,64},{96,80},{112,96},{1... | collective-permute-start | bytes 196616 | tf_op jit(solution)/shard_map/ppermute | solution.py:63
  13.9 10.8 %collective-permute-start.5 = (bf16[512,64]{0,1:T(8,128)(2,1)}, bf16[512,64]{0,1:T(8,128)(2,1)S(1)}, u32[]{:S(2)}, u32[]{:S(2)}) collective-permute-start(bf16[512,64]{0,1:T(8,128)(2,1)} %param.13), channel_id=1, source_target_pairs={{0,16},{16,32},{32,48},{48,64},{64,80},{80,96},{96,112},{112,0},{1... | collective-permute-start | bytes 196616 | tf_op jit(solution)/shard_map/ppermute | solution.py:63
  17.9 14.0 %collective-permute-start = (bf16[128,512]{1,0:T(8,128)(2,1)S(1)}, bf16[128,512]{1,0:T(8,128)(2,1)S(1)}, u32[]{:S(2)}, u32[]{:S(2)}) collective-permute-start(bf16[128,512]{1,0:T(8,128)(2,1)S(1)} %multiply_convert_fusion.2), channel_id=1, source_target_pairs={{0,8},{8,0},{1,9},{9,1},{2,10},{10,2},{3,11},{11,3},{4,12},{12,4},... | collective-permute-start | bytes 393224 | tf_op jit(solution)/shard_map/ppermute | solution.py:112
  24.8 14.4 %collective-permute-start.6 = (bf16[3,512,64]{1,2,0:T(8,128)(2,1)S(1)}, bf16[3,512,64]{1,2,0:T(8,128)(2,1)S(1)}, u32[]{:S(2)}, u32[]{:S(2)}) collective-permute-start(bf16[3,512,64]{1,2,0:T(8,128)(2,1)S(1)} %pad_maximum_fusion.3), channel_id=1, source_target_pairs={{0,80},{16,96},{32,112},{48,0},{64,16},{80,32},{96,48},{112,64},{1... | collective-permute-start | bytes 589832 | tf_op jit(solution)/shard_map/ppermute | solution.py:63
  26.7 19.7 %collective-permute-start.7 = (bf16[3,512,64]{1,2,0:T(8,128)(2,1)S(1)}, bf16[3,512,64]{1,2,0:T(8,128)(2,1)S(1)}, u32[]{:S(2)}, u32[]{:S(2)}) collective-permute-start(bf16[3,512,64]{1,2,0:T(8,128)(2,1)S(1)} %pad_maximum_fusion.3), channel_id=1, source_target_pairs={{0,48},{16,64},{32,80},{48,96},{64,112},{80,0},{96,16},{112,32},{1... | collective-permute-start | bytes 589832 | tf_op jit(solution)/shard_map/ppermute | solution.py:63
  32.0 14.5 %collective-permute-start.1 = (bf16[2,128,512]{2,1,0:T(8,128)(2,1)S(1)}, bf16[2,128,512]{2,1,0:T(8,128)(2,1)S(1)}, u32[]{:S(2)}, u32[]{:S(2)}) collective-permute-start(bf16[2,128,512]{2,1,0:T(8,128)(2,1)S(1)} %get-tuple-element.24), channel_id=1, source_target_pairs={{0,384},{128,0},{256,128},{384,256},{1,385},{129,1},{257,129},{385... | collective-permute-start | bytes 786440 | tf_op jit(solution)/shard_map/ppermute | solution.py:63
  33.9 12.6 %collective-permute-start.2 = (bf16[2,128,512]{2,1,0:T(8,128)(2,1)S(1)}, bf16[2,128,512]{2,1,0:T(8,128)(2,1)S(1)}, u32[]{:S(2)}, u32[]{:S(2)}) collective-permute-start(bf16[2,128,512]{2,1,0:T(8,128)(2,1)S(1)} %get-tuple-element.24), channel_id=1, source_target_pairs={{0,256},{128,384},{256,0},{384,128},{1,257},{129,385},{257,1},{385... | collective-permute-start | bytes 786440 | tf_op jit(solution)/shard_map/ppermute | solution.py:63
  35.8 15.4 %collective-permute-start.3 = (bf16[2,128,512]{2,1,0:T(8,128)(2,1)S(1)}, bf16[2,128,512]{2,1,0:T(8,128)(2,1)S(1)}, u32[]{:S(2)}, u32[]{:S(2)}) collective-permute-start(bf16[2,128,512]{2,1,0:T(8,128)(2,1)S(1)} %get-tuple-element.24), channel_id=1, source_target_pairs={{0,128},{128,256},{256,384},{384,0},{1,129},{129,257},{257,385},{3... | collective-permute-start | bytes 786440 | tf_op jit(solution)/shard_map/ppermute | solution.py:63
  52.1 3.8 %collective-permute-start.8 = (bf16[4,128,8,64]{1,3,2,0:T(8,128)(2,1)S(1)}, bf16[4,128,8,64]{1,3,2,0:T(8,128)(2,1)S(1)}, u32[]{:S(2)}, u32[]{:S(2)}) collective-permute-start(bf16[4,128,8,64]{1,3,2,0:T(8,128)(2,1)S(1)} %get-tuple-element.20), channel_id=1, source_target_pairs={{0,8},{8,0},{1,9},{9,1},{2,10},{10,2},{3,11},{11,3},{4,12},{12,4},... | collective-permute-start | bytes 1572872 | tf_op jit(solution)/shard_map/ppermute | solution.py:118
  56.0 9.4 %collective-permute-start.9 = (bf16[128,8,2,64]{0,3,1,2:T(8,128)(2,1)S(1)}, bf16[128,8,2,64]{0,3,1,2:T(8,128)(2,1)S(1)}, u32[]{:S(2)}, u32[]{:S(2)}) collective-permute-start(bf16[128,8,2,64]{0,3,1,2:T(8,128)(2,1)S(1)} %get-tuple-element.16), channel_id=1, source_target_pairs={{0,384},{128,0},{256,128},{384,256},{1,385},{129,1},{257,129},{385... | collective-permute-start | bytes 786440 | tf_op jit(solution)/shard_map/ppermute | solution.py:63
  58.2 10.6 %collective-permute-start.10 = (bf16[128,8,2,64]{0,3,1,2:T(8,128)(2,1)S(1)}, bf16[128,8,2,64]{0,3,1,2:T(8,128)(2,1)S(1)}, u32[]{:S(2)}, u32[]{:S(2)}) collective-permute-start(bf16[128,8,2,64]{0,3,1,2:T(8,128)(2,1)S(1)} %get-tuple-element.18), channel_id=1, source_target_pairs={{0,256},{128,384},{256,0},{384,128},{1,257},{129,385},{257,1},{385... | collective-permute-start | bytes 786440 | tf_op jit(solution)/shard_map/ppermute | solution.py:63
  60.1 15.3 %collective-permute-start.11 = (bf16[128,8,2,64]{0,3,1,2:T(8,128)(2,1)S(1)}, bf16[128,8,2,64]{0,3,1,2:T(8,128)(2,1)S(1)}, u32[]{:S(2)}, u32[]{:S(2)}) collective-permute-start(bf16[128,8,2,64]{0,3,1,2:T(8,128)(2,1)S(1)} %get-tuple-element.17), channel_id=1, source_target_pairs={{0,128},{128,256},{256,384},{384,0},{1,129},{129,257},{257,385},{3... | collective-permute-start | bytes 786440 | tf_op jit(solution)/shard_map/ppermute | solution.py:63
  76.7 9.8 %copy-start.4 = (s32[128,2]{0,1:T(2,128)S(1)}, s32[128,2]{0,1:T(2,128)}, u32[]{:S(2)}) copy-start(s32[128,2]{0,1:T(2,128)} %param.18) | copy-start | bytes 3076
  76.7 9.8 %copy-start.5 = (s32[128]{0:T(128)S(1)}, s32[128]{0:T(128)}, u32[]{:S(2)}) copy-start(s32[128]{0:T(128)} %param.19) | copy-start | bytes 1540
  76.7 11.5 %copy-start = (bf16[512,512]{1,0:T(8,128)(2,1)S(1)}, bf16[512,512]{1,0:T(8,128)(2,1)}, u32[]{:S(2)}) copy-start(bf16[512,512]{1,0:T(8,128)(2,1)} %param.12) | copy-start | bytes 1572868
  77.8 37.9 %all-to-all-start = ((bf16[8,128,512]{1,2,0:T(8,128)(2,1)}), bf16[8,128,512]{1,2,0:T(8,128)(2,1)S(1)}, u32[]{:S(2)}, u32[]{:S(2)}) async-start(bf16[8,128,512]{1,2,0:T(8,128)(2,1)} %bitcast.27), calls=%async_computation | async-start | bytes 2097152 | tf_op jit(solution)/shard_map/all_to_all | solution.py:133
  88.2 27.8 %copy-start.3 = (f32[512]{0:T(512)S(1)}, f32[512]{0:T(512)}, u32[]{:S(2)}) copy-start(f32[512]{0:T(512)} %param.14) | copy-start | bytes 6148
  116.9 17.9 %all-to-all-start.1 = ((bf16[64,2,512]{2,1,0:T(2,128)(2,1)}), bf16[64,2,512]{2,1,0:T(2,128)(2,1)S(1)}, u32[]{:S(2)}, u32[]{:S(2)}) async-start(bf16[64,2,512]{2,1,0:T(2,128)(2,1)} %reshape.235), calls=%async_computation.1 | async-start | bytes 262144 | tf_op jit(solution)/shard_map/all_to_all | solution.py:151
  136.1 30.8 %all-to-all-start.2 = ((bf16[8,128,512]{1,2,0:T(8,128)(2,1)}), bf16[8,128,512]{1,2,0:T(8,128)(2,1)S(1)}, u32[]{:S(2)}, u32[]{:S(2)}) async-start(bf16[8,128,512]{1,2,0:T(8,128)(2,1)} %broadcast_in_dim.28), calls=%async_computation.2 | async-start | bytes 2097152 | tf_op jit(solution)/shard_map/all_to_all | solution.py:57
  140.5 8.9 %copy-start.2 = (f32[4096]{0:T(1024)S(1)}, f32[4096]{0:T(1024)}, u32[]{:S(2)}) copy-start(f32[4096]{0:T(1024)} %param.20) | copy-start | bytes 49156
Sparse Core Ops, SparseCore 0:
  9.4 46.0 all-gather.5
  58.9 90.4 all-gather.3
